TPU v7x, 32 devices: a whole 2x2x4 slice. The times are simulated.
32 devices in a mesh: leaf: 16 (over z, y, x), rows: 2 (over core).
Axes of the slice: x: 2, y: 2, z: 4, core: 2. Of those that a mesh axis runs over, the one named last changes fastest.
Arguments:
- leaf_factor: float32 [16384, 1024], P(('leaf', 'rows')), may hold values from -2 to 2, as said below
- leaf_rhs: float32 [16384, 256], P(('leaf', 'rows')), may hold values from -6 to 6
- update_panel: float32 [16384, 1024], P('leaf', 'rows'), may hold values from -0.1875 to 0.1875
- update_blocks: int32 [16, 8], P('leaf'), may hold values from 0 to 7, each once within a row
- parent_factor: float32 [16384, 1024], P(('leaf', 'rows')), may hold values from -2 to 2, as said below
- parent_rhs: float32 [16384, 128], P(('leaf', 'rows')), may hold values from -6 to 6
Outputs:
- leaf_solution: float32 [16384, 256], P(('leaf', 'rows'))
- parent_solution: float32 [16384, 128], P(('leaf', 'rows'))
Inputs may be any that keep to these rules, and one draw needn't show every extreme that they name: `parent_factor`: tiles on the block diagonal are near the identity. Groups 2 q and 2 q + 1 hold equal copies of one parent factor: rows 2 q * 1024 onward equal rows (2 q + 1) * 1024 onward. `leaf_factor`: tiles on the block diagonal are near the identity.
All inputs are finite; a program needn't handle non-finite values.
Results may differ from a plain program's by a relative error of at most 0.0003.
Values sent between devices are 32-bit elements; how exact they have to be, the bound alone decides.
No kernel may reach another device: no remote copies, remote signals or barrier semaphores. Data moves between devices by JAX's collectives and lax.ppermute only.
A program may use at most 64 MiB of HBM per device.

v0:
```python
import jax
import jax.numpy as jnp
from jax import lax
from jax.sharding import PartitionSpec as P

ROW_BLOCK = 128


def passed_along(array, axis, by):
    size = lax.axis_size(axis)
    pairs = [(i, i + by) for i in range(size) if 0 <= i + by < size]
    return lax.ppermute(array, axis, pairs)


def swapped(block, axis, apart):
    count = lax.axis_size(axis)
    route = []
    for low in range(count):
        high = low | 1 << apart
        if high != low and high < count:
            route += [(low, high), (high, low)]
    return lax.ppermute(block, axis, route)


def matmul(left, right):
    return jnp.dot(left, right, precision=lax.Precision.HIGHEST, preferred_element_type=jnp.float32)


def leaf_pass(outgoing):
    return passed_along(outgoing, "rows", 1)


def parent_pass(outgoing):
    return passed_along(outgoing, "rows", 1)


def front_forward(factor, right_side, section, sections, pass_tile):
    tile_rows = right_side.shape[0]

    def advance(tick, state):
        pending, solution, incoming = state
        source = tick - section
        useful = jnp.logical_and(source >= 0, source < section)
        safe_source = jnp.clip(source, 0, sections - 1)

        def apply_tile(values):
            factor_tile = lax.dynamic_slice_in_dim(factor, safe_source * tile_rows, tile_rows, 1)
            return values - matmul(factor_tile, incoming)

        pending = lax.cond(useful, apply_tile, lambda values: values, pending)
        own_turn = tick == 2 * section

        def solve_own(values):
            diagonal_tile = lax.dynamic_slice_in_dim(factor, section * tile_rows, tile_rows, 1)
            return matmul(diagonal_tile, values)

        solution = lax.cond(own_turn, solve_own, lambda values: solution, pending)
        outgoing = jnp.where(
            own_turn, solution, jnp.where(useful, incoming, jnp.zeros_like(incoming))
        )
        incoming = pass_tile(outgoing)
        return (pending, solution, incoming)

    initial = (right_side, jnp.zeros_like(right_side), jnp.zeros_like(right_side))
    return lax.fori_loop(0, 2 * sections - 1, advance, initial)[1]


def split_halves(values, sibling, column_half):
    lower_half = values[:, :column_half]
    upper_half = values[:, column_half:]
    kept_half = jnp.where(sibling == 0, lower_half, upper_half)
    sent_half = jnp.where(sibling == 0, upper_half, lower_half)
    return (kept_half, sent_half)


def shards(leaf_factor, leaf_rhs, update_panel, update_blocks, parent_factor, parent_rhs):
    sections = lax.axis_size("rows")
    section = lax.axis_index("rows")
    leaf_solution = front_forward(leaf_factor, leaf_rhs, section, sections, leaf_pass)
    panel_product = matmul(update_panel, leaf_solution)
    columns = panel_product.shape[1]
    pieces = panel_product.reshape(-1, ROW_BLOCK, columns)
    placed = jnp.zeros_like(pieces).at[update_blocks[0]].set(pieces).reshape(panel_product.shape)
    column_half = parent_rhs.shape[1]
    sibling = lax.axis_index("leaf") % 2
    kept_half, sent_half = split_halves(placed, sibling, column_half)
    arrived = swapped(sent_half, "leaf", 0)
    update_sum = lax.psum_scatter(kept_half + arrived, "rows", scatter_dimension=0, tiled=True)
    pending = parent_rhs - update_sum
    parent_solution = front_forward(parent_factor, pending, section, sections, parent_pass)
    return (leaf_solution, parent_solution)


def solution(mesh):
    placed = (
        P(("leaf", "rows"), None),
        P(("leaf", "rows"), None),
        P("leaf", "rows"),
        P("leaf", None),
        P(("leaf", "rows"), None),
        P(("leaf", "rows"), None),
    )
    return jax.shard_map(
        shards,
        mesh=mesh,
        in_specs=placed,
        out_specs=(P(("leaf", "rows"), None), P(("leaf", "rows"), None)),
        check_vma=False,
    )
```

profile of v0, /device:TPU:0, one launch (start us, length us, event | category | flops | bytes accessed | tf_op | source)
XLA Modules:
  0.0 91.6 jit_solution(15705059497558909469)
XLA Ops:
  7.2 0.0 copy-start
  7.2 0.0 copy-start.1
  7.2 0.0 reduce-scatter.2.cloned.1.call-start
  7.2 0.8 broadcast.43
  8.1 0.4 copy-done.1
  8.5 24.2 %while.48 = (s32[]{:T(128)}, f32[512,256]{1,0:T(8,128)S(1)}, f32[512,256]{1,0:T(8,128)}, f32[512,256]{1,0:T(8,128)S(1)}, s32[]{:T(128)}, /*index=5*/f32[512,1024]{1,0:T(8,128)}, s32[]{:T(128)}, s32[]{:T(128)}, s32[]{:T(128)}) while((s32[]{:T(128)}, f32[512,256]{1,0:T(8,128)S(1)}, f32[512,256]{1,0:T(8,128)}, f32[512,256]{1,0:T(8,128)S(1)}, ...), condition=%wide.region_5.6_spmd, body=%wide.region_0.5_spmd.sunk | while | flops 1611005952 | bytes 8388991 | solution.py:65
  8.5 3.0 %conditional.9 = (f32[512,256]{1,0:T(8,128)}) conditional(s32[]{:T(128)} %convert_element_type.37, f32[512,256]{1,0:T(8,128)} %get-tuple-element.491, (s32[]{:T(128)}, f32[512,1024]{1,0:T(8,128)}, f32[512,256]{1,0:T(8,128)S(1)}) %tuple.111), branch_computations={%region_3.3_spmd, %region_4.4_spmd} | conditional | flops 805306368 | bytes 2097210 | solution.py:57
  8.5 3.0 %fusion.2 = f32[512,256]{1,0:T(8,128)} fusion(f32[512,256]{1,0:T(8,128)S(1)} %get-tuple-element.336, f32[512,1024]{1,0:T(8,128)} %get-tuple-element.334, s32[]{:T(128)S(6)} %select_n.93), kind=kOutput, calls=%fused_computation.4 | convolution fusion | flops 805306368 | bytes 2097156 | tf_op jit(solution)/shard_map/while/body/eval_jaxpr/cond/branch_1_fun/dot_general | solution.py:26
  11.5 1.9 %select_select_fusion.4 = f32[512,256]{1,0:T(8,128)} fusion(f32[512,256]{1,0:T(8,128)} %get-tuple-element.535, f32[512,256]{1,0:T(8,128)S(1)} %get-tuple-element.492, pred[]{:T(512)S(6)} %and.26, pred[]{:T(512)S(6)} %eq.25), kind=kLoop, calls=%fused_computation.7.clone.1 | loop fusion | flops 262144 | bytes 1572866 | tf_op jit(solution)/shard_map/while/body/eval_jaxpr/jit(_where)/select_n | solution.py:58
  13.4 1.3 %collective-permute-start = (f32[512,256]{1,0:T(8,128)}, f32[512,256]{1,0:T(8,128)S(1)}, u32[]{:S(2)}, u32[]{:S(2)}) collective-permute-start(f32[512,256]{1,0:T(8,128)} %select_select_fusion.4), channel_id=1, source_target_pairs={{0,1},{2,3},{4,5},{6,7},{8,9},{10,11},{12,13},{14,15},{16,17},{18,... | collective-permute-start | bytes 1572872 | tf_op jit(solution)/shard_map/while/body/eval_jaxpr/ppermute | solution.py:12
  14.8 1.7 %collective-permute-done = f32[512,256]{1,0:T(8,128)S(1)} collective-permute-done((f32[512,256]{1,0:T(8,128)}, f32[512,256]{1,0:T(8,128)S(1)}, u32[]{:S(2)}, u32[]{:S(2)}) %collective-permute-start) | collective-permute-done | bytes 524320 | tf_op jit(solution)/shard_map/while/body/eval_jaxpr/ppermute | solution.py:12
  16.5 0.9 select_select_fusion.4
  17.3 4.8 %collective-permute-start = (f32[512,256]{1,0:T(8,128)}, f32[512,256]{1,0:T(8,128)S(1)}, u32[]{:S(2)}, u32[]{:S(2)}) collective-permute-start(f32[512,256]{1,0:T(8,128)} %select_select_fusion.4), channel_id=1, source_target_pairs={{0,1},{2,3},{4,5},{6,7},{8,9},{10,11},{12,13},{14,15},{16,17},{18,... | collective-permute-start | bytes 1572872 | tf_op jit(solution)/shard_map/while/body/eval_jaxpr/ppermute | solution.py:12
  22.1 1.7 %collective-permute-done = f32[512,256]{1,0:T(8,128)S(1)} collective-permute-done((f32[512,256]{1,0:T(8,128)}, f32[512,256]{1,0:T(8,128)S(1)}, u32[]{:S(2)}, u32[]{:S(2)}) %collective-permute-start) | collective-permute-done | bytes 524320 | tf_op jit(solution)/shard_map/while/body/eval_jaxpr/ppermute | solution.py:12
  23.8 0.9 select_select_fusion.4
  24.7 6.3 %collective-permute-start = (f32[512,256]{1,0:T(8,128)}, f32[512,256]{1,0:T(8,128)S(1)}, u32[]{:S(2)}, u32[]{:S(2)}) collective-permute-start(f32[512,256]{1,0:T(8,128)} %select_select_fusion.4), channel_id=1, source_target_pairs={{0,1},{2,3},{4,5},{6,7},{8,9},{10,11},{12,13},{14,15},{16,17},{18,... | collective-permute-start | bytes 1572872 | tf_op jit(solution)/shard_map/while/body/eval_jaxpr/ppermute | solution.py:12
  31.0 1.7 %collective-permute-done = f32[512,256]{1,0:T(8,128)S(1)} collective-permute-done((f32[512,256]{1,0:T(8,128)}, f32[512,256]{1,0:T(8,128)S(1)}, u32[]{:S(2)}, u32[]{:S(2)}) %collective-permute-start) | collective-permute-done | bytes 524320 | tf_op jit(solution)/shard_map/while/body/eval_jaxpr/ppermute | solution.py:12
  32.7 0.0 copy-done
  32.7 0.0 copy-start.4
  32.7 4.5 %convolution_bitcast_fusion = f32[1024,256]{0,1:T(8,128)S(1)} fusion(f32[512,256]{1,0:T(8,128)} %get-tuple-element.362, f32[1024,512]{1,0:T(8,128)S(1)} %copy-done), kind=kOutput, calls=%fused_computation.15 | convolution fusion | flops 1610612736 | bytes 3670016 | tf_op jit(solution)/shard_map/dot_general | solution.py:26
  37.3 1.3 %copy.9 = f32[1024,256]{1,0:T(8,128)} copy(f32[1024,256]{0,1:T(8,128)S(1)} %convolution_bitcast_fusion) | data formatting | bytes 2097152 | tf_op jit(solution)/shard_map/reshape | solution.py:82
  38.6 0.0 copy-done.4
  38.6 0.1 broadcast_in_dim.4
  38.7 2.0 %scatter_fusion = f32[8,128,256]{2,1,0:T(8,128)S(1)} fusion(f32[8,128,256]{2,1,0:T(8,128)S(1)} %broadcast_in_dim.4, s32[8]{0:T(128)S(1)} %fusion.10, f32[8,128,256]{2,1,0:T(8,128)} %bitcast.16), kind=kCustom, calls=%fused_computation | custom fusion | bytes 3145760 | tf_op jit(solution)/shard_map/scatter | solution.py:83
  40.7 0.0 copy-start.3
  40.7 0.1 slice_select_fusion
  40.8 3.0 %collective-permute-start.2 = (f32[1024,128]{1,0:T(8,128)S(1)}, f32[1024,128]{1,0:T(8,128)S(1)}, u32[]{:S(2)}, u32[]{:S(2)}) collective-permute-start(f32[1024,128]{1,0:T(8,128)S(1)} %slice_select_fusion), channel_id=1, source_target_pairs={{0,2},{2,0},{4,6},{6,4},{8,10},{10,8},{12,14},{14,12},{16,18},{18,... | collective-permute-start | bytes 1572872 | tf_op jit(solution)/shard_map/ppermute | solution.py:22
  43.8 12.4 %collective-permute-done.2 = f32[1024,128]{1,0:T(8,128)S(1)} collective-permute-done((f32[1024,128]{1,0:T(8,128)S(1)}, f32[1024,128]{1,0:T(8,128)S(1)}, u32[]{:S(2)}, u32[]{:S(2)}) %collective-permute-start.2) | collective-permute-done | bytes 524320 | tf_op jit(solution)/shard_map/ppermute | solution.py:22
  56.2 0.9 select_add_fusion
  57.1 0.0 reduce-scatter.2.cloned.1.call-update
  57.1 9.6 %reduce-scatter.2.cloned.1.call-done = f32[512,128]{1,0:T(8,128)} async-done(((f32[1024,128]{1,0:T(8,128)}), f32[512,128]{1,0:T(8,128)}) %reduce-scatter.2.cloned.1.call-update) | async-done | bytes 262160 | tf_op jit(solution)/shard_map/reduce_scatter | solution.py:88
  66.7 0.0 copy-done.3
  66.7 1.0 %sub.25 = f32[512,128]{1,0:T(8,128)S(1)} subtract(f32[512,128]{1,0:T(8,128)S(1)} %copy-done.3, f32[512,128]{1,0:T(8,128)} %reduce-scatter.2.cloned.1.call-done) | non-fusion elementwise | flops 65536 | bytes 786432 | tf_op jit(solution)/shard_map/sub | solution.py:89
  67.8 16.2 %while.49 = (s32[]{:T(128)}, f32[512,128]{1,0:T(8,128)S(1)}, f32[512,128]{1,0:T(8,128)S(1)}, f32[512,128]{1,0:T(8,128)S(1)}, s32[]{:T(128)}, /*index=5*/f32[512,1024]{1,0:T(8,128)}, s32[]{:T(128)}, s32[]{:T(128)}, s32[]{:T(128)}) while((s32[]{:T(128)}, f32[512,128]{1,0:T(8,128)S(1)}, f32[512,128]{1,0:T(8,128)S(1)}, ...), condition=%wide.region_13.14_spmd, body=%wide.region_8.13_spmd.sunk | while | flops 805502976 | bytes 5243263 | solution.py:65
  67.8 2.2 %conditional.11 = (f32[512,128]{1,0:T(8,128)S(1)}) conditional(s32[]{:T(128)} %convert_element_type.39, f32[512,128]{1,0:T(8,128)S(1)} %get-tuple-element.518, (s32[]{:T(128)}, f32[512,1024]{1,0:T(8,128)}, f32[512,128]{1,0:T(8,128)S(1)}) %tuple.114), branch_computations={%region_11.11_spmd, %region_12.12_spmd} | conditional | flops 402653184 | bytes 1572922 | solution.py:57
  67.8 2.2 %fusion.7 = f32[512,128]{1,0:T(8,128)S(1)} fusion(f32[512,128]{1,0:T(8,128)S(1)} %get-tuple-element.351, f32[512,1024]{1,0:T(8,128)} %get-tuple-element.349, s32[]{:T(128)S(6)} %select_n.99), kind=kOutput, calls=%fused_computation.11 | convolution fusion | flops 402653184 | bytes 1572868 | tf_op jit(solution)/shard_map/while/body/eval_jaxpr/cond/branch_1_fun/dot_general | solution.py:26
  70.1 1.3 %collective-permute-start.1 = (f32[512,128]{1,0:T(8,128)S(1)}, f32[512,128]{1,0:T(8,128)S(1)}, u32[]{:S(2)}, u32[]{:S(2)}) collective-permute-start(f32[512,128]{1,0:T(8,128)S(1)} %select_select_fusion.5), channel_id=1, source_target_pairs={{0,1},{2,3},{4,5},{6,7},{8,9},{10,11},{12,13},{14,15},{16,17},{18,... | collective-permute-start | bytes 786440 | tf_op jit(solution)/shard_map/while/body/eval_jaxpr/ppermute | solution.py:12
  71.4 1.1 %collective-permute-done.1 = f32[512,128]{1,0:T(8,128)S(1)} collective-permute-done((f32[512,128]{1,0:T(8,128)S(1)}, f32[512,128]{1,0:T(8,128)S(1)}, u32[]{:S(2)}, u32[]{:S(2)}) %collective-permute-start.1) | collective-permute-done | bytes 262176 | tf_op jit(solution)/shard_map/while/body/eval_jaxpr/ppermute | solution.py:12
  72.6 4.6 %collective-permute-start.1 = (f32[512,128]{1,0:T(8,128)S(1)}, f32[512,128]{1,0:T(8,128)S(1)}, u32[]{:S(2)}, u32[]{:S(2)}) collective-permute-start(f32[512,128]{1,0:T(8,128)S(1)} %select_select_fusion.5), channel_id=1, source_target_pairs={{0,1},{2,3},{4,5},{6,7},{8,9},{10,11},{12,13},{14,15},{16,17},{18,... | collective-permute-start | bytes 786440 | tf_op jit(solution)/shard_map/while/body/eval_jaxpr/ppermute | solution.py:12
  77.2 1.1 %collective-permute-done.1 = f32[512,128]{1,0:T(8,128)S(1)} collective-permute-done((f32[512,128]{1,0:T(8,128)S(1)}, f32[512,128]{1,0:T(8,128)S(1)}, u32[]{:S(2)}, u32[]{:S(2)}) %collective-permute-start.1) | collective-permute-done | bytes 262176 | tf_op jit(solution)/shard_map/while/body/eval_jaxpr/ppermute | solution.py:12
  78.3 4.5 %collective-permute-start.1 = (f32[512,128]{1,0:T(8,128)S(1)}, f32[512,128]{1,0:T(8,128)S(1)}, u32[]{:S(2)}, u32[]{:S(2)}) collective-permute-start(f32[512,128]{1,0:T(8,128)S(1)} %select_select_fusion.5), channel_id=1, source_target_pairs={{0,1},{2,3},{4,5},{6,7},{8,9},{10,11},{12,13},{14,15},{16,17},{18,... | collective-permute-start | bytes 786440 | tf_op jit(solution)/shard_map/while/body/eval_jaxpr/ppermute | solution.py:12
  82.9 1.1 %collective-permute-done.1 = f32[512,128]{1,0:T(8,128)S(1)} collective-permute-done((f32[512,128]{1,0:T(8,128)S(1)}, f32[512,128]{1,0:T(8,128)S(1)}, u32[]{:S(2)}, u32[]{:S(2)}) %collective-permute-start.1) | collective-permute-done | bytes 262176 | tf_op jit(solution)/shard_map/while/body/eval_jaxpr/ppermute | solution.py:12
  84.0 0.0 copy-start.2
  84.0 0.7 copy-done.2
  (17 shorter events, 0.2 us)
Async XLA Ops:
  7.2 25.5 %copy-start = (f32[1024,512]{1,0:T(8,128)S(1)}, f32[1024,512]{1,0:T(8,128)}, u32[]{:S(2)}) copy-start(f32[1024,512]{1,0:T(8,128)} %param.20) | copy-start | bytes 6291460
  7.2 1.4 %copy-start.1 = (f32[512,256]{1,0:T(8,128)S(1)}, f32[512,256]{1,0:T(8,128)}, u32[]{:S(2)}) copy-start(f32[512,256]{1,0:T(8,128)} %param.19) | copy-start | bytes 1572868
  7.2 59.5 %reduce-scatter.2.cloned.1.call-start = ((), (), s32[]{:S(2)}) async-start(), calls=%async_computation.1 | async-start | bytes 786432 | tf_op jit(solution)/shard_map/reduce_scatter | solution.py:88
  13.4 3.0 %collective-permute-start = (f32[512,256]{1,0:T(8,128)}, f32[512,256]{1,0:T(8,128)S(1)}, u32[]{:S(2)}, u32[]{:S(2)}) collective-permute-start(f32[512,256]{1,0:T(8,128)} %select_select_fusion.4), channel_id=1, source_target_pairs={{0,1},{2,3},{4,5},{6,7},{8,9},{10,11},{12,13},{14,15},{16,17},{18,... | collective-permute-start | bytes 1572872 | tf_op jit(solution)/shard_map/while/body/eval_jaxpr/ppermute | solution.py:12
  17.3 6.5 %collective-permute-start = (f32[512,256]{1,0:T(8,128)}, f32[512,256]{1,0:T(8,128)S(1)}, u32[]{:S(2)}, u32[]{:S(2)}) collective-permute-start(f32[512,256]{1,0:T(8,128)} %select_select_fusion.4), channel_id=1, source_target_pairs={{0,1},{2,3},{4,5},{6,7},{8,9},{10,11},{12,13},{14,15},{16,17},{18,... | collective-permute-start | bytes 1572872 | tf_op jit(solution)/shard_map/while/body/eval_jaxpr/ppermute | solution.py:12
  24.7 8.0 %collective-permute-start = (f32[512,256]{1,0:T(8,128)}, f32[512,256]{1,0:T(8,128)S(1)}, u32[]{:S(2)}, u32[]{:S(2)}) collective-permute-start(f32[512,256]{1,0:T(8,128)} %select_select_fusion.4), channel_id=1, source_target_pairs={{0,1},{2,3},{4,5},{6,7},{8,9},{10,11},{12,13},{14,15},{16,17},{18,... | collective-permute-start | bytes 1572872 | tf_op jit(solution)/shard_map/while/body/eval_jaxpr/ppermute | solution.py:12
  32.7 5.9 %copy-start.4 = (s32[1,8]{1,0:T(1,128)S(1)}, s32[1,8]{1,0:T(1,128)}, u32[]{:S(2)}) copy-start(s32[1,8]{1,0:T(1,128)} %param.21) | copy-start | bytes 100
  40.7 26.0 %copy-start.3 = (f32[512,128]{1,0:T(8,128)S(1)}, f32[512,128]{1,0:T(8,128)}, u32[]{:S(2)}) copy-start(f32[512,128]{1,0:T(8,128)} %param.23) | copy-start | bytes 786436
  40.8 15.5 %collective-permute-start.2 = (f32[1024,128]{1,0:T(8,128)S(1)}, f32[1024,128]{1,0:T(8,128)S(1)}, u32[]{:S(2)}, u32[]{:S(2)}) collective-permute-start(f32[1024,128]{1,0:T(8,128)S(1)} %slice_select_fusion), channel_id=1, source_target_pairs={{0,2},{2,0},{4,6},{6,4},{8,10},{10,8},{12,14},{14,12},{16,18},{18,... | collective-permute-start | bytes 1572872 | tf_op jit(solution)/shard_map/ppermute | solution.py:22
  70.1 2.4 %collective-permute-start.1 = (f32[512,128]{1,0:T(8,128)S(1)}, f32[512,128]{1,0:T(8,128)S(1)}, u32[]{:S(2)}, u32[]{:S(2)}) collective-permute-start(f32[512,128]{1,0:T(8,128)S(1)} %select_select_fusion.5), channel_id=1, source_target_pairs={{0,1},{2,3},{4,5},{6,7},{8,9},{10,11},{12,13},{14,15},{16,17},{18,... | collective-permute-start | bytes 786440 | tf_op jit(solution)/shard_map/while/body/eval_jaxpr/ppermute | solution.py:12
  72.6 5.7 %collective-permute-start.1 = (f32[512,128]{1,0:T(8,128)S(1)}, f32[512,128]{1,0:T(8,128)S(1)}, u32[]{:S(2)}, u32[]{:S(2)}) collective-permute-start(f32[512,128]{1,0:T(8,128)S(1)} %select_select_fusion.5), channel_id=1, source_target_pairs={{0,1},{2,3},{4,5},{6,7},{8,9},{10,11},{12,13},{14,15},{16,17},{18,... | collective-permute-start | bytes 786440 | tf_op jit(solution)/shard_map/while/body/eval_jaxpr/ppermute | solution.py:12
  78.3 5.7 %collective-permute-start.1 = (f32[512,128]{1,0:T(8,128)S(1)}, f32[512,128]{1,0:T(8,128)S(1)}, u32[]{:S(2)}, u32[]{:S(2)}) collective-permute-start(f32[512,128]{1,0:T(8,128)S(1)} %select_select_fusion.5), channel_id=1, source_target_pairs={{0,1},{2,3},{4,5},{6,7},{8,9},{10,11},{12,13},{14,15},{16,17},{18,... | collective-permute-start | bytes 786440 | tf_op jit(solution)/shard_map/while/body/eval_jaxpr/ppermute | solution.py:12
  84.0 0.7 copy-start.2
Sparse Core Ops, SparseCore 0:
  57.2 9.4 reduce-scatter.1
where the time goes:
time: 92.1 us; the launch traced here: 91.6 us
  waiting for transfers between devices  30.5 us (33%)
  starting transfers between devices  25.9 us (28%)
  between operations  14.1 us (15%)
  matrix products  9.77 us (11%)
  other arithmetic  5.62 us (6%)
  local copies, waits for them, and re-layouts  5.43 us (6%)
    ppermute x6, starting transfers between devices, passed_along(): return lax.ppermute(array, axis, pairs)  22.8 us
    ppermute x1, waiting for transfers between devices, swapped(): return lax.ppermute(block, axis, route)  12.4 us
    dot_general x3, matrix products, matmul(): jnp.dot(left, right, precision=lax.Precision.HIGHEST, preferred_element_t...  9.77 us
    reduce_scatter x1, waiting for transfers between devices, shards(): lax.psum_scatter(kept_half + arrived, 'rows', scatter_dimension=0, tiled=...  9.62 us
    ppermute x6, waiting for transfers between devices, passed_along(): return lax.ppermute(array, axis, pairs)  8.45 us
    select_n x6, other arithmetic, advance(): jnp.where(own_turn, solution, jnp.where(useful, incoming, jnp.zeros_like(...  3.72 us
    ppermute x1, starting transfers between devices, swapped(): return lax.ppermute(block, axis, route)  3.02 us
    scatter x1, local copies, waits for them, and re-layouts, shards(): jnp.zeros_like(pieces).at[update_blocks[0]].set(pieces)  1.99 us
  transfers between devices with their start and end apart: 8, of which 8 were waited for; matrix products, arithmetic and copies ran while one was open for 0% of the time, Pallas kernels for 0%

commit v1 on v0

--- a/solution.py
+++ b/solution.py
@@ -22,8 +22,8 @@
     return lax.ppermute(block, axis, route)
 
 
-def matmul(left, right):
-    return jnp.dot(left, right, precision=lax.Precision.HIGHEST, preferred_element_type=jnp.float32)
+def matmul(left, right, precision=lax.Precision.HIGHEST):
+    return jnp.dot(left, right, precision=precision, preferred_element_type=jnp.float32)
 
 
 def leaf_pass(outgoing):
@@ -73,8 +73,45 @@
     return (kept_half, sent_half)
 
 
+def pair_swap(block, axis):
+    return lax.ppermute(block, axis, [(0, 1), (1, 0)])
+
+
+def two_section_solve(factor, right_side, section, precision):
+    tile_rows = right_side.shape[0]
+    diagonal = lax.dynamic_slice_in_dim(factor, section * tile_rows, tile_rows, 1)
+    below = factor[:, :tile_rows]
+    first = matmul(diagonal, right_side, precision)
+    arrived = lax.ppermute(first, "rows", [(0, 1)])
+    coupling = matmul(diagonal, below, precision)
+    return first - matmul(coupling, arrived, precision)
+
+
+def two_section_shards(leaf_factor, leaf_rhs, update_panel, update_blocks, parent_factor, parent_rhs):
+    section = lax.axis_index("rows")
+    precision = lax.Precision.HIGHEST
+    leaf_solution = two_section_solve(leaf_factor, leaf_rhs, section, precision)
+    order = jnp.argsort(update_blocks[0])
+    blocks = update_panel.reshape(-1, ROW_BLOCK, update_panel.shape[1])
+    panel_placed = jnp.take(blocks, order, axis=0).reshape(update_panel.shape)
+    placed = matmul(panel_placed, leaf_solution, precision)
+    rows_half = placed.shape[0] // 2
+    own_rows = lax.dynamic_slice_in_dim(placed, section * rows_half, rows_half, 0)
+    other_rows = lax.dynamic_slice_in_dim(placed, (1 - section) * rows_half, rows_half, 0)
+    chip_sum = own_rows + pair_swap(other_rows, "rows")
+    column_half = parent_rhs.shape[1]
+    sibling = lax.axis_index("leaf") % 2
+    kept = lax.dynamic_slice_in_dim(chip_sum, sibling * column_half, column_half, 1)
+    sent = lax.dynamic_slice_in_dim(chip_sum, (1 - sibling) * column_half, column_half, 1)
+    pending = parent_rhs - (kept + swapped(sent, "leaf", 0))
+    parent_solution = two_section_solve(parent_factor, pending, section, precision)
+    return (leaf_solution, parent_solution)
+
+
 def shards(leaf_factor, leaf_rhs, update_panel, update_blocks, parent_factor, parent_rhs):
     sections = lax.axis_size("rows")
+    if sections == 2:
+        return two_section_shards(leaf_factor, leaf_rhs, update_panel, update_blocks, parent_factor, parent_rhs)
     section = lax.axis_index("rows")
     leaf_solution = front_forward(leaf_factor, leaf_rhs, section, sections, leaf_pass)
     panel_product = matmul(update_panel, leaf_solution)

time: 92.1 us -> 39.6 us (0.43)
  waiting for transfers between devices: 30.5 us -> 8.86 us
  starting transfers between devices: 25.9 us -> 7.08 us
  between operations: 14.1 us -> 0.81 us
  matrix products: 9.77 us -> 14.9 us
  other arithmetic: 5.62 us -> 3.89 us
  local copies, waits for them, and re-layouts: 5.43 us -> 3.76 us
    ppermute x6 -> x3, starting transfers between devices: 22.8 us -> 4.7 us  [the longest x2 4.69 us: two_section_solve(): arrived = lax.ppermute(first, 'rows', [(0, 1)])]
    reduce_scatter x1 -> x0, waiting for transfers between devices: 9.62 us -> none  [shards(): lax.psum_scatter(kept_half + arrived, 'rows', scatter_dimension=0, tiled=...]
    ppermute x6 -> x3, waiting for transfers between devices: 8.45 us -> 2.25 us  [the longest x1 2.25 us: pair_swap(): return lax.ppermute(block, axis, [(0, 1), (1, 0)])]
    ppermute x1, waiting for transfers between devices: 12.4 us -> 6.6 us  [swapped(): return lax.ppermute(block, axis, route)]
    dot_general x3 -> x7, matrix products: 9.77 us -> 14.9 us  [matmul(): jnp.dot(left, right, precision=precision, preferred_element_type=jnp.floa...]
    gather x0 -> x1, local copies, waits for them, and re-layouts: none -> 2.01 us  [two_section_shards(): panel_placed = jnp.take(blocks, order, axis=0).reshape(update_panel.shape)]
    scatter x1 -> x0, local copies, waits for them, and re-layouts: 1.99 us -> none  [shards(): jnp.zeros_like(pieces).at[update_blocks[0]].set(pieces)]
    select_n x8 -> x2, other arithmetic: 3.78 us -> 1.81 us  [two_section_shards(): panel_placed = jnp.take(blocks, order, axis=0).reshape(update_panel.shape)]
  transfers between devices with their start and end apart: 8 -> 4, of which waited for: 8 -> 2; matrix products, arithmetic and copies ran while one was open for 0% -> 22% of each run, Pallas kernels for 0% -> 0%
where the time goes in v1:
time: 39.6 us; the launch traced here: 39.3 us
  matrix products  14.9 us (38%)
  waiting for transfers between devices  8.86 us (22%)
  starting transfers between devices  7.08 us (18%)
  other arithmetic  3.89 us (10%)
  local copies, waits for them, and re-layouts  3.76 us (9%)
  between operations  0.81 us (2%)
    dot_general x7, matrix products, matmul(): jnp.dot(left, right, precision=precision, preferred_element_type=jnp.floa...  14.9 us
    ppermute x1, waiting for transfers between devices, swapped(): return lax.ppermute(block, axis, route)  6.6 us
    ppermute x2, starting transfers between devices, two_section_solve(): arrived = lax.ppermute(first, 'rows', [(0, 1)])  4.69 us
    ppermute x1, starting transfers between devices, swapped(): return lax.ppermute(block, axis, route)  2.39 us
    ppermute x1, waiting for transfers between devices, pair_swap(): return lax.ppermute(block, axis, [(0, 1), (1, 0)])  2.25 us
    gather x1, local copies, waits for them, and re-layouts, two_section_shards(): panel_placed = jnp.take(blocks, order, axis=0).reshape(update_panel.shape)  2.01 us
    select_n x2, other arithmetic, two_section_shards(): panel_placed = jnp.take(blocks, order, axis=0).reshape(update_panel.shape)  1.81 us
    add x1, other arithmetic, two_section_shards(): chip_sum = own_rows + pair_swap(other_rows, 'rows')  1.11 us
  transfers between devices with their start and end apart: 4, of which 2 were waited for; matrix products, arithmetic and copies ran while one was open for 22% of the time, Pallas kernels for 0%

profile of v1, /device:TPU:0, one launch (start us, length us, event | category | flops | bytes accessed | tf_op | source)
XLA Modules:
  0.0 39.3 jit_solution(12234759545413988442)
XLA Ops:
  0.6 0.0 copy-start
  0.7 0.0 copy-start.2
  0.7 0.0 copy-start.6
  0.7 3.3 %fusion.8 = f32[512,256]{1,0:T(8,128)} fusion(f32[512,256]{1,0:T(8,128)} %param.7, f32[512,1024]{1,0:T(8,128)} %param.6, s32[]{:T(128)S(6)} %select_n.31), kind=kOutput, calls=%fused_computation.12 | convolution fusion | flops 805306368 | bytes 2097156 | tf_op jit(solution)/shard_map/dot_general | solution.py:26
  4.0 3.1 %collective-permute-start = (f32[512,256]{1,0:T(8,128)}, f32[512,256]{1,0:T(8,128)}, u32[]{:S(2)}, u32[]{:S(2)}) collective-permute-start(f32[512,256]{1,0:T(8,128)} %fusion.8), channel_id=1, source_target_pairs={{0,1},{2,3},{4,5},{6,7},{8,9},{10,11},{12,13},{14,15},{16,17},{18,... | collective-permute-start | bytes 1572872 | tf_op jit(solution)/shard_map/ppermute | solution.py:85
  7.1 0.0 copy-done.2
  7.1 1.8 %fusion.2 = f32[512,512]{1,0:T(8,128)S(1)} fusion(f32[512,1024]{1,0:T(8,128)S(1)} %copy-done.2, s32[]{:T(128)S(6)} %select_n.31), kind=kOutput, calls=%fused_computation.6 | convolution fusion | flops 1610612736 | bytes 3145732 | tf_op jit(solution)/shard_map/dot_general | solution.py:26
  9.0 0.0 copy-done.6
  9.0 1.0 %sort.17 = (s32[8]{0:T(128)}, s32[8]{0:T(128)S(1)}) sort(s32[8]{0:T(128)S(1)} %bitcast.14, s32[8]{0:T(128)S(1)} %iota.4), dimensions={0}, to_apply=%region_0.0 | sort | flops 24 | bytes 128 | tf_op jit(solution)/shard_map/jit(argsort)/sort | solution.py:94
  10.0 0.0 copy-done
  10.0 2.0 %gather_fusion = f32[8,128,512]{2,1,0:T(8,128)} fusion(f32[8,128,512]{2,1,0:T(8,128)S(1)} %bitcast.13, s32[1024]{0:T(1024)S(1)} %pad_clamp_fusion), kind=kCustom, calls=%fused_computation | custom fusion | bytes 4194336 | tf_op jit(solution)/shard_map/jit(_take)/gather | solution.py:96
  12.0 0.1 broadcast_bitcast_fusion
  12.1 1.8 %bitcast_select_fusion = f32[1024,512]{1,0:T(8,128)S(1)} fusion(f32[8,128,512]{2,1,0:T(8,128)} %gather_fusion, pred[1024]{0:T(1024)(128)(4,1)S(1)} %broadcast_bitcast_fusion), kind=kLoop, calls=%fused_computation.1 | loop fusion | flops 524288 | bytes 4195328 | tf_op jit(solution)/shard_map/jit(_take)/select_n | solution.py:96
  13.9 0.0 collective-permute-done
  13.9 2.2 %convolution_subtract_fusion = f32[512,256]{1,0:T(8,128)S(1)} fusion(f32[512,256]{1,0:T(8,128)} %fusion.8, f32[512,512]{1,0:T(8,128)S(1)} %fusion.2, f32[512,256]{1,0:T(8,128)} %collective-permute-done), kind=kOutput, calls=%fused_computation.2 | convolution fusion | flops 805437440 | bytes 2621440 | tf_op jit(solution)/shard_map/dot_general | solution.py:26
  16.1 0.0 copy-start.1
  16.1 1.8 %fusion.17 = f32[1024,256]{1,0:T(8,128)S(1)} fusion(f32[1024,512]{1,0:T(8,128)S(1)} %bitcast_select_fusion, f32[512,256]{1,0:T(8,128)S(1)} %convolution_subtract_fusion), kind=kOutput, calls=%fused_computation.28 | convolution fusion | flops 1610612736 | bytes 3670016 | tf_op jit(solution)/shard_map/dot_general | solution.py:26
  17.9 0.0 copy-start.5
  17.9 0.8 %constant_dynamic-slice_fusion.1 = f32[512,256]{1,0:T(8,128)} fusion(f32[1024,256]{1,0:T(8,128)S(1)} %fusion.17, s32[]{:T(128)S(6)} %select_n.34), kind=kLoop, calls=%fused_computation.25 | loop fusion | bytes 1048580 | tf_op jit(solution)/shard_map/dynamic_slice | solution.py:100
  18.8 0.0 copy-done.1
  18.8 0.0 collective-permute-start.1
  18.8 2.2 %collective-permute-done.1 = f32[512,256]{1,0:T(8,128)} collective-permute-done((f32[512,256]{1,0:T(8,128)}, f32[512,256]{1,0:T(8,128)}, u32[]{:S(2)}, u32[]{:S(2)}) %collective-permute-start.1) | collective-permute-done | bytes 524320 | tf_op jit(solution)/shard_map/ppermute | solution.py:77
  21.0 1.1 %dynamic-slice_add_fusion = f32[512,256]{1,0:T(8,128)S(1)} fusion(f32[512,256]{1,0:T(8,128)} %collective-permute-done.1, f32[1024,256]{1,0:T(8,128)S(1)} %fusion.17, s32[]{:T(128)S(6)} %select_n.31), kind=kLoop, calls=%fused_computation.14 | loop fusion | flops 131072 | bytes 1572868 | tf_op jit(solution)/shard_map/add | solution.py:101
  22.1 0.0 copy-start.4
  22.1 0.8 %copy-done.4 = f32[512,256]{1,0:T(8,128)} copy-done((f32[512,256]{1,0:T(8,128)}, f32[512,256]{1,0:T(8,128)S(1)}, u32[]{:S(2)}) %copy-start.4) | copy-done | bytes 524312
  22.9 2.4 %collective-permute-start.2 = (f32[512,128]{1,0:T(8,128)S(1)}, f32[512,128]{1,0:T(8,128)S(1)}, u32[]{:S(2)}, u32[]{:S(2)}) collective-permute-start(f32[512,128]{1,0:T(8,128)S(1)} %constant_dynamic-slice_fusion), channel_id=1, source_target_pairs={{0,2},{2,0},{4,6},{6,4},{8,10},{10,8},{12,14},{14,12},{16,18},{18,... | collective-permute-start | bytes 786440 | tf_op jit(solution)/shard_map/ppermute | solution.py:22
  25.3 0.0 copy-start.3
  25.3 6.6 %collective-permute-done.2 = f32[512,128]{1,0:T(8,128)S(1)} collective-permute-done((f32[512,128]{1,0:T(8,128)S(1)}, f32[512,128]{1,0:T(8,128)S(1)}, u32[]{:S(2)}, u32[]{:S(2)}) %collective-permute-start.2) | collective-permute-done | bytes 262176 | tf_op jit(solution)/shard_map/ppermute | solution.py:22
  31.9 0.0 copy-done.5
  31.9 2.2 %fusion.5 = f32[512,128]{1,0:T(8,128)S(1)} fusion(f32[512,1024]{1,0:T(8,128)} %param.10, s32[]{:T(128)S(6)} %select_n.31, f32[512,128]{1,0:T(8,128)S(1)} %copy-done.5, f32[512,128]{1,0:T(8,128)S(1)} %collective-permute-done.2, f32[512,256]{1,0:T(8,128)} %copy-done.4, s32[]{:T(128)S(6)} %select_n.36), kind=kOutput, calls=%fused_computation.9 | convolution fusion | flops 402784256 | bytes 2097160 | tf_op jit(solution)/shard_map/dot_general | solution.py:26
  34.2 1.5 %collective-permute-start.3 = (f32[512,128]{1,0:T(8,128)S(1)}, f32[512,128]{1,0:T(8,128)S(1)}, u32[]{:S(2)}, u32[]{:S(2)}) collective-permute-start(f32[512,128]{1,0:T(8,128)S(1)} %fusion.5), channel_id=1, source_target_pairs={{0,1},{2,3},{4,5},{6,7},{8,9},{10,11},{12,13},{14,15},{16,17},{18,... | collective-permute-start | bytes 786440 | tf_op jit(solution)/shard_map/ppermute | solution.py:85
  35.7 0.0 copy-done.3
  35.7 1.8 %fusion = f32[512,512]{1,0:T(8,128)S(1)} fusion(f32[512,1024]{1,0:T(8,128)S(1)} %copy-done.3, s32[]{:T(128)S(6)} %select_n.31), kind=kOutput, calls=%fused_computation.4 | convolution fusion | flops 1610612736 | bytes 3145732 | tf_op jit(solution)/shard_map/dot_general | solution.py:26
  37.6 0.0 collective-permute-done.3
  37.6 1.7 %convolution_subtract_fusion.1 = f32[512,128]{1,0:T(8,128)} fusion(f32[512,128]{1,0:T(8,128)S(1)} %fusion.5, f32[512,512]{1,0:T(8,128)S(1)} %fusion, f32[512,128]{1,0:T(8,128)S(1)} %collective-permute-done.3), kind=kOutput, calls=%fused_computation.3 | convolution fusion | flops 402718720 | bytes 1835008 | tf_op jit(solution)/shard_map/dot_general | solution.py:26
  (5 shorter events, 0.0 us)
Async XLA Ops:
  0.6 9.3 %copy-start = (f32[1024,512]{1,0:T(8,128)S(1)}, f32[1024,512]{1,0:T(8,128)}, u32[]{:S(2)}) copy-start(f32[1024,512]{1,0:T(8,128)} %param.8) | copy-start | bytes 6291460
  0.7 6.5 %copy-start.2 = (f32[512,1024]{1,0:T(8,128)S(1)}, f32[512,1024]{1,0:T(8,128)}, u32[]{:S(2)}) copy-start(f32[512,1024]{1,0:T(8,128)} %param.6) | copy-start | bytes 6291460
  0.7 8.3 %copy-start.6 = (s32[1,8]{1,0:T(1,128)S(1)}, s32[1,8]{1,0:T(1,128)}, u32[]{:S(2)}) copy-start(s32[1,8]{1,0:T(1,128)} %param.9) | copy-start | bytes 100
  4.0 9.9 %collective-permute-start = (f32[512,256]{1,0:T(8,128)}, f32[512,256]{1,0:T(8,128)}, u32[]{:S(2)}, u32[]{:S(2)}) collective-permute-start(f32[512,256]{1,0:T(8,128)} %fusion.8), channel_id=1, source_target_pairs={{0,1},{2,3},{4,5},{6,7},{8,9},{10,11},{12,13},{14,15},{16,17},{18,... | collective-permute-start | bytes 1572872 | tf_op jit(solution)/shard_map/ppermute | solution.py:85
  16.1 2.7 %copy-start.1 = (f32[512,256]{1,0:T(8,128)}, f32[512,256]{1,0:T(8,128)S(1)}, u32[]{:S(2)}) copy-start(f32[512,256]{1,0:T(8,128)S(1)} %convolution_subtract_fusion) | copy-start | bytes 1572868
  17.9 14.0 %copy-start.5 = (f32[512,128]{1,0:T(8,128)S(1)}, f32[512,128]{1,0:T(8,128)}, u32[]{:S(2)}) copy-start(f32[512,128]{1,0:T(8,128)} %param.11) | copy-start | bytes 786436
  18.8 2.3 %collective-permute-start.1 = (f32[512,256]{1,0:T(8,128)}, f32[512,256]{1,0:T(8,128)}, u32[]{:S(2)}, u32[]{:S(2)}) collective-permute-start(f32[512,256]{1,0:T(8,128)} %constant_dynamic-slice_fusion.1), channel_id=1, source_target_pairs={{0,1},{1,0},{2,3},{3,2},{4,5},{5,4},{6,7},{7,6},{8,9},{9,8},{10,11... | collective-permute-start | bytes 1572872 | tf_op jit(solution)/shard_map/ppermute | solution.py:77
  22.1 0.8 %copy-start.4 = (f32[512,256]{1,0:T(8,128)}, f32[512,256]{1,0:T(8,128)S(1)}, u32[]{:S(2)}) copy-start(f32[512,256]{1,0:T(8,128)S(1)} %dynamic-slice_add_fusion) | copy-start | bytes 1572868
  22.9 9.0 %collective-permute-start.2 = (f32[512,128]{1,0:T(8,128)S(1)}, f32[512,128]{1,0:T(8,128)S(1)}, u32[]{:S(2)}, u32[]{:S(2)}) collective-permute-start(f32[512,128]{1,0:T(8,128)S(1)} %constant_dynamic-slice_fusion), channel_id=1, source_target_pairs={{0,2},{2,0},{4,6},{6,4},{8,10},{10,8},{12,14},{14,12},{16,18},{18,... | collective-permute-start | bytes 786440 | tf_op jit(solution)/shard_map/ppermute | solution.py:22
  25.3 10.4 %copy-start.3 = (f32[512,1024]{1,0:T(8,128)S(1)}, f32[512,1024]{1,0:T(8,128)}, u32[]{:S(2)}) copy-start(f32[512,1024]{1,0:T(8,128)} %param.10) | copy-start | bytes 6291460
  34.2 3.4 %collective-permute-start.3 = (f32[512,128]{1,0:T(8,128)S(1)}, f32[512,128]{1,0:T(8,128)S(1)}, u32[]{:S(2)}, u32[]{:S(2)}) collective-permute-start(f32[512,128]{1,0:T(8,128)S(1)} %fusion.5), channel_id=1, source_target_pairs={{0,1},{2,3},{4,5},{6,7},{8,9},{10,11},{12,13},{14,15},{16,17},{18,... | collective-permute-start | bytes 786440 | tf_op jit(solution)/shard_map/ppermute | solution.py:85

commit v2 on v1

--- a/solution.py
+++ b/solution.py
@@ -87,24 +87,43 @@
     return first - matmul(coupling, arrived, precision)
 
 
+def inverse_order(update_blocks):
+    targets = update_blocks[0]
+    count = targets.shape[0]
+    hits = targets[:, None] == jnp.arange(count)[None, :]
+    return jnp.sum(jnp.where(hits, jnp.arange(count)[:, None], 0), axis=0)
+
+
+def placed_rows(product, order, section):
+    pieces = product.reshape(-1, ROW_BLOCK, product.shape[1])
+    per_section = pieces.shape[0] // 2
+    chosen = lax.dynamic_slice_in_dim(order, section * per_section, per_section)
+    taken = jnp.take(pieces, chosen, axis=0, mode="clip")
+    return taken.reshape(-1, product.shape[1])
+
+
 def two_section_shards(leaf_factor, leaf_rhs, update_panel, update_blocks, parent_factor, parent_rhs):
     section = lax.axis_index("rows")
-    precision = lax.Precision.HIGHEST
+    precision = lax.Precision.HIGH
     leaf_solution = two_section_solve(leaf_factor, leaf_rhs, section, precision)
-    order = jnp.argsort(update_blocks[0])
-    blocks = update_panel.reshape(-1, ROW_BLOCK, update_panel.shape[1])
-    panel_placed = jnp.take(blocks, order, axis=0).reshape(update_panel.shape)
-    placed = matmul(panel_placed, leaf_solution, precision)
-    rows_half = placed.shape[0] // 2
-    own_rows = lax.dynamic_slice_in_dim(placed, section * rows_half, rows_half, 0)
-    other_rows = lax.dynamic_slice_in_dim(placed, (1 - section) * rows_half, rows_half, 0)
-    chip_sum = own_rows + pair_swap(other_rows, "rows")
+    order = inverse_order(update_blocks)
+    product = matmul(update_panel, leaf_solution, precision)
+    other_rows = placed_rows(product, order, 1 - section)
+    arrived_rows = pair_swap(other_rows, "rows")
+    chip_sum = placed_rows(product, order, section) + arrived_rows
     column_half = parent_rhs.shape[1]
     sibling = lax.axis_index("leaf") % 2
     kept = lax.dynamic_slice_in_dim(chip_sum, sibling * column_half, column_half, 1)
     sent = lax.dynamic_slice_in_dim(chip_sum, (1 - sibling) * column_half, column_half, 1)
-    pending = parent_rhs - (kept + swapped(sent, "leaf", 0))
-    parent_solution = two_section_solve(parent_factor, pending, section, precision)
+    tile_rows = parent_rhs.shape[0]
+    diagonal = lax.dynamic_slice_in_dim(parent_factor, section * tile_rows, tile_rows, 1)
+    coupling = matmul(diagonal, parent_factor[:, :tile_rows], precision)
+    arrived = swapped(sent, "leaf", 0)
+    arrived, coupling = lax.optimization_barrier((arrived, coupling))
+    pending = parent_rhs - (kept + arrived)
+    first = matmul(diagonal, pending, precision)
+    arrived = lax.ppermute(first, "rows", [(0, 1)])
+    parent_solution = first - matmul(coupling, arrived, precision)
     return (leaf_solution, parent_solution)
 
 

time: 39.6 us -> 31.5 us (0.80)
  matrix products: 14.9 us -> 10.1 us
  other arithmetic: 3.89 us -> 0.16 us
  local copies, waits for them, and re-layouts: 3.76 us -> 6.64 us
  waiting for transfers between devices: 8.86 us -> 7.1 us
  starting transfers between devices: 7.08 us -> 6.45 us
    dot_general x7, matrix products: 14.9 us -> 10.1 us  [matmul(): jnp.dot(left, right, precision=precision, preferred_element_type=jnp.floa...]
    gather x1 -> x2, local copies, waits for them, and re-layouts: 2.01 us -> 4.42 us  [placed_rows(): taken = jnp.take(pieces, chosen, axis=0, mode='clip')]
    ppermute x2 -> x1, starting transfers between devices: 4.69 us -> 2.39 us  [two_section_solve(): arrived = lax.ppermute(first, 'rows', [(0, 1)])]
    ppermute x1, waiting for transfers between devices: 2.25 us -> 0.27 us  [pair_swap(): return lax.ppermute(block, axis, [(0, 1), (1, 0)])]
    select_n x2 -> x0, other arithmetic: 1.81 us -> none  [two_section_shards(): panel_placed = jnp.take(blocks, order, axis=0).reshape(update_panel.shape)]
    ppermute x0 -> x1, starting transfers between devices: none -> 1.67 us  [two_section_shards(): arrived = lax.ppermute(first, 'rows', [(0, 1)])]
    reshape x0 -> x1, local copies, waits for them, and re-layouts: none -> 1.3 us  [placed_rows(): pieces = product.reshape(-1, ROW_BLOCK, product.shape[1])]
    ppermute x0 -> x1, waiting for transfers between devices: none -> 1.13 us  [two_section_shards(): arrived = lax.ppermute(first, 'rows', [(0, 1)])]
  transfers between devices with their start and end apart: 4 -> 4, of which waited for: 2 -> 3; matrix products, arithmetic and copies ran while one was open for 22% -> 18% of each run, Pallas kernels for 0% -> 0%
where the time goes in v2:
time: 31.5 us; the launch traced here: 31.2 us
  matrix products  10.1 us (32%)
  waiting for transfers between devices  7.1 us (23%)
  local copies, waits for them, and re-layouts  6.64 us (21%)
  starting transfers between devices  6.45 us (20%)
  between operations  0.78 us (2%)
    dot_general x7, matrix products, matmul(): jnp.dot(left, right, precision=precision, preferred_element_type=jnp.floa...  10.1 us
    ppermute x1, waiting for transfers between devices, swapped(): return lax.ppermute(block, axis, route)  5.7 us
    gather x2, local copies, waits for them, and re-layouts, placed_rows(): taken = jnp.take(pieces, chosen, axis=0, mode='clip')  4.42 us
    ppermute x1, starting transfers between devices, two_section_solve(): arrived = lax.ppermute(first, 'rows', [(0, 1)])  2.39 us
    ppermute x1, starting transfers between devices, swapped(): return lax.ppermute(block, axis, route)  2.39 us
    ppermute x1, starting transfers between devices, two_section_shards(): arrived = lax.ppermute(first, 'rows', [(0, 1)])  1.67 us
    reshape x1, local copies, waits for them, and re-layouts, placed_rows(): pieces = product.reshape(-1, ROW_BLOCK, product.shape[1])  1.3 us
    ppermute x1, waiting for transfers between devices, two_section_shards(): arrived = lax.ppermute(first, 'rows', [(0, 1)])  1.13 us
  transfers between devices with their start and end apart: 4, of which 3 were waited for; matrix products, arithmetic and copies ran while one was open for 18% of the time, Pallas kernels for 0%

profile of v2, /device:TPU:0, one launch (start us, length us, event | category | flops | bytes accessed | tf_op | source)
XLA Modules:
  0.0 31.2 jit_solution(13888707618969024709)
XLA Ops:
  0.6 0.0 copy-start
  0.6 0.0 copy-start.4
  0.7 2.1 %fusion.8 = f32[512,256]{1,0:T(8,128)S(1)} fusion(f32[512,256]{1,0:T(8,128)} %param.7, f32[512,1024]{1,0:T(8,128)} %param.6, s32[]{:T(128)S(6)} %select_n.27), kind=kOutput, calls=%fused_computation.13 | convolution fusion | flops 402653184 | bytes 2097156 | tf_op jit(solution)/shard_map/dot_general | solution.py:26
  2.8 2.4 %collective-permute-start = (f32[512,256]{1,0:T(8,128)S(1)}, f32[512,256]{1,0:T(8,128)S(1)}, u32[]{:S(2)}, u32[]{:S(2)}) collective-permute-start(f32[512,256]{1,0:T(8,128)S(1)} %fusion.8), channel_id=1, source_target_pairs={{0,1},{2,3},{4,5},{6,7},{8,9},{10,11},{12,13},{14,15},{16,17},{18,... | collective-permute-start | bytes 1572872 | tf_op jit(solution)/shard_map/ppermute | solution.py:85
  5.2 0.0 copy-done.4
  5.2 0.1 select_reduce_fusion
  5.3 0.1 fusion.17
  5.4 2.6 %fusion.2 = f32[512,512]{1,0:T(8,128)S(1)} fusion(f32[512,1024]{1,0:T(8,128)} %param.6, s32[]{:T(128)S(6)} %select_n.27), kind=kOutput, calls=%fused_computation.7 | convolution fusion | flops 805306368 | bytes 3145732 | tf_op jit(solution)/shard_map/dot_general | solution.py:26
  8.0 0.0 collective-permute-done
  8.0 0.6 %convolution_subtract_fusion = f32[512,256]{1,0:T(8,128)S(1)} fusion(f32[512,256]{1,0:T(8,128)S(1)} %fusion.8, f32[512,512]{1,0:T(8,128)S(1)} %fusion.2, f32[512,256]{1,0:T(8,128)S(1)} %collective-permute-done), kind=kOutput, calls=%fused_computation.3 | convolution fusion | flops 402784256 | bytes 2621440 | tf_op jit(solution)/shard_map/dot_general | solution.py:26
  8.6 0.0 copy-start.1
  8.6 0.8 %copy-done.1 = f32[512,256]{1,0:T(8,128)} copy-done((f32[512,256]{1,0:T(8,128)}, f32[512,256]{1,0:T(8,128)S(1)}, u32[]{:S(2)}) %copy-start.1) | copy-done | bytes 524312
  9.4 0.0 copy-done
  9.4 1.9 %convolution_bitcast_fusion = f32[1024,256]{0,1:T(8,128)S(1)} fusion(f32[512,256]{1,0:T(8,128)S(1)} %convolution_subtract_fusion, f32[1024,512]{1,0:T(8,128)S(1)} %copy-done), kind=kOutput, calls=%fused_computation.2 | convolution fusion | flops 805306368 | bytes 3670016 | tf_op jit(solution)/shard_map/dot_general | solution.py:26
  11.3 1.3 %copy.14 = f32[1024,256]{1,0:T(8,128)} copy(f32[1024,256]{0,1:T(8,128)S(1)} %convolution_bitcast_fusion) | data formatting | bytes 2097152 | tf_op jit(solution)/shard_map/reshape | solution.py:98
  12.6 2.6 %gather_fusion.1 = f32[4,128,256]{2,1,0:T(8,128)} fusion(f32[8,128,256]{2,1,0:T(8,128)} %bitcast.14, s32[1024]{0:T(1024)S(1)} %pad_clamp_fusion), kind=kCustom, calls=%fused_computation.1 | custom fusion | bytes 1048592 | tf_op jit(solution)/shard_map/jit(_take)/gather | solution.py:101
  15.2 0.0 collective-permute-start.1
  15.2 1.8 %gather_fusion = f32[4,128,256]{2,1,0:T(8,128)S(1)} fusion(f32[8,128,256]{2,1,0:T(8,128)} %bitcast.15, s32[1024]{0:T(1024)S(1)} %pad_clamp_fusion.1), kind=kCustom, calls=%fused_computation | custom fusion | bytes 1048592 | tf_op jit(solution)/shard_map/jit(_take)/gather | solution.py:101
  17.0 0.0 copy-start.2
  17.0 0.0 copy-start.3
  17.1 0.3 collective-permute-done.1
  17.3 0.1 bitcast_add_fusion
  17.4 2.4 %collective-permute-start.2 = (f32[512,128]{1,0:T(8,128)S(1)}, f32[512,128]{1,0:T(8,128)S(1)}, u32[]{:S(2)}, u32[]{:S(2)}) collective-permute-start(f32[512,128]{1,0:T(8,128)S(1)} %constant_dynamic-slice_fusion), channel_id=1, source_target_pairs={{0,2},{2,0},{4,6},{6,4},{8,10},{10,8},{12,14},{14,12},{16,18},{18,... | collective-permute-start | bytes 786440 | tf_op jit(solution)/shard_map/ppermute | solution.py:22
  19.8 0.0 copy-done.2
  19.8 1.0 %fusion = f32[512,512]{1,0:T(8,128)S(1)} fusion(f32[512,1024]{1,0:T(8,128)S(1)} %copy-done.2, s32[]{:T(128)S(6)} %select_n.27), kind=kOutput, calls=%fused_computation.5 | convolution fusion | flops 805306368 | bytes 3145732 | tf_op jit(solution)/shard_map/dot_general | solution.py:26
  20.8 5.7 %collective-permute-done.2 = f32[512,128]{1,0:T(8,128)S(1)} collective-permute-done((f32[512,128]{1,0:T(8,128)S(1)}, f32[512,128]{1,0:T(8,128)S(1)}, u32[]{:S(2)}, u32[]{:S(2)}) %collective-permute-start.2) | collective-permute-done | bytes 262176 | tf_op jit(solution)/shard_map/ppermute | solution.py:22
  26.5 0.0 copy-done.3
  26.5 0.6 %fusion.4 = f32[512,128]{1,0:T(8,128)S(1)} fusion(f32[512,1024]{1,0:T(8,128)S(1)} %copy-done.2, s32[]{:T(128)S(6)} %select_n.27, f32[512,128]{1,0:T(8,128)S(1)} %copy-done.3, f32[512,128]{1,0:T(8,128)S(1)} %collective-permute-done.2, f32[512,256]{1,0:T(8,128)S(1)} %bitcast_add_fusion, s32[]{:T(128)S(6)} %select_n.32), kind=kOutput, calls=%fused_computation.9 | convolution fusion | flops 201457664 | bytes 2097160 | tf_op jit(solution)/shard_map/dot_general | solution.py:26
  27.1 1.7 %collective-permute-start.3 = (f32[512,128]{1,0:T(8,128)S(1)}, f32[512,128]{1,0:T(8,128)S(1)}, u32[]{:S(2)}, u32[]{:S(2)}) collective-permute-start(f32[512,128]{1,0:T(8,128)S(1)} %fusion.4), channel_id=1, source_target_pairs={{0,1},{2,3},{4,5},{6,7},{8,9},{10,11},{12,13},{14,15},{16,17},{18,... | collective-permute-start | bytes 786440 | tf_op jit(solution)/shard_map/ppermute | solution.py:125
  28.8 1.1 %collective-permute-done.3 = f32[512,128]{1,0:T(8,128)S(1)} collective-permute-done((f32[512,128]{1,0:T(8,128)S(1)}, f32[512,128]{1,0:T(8,128)S(1)}, u32[]{:S(2)}, u32[]{:S(2)}) %collective-permute-start.3) | collective-permute-done | bytes 262176 | tf_op jit(solution)/shard_map/ppermute | solution.py:125
  30.0 1.3 %convolution_subtract_fusion.1 = f32[512,128]{1,0:T(8,128)} fusion(f32[512,128]{1,0:T(8,128)S(1)} %fusion.4, f32[512,512]{1,0:T(8,128)S(1)} %fusion, f32[512,128]{1,0:T(8,128)S(1)} %collective-permute-done.3), kind=kOutput, calls=%fused_computation.4 | convolution fusion | flops 201392128 | bytes 1835008 | tf_op jit(solution)/shard_map/dot_general | solution.py:26
  (3 shorter events, 0.0 us)
Async XLA Ops:
  0.6 8.8 %copy-start = (f32[1024,512]{1,0:T(8,128)S(1)}, f32[1024,512]{1,0:T(8,128)}, u32[]{:S(2)}) copy-start(f32[1024,512]{1,0:T(8,128)} %param.8) | copy-start | bytes 6291460
  0.6 4.5 %copy-start.4 = (s32[1,8]{1,0:T(1,128)S(1)}, s32[1,8]{1,0:T(1,128)}, u32[]{:S(2)}) copy-start(s32[1,8]{1,0:T(1,128)} %param.9) | copy-start | bytes 100
  2.8 5.2 %collective-permute-start = (f32[512,256]{1,0:T(8,128)S(1)}, f32[512,256]{1,0:T(8,128)S(1)}, u32[]{:S(2)}, u32[]{:S(2)}) collective-permute-start(f32[512,256]{1,0:T(8,128)S(1)} %fusion.8), channel_id=1, source_target_pairs={{0,1},{2,3},{4,5},{6,7},{8,9},{10,11},{12,13},{14,15},{16,17},{18,... | collective-permute-start | bytes 1572872 | tf_op jit(solution)/shard_map/ppermute | solution.py:85
  8.6 0.8 %copy-start.1 = (f32[512,256]{1,0:T(8,128)}, f32[512,256]{1,0:T(8,128)S(1)}, u32[]{:S(2)}) copy-start(f32[512,256]{1,0:T(8,128)S(1)} %convolution_subtract_fusion) | copy-start | bytes 1572868
  15.2 2.1 %collective-permute-start.1 = (f32[512,256]{1,0:T(8,128)}, f32[512,256]{1,0:T(8,128)S(1)}, u32[]{:S(2)}, u32[]{:S(2)}) collective-permute-start(f32[512,256]{1,0:T(8,128)} %bitcast.3), channel_id=1, source_target_pairs={{0,1},{1,0},{2,3},{3,2},{4,5},{5,4},{6,7},{7,6},{8,9},{9,8},{10,11... | collective-permute-start | bytes 1572872 | tf_op jit(solution)/shard_map/ppermute | solution.py:77
  17.0 2.8 %copy-start.2 = (f32[512,1024]{1,0:T(8,128)S(1)}, f32[512,1024]{1,0:T(8,128)}, u32[]{:S(2)}) copy-start(f32[512,1024]{1,0:T(8,128)} %param.10) | copy-start | bytes 6291460
  17.0 9.5 %copy-start.3 = (f32[512,128]{1,0:T(8,128)S(1)}, f32[512,128]{1,0:T(8,128)}, u32[]{:S(2)}) copy-start(f32[512,128]{1,0:T(8,128)} %param.11) | copy-start | bytes 786436
  17.4 9.1 %collective-permute-start.2 = (f32[512,128]{1,0:T(8,128)S(1)}, f32[512,128]{1,0:T(8,128)S(1)}, u32[]{:S(2)}, u32[]{:S(2)}) collective-permute-start(f32[512,128]{1,0:T(8,128)S(1)} %constant_dynamic-slice_fusion), channel_id=1, source_target_pairs={{0,2},{2,0},{4,6},{6,4},{8,10},{10,8},{12,14},{14,12},{16,18},{18,... | collective-permute-start | bytes 786440 | tf_op jit(solution)/shard_map/ppermute | solution.py:22
  27.1 2.8 %collective-permute-start.3 = (f32[512,128]{1,0:T(8,128)S(1)}, f32[512,128]{1,0:T(8,128)S(1)}, u32[]{:S(2)}, u32[]{:S(2)}) collective-permute-start(f32[512,128]{1,0:T(8,128)S(1)} %fusion.4), channel_id=1, source_target_pairs={{0,1},{2,3},{4,5},{6,7},{8,9},{10,11},{12,13},{14,15},{16,17},{18,... | collective-permute-start | bytes 786440 | tf_op jit(solution)/shard_map/ppermute | solution.py:125

commit v3 on v2

--- a/solution.py
+++ b/solution.py
@@ -77,14 +77,13 @@
     return lax.ppermute(block, axis, [(0, 1), (1, 0)])
 
 
-def two_section_solve(factor, right_side, section, precision):
+def two_section_leaf(factor, right_side, section, precision):
     tile_rows = right_side.shape[0]
     diagonal = lax.dynamic_slice_in_dim(factor, section * tile_rows, tile_rows, 1)
-    below = factor[:, :tile_rows]
     first = matmul(diagonal, right_side, precision)
     arrived = lax.ppermute(first, "rows", [(0, 1)])
-    coupling = matmul(diagonal, below, precision)
-    return first - matmul(coupling, arrived, precision)
+    target = right_side - matmul(factor[:, :tile_rows], arrived, precision)
+    return matmul(diagonal, target, precision)
 
 
 def inverse_order(update_blocks):
@@ -95,17 +94,18 @@
 
 
 def placed_rows(product, order, section):
-    pieces = product.reshape(-1, ROW_BLOCK, product.shape[1])
-    per_section = pieces.shape[0] // 2
-    chosen = lax.dynamic_slice_in_dim(order, section * per_section, per_section)
-    taken = jnp.take(pieces, chosen, axis=0, mode="clip")
-    return taken.reshape(-1, product.shape[1])
+    per_section = product.shape[0] // ROW_BLOCK // 2
+    pieces = []
+    for k in range(per_section):
+        block = lax.dynamic_index_in_dim(order, section * per_section + k, keepdims=False)
+        pieces.append(lax.dynamic_slice_in_dim(product, block * ROW_BLOCK, ROW_BLOCK, 0))
+    return jnp.concatenate(pieces, 0)
 
 
 def two_section_shards(leaf_factor, leaf_rhs, update_panel, update_blocks, parent_factor, parent_rhs):
     section = lax.axis_index("rows")
     precision = lax.Precision.HIGH
-    leaf_solution = two_section_solve(leaf_factor, leaf_rhs, section, precision)
+    leaf_solution = two_section_leaf(leaf_factor, leaf_rhs, section, precision)
     order = inverse_order(update_blocks)
     product = matmul(update_panel, leaf_solution, precision)
     other_rows = placed_rows(product, order, 1 - section)

time: 31.5 us -> 33.3 us (1.057)
  between operations: 0.78 us -> 5.85 us
  local copies, waits for them, and re-layouts: 6.64 us -> 1.97 us
  other arithmetic: 0.16 us -> 0.98 us
  waiting for transfers between devices: 7.1 us -> 7.73 us
    gather x2 -> x0, local copies, waits for them, and re-layouts: 4.42 us -> none  [placed_rows(): taken = jnp.take(pieces, chosen, axis=0, mode='clip')]
    reshape x1 -> x0, local copies, waits for them, and re-layouts: 1.3 us -> none  [placed_rows(): pieces = product.reshape(-1, ROW_BLOCK, product.shape[1])]
    concatenate x0 -> x1, other arithmetic: none -> 0.83 us  [placed_rows(): return jnp.concatenate(pieces, 0)]
    dynamic_slice x1 -> x2, local copies, waits for them, and re-layouts: 0.08 us -> 0.83 us  [the longest x1 0.67 us: placed_rows(): lax.dynamic_index_in_dim(order, section * per_section + k, keepdims=False)]
    ppermute x1, waiting for transfers between devices: 0.27 us -> 1.01 us  [pair_swap(): return lax.ppermute(block, axis, [(0, 1), (1, 0)])]
    unnamed x10 -> x13, local copies, waits for them, and re-layouts: 0.81 us -> 1.11 us
  transfers between devices with their start and end apart: 4 -> 4, of which waited for: 3 -> 3; matrix products, arithmetic and copies ran while one was open for 18% -> 9% of each run, Pallas kernels for 0% -> 0%
where the time goes in v3:
time: 33.3 us; the launch traced here: 33.1 us
  matrix products  10.2 us (31%)
  waiting for transfers between devices  7.73 us (23%)
  starting transfers between devices  6.32 us (19%)
  between operations  5.85 us (18%)
  local copies, waits for them, and re-layouts  1.97 us (6%)
  other arithmetic  0.98 us (3%)
    dot_general x7, matrix products, matmul(): jnp.dot(left, right, precision=precision, preferred_element_type=jnp.floa...  10.2 us
    ppermute x1, waiting for transfers between devices, swapped(): return lax.ppermute(block, axis, route)  5.59 us
    ppermute x1, starting transfers between devices, swapped(): return lax.ppermute(block, axis, route)  2.4 us
    ppermute x1, starting transfers between devices, two_section_leaf(): arrived = lax.ppermute(first, 'rows', [(0, 1)])  2.38 us
    ppermute x1, starting transfers between devices, two_section_shards(): arrived = lax.ppermute(first, 'rows', [(0, 1)])  1.54 us
    ppermute x1, waiting for transfers between devices, two_section_shards(): arrived = lax.ppermute(first, 'rows', [(0, 1)])  1.13 us
    unnamed x13, local copies, waits for them, and re-layouts  1.11 us
    ppermute x1, waiting for transfers between devices, pair_swap(): return lax.ppermute(block, axis, [(0, 1), (1, 0)])  1.01 us
  transfers between devices with their start and end apart: 4, of which 3 were waited for; matrix products, arithmetic and copies ran while one was open for 9% of the time, Pallas kernels for 0%

profile of v3, /device:TPU:0, one launch (start us, length us, event | category | flops | bytes accessed | tf_op | source)
XLA Modules:
  0.0 33.1 jit_solution(4630865416413870433)
XLA Ops:
  0.6 0.0 copy-start
  0.6 0.0 copy-start.2
  0.7 0.0 copy-start.5
  0.7 2.9 %fusion.9 = f32[512,256]{1,0:T(8,128)} fusion(f32[512,256]{1,0:T(8,128)} %param.7, f32[512,1024]{1,0:T(8,128)} %param.6, s32[]{:T(128)S(6)} %select_n.70), kind=kOutput, calls=%fused_computation.11 | convolution fusion | flops 402653184 | bytes 2097156 | tf_op jit(solution)/shard_map/dot_general | solution.py:26
  3.6 2.4 %collective-permute-start = (f32[512,256]{1,0:T(8,128)}, f32[512,256]{1,0:T(8,128)S(1)}, u32[]{:S(2)}, u32[]{:S(2)}) collective-permute-start(f32[512,256]{1,0:T(8,128)} %fusion.9), channel_id=1, source_target_pairs={{0,1},{2,3},{4,5},{6,7},{8,9},{10,11},{12,13},{14,15},{16,17},{18,... | collective-permute-start | bytes 1572872 | tf_op jit(solution)/shard_map/ppermute | solution.py:84
  6.0 0.0 copy-done.5
  6.0 0.1 select_reduce_fusion
  6.1 0.7 %fusion.18 = (s32[1]{0:T(128)}, s32[1]{0:T(128)}, s32[1]{0:T(128)}, s32[1]{0:T(128)}, s32[1]{0:T(128)}, /*index=5*/s32[1]{0:T(128)}, s32[1]{0:T(128)}, s32[1]{0:T(128)}) fusion(s32[8]{0:T(128)S(1)} %select_reduce_fusion, s32[]{:T(128)S(6)} %select_n.72, s32[]{:T(128)S(6)} %select_n.86, s32[]{:T(128)S(6)} %select_n.84, s32[]{:T(128)S(6)} %select_n.82, ...), kind=kLoop, calls=%fused_computation.33 | loop fusion | bytes 96 | tf_op jit(solution)/shard_map/jit(dynamic_index_in_dim)/dynamic_slice | solution.py:100
  11.7 0.0 copy-start.1
  11.8 0.0 collective-permute-done
  11.8 0.0 copy-done.2
  11.8 2.0 %fusion = f32[512,256]{1,0:T(8,128)S(1)} fusion(f32[512,256]{1,0:T(8,128)S(1)} %copy-done.2, f32[512,256]{1,0:T(8,128)S(1)} %collective-permute-done, f32[512,1024]{1,0:T(8,128)} %param.6), kind=kOutput, calls=%fused_computation.1 | convolution fusion | flops 402784256 | bytes 2621440 | tf_op jit(solution)/shard_map/dot_general | solution.py:26
  13.7 0.0 copy-done.1
  13.8 0.6 %fusion.7 = f32[512,256]{1,0:T(8,128)S(1)} fusion(f32[512,256]{1,0:T(8,128)S(1)} %fusion, f32[512,1024]{1,0:T(8,128)S(1)} %copy-done.1, s32[]{:T(128)S(6)} %select_n.70), kind=kOutput, calls=%fused_computation.9 | convolution fusion | flops 402653184 | bytes 2097156 | tf_op jit(solution)/shard_map/dot_general | solution.py:26
  14.4 0.0 copy-done
  14.4 0.0 copy-start.3
  14.4 1.9 %fusion.19 = f32[256,1024]{1,0:T(8,128)S(1)} fusion(f32[512,256]{1,0:T(8,128)S(1)} %fusion.7, f32[1024,512]{1,0:T(8,128)S(1)} %copy-done), kind=kOutput, calls=%fused_computation.34 | convolution fusion | flops 805306368 | bytes 3670016 | tf_op jit(solution)/shard_map/dot_general | solution.py:26
  16.3 0.2 dynamic-slice_bitcast_fusion.7
  16.4 0.0 copy-done.3
  16.4 0.8 %pad_maximum_fusion = f32[512,256]{0,1:T(8,128)} fusion(f32[128,256]{0,1:T(8,128)S(1)} %get-tuple-element.7, f32[128,256]{0,1:T(8,128)S(1)} %get-tuple-element.8, f32[128,256]{0,1:T(8,128)S(1)} %get-tuple-element.9, f32[128,256]{0,1:T(8,128)S(1)} %get-tuple-element.10), kind=kLoop, calls=%fused_computation.14 | loop fusion | flops 393216 | bytes 1048576 | tf_op jit(solution)/shard_map/concatenate | solution.py:102
  17.3 0.0 collective-permute-start.1
  17.3 1.1 %copy.9 = f32[512,128]{0,1:T(8,128)S(1)} copy(f32[512,128]{1,0:T(8,128)} %param.11) | data formatting | bytes 524288 | tf_op args[5]
  18.4 0.0 copy-start.4
  18.4 1.0 %collective-permute-done.1 = f32[512,256]{0,1:T(8,128)S(1)} collective-permute-done((f32[512,256]{0,1:T(8,128)}, f32[512,256]{0,1:T(8,128)S(1)}, u32[]{:S(2)}, u32[]{:S(2)}) %collective-permute-start.1) | collective-permute-done | bytes 524320 | tf_op jit(solution)/shard_map/ppermute | solution.py:77
  19.4 0.1 maximum_add_fusion
  19.5 2.4 %collective-permute-start.2 = (f32[512,128]{0,1:T(8,128)S(1)}, f32[512,128]{0,1:T(8,128)S(1)}, u32[]{:S(2)}, u32[]{:S(2)}) collective-permute-start(f32[512,128]{0,1:T(8,128)S(1)} %constant_dynamic-slice_fusion), channel_id=1, source_target_pairs={{0,2},{2,0},{4,6},{6,4},{8,10},{10,8},{12,14},{14,12},{16,18},{18,... | collective-permute-start | bytes 786440 | tf_op jit(solution)/shard_map/ppermute | solution.py:22
  21.9 0.0 copy-done.4
  21.9 1.0 %fusion.1 = f32[512,512]{1,0:T(8,128)S(1)} fusion(f32[512,1024]{1,0:T(8,128)S(1)} %copy-done.4, s32[]{:T(128)S(6)} %select_n.70), kind=kOutput, calls=%fused_computation.3 | convolution fusion | flops 805306368 | bytes 3145732 | tf_op jit(solution)/shard_map/dot_general | solution.py:26
  22.9 5.6 %collective-permute-done.2 = f32[512,128]{0,1:T(8,128)S(1)} collective-permute-done((f32[512,128]{0,1:T(8,128)S(1)}, f32[512,128]{0,1:T(8,128)S(1)}, u32[]{:S(2)}, u32[]{:S(2)}) %collective-permute-start.2) | collective-permute-done | bytes 262176 | tf_op jit(solution)/shard_map/ppermute | solution.py:22
  28.5 0.6 %fusion.4 = f32[512,128]{1,0:T(8,128)S(1)} fusion(f32[512,1024]{1,0:T(8,128)S(1)} %copy-done.4, s32[]{:T(128)S(6)} %select_n.70, f32[512,128]{0,1:T(8,128)S(1)} %copy.9, f32[512,128]{0,1:T(8,128)S(1)} %collective-permute-done.2, f32[512,256]{0,1:T(8,128)S(1)} %maximum_add_fusion, s32[]{:T(128)S(6)} %select_n.89), kind=kOutput, calls=%fused_computation.6 | convolution fusion | flops 201457664 | bytes 2097160 | tf_op jit(solution)/shard_map/dot_general | solution.py:26
  29.1 1.5 %collective-permute-start.3 = (f32[512,128]{1,0:T(8,128)S(1)}, f32[512,128]{1,0:T(8,128)S(1)}, u32[]{:S(2)}, u32[]{:S(2)}) collective-permute-start(f32[512,128]{1,0:T(8,128)S(1)} %fusion.4), channel_id=1, source_target_pairs={{0,1},{2,3},{4,5},{6,7},{8,9},{10,11},{12,13},{14,15},{16,17},{18,... | collective-permute-start | bytes 786440 | tf_op jit(solution)/shard_map/ppermute | solution.py:125
  30.6 1.1 %collective-permute-done.3 = f32[512,128]{1,0:T(8,128)S(1)} collective-permute-done((f32[512,128]{1,0:T(8,128)S(1)}, f32[512,128]{1,0:T(8,128)S(1)}, u32[]{:S(2)}, u32[]{:S(2)}) %collective-permute-start.3) | collective-permute-done | bytes 262176 | tf_op jit(solution)/shard_map/ppermute | solution.py:125
  31.8 1.3 %convolution_subtract_fusion = f32[512,128]{1,0:T(8,128)} fusion(f32[512,128]{1,0:T(8,128)S(1)} %fusion.4, f32[512,512]{1,0:T(8,128)S(1)} %fusion.1, f32[512,128]{1,0:T(8,128)S(1)} %collective-permute-done.3), kind=kOutput, calls=%fused_computation.2 | convolution fusion | flops 201392128 | bytes 1835008 | tf_op jit(solution)/shard_map/dot_general | solution.py:26
  (1 shorter events, 0.0 us)
Async XLA Ops:
  0.6 13.7 %copy-start = (f32[1024,512]{1,0:T(8,128)S(1)}, f32[1024,512]{1,0:T(8,128)}, u32[]{:S(2)}) copy-start(f32[1024,512]{1,0:T(8,128)} %param.8) | copy-start | bytes 6291460
  0.6 11.1 %copy-start.2 = (f32[512,256]{1,0:T(8,128)S(1)}, f32[512,256]{1,0:T(8,128)}, u32[]{:S(2)}) copy-start(f32[512,256]{1,0:T(8,128)} %param.7) | copy-start | bytes 1572868
  0.7 5.3 %copy-start.5 = (s32[1,8]{1,0:T(1,128)S(1)}, s32[1,8]{1,0:T(1,128)}, u32[]{:S(2)}) copy-start(s32[1,8]{1,0:T(1,128)} %param.9) | copy-start | bytes 100
  3.6 8.2 %collective-permute-start = (f32[512,256]{1,0:T(8,128)}, f32[512,256]{1,0:T(8,128)S(1)}, u32[]{:S(2)}, u32[]{:S(2)}) collective-permute-start(f32[512,256]{1,0:T(8,128)} %fusion.9), channel_id=1, source_target_pairs={{0,1},{2,3},{4,5},{6,7},{8,9},{10,11},{12,13},{14,15},{16,17},{18,... | collective-permute-start | bytes 1572872 | tf_op jit(solution)/shard_map/ppermute | solution.py:84
  11.7 2.0 %copy-start.1 = (f32[512,1024]{1,0:T(8,128)S(1)}, f32[512,1024]{1,0:T(8,128)}, u32[]{:S(2)}) copy-start(f32[512,1024]{1,0:T(8,128)} %param.6) | copy-start | bytes 6291460
  14.4 2.1 %copy-start.3 = (f32[512,256]{1,0:T(8,128)}, f32[512,256]{1,0:T(8,128)S(1)}, u32[]{:S(2)}) copy-start(f32[512,256]{1,0:T(8,128)S(1)} %fusion.7) | copy-start | bytes 1572868
  17.3 2.1 %collective-permute-start.1 = (f32[512,256]{0,1:T(8,128)}, f32[512,256]{0,1:T(8,128)S(1)}, u32[]{:S(2)}, u32[]{:S(2)}) collective-permute-start(f32[512,256]{0,1:T(8,128)} %pad_maximum_fusion), channel_id=1, source_target_pairs={{0,1},{1,0},{2,3},{3,2},{4,5},{5,4},{6,7},{7,6},{8,9},{9,8},{10,11... | collective-permute-start | bytes 1572872 | tf_op jit(solution)/shard_map/ppermute | solution.py:77
  18.4 3.5 %copy-start.4 = (f32[512,1024]{1,0:T(8,128)S(1)}, f32[512,1024]{1,0:T(8,128)}, u32[]{:S(2)}) copy-start(f32[512,1024]{1,0:T(8,128)} %param.10) | copy-start | bytes 6291460
  19.5 9.0 %collective-permute-start.2 = (f32[512,128]{0,1:T(8,128)S(1)}, f32[512,128]{0,1:T(8,128)S(1)}, u32[]{:S(2)}, u32[]{:S(2)}) collective-permute-start(f32[512,128]{0,1:T(8,128)S(1)} %constant_dynamic-slice_fusion), channel_id=1, source_target_pairs={{0,2},{2,0},{4,6},{6,4},{8,10},{10,8},{12,14},{14,12},{16,18},{18,... | collective-permute-start | bytes 786440 | tf_op jit(solution)/shard_map/ppermute | solution.py:22
  29.1 2.7 %collective-permute-start.3 = (f32[512,128]{1,0:T(8,128)S(1)}, f32[512,128]{1,0:T(8,128)S(1)}, u32[]{:S(2)}, u32[]{:S(2)}) collective-permute-start(f32[512,128]{1,0:T(8,128)S(1)} %fusion.4), channel_id=1, source_target_pairs={{0,1},{2,3},{4,5},{6,7},{8,9},{10,11},{12,13},{14,15},{16,17},{18,... | collective-permute-start | bytes 786440 | tf_op jit(solution)/shard_map/ppermute | solution.py:125

commit v4 on v3

--- a/solution.py
+++ b/solution.py
@@ -77,13 +77,13 @@
     return lax.ppermute(block, axis, [(0, 1), (1, 0)])
 
 
-def two_section_leaf(factor, right_side, section, precision):
+def two_section_solve(factor, right_side, section, precision):
     tile_rows = right_side.shape[0]
     diagonal = lax.dynamic_slice_in_dim(factor, section * tile_rows, tile_rows, 1)
     first = matmul(diagonal, right_side, precision)
     arrived = lax.ppermute(first, "rows", [(0, 1)])
-    target = right_side - matmul(factor[:, :tile_rows], arrived, precision)
-    return matmul(diagonal, target, precision)
+    coupling = matmul(diagonal, factor[:, :tile_rows], precision)
+    return first - matmul(coupling, arrived, precision)
 
 
 def inverse_order(update_blocks):
@@ -105,7 +105,7 @@
 def two_section_shards(leaf_factor, leaf_rhs, update_panel, update_blocks, parent_factor, parent_rhs):
     section = lax.axis_index("rows")
     precision = lax.Precision.HIGH
-    leaf_solution = two_section_leaf(leaf_factor, leaf_rhs, section, precision)
+    leaf_solution = two_section_solve(leaf_factor, leaf_rhs, section, precision)
     order = inverse_order(update_blocks)
     product = matmul(update_panel, leaf_solution, precision)
     other_rows = placed_rows(product, order, 1 - section)

time: 33.3 us -> 33.1 us (level)
    unnamed x13 -> x9, local copies, waits for them, and re-layouts: 1.11 us -> 1.1 us
  transfers between devices with their start and end apart: 4 -> 4, of which waited for: 3 -> 3; matrix products, arithmetic and copies ran while one was open for 9% -> 16% of each run, Pallas kernels for 0% -> 0%
where the time goes in v4:
time: 33.1 us; the launch traced here: 32.8 us
  matrix products  10 us (30%)
  waiting for transfers between devices  7.73 us (23%)
  starting transfers between devices  6.33 us (19%)
  between operations  5.78 us (17%)
  local copies, waits for them, and re-layouts  1.96 us (6%)
  other arithmetic  0.97 us (3%)
    dot_general x7, matrix products, matmul(): jnp.dot(left, right, precision=precision, preferred_element_type=jnp.floa...  10 us
    ppermute x1, waiting for transfers between devices, swapped(): return lax.ppermute(block, axis, route)  5.59 us
    ppermute x1, starting transfers between devices, two_section_solve(): arrived = lax.ppermute(first, 'rows', [(0, 1)])  2.39 us
    ppermute x1, starting transfers between devices, swapped(): return lax.ppermute(block, axis, route)  2.38 us
    ppermute x1, starting transfers between devices, two_section_shards(): arrived = lax.ppermute(first, 'rows', [(0, 1)])  1.55 us
    ppermute x1, waiting for transfers between devices, two_section_shards(): arrived = lax.ppermute(first, 'rows', [(0, 1)])  1.13 us
    unnamed x9, local copies, waits for them, and re-layouts  1.1 us
    ppermute x1, waiting for transfers between devices, pair_swap(): return lax.ppermute(block, axis, [(0, 1), (1, 0)])  1.01 us
  transfers between devices with their start and end apart: 4, of which 3 were waited for; matrix products, arithmetic and copies ran while one was open for 16% of the time, Pallas kernels for 0%

profile of v4, /device:TPU:0, one launch (start us, length us, event | category | flops | bytes accessed | tf_op | source)
XLA Modules:
  0.0 32.8 jit_solution(10999995118601354406)
XLA Ops:
  0.6 0.0 copy-start
  0.6 0.0 copy-start.3
  0.7 2.1 %fusion.8 = f32[512,256]{1,0:T(8,128)S(1)} fusion(f32[512,256]{1,0:T(8,128)} %param.7, f32[512,1024]{1,0:T(8,128)} %param.6, s32[]{:T(128)S(6)} %select_n.70), kind=kOutput, calls=%fused_computation.10 | convolution fusion | flops 402653184 | bytes 2097156 | tf_op jit(solution)/shard_map/dot_general | solution.py:26
  2.8 2.4 %collective-permute-start = (f32[512,256]{1,0:T(8,128)S(1)}, f32[512,256]{1,0:T(8,128)S(1)}, u32[]{:S(2)}, u32[]{:S(2)}) collective-permute-start(f32[512,256]{1,0:T(8,128)S(1)} %fusion.8), channel_id=1, source_target_pairs={{0,1},{2,3},{4,5},{6,7},{8,9},{10,11},{12,13},{14,15},{16,17},{18,... | collective-permute-start | bytes 1572872 | tf_op jit(solution)/shard_map/ppermute | solution.py:84
  5.2 0.0 copy-done.3
  5.2 0.1 select_reduce_fusion
  5.3 0.7 %fusion.17 = (s32[1]{0:T(128)}, s32[1]{0:T(128)}, s32[1]{0:T(128)}, s32[1]{0:T(128)}, s32[1]{0:T(128)}, /*index=5*/s32[1]{0:T(128)}, s32[1]{0:T(128)}, s32[1]{0:T(128)}) fusion(s32[8]{0:T(128)S(1)} %select_reduce_fusion, s32[]{:T(128)S(6)} %select_n.72, s32[]{:T(128)S(6)} %select_n.86, s32[]{:T(128)S(6)} %select_n.84, s32[]{:T(128)S(6)} %select_n.82, ...), kind=kLoop, calls=%fused_computation.32 | loop fusion | bytes 96 | tf_op jit(solution)/shard_map/jit(dynamic_index_in_dim)/dynamic_slice | solution.py:100
  10.9 2.5 %fusion.2 = f32[512,512]{1,0:T(8,128)S(1)} fusion(f32[512,1024]{1,0:T(8,128)} %param.6, s32[]{:T(128)S(6)} %select_n.70), kind=kOutput, calls=%fused_computation.4 | convolution fusion | flops 805306368 | bytes 3145732 | tf_op jit(solution)/shard_map/dot_general | solution.py:26
  13.5 0.0 collective-permute-done
  13.5 0.6 %convolution_subtract_fusion = f32[512,256]{1,0:T(8,128)S(1)} fusion(f32[512,256]{1,0:T(8,128)S(1)} %fusion.8, f32[512,512]{1,0:T(8,128)S(1)} %fusion.2, f32[512,256]{1,0:T(8,128)S(1)} %collective-permute-done), kind=kOutput, calls=%fused_computation | convolution fusion | flops 402784256 | bytes 2621440 | tf_op jit(solution)/shard_map/dot_general | solution.py:26
  14.1 0.0 copy-done
  14.1 0.0 copy-start.1
  14.1 1.9 %fusion.18 = f32[256,1024]{1,0:T(8,128)S(1)} fusion(f32[512,256]{1,0:T(8,128)S(1)} %convolution_subtract_fusion, f32[1024,512]{1,0:T(8,128)S(1)} %copy-done), kind=kOutput, calls=%fused_computation.33 | convolution fusion | flops 805306368 | bytes 3670016 | tf_op jit(solution)/shard_map/dot_general | solution.py:26
  16.0 0.2 dynamic-slice_bitcast_fusion.7
  16.1 0.0 copy-done.1
  16.2 0.8 %pad_maximum_fusion = f32[512,256]{0,1:T(8,128)} fusion(f32[128,256]{0,1:T(8,128)S(1)} %get-tuple-element.7, f32[128,256]{0,1:T(8,128)S(1)} %get-tuple-element.8, f32[128,256]{0,1:T(8,128)S(1)} %get-tuple-element.9, f32[128,256]{0,1:T(8,128)S(1)} %get-tuple-element.10), kind=kLoop, calls=%fused_computation.13 | loop fusion | flops 393216 | bytes 1048576 | tf_op jit(solution)/shard_map/concatenate | solution.py:102
  17.0 0.0 collective-permute-start.1
  17.0 1.1 %copy.9 = f32[512,128]{0,1:T(8,128)S(1)} copy(f32[512,128]{1,0:T(8,128)} %param.11) | data formatting | bytes 524288 | tf_op args[5]
  18.1 0.0 copy-start.2
  18.1 1.0 %collective-permute-done.1 = f32[512,256]{0,1:T(8,128)S(1)} collective-permute-done((f32[512,256]{0,1:T(8,128)}, f32[512,256]{0,1:T(8,128)S(1)}, u32[]{:S(2)}, u32[]{:S(2)}) %collective-permute-start.1) | collective-permute-done | bytes 524320 | tf_op jit(solution)/shard_map/ppermute | solution.py:77
  19.1 0.1 maximum_add_fusion
  19.2 2.4 %collective-permute-start.2 = (f32[512,128]{0,1:T(8,128)S(1)}, f32[512,128]{0,1:T(8,128)S(1)}, u32[]{:S(2)}, u32[]{:S(2)}) collective-permute-start(f32[512,128]{0,1:T(8,128)S(1)} %constant_dynamic-slice_fusion), channel_id=1, source_target_pairs={{0,2},{2,0},{4,6},{6,4},{8,10},{10,8},{12,14},{14,12},{16,18},{18,... | collective-permute-start | bytes 786440 | tf_op jit(solution)/shard_map/ppermute | solution.py:22
  21.6 0.0 copy-done.2
  21.6 1.0 %fusion = f32[512,512]{1,0:T(8,128)S(1)} fusion(f32[512,1024]{1,0:T(8,128)S(1)} %copy-done.2, s32[]{:T(128)S(6)} %select_n.70), kind=kOutput, calls=%fused_computation.2 | convolution fusion | flops 805306368 | bytes 3145732 | tf_op jit(solution)/shard_map/dot_general | solution.py:26
  22.6 5.6 %collective-permute-done.2 = f32[512,128]{0,1:T(8,128)S(1)} collective-permute-done((f32[512,128]{0,1:T(8,128)S(1)}, f32[512,128]{0,1:T(8,128)S(1)}, u32[]{:S(2)}, u32[]{:S(2)}) %collective-permute-start.2) | collective-permute-done | bytes 262176 | tf_op jit(solution)/shard_map/ppermute | solution.py:22
  28.2 0.6 %fusion.4 = f32[512,128]{1,0:T(8,128)S(1)} fusion(f32[512,1024]{1,0:T(8,128)S(1)} %copy-done.2, s32[]{:T(128)S(6)} %select_n.70, f32[512,128]{0,1:T(8,128)S(1)} %copy.9, f32[512,128]{0,1:T(8,128)S(1)} %collective-permute-done.2, f32[512,256]{0,1:T(8,128)S(1)} %maximum_add_fusion, s32[]{:T(128)S(6)} %select_n.89), kind=kOutput, calls=%fused_computation.6 | convolution fusion | flops 201457664 | bytes 2097160 | tf_op jit(solution)/shard_map/dot_general | solution.py:26
  28.8 1.6 %collective-permute-start.3 = (f32[512,128]{1,0:T(8,128)S(1)}, f32[512,128]{1,0:T(8,128)S(1)}, u32[]{:S(2)}, u32[]{:S(2)}) collective-permute-start(f32[512,128]{1,0:T(8,128)S(1)} %fusion.4), channel_id=1, source_target_pairs={{0,1},{2,3},{4,5},{6,7},{8,9},{10,11},{12,13},{14,15},{16,17},{18,... | collective-permute-start | bytes 786440 | tf_op jit(solution)/shard_map/ppermute | solution.py:125
  30.3 1.1 %collective-permute-done.3 = f32[512,128]{1,0:T(8,128)S(1)} collective-permute-done((f32[512,128]{1,0:T(8,128)S(1)}, f32[512,128]{1,0:T(8,128)S(1)}, u32[]{:S(2)}, u32[]{:S(2)}) %collective-permute-start.3) | collective-permute-done | bytes 262176 | tf_op jit(solution)/shard_map/ppermute | solution.py:125
  31.5 1.3 %convolution_subtract_fusion.1 = f32[512,128]{1,0:T(8,128)} fusion(f32[512,128]{1,0:T(8,128)S(1)} %fusion.4, f32[512,512]{1,0:T(8,128)S(1)} %fusion, f32[512,128]{1,0:T(8,128)S(1)} %collective-permute-done.3), kind=kOutput, calls=%fused_computation.1 | convolution fusion | flops 201392128 | bytes 1835008 | tf_op jit(solution)/shard_map/dot_general | solution.py:26
  (1 shorter events, 0.0 us)
Async XLA Ops:
  0.6 13.4 %copy-start = (f32[1024,512]{1,0:T(8,128)S(1)}, f32[1024,512]{1,0:T(8,128)}, u32[]{:S(2)}) copy-start(f32[1024,512]{1,0:T(8,128)} %param.8) | copy-start | bytes 6291460
  0.6 4.5 %copy-start.3 = (s32[1,8]{1,0:T(1,128)S(1)}, s32[1,8]{1,0:T(1,128)}, u32[]{:S(2)}) copy-start(s32[1,8]{1,0:T(1,128)} %param.9) | copy-start | bytes 100
  2.8 10.7 %collective-permute-start = (f32[512,256]{1,0:T(8,128)S(1)}, f32[512,256]{1,0:T(8,128)S(1)}, u32[]{:S(2)}, u32[]{:S(2)}) collective-permute-start(f32[512,256]{1,0:T(8,128)S(1)} %fusion.8), channel_id=1, source_target_pairs={{0,1},{2,3},{4,5},{6,7},{8,9},{10,11},{12,13},{14,15},{16,17},{18,... | collective-permute-start | bytes 1572872 | tf_op jit(solution)/shard_map/ppermute | solution.py:84
  14.1 2.1 %copy-start.1 = (f32[512,256]{1,0:T(8,128)}, f32[512,256]{1,0:T(8,128)S(1)}, u32[]{:S(2)}) copy-start(f32[512,256]{1,0:T(8,128)S(1)} %convolution_subtract_fusion) | copy-start | bytes 1572868
  17.0 2.1 %collective-permute-start.1 = (f32[512,256]{0,1:T(8,128)}, f32[512,256]{0,1:T(8,128)S(1)}, u32[]{:S(2)}, u32[]{:S(2)}) collective-permute-start(f32[512,256]{0,1:T(8,128)} %pad_maximum_fusion), channel_id=1, source_target_pairs={{0,1},{1,0},{2,3},{3,2},{4,5},{5,4},{6,7},{7,6},{8,9},{9,8},{10,11... | collective-permute-start | bytes 1572872 | tf_op jit(solution)/shard_map/ppermute | solution.py:77
  18.1 3.5 %copy-start.2 = (f32[512,1024]{1,0:T(8,128)S(1)}, f32[512,1024]{1,0:T(8,128)}, u32[]{:S(2)}) copy-start(f32[512,1024]{1,0:T(8,128)} %param.10) | copy-start | bytes 6291460
  19.2 9.0 %collective-permute-start.2 = (f32[512,128]{0,1:T(8,128)S(1)}, f32[512,128]{0,1:T(8,128)S(1)}, u32[]{:S(2)}, u32[]{:S(2)}) collective-permute-start(f32[512,128]{0,1:T(8,128)S(1)} %constant_dynamic-slice_fusion), channel_id=1, source_target_pairs={{0,2},{2,0},{4,6},{6,4},{8,10},{10,8},{12,14},{14,12},{16,18},{18,... | collective-permute-start | bytes 786440 | tf_op jit(solution)/shard_map/ppermute | solution.py:22
  28.8 2.7 %collective-permute-start.3 = (f32[512,128]{1,0:T(8,128)S(1)}, f32[512,128]{1,0:T(8,128)S(1)}, u32[]{:S(2)}, u32[]{:S(2)}) collective-permute-start(f32[512,128]{1,0:T(8,128)S(1)} %fusion.4), channel_id=1, source_target_pairs={{0,1},{2,3},{4,5},{6,7},{8,9},{10,11},{12,13},{14,15},{16,17},{18,... | collective-permute-start | bytes 786440 | tf_op jit(solution)/shard_map/ppermute | solution.py:125

commit v5 on v4

--- a/solution.py
+++ b/solution.py
@@ -93,24 +93,17 @@
     return jnp.sum(jnp.where(hits, jnp.arange(count)[:, None], 0), axis=0)
 
 
-def placed_rows(product, order, section):
-    per_section = product.shape[0] // ROW_BLOCK // 2
-    pieces = []
-    for k in range(per_section):
-        block = lax.dynamic_index_in_dim(order, section * per_section + k, keepdims=False)
-        pieces.append(lax.dynamic_slice_in_dim(product, block * ROW_BLOCK, ROW_BLOCK, 0))
-    return jnp.concatenate(pieces, 0)
-
-
 def two_section_shards(leaf_factor, leaf_rhs, update_panel, update_blocks, parent_factor, parent_rhs):
     section = lax.axis_index("rows")
     precision = lax.Precision.HIGH
     leaf_solution = two_section_solve(leaf_factor, leaf_rhs, section, precision)
-    order = inverse_order(update_blocks)
-    product = matmul(update_panel, leaf_solution, precision)
-    other_rows = placed_rows(product, order, 1 - section)
-    arrived_rows = pair_swap(other_rows, "rows")
-    chip_sum = placed_rows(product, order, section) + arrived_rows
+    blocks = update_panel.reshape(-1, ROW_BLOCK, update_panel.shape[1])
+    panel_placed = jnp.take(blocks, inverse_order(update_blocks), axis=0, mode="clip")
+    placed = matmul(panel_placed.reshape(update_panel.shape), leaf_solution, precision)
+    rows_half = placed.shape[0] // 2
+    own_rows = lax.dynamic_slice_in_dim(placed, section * rows_half, rows_half, 0)
+    other_rows = lax.dynamic_slice_in_dim(placed, (1 - section) * rows_half, rows_half, 0)
+    chip_sum = own_rows + pair_swap(other_rows, "rows")
     column_half = parent_rhs.shape[1]
     sibling = lax.axis_index("leaf") % 2
     kept = lax.dynamic_slice_in_dim(chip_sum, sibling * column_half, column_half, 1)

time: 33.1 us -> 29.6 us (0.89)
  between operations: 5.78 us -> 0.77 us
  waiting for transfers between devices: 7.73 us -> 8.96 us
  local copies, waits for them, and re-layouts: 1.96 us -> 2.92 us
  matrix products: 10 us -> 9.27 us
    gather x0 -> x1, local copies, waits for them, and re-layouts: none -> 2.03 us  [two_section_shards(): jnp.take(blocks, inverse_order(update_blocks), axis=0, mode='clip')]
    ppermute x1, waiting for transfers between devices: 1.01 us -> 2.24 us  [pair_swap(): return lax.ppermute(block, axis, [(0, 1), (1, 0)])]
    unnamed x9 -> x12, local copies, waits for them, and re-layouts: 1.1 us -> 0.03 us
    add x1, other arithmetic: 0.06 us -> 1.11 us  [two_section_shards(): chip_sum = own_rows + pair_swap(other_rows, 'rows')]
    concatenate x1 -> x0, other arithmetic: 0.83 us -> none  [placed_rows(): return jnp.concatenate(pieces, 0)]
    dot_general x7, matrix products: 10 us -> 9.27 us  [matmul(): jnp.dot(left, right, precision=precision, preferred_element_type=jnp.floa...]
    dynamic_slice x2 -> x1, local copies, waits for them, and re-layouts: 0.83 us -> 0.83 us  [two_section_shards(): lax.dynamic_slice_in_dim(placed, (1 - section) * rows_half, rows_half, 0)]
  transfers between devices with their start and end apart: 4 -> 4, of which waited for: 3 -> 3; matrix products, arithmetic and copies ran while one was open for 16% -> 20% of each run, Pallas kernels for 0% -> 0%
where the time goes in v5:
time: 29.6 us; the launch traced here: 29.4 us
  matrix products  9.27 us (31%)
  waiting for transfers between devices  8.96 us (30%)
  starting transfers between devices  6.31 us (21%)
  local copies, waits for them, and re-layouts  2.92 us (10%)
  other arithmetic  1.2 us (4%)
  between operations  0.77 us (3%)
    dot_general x7, matrix products, matmul(): jnp.dot(left, right, precision=precision, preferred_element_type=jnp.floa...  9.27 us
    ppermute x1, waiting for transfers between devices, swapped(): return lax.ppermute(block, axis, route)  5.59 us
    ppermute x1, starting transfers between devices, two_section_solve(): arrived = lax.ppermute(first, 'rows', [(0, 1)])  2.39 us
    ppermute x1, starting transfers between devices, swapped(): return lax.ppermute(block, axis, route)  2.38 us
    ppermute x1, waiting for transfers between devices, pair_swap(): return lax.ppermute(block, axis, [(0, 1), (1, 0)])  2.24 us
    gather x1, local copies, waits for them, and re-layouts, two_section_shards(): jnp.take(blocks, inverse_order(update_blocks), axis=0, mode='clip')  2.03 us
    ppermute x1, starting transfers between devices, two_section_shards(): arrived = lax.ppermute(first, 'rows', [(0, 1)])  1.54 us
    ppermute x1, waiting for transfers between devices, two_section_shards(): arrived = lax.ppermute(first, 'rows', [(0, 1)])  1.13 us
  transfers between devices with their start and end apart: 4, of which 3 were waited for; matrix products, arithmetic and copies ran while one was open for 20% of the time, Pallas kernels for 0%

profile of v5, /device:TPU:0, one launch (start us, length us, event | category | flops | bytes accessed | tf_op | source)
XLA Modules:
  0.0 29.4 jit_solution(9983037614326404194)
XLA Ops:
  0.6 0.0 copy-start
  0.6 0.0 copy-start.5
  0.7 2.1 %fusion.8 = f32[512,256]{1,0:T(8,128)S(1)} fusion(f32[512,256]{1,0:T(8,128)} %param.7, f32[512,1024]{1,0:T(8,128)} %param.6, s32[]{:T(128)S(6)} %select_n.25), kind=kOutput, calls=%fused_computation.11 | convolution fusion | flops 402653184 | bytes 2097156 | tf_op jit(solution)/shard_map/dot_general | solution.py:26
  2.8 2.4 %collective-permute-start = (f32[512,256]{1,0:T(8,128)S(1)}, f32[512,256]{1,0:T(8,128)S(1)}, u32[]{:S(2)}, u32[]{:S(2)}) collective-permute-start(f32[512,256]{1,0:T(8,128)S(1)} %fusion.8), channel_id=1, source_target_pairs={{0,1},{2,3},{4,5},{6,7},{8,9},{10,11},{12,13},{14,15},{16,17},{18,... | collective-permute-start | bytes 1572872 | tf_op jit(solution)/shard_map/ppermute | solution.py:84
  5.2 0.0 copy-done.5
  5.2 0.1 select_reduce_fusion
  5.3 0.0 copy-done
  5.3 2.0 %gather_fusion = f32[8,128,512]{2,1,0:T(8,128)} fusion(f32[8,128,512]{2,1,0:T(8,128)S(1)} %bitcast.10, s32[1024]{0:T(1024)S(1)} %pad_clamp_fusion), kind=kCustom, calls=%fused_computation | custom fusion | bytes 4194336 | tf_op jit(solution)/shard_map/jit(_take)/gather | solution.py:101
  7.3 0.0 copy-start.1
  7.3 2.7 %fusion.2 = f32[512,512]{1,0:T(8,128)S(1)} fusion(f32[512,1024]{1,0:T(8,128)} %param.6, s32[]{:T(128)S(6)} %select_n.25), kind=kOutput, calls=%fused_computation.5 | convolution fusion | flops 805306368 | bytes 3145732 | tf_op jit(solution)/shard_map/dot_general | solution.py:26
  10.0 0.0 collective-permute-done
  10.0 0.6 %convolution_subtract_fusion = f32[512,256]{1,0:T(8,128)S(1)} fusion(f32[512,256]{1,0:T(8,128)S(1)} %fusion.8, f32[512,512]{1,0:T(8,128)S(1)} %fusion.2, f32[512,256]{1,0:T(8,128)S(1)} %collective-permute-done), kind=kOutput, calls=%fused_computation.1 | convolution fusion | flops 402784256 | bytes 2621440 | tf_op jit(solution)/shard_map/dot_general | solution.py:26
  10.6 0.0 copy-start.2
  10.6 0.0 copy-done.1
  10.6 1.0 %fusion.17 = f32[1024,256]{1,0:T(8,128)S(1)} fusion(f32[1024,512]{1,0:T(8,128)S(1)} %bitcast.11, f32[512,256]{1,0:T(8,128)S(1)} %convolution_subtract_fusion), kind=kOutput, calls=%fused_computation.26 | convolution fusion | flops 805306368 | bytes 3670016 | tf_op jit(solution)/shard_map/dot_general | solution.py:26
  11.6 0.8 %constant_dynamic-slice_fusion.1 = f32[512,256]{1,0:T(8,128)} fusion(f32[1024,256]{1,0:T(8,128)S(1)} %fusion.17, s32[]{:T(128)S(6)} %select_n.27), kind=kLoop, calls=%fused_computation.22 | loop fusion | bytes 1048580 | tf_op jit(solution)/shard_map/dynamic_slice | solution.py:105
  12.5 0.0 copy-done.2
  12.5 0.0 collective-permute-start.1
  12.5 0.0 copy-start.3
  12.5 0.0 copy-start.4
  12.5 2.2 %collective-permute-done.1 = f32[512,256]{1,0:T(8,128)} collective-permute-done((f32[512,256]{1,0:T(8,128)}, f32[512,256]{1,0:T(8,128)}, u32[]{:S(2)}, u32[]{:S(2)}) %collective-permute-start.1) | collective-permute-done | bytes 524320 | tf_op jit(solution)/shard_map/ppermute | solution.py:77
  14.7 1.1 %dynamic-slice_add_fusion = f32[512,256]{1,0:T(8,128)S(1)} fusion(f32[512,256]{1,0:T(8,128)} %collective-permute-done.1, f32[1024,256]{1,0:T(8,128)S(1)} %fusion.17, s32[]{:T(128)S(6)} %select_n.25), kind=kLoop, calls=%fused_computation.13 | loop fusion | flops 131072 | bytes 1572868 | tf_op jit(solution)/shard_map/add | solution.py:106
  15.9 2.4 %collective-permute-start.2 = (f32[512,128]{1,0:T(8,128)S(1)}, f32[512,128]{1,0:T(8,128)S(1)}, u32[]{:S(2)}, u32[]{:S(2)}) collective-permute-start(f32[512,128]{1,0:T(8,128)S(1)} %constant_dynamic-slice_fusion), channel_id=1, source_target_pairs={{0,2},{2,0},{4,6},{6,4},{8,10},{10,8},{12,14},{14,12},{16,18},{18,... | collective-permute-start | bytes 786440 | tf_op jit(solution)/shard_map/ppermute | solution.py:22
  18.3 0.0 copy-done.3
  18.3 1.0 %fusion = f32[512,512]{1,0:T(8,128)S(1)} fusion(f32[512,1024]{1,0:T(8,128)S(1)} %copy-done.3, s32[]{:T(128)S(6)} %select_n.25), kind=kOutput, calls=%fused_computation.3 | convolution fusion | flops 805306368 | bytes 3145732 | tf_op jit(solution)/shard_map/dot_general | solution.py:26
  19.3 5.6 %collective-permute-done.2 = f32[512,128]{1,0:T(8,128)S(1)} collective-permute-done((f32[512,128]{1,0:T(8,128)S(1)}, f32[512,128]{1,0:T(8,128)S(1)}, u32[]{:S(2)}, u32[]{:S(2)}) %collective-permute-start.2) | collective-permute-done | bytes 262176 | tf_op jit(solution)/shard_map/ppermute | solution.py:22
  24.9 0.0 copy-done.4
  24.9 0.6 %fusion.4 = f32[512,128]{1,0:T(8,128)S(1)} fusion(f32[512,1024]{1,0:T(8,128)S(1)} %copy-done.3, s32[]{:T(128)S(6)} %select_n.25, f32[512,128]{1,0:T(8,128)S(1)} %copy-done.4, f32[512,128]{1,0:T(8,128)S(1)} %collective-permute-done.2, f32[512,256]{1,0:T(8,128)S(1)} %dynamic-slice_add_fusion, s32[]{:T(128)S(6)} %select_n.29), kind=kOutput, calls=%fused_computation.7 | convolution fusion | flops 201457664 | bytes 2097160 | tf_op jit(solution)/shard_map/dot_general | solution.py:26
  25.5 1.5 %collective-permute-start.3 = (f32[512,128]{1,0:T(8,128)S(1)}, f32[512,128]{1,0:T(8,128)S(1)}, u32[]{:S(2)}, u32[]{:S(2)}) collective-permute-start(f32[512,128]{1,0:T(8,128)S(1)} %fusion.4), channel_id=1, source_target_pairs={{0,1},{2,3},{4,5},{6,7},{8,9},{10,11},{12,13},{14,15},{16,17},{18,... | collective-permute-start | bytes 786440 | tf_op jit(solution)/shard_map/ppermute | solution.py:118
  27.0 1.1 %collective-permute-done.3 = f32[512,128]{1,0:T(8,128)S(1)} collective-permute-done((f32[512,128]{1,0:T(8,128)S(1)}, f32[512,128]{1,0:T(8,128)S(1)}, u32[]{:S(2)}, u32[]{:S(2)}) %collective-permute-start.3) | collective-permute-done | bytes 262176 | tf_op jit(solution)/shard_map/ppermute | solution.py:118
  28.1 1.3 %convolution_subtract_fusion.1 = f32[512,128]{1,0:T(8,128)} fusion(f32[512,128]{1,0:T(8,128)S(1)} %fusion.4, f32[512,512]{1,0:T(8,128)S(1)} %fusion, f32[512,128]{1,0:T(8,128)S(1)} %collective-permute-done.3), kind=kOutput, calls=%fused_computation.2 | convolution fusion | flops 201392128 | bytes 1835008 | tf_op jit(solution)/shard_map/dot_general | solution.py:26
  (2 shorter events, 0.0 us)
Async XLA Ops:
  0.6 4.6 %copy-start = (f32[1024,512]{1,0:T(8,128)S(1)}, f32[1024,512]{1,0:T(8,128)}, u32[]{:S(2)}) copy-start(f32[1024,512]{1,0:T(8,128)} %param.8) | copy-start | bytes 6291460
  0.6 4.5 %copy-start.5 = (s32[1,8]{1,0:T(1,128)S(1)}, s32[1,8]{1,0:T(1,128)}, u32[]{:S(2)}) copy-start(s32[1,8]{1,0:T(1,128)} %param.9) | copy-start | bytes 100
  2.8 7.2 %collective-permute-start = (f32[512,256]{1,0:T(8,128)S(1)}, f32[512,256]{1,0:T(8,128)S(1)}, u32[]{:S(2)}, u32[]{:S(2)}) collective-permute-start(f32[512,256]{1,0:T(8,128)S(1)} %fusion.8), channel_id=1, source_target_pairs={{0,1},{2,3},{4,5},{6,7},{8,9},{10,11},{12,13},{14,15},{16,17},{18,... | collective-permute-start | bytes 1572872 | tf_op jit(solution)/shard_map/ppermute | solution.py:84
  7.3 3.3 %copy-start.1 = (f32[8,128,512]{2,1,0:T(8,128)S(1)}, f32[8,128,512]{2,1,0:T(8,128)}, u32[]{:S(2)}) copy-start(f32[8,128,512]{2,1,0:T(8,128)} %gather_fusion) | copy-start | bytes 6291460
  10.6 1.9 %copy-start.2 = (f32[512,256]{1,0:T(8,128)}, f32[512,256]{1,0:T(8,128)S(1)}, u32[]{:S(2)}) copy-start(f32[512,256]{1,0:T(8,128)S(1)} %convolution_subtract_fusion) | copy-start | bytes 1572868
  12.5 2.3 %collective-permute-start.1 = (f32[512,256]{1,0:T(8,128)}, f32[512,256]{1,0:T(8,128)}, u32[]{:S(2)}, u32[]{:S(2)}) collective-permute-start(f32[512,256]{1,0:T(8,128)} %constant_dynamic-slice_fusion.1), channel_id=1, source_target_pairs={{0,1},{1,0},{2,3},{3,2},{4,5},{5,4},{6,7},{7,6},{8,9},{9,8},{10,11... | collective-permute-start | bytes 1572872 | tf_op jit(solution)/shard_map/ppermute | solution.py:77
  12.5 5.8 %copy-start.3 = (f32[512,1024]{1,0:T(8,128)S(1)}, f32[512,1024]{1,0:T(8,128)}, u32[]{:S(2)}) copy-start(f32[512,1024]{1,0:T(8,128)} %param.10) | copy-start | bytes 6291460
  12.5 12.4 %copy-start.4 = (f32[512,128]{1,0:T(8,128)S(1)}, f32[512,128]{1,0:T(8,128)}, u32[]{:S(2)}) copy-start(f32[512,128]{1,0:T(8,128)} %param.11) | copy-start | bytes 786436
  15.9 9.0 %collective-permute-start.2 = (f32[512,128]{1,0:T(8,128)S(1)}, f32[512,128]{1,0:T(8,128)S(1)}, u32[]{:S(2)}, u32[]{:S(2)}) collective-permute-start(f32[512,128]{1,0:T(8,128)S(1)} %constant_dynamic-slice_fusion), channel_id=1, source_target_pairs={{0,2},{2,0},{4,6},{6,4},{8,10},{10,8},{12,14},{14,12},{16,18},{18,... | collective-permute-start | bytes 786440 | tf_op jit(solution)/shard_map/ppermute | solution.py:22
  25.5 2.7 %collective-permute-start.3 = (f32[512,128]{1,0:T(8,128)S(1)}, f32[512,128]{1,0:T(8,128)S(1)}, u32[]{:S(2)}, u32[]{:S(2)}) collective-permute-start(f32[512,128]{1,0:T(8,128)S(1)} %fusion.4), channel_id=1, source_target_pairs={{0,1},{2,3},{4,5},{6,7},{8,9},{10,11},{12,13},{14,15},{16,17},{18,... | collective-permute-start | bytes 786440 | tf_op jit(solution)/shard_map/ppermute | solution.py:118

commit v6 on v5

--- a/solution.py
+++ b/solution.py
@@ -77,12 +77,18 @@
     return lax.ppermute(block, axis, [(0, 1), (1, 0)])
 
 
+def lower_coupling(factor, diagonal, section, precision):
+    tile_rows = diagonal.shape[0]
+    below = jnp.where(section > 0, factor[:, :tile_rows], jnp.zeros_like(diagonal))
+    return matmul(diagonal, below, precision)
+
+
 def two_section_solve(factor, right_side, section, precision):
     tile_rows = right_side.shape[0]
     diagonal = lax.dynamic_slice_in_dim(factor, section * tile_rows, tile_rows, 1)
     first = matmul(diagonal, right_side, precision)
-    arrived = lax.ppermute(first, "rows", [(0, 1)])
-    coupling = matmul(diagonal, factor[:, :tile_rows], precision)
+    arrived = pair_swap(first, "rows")
+    coupling = lower_coupling(factor, diagonal, section, precision)
     return first - matmul(coupling, arrived, precision)
 
 
@@ -110,12 +116,12 @@
     sent = lax.dynamic_slice_in_dim(chip_sum, (1 - sibling) * column_half, column_half, 1)
     tile_rows = parent_rhs.shape[0]
     diagonal = lax.dynamic_slice_in_dim(parent_factor, section * tile_rows, tile_rows, 1)
-    coupling = matmul(diagonal, parent_factor[:, :tile_rows], precision)
+    coupling = lower_coupling(parent_factor, diagonal, section, precision)
     arrived = swapped(sent, "leaf", 0)
     arrived, coupling = lax.optimization_barrier((arrived, coupling))
     pending = parent_rhs - (kept + arrived)
     first = matmul(diagonal, pending, precision)
-    arrived = lax.ppermute(first, "rows", [(0, 1)])
+    arrived = pair_swap(first, "rows")
     parent_solution = first - matmul(coupling, arrived, precision)
     return (leaf_solution, parent_solution)
 

time: 29.6 us -> 27.2 us (0.919)
  starting transfers between devices: 6.31 us -> 3.34 us
  waiting for transfers between devices: 8.96 us -> 9.52 us
    ppermute x2 -> x0, starting transfers between devices: 3.93 us -> none  [the longest x1 2.39 us: two_section_solve(): arrived = lax.ppermute(first, 'rows', [(0, 1)])]
    ppermute x1 -> x3, waiting for transfers between devices: 2.24 us -> 3.72 us  [pair_swap(): return lax.ppermute(block, axis, [(0, 1), (1, 0)])]
    ppermute x2 -> x0, waiting for transfers between devices: 1.13 us -> none  [the longest x1 1.13 us: two_section_shards(): arrived = lax.ppermute(first, 'rows', [(0, 1)])]
    ppermute x1 -> x3, starting transfers between devices: 0.01 us -> 0.64 us  [pair_swap(): return lax.ppermute(block, axis, [(0, 1), (1, 0)])]
    ppermute x1, starting transfers between devices: 2.38 us -> 2.7 us  [swapped(): return lax.ppermute(block, axis, route)]
  transfers between devices with their start and end apart: 4 -> 4, of which waited for: 3 -> 3; matrix products, arithmetic and copies ran while one was open for 20% -> 22% of each run, Pallas kernels for 0% -> 0%
where the time goes in v6:
time: 27.2 us; the launch traced here: 27 us
  waiting for transfers between devices  9.52 us (35%)
  matrix products  9.29 us (34%)
  starting transfers between devices  3.34 us (12%)
  local copies, waits for them, and re-layouts  2.92 us (11%)
  other arithmetic  1.2 us (4%)
  between operations  0.75 us (3%)
    dot_general x7, matrix products, matmul(): jnp.dot(left, right, precision=precision, preferred_element_type=jnp.floa...  9.29 us
    ppermute x1, waiting for transfers between devices, swapped(): return lax.ppermute(block, axis, route)  5.8 us
    ppermute x3, waiting for transfers between devices, pair_swap(): return lax.ppermute(block, axis, [(0, 1), (1, 0)])  3.72 us
    ppermute x1, starting transfers between devices, swapped(): return lax.ppermute(block, axis, route)  2.7 us
    gather x1, local copies, waits for them, and re-layouts, two_section_shards(): jnp.take(blocks, inverse_order(update_blocks), axis=0, mode='clip')  2.03 us
    add x1, other arithmetic, two_section_shards(): chip_sum = own_rows + pair_swap(other_rows, 'rows')  1.11 us
    dynamic_slice x1, local copies, waits for them, and re-layouts, two_section_shards(): lax.dynamic_slice_in_dim(placed, (1 - section) * rows_half, rows_half, 0)  0.83 us
    ppermute x3, starting transfers between devices, pair_swap(): return lax.ppermute(block, axis, [(0, 1), (1, 0)])  0.64 us
  transfers between devices with their start and end apart: 4, of which 3 were waited for; matrix products, arithmetic and copies ran while one was open for 22% of the time, Pallas kernels for 0%

profile of v6, /device:TPU:0, one launch (start us, length us, event | category | flops | bytes accessed | tf_op | source)
XLA Modules:
  0.0 27.0 jit_solution(6280932347753564514)
XLA Ops:
  0.6 0.0 copy-start
  0.6 0.0 copy-start.5
  0.7 2.1 %fusion.10 = f32[512,256]{1,0:T(8,128)S(1)} fusion(f32[512,256]{1,0:T(8,128)} %param.7, f32[512,1024]{1,0:T(8,128)} %param.6, s32[]{:T(128)S(6)} %select_n.37), kind=kOutput, calls=%fused_computation.13 | convolution fusion | flops 402653184 | bytes 2097156 | tf_op jit(solution)/shard_map/dot_general | solution.py:26
  2.8 0.5 %collective-permute-start = (f32[512,256]{1,0:T(8,128)S(1)}, f32[512,256]{1,0:T(8,128)S(1)}, u32[]{:S(2)}, u32[]{:S(2)}) collective-permute-start(f32[512,256]{1,0:T(8,128)S(1)} %fusion.10), channel_id=1, source_target_pairs={{0,1},{1,0},{2,3},{3,2},{4,5},{5,4},{6,7},{7,6},{8,9},{9,8},{10,11... | collective-permute-start | bytes 1572872 | tf_op jit(solution)/shard_map/ppermute | solution.py:77
  3.3 0.0 copy-done.5
  3.3 0.1 select_reduce_fusion
  3.4 0.0 copy-done
  3.4 2.0 %gather_fusion = f32[8,128,512]{2,1,0:T(8,128)} fusion(f32[8,128,512]{2,1,0:T(8,128)S(1)} %bitcast.10, s32[1024]{0:T(1024)S(1)} %pad_clamp_fusion), kind=kCustom, calls=%fused_computation | custom fusion | bytes 4194336 | tf_op jit(solution)/shard_map/jit(_take)/gather | solution.py:107
  5.4 0.0 copy-start.1
  5.4 2.7 %fusion.3 = f32[512,512]{1,0:T(8,128)S(1)} fusion(f32[512,1024]{1,0:T(8,128)} %param.6, s32[]{:T(128)S(6)} %select_n.37, pred[]{:T(512)S(6)} %gt.4), kind=kOutput, calls=%fused_computation.6 | convolution fusion | flops 805568512 | bytes 3145733 | tf_op jit(solution)/shard_map/dot_general | solution.py:26
  8.1 0.0 collective-permute-done
  8.1 0.6 %convolution_subtract_fusion = f32[512,256]{1,0:T(8,128)S(1)} fusion(f32[512,256]{1,0:T(8,128)S(1)} %fusion.10, f32[512,512]{1,0:T(8,128)S(1)} %fusion.3, f32[512,256]{1,0:T(8,128)S(1)} %collective-permute-done), kind=kOutput, calls=%fused_computation.1 | convolution fusion | flops 402784256 | bytes 2621440 | tf_op jit(solution)/shard_map/dot_general | solution.py:26
  8.7 0.0 copy-start.2
  8.7 0.0 copy-done.1
  8.8 1.0 %fusion.25 = f32[1024,256]{1,0:T(8,128)S(1)} fusion(f32[1024,512]{1,0:T(8,128)S(1)} %bitcast.11, f32[512,256]{1,0:T(8,128)S(1)} %convolution_subtract_fusion), kind=kOutput, calls=%fused_computation.34 | convolution fusion | flops 805306368 | bytes 3670016 | tf_op jit(solution)/shard_map/dot_general | solution.py:26
  9.8 0.8 %constant_dynamic-slice_fusion.1 = f32[512,256]{1,0:T(8,128)} fusion(f32[1024,256]{1,0:T(8,128)S(1)} %fusion.25, s32[]{:T(128)S(6)} %select_n.41), kind=kLoop, calls=%fused_computation.28 | loop fusion | bytes 1048580 | tf_op jit(solution)/shard_map/dynamic_slice | solution.py:111
  10.6 0.0 copy-done.2
  10.6 0.1 collective-permute-start.1
  10.7 0.0 copy-start.3
  10.7 0.0 copy-start.4
  10.7 2.2 %collective-permute-done.1 = f32[512,256]{1,0:T(8,128)} collective-permute-done((f32[512,256]{1,0:T(8,128)}, f32[512,256]{1,0:T(8,128)}, u32[]{:S(2)}, u32[]{:S(2)}) %collective-permute-start.1) | collective-permute-done | bytes 524320 | tf_op jit(solution)/shard_map/ppermute | solution.py:77
  12.9 1.1 %dynamic-slice_add_fusion = f32[512,256]{1,0:T(8,128)S(1)} fusion(f32[512,256]{1,0:T(8,128)} %collective-permute-done.1, f32[1024,256]{1,0:T(8,128)S(1)} %fusion.25, s32[]{:T(128)S(6)} %select_n.37), kind=kLoop, calls=%fused_computation.15 | loop fusion | flops 131072 | bytes 1572868 | tf_op jit(solution)/shard_map/add | solution.py:112
  14.0 2.7 %collective-permute-start.2 = (f32[512,128]{1,0:T(8,128)S(1)}, f32[512,128]{1,0:T(8,128)S(1)}, u32[]{:S(2)}, u32[]{:S(2)}) collective-permute-start(f32[512,128]{1,0:T(8,128)S(1)} %constant_dynamic-slice_fusion), channel_id=1, source_target_pairs={{0,2},{2,0},{4,6},{6,4},{8,10},{10,8},{12,14},{14,12},{16,18},{18,... | collective-permute-start | bytes 786440 | tf_op jit(solution)/shard_map/ppermute | solution.py:22
  16.7 0.0 copy-done.3
  16.7 1.0 %fusion = f32[512,512]{1,0:T(8,128)S(1)} fusion(f32[512,1024]{1,0:T(8,128)S(1)} %copy-done.3, s32[]{:T(128)S(6)} %select_n.37, pred[]{:T(512)S(6)} %gt.4), kind=kOutput, calls=%fused_computation.3 | convolution fusion | flops 805568512 | bytes 3145733 | tf_op jit(solution)/shard_map/dot_general | solution.py:26
  17.7 5.8 %collective-permute-done.2 = f32[512,128]{1,0:T(8,128)S(1)} collective-permute-done((f32[512,128]{1,0:T(8,128)S(1)}, f32[512,128]{1,0:T(8,128)S(1)}, u32[]{:S(2)}, u32[]{:S(2)}) %collective-permute-start.2) | collective-permute-done | bytes 262176 | tf_op jit(solution)/shard_map/ppermute | solution.py:22
  23.5 0.0 copy-done.4
  23.5 0.6 %fusion.6 = f32[512,128]{1,0:T(8,128)S(1)} fusion(f32[512,1024]{1,0:T(8,128)S(1)} %copy-done.3, s32[]{:T(128)S(6)} %select_n.37, f32[512,128]{1,0:T(8,128)S(1)} %copy-done.4, f32[512,128]{1,0:T(8,128)S(1)} %collective-permute-done.2, f32[512,256]{1,0:T(8,128)S(1)} %dynamic-slice_add_fusion, s32[]{:T(128)S(6)} %select_n.43), kind=kOutput, calls=%fused_computation.9 | convolution fusion | flops 201457664 | bytes 2097160 | tf_op jit(solution)/shard_map/dot_general | solution.py:26
  24.1 0.1 collective-permute-start.3
  24.2 1.5 %collective-permute-done.3 = f32[512,128]{1,0:T(8,128)S(1)} collective-permute-done((f32[512,128]{1,0:T(8,128)S(1)}, f32[512,128]{1,0:T(8,128)S(1)}, u32[]{:S(2)}, u32[]{:S(2)}) %collective-permute-start.3) | collective-permute-done | bytes 262176 | tf_op jit(solution)/shard_map/ppermute | solution.py:77
  25.7 1.3 %convolution_subtract_fusion.1 = f32[512,128]{1,0:T(8,128)} fusion(f32[512,128]{1,0:T(8,128)S(1)} %fusion.6, f32[512,512]{1,0:T(8,128)S(1)} %fusion, f32[512,128]{1,0:T(8,128)S(1)} %collective-permute-done.3), kind=kOutput, calls=%fused_computation.2 | convolution fusion | flops 201392128 | bytes 1835008 | tf_op jit(solution)/shard_map/dot_general | solution.py:26
  (2 shorter events, 0.0 us)
Async XLA Ops:
  0.6 2.8 %copy-start = (f32[1024,512]{1,0:T(8,128)S(1)}, f32[1024,512]{1,0:T(8,128)}, u32[]{:S(2)}) copy-start(f32[1024,512]{1,0:T(8,128)} %param.8) | copy-start | bytes 6291460
  0.6 2.6 %copy-start.5 = (s32[1,8]{1,0:T(1,128)S(1)}, s32[1,8]{1,0:T(1,128)}, u32[]{:S(2)}) copy-start(s32[1,8]{1,0:T(1,128)} %param.9) | copy-start | bytes 100
  2.8 5.4 %collective-permute-start = (f32[512,256]{1,0:T(8,128)S(1)}, f32[512,256]{1,0:T(8,128)S(1)}, u32[]{:S(2)}, u32[]{:S(2)}) collective-permute-start(f32[512,256]{1,0:T(8,128)S(1)} %fusion.10), channel_id=1, source_target_pairs={{0,1},{1,0},{2,3},{3,2},{4,5},{5,4},{6,7},{7,6},{8,9},{9,8},{10,11... | collective-permute-start | bytes 1572872 | tf_op jit(solution)/shard_map/ppermute | solution.py:77
  5.4 3.3 %copy-start.1 = (f32[8,128,512]{2,1,0:T(8,128)S(1)}, f32[8,128,512]{2,1,0:T(8,128)}, u32[]{:S(2)}) copy-start(f32[8,128,512]{2,1,0:T(8,128)} %gather_fusion) | copy-start | bytes 6291460
  8.7 1.9 %copy-start.2 = (f32[512,256]{1,0:T(8,128)}, f32[512,256]{1,0:T(8,128)S(1)}, u32[]{:S(2)}) copy-start(f32[512,256]{1,0:T(8,128)S(1)} %convolution_subtract_fusion) | copy-start | bytes 1572868
  10.6 2.3 %collective-permute-start.1 = (f32[512,256]{1,0:T(8,128)}, f32[512,256]{1,0:T(8,128)}, u32[]{:S(2)}, u32[]{:S(2)}) collective-permute-start(f32[512,256]{1,0:T(8,128)} %constant_dynamic-slice_fusion.1), channel_id=1, source_target_pairs={{0,1},{1,0},{2,3},{3,2},{4,5},{5,4},{6,7},{7,6},{8,9},{9,8},{10,11... | collective-permute-start | bytes 1572872 | tf_op jit(solution)/shard_map/ppermute | solution.py:77
  10.7 6.0 %copy-start.3 = (f32[512,1024]{1,0:T(8,128)S(1)}, f32[512,1024]{1,0:T(8,128)}, u32[]{:S(2)}) copy-start(f32[512,1024]{1,0:T(8,128)} %param.10) | copy-start | bytes 6291460
  10.7 12.9 %copy-start.4 = (f32[512,128]{1,0:T(8,128)S(1)}, f32[512,128]{1,0:T(8,128)}, u32[]{:S(2)}) copy-start(f32[512,128]{1,0:T(8,128)} %param.11) | copy-start | bytes 786436
  14.0 9.5 %collective-permute-start.2 = (f32[512,128]{1,0:T(8,128)S(1)}, f32[512,128]{1,0:T(8,128)S(1)}, u32[]{:S(2)}, u32[]{:S(2)}) collective-permute-start(f32[512,128]{1,0:T(8,128)S(1)} %constant_dynamic-slice_fusion), channel_id=1, source_target_pairs={{0,2},{2,0},{4,6},{6,4},{8,10},{10,8},{12,14},{14,12},{16,18},{18,... | collective-permute-start | bytes 786440 | tf_op jit(solution)/shard_map/ppermute | solution.py:22
  24.1 1.6 %collective-permute-start.3 = (f32[512,128]{1,0:T(8,128)S(1)}, f32[512,128]{1,0:T(8,128)S(1)}, u32[]{:S(2)}, u32[]{:S(2)}) collective-permute-start(f32[512,128]{1,0:T(8,128)S(1)} %fusion.6), channel_id=1, source_target_pairs={{0,1},{1,0},{2,3},{3,2},{4,5},{5,4},{6,7},{7,6},{8,9},{9,8},{10,11... | collective-permute-start | bytes 786440 | tf_op jit(solution)/shard_map/ppermute | solution.py:77

commit v7 on v6

--- a/solution.py
+++ b/solution.py
@@ -83,13 +83,13 @@
     return matmul(diagonal, below, precision)
 
 
-def two_section_solve(factor, right_side, section, precision):
+def two_section_leaf(factor, right_side, section, precision):
     tile_rows = right_side.shape[0]
     diagonal = lax.dynamic_slice_in_dim(factor, section * tile_rows, tile_rows, 1)
     first = matmul(diagonal, right_side, precision)
     arrived = pair_swap(first, "rows")
-    coupling = lower_coupling(factor, diagonal, section, precision)
-    return first - matmul(coupling, arrived, precision)
+    below = jnp.where(section > 0, factor[:, :tile_rows], jnp.zeros_like(diagonal))
+    return matmul(diagonal, right_side - matmul(below, arrived, precision), precision)
 
 
 def inverse_order(update_blocks):
@@ -102,14 +102,19 @@
 def two_section_shards(leaf_factor, leaf_rhs, update_panel, update_blocks, parent_factor, parent_rhs):
     section = lax.axis_index("rows")
     precision = lax.Precision.HIGH
-    leaf_solution = two_section_solve(leaf_factor, leaf_rhs, section, precision)
+    leaf_solution = two_section_leaf(leaf_factor, leaf_rhs, section, precision)
     blocks = update_panel.reshape(-1, ROW_BLOCK, update_panel.shape[1])
-    panel_placed = jnp.take(blocks, inverse_order(update_blocks), axis=0, mode="clip")
-    placed = matmul(panel_placed.reshape(update_panel.shape), leaf_solution, precision)
-    rows_half = placed.shape[0] // 2
-    own_rows = lax.dynamic_slice_in_dim(placed, section * rows_half, rows_half, 0)
-    other_rows = lax.dynamic_slice_in_dim(placed, (1 - section) * rows_half, rows_half, 0)
-    chip_sum = own_rows + pair_swap(other_rows, "rows")
+    order = inverse_order(update_blocks)
+    per_section = blocks.shape[0] // 2
+
+    def section_panel(rows_of):
+        chosen = lax.dynamic_slice_in_dim(order, rows_of * per_section, per_section)
+        taken = jnp.take(blocks, chosen, axis=0, mode="clip")
+        return taken.reshape(-1, update_panel.shape[1])
+
+    other_rows = matmul(section_panel(1 - section), leaf_solution, precision)
+    arrived_rows = pair_swap(other_rows, "rows")
+    chip_sum = matmul(section_panel(section), leaf_solution, precision) + arrived_rows
     column_half = parent_rhs.shape[1]
     sibling = lax.axis_index("leaf") % 2
     kept = lax.dynamic_slice_in_dim(chip_sum, sibling * column_half, column_half, 1)

time: 27.2 us -> 26.5 us (0.974)
  waiting for transfers between devices: 9.52 us -> 7.47 us
  matrix products: 9.29 us -> 11.1 us
  other arithmetic: 1.2 us -> 0.09 us
  local copies, waits for them, and re-layouts: 2.92 us -> 3.31 us
  starting transfers between devices: 3.34 us -> 3.69 us
    ppermute x3, waiting for transfers between devices: 3.72 us -> 1.79 us  [pair_swap(): return lax.ppermute(block, axis, [(0, 1), (1, 0)])]
    dot_general x7 -> x8, matrix products: 9.29 us -> 11.1 us  [matmul(): jnp.dot(left, right, precision=precision, preferred_element_type=jnp.floa...]
    gather x1 -> x2, local copies, waits for them, and re-layouts: 2.03 us -> 3.17 us  [section_panel(): taken = jnp.take(blocks, chosen, axis=0, mode='clip')]
    add x1 -> x0, other arithmetic: 1.11 us -> none  [two_section_shards(): chip_sum = own_rows + pair_swap(other_rows, 'rows')]
    dynamic_slice x1, local copies, waits for them, and re-layouts: 0.83 us -> 0.08 us  [section_panel(): chosen = lax.dynamic_slice_in_dim(order, rows_of * per_section, per_section)]
  transfers between devices with their start and end apart: 4 -> 4, of which waited for: 3 -> 3; matrix products, arithmetic and copies ran while one was open for 22% -> 16% of each run, Pallas kernels for 0% -> 0%
where the time goes in v7:
time: 26.5 us; the launch traced here: 26.4 us
  matrix products  11.1 us (42%)
  waiting for transfers between devices  7.47 us (28%)
  starting transfers between devices  3.69 us (14%)
  local copies, waits for them, and re-layouts  3.31 us (12%)
  between operations  0.76 us (3%)
    dot_general x8, matrix products, matmul(): jnp.dot(left, right, precision=precision, preferred_element_type=jnp.floa...  11.1 us
    ppermute x1, waiting for transfers between devices, swapped(): return lax.ppermute(block, axis, route)  5.68 us
    gather x2, local copies, waits for them, and re-layouts, section_panel(): taken = jnp.take(blocks, chosen, axis=0, mode='clip')  3.17 us
    ppermute x1, starting transfers between devices, swapped(): return lax.ppermute(block, axis, route)  2.82 us
    ppermute x3, waiting for transfers between devices, pair_swap(): return lax.ppermute(block, axis, [(0, 1), (1, 0)])  1.79 us
    ppermute x3, starting transfers between devices, pair_swap(): return lax.ppermute(block, axis, [(0, 1), (1, 0)])  0.86 us
  transfers between devices with their start and end apart: 4, of which 3 were waited for; matrix products, arithmetic and copies ran while one was open for 16% of the time, Pallas kernels for 0%

profile of v7, /device:TPU:0, one launch (start us, length us, event | category | flops | bytes accessed | tf_op | source)
XLA Modules:
  0.0 26.4 jit_solution(3233229369597125821)
XLA Ops:
  0.6 0.0 copy-start
  0.6 0.0 copy-start.7
  0.7 0.0 copy-start.4
  0.7 2.1 %fusion.10 = f32[512,256]{1,0:T(8,128)S(1)} fusion(f32[512,256]{1,0:T(8,128)} %param.7, f32[512,1024]{1,0:T(8,128)} %param.6, s32[]{:T(128)S(6)} %select_n.39), kind=kOutput, calls=%fused_computation.15 | convolution fusion | flops 402653184 | bytes 2097156 | tf_op jit(solution)/shard_map/dot_general | solution.py:26
  2.8 0.5 %collective-permute-start = (f32[512,256]{1,0:T(8,128)S(1)}, f32[512,256]{1,0:T(8,128)}, u32[]{:S(2)}, u32[]{:S(2)}) collective-permute-start(f32[512,256]{1,0:T(8,128)S(1)} %fusion.10), channel_id=1, source_target_pairs={{0,1},{1,0},{2,3},{3,2},{4,5},{5,4},{6,7},{7,6},{8,9},{9,8},{10,11... | collective-permute-start | bytes 1572872 | tf_op jit(solution)/shard_map/ppermute | solution.py:77
  3.3 0.0 copy-done.7
  3.3 0.1 select_reduce_fusion
  3.4 0.1 fusion.25
  3.5 0.0 copy-done
  3.5 1.6 %gather_fusion.1 = f32[4,128,512]{2,1,0:T(8,128)} fusion(f32[8,128,512]{2,1,0:T(8,128)S(1)} %bitcast.14, s32[1024]{0:T(1024)S(1)} %get-tuple-element.8), kind=kCustom, calls=%fused_computation.1 | custom fusion | bytes 2097168 | tf_op jit(solution)/shard_map/jit(_take)/gather | solution.py:112
  5.1 0.0 copy-start.1
  5.1 0.0 copy-start.3
  5.1 0.0 collective-permute-done
  5.1 0.0 copy-done.4
  5.1 2.1 %convolution_subtract_fusion = f32[512,256]{1,0:T(8,128)S(1)} fusion(f32[512,256]{1,0:T(8,128)S(1)} %copy-done.4, f32[512,256]{1,0:T(8,128)} %collective-permute-done, f32[512,1024]{1,0:T(8,128)} %param.6, pred[]{:T(512)S(6)} %gt.4), kind=kOutput, calls=%fused_computation.3 | convolution fusion | flops 403046400 | bytes 2621441 | tf_op jit(solution)/shard_map/dot_general | solution.py:26
  7.2 0.0 copy-done.1
  7.2 0.6 %fusion.8 = f32[512,256]{1,0:T(8,128)S(1)} fusion(f32[512,256]{1,0:T(8,128)S(1)} %convolution_subtract_fusion, f32[512,1024]{1,0:T(8,128)S(1)} %copy-done.1, s32[]{:T(128)S(6)} %select_n.39), kind=kOutput, calls=%fused_computation.13 | convolution fusion | flops 402653184 | bytes 2097156 | tf_op jit(solution)/shard_map/dot_general | solution.py:26
  7.8 0.0 copy-start.2
  7.8 0.0 copy-done.3
  7.8 1.4 %fusion.26 = f32[512,256]{1,0:T(8,128)} fusion(f32[512,512]{1,0:T(8,128)S(1)} %bitcast.16, f32[512,256]{1,0:T(8,128)S(1)} %fusion.8), kind=kOutput, calls=%fused_computation.36 | convolution fusion | flops 402653184 | bytes 2097152 | tf_op jit(solution)/shard_map/dot_general | solution.py:26
  9.2 0.3 %collective-permute-start.1 = (f32[512,256]{1,0:T(8,128)}, f32[512,256]{1,0:T(8,128)S(1)}, u32[]{:S(2)}, u32[]{:S(2)}) collective-permute-start(f32[512,256]{1,0:T(8,128)} %fusion.26), channel_id=1, source_target_pairs={{0,1},{1,0},{2,3},{3,2},{4,5},{5,4},{6,7},{7,6},{8,9},{9,8},{10,11... | collective-permute-start | bytes 1572872 | tf_op jit(solution)/shard_map/ppermute | solution.py:77
  9.5 1.6 %gather_fusion = f32[4,128,512]{2,1,0:T(8,128)} fusion(f32[8,128,512]{2,1,0:T(8,128)S(1)} %bitcast.13, s32[1024]{0:T(1024)S(1)} %get-tuple-element.9), kind=kCustom, calls=%fused_computation | custom fusion | bytes 2097168 | tf_op jit(solution)/shard_map/jit(_take)/gather | solution.py:112
  11.1 0.0 copy-start.5
  11.1 0.3 %collective-permute-done.1 = f32[512,256]{1,0:T(8,128)S(1)} collective-permute-done((f32[512,256]{1,0:T(8,128)}, f32[512,256]{1,0:T(8,128)S(1)}, u32[]{:S(2)}, u32[]{:S(2)}) %collective-permute-start.1) | collective-permute-done | bytes 524320 | tf_op jit(solution)/shard_map/ppermute | solution.py:77
  11.4 0.0 copy-done.2
  11.4 0.0 copy-start.6
  11.4 2.0 %convolution_add_fusion = f32[512,256]{1,0:T(8,128)S(1)} fusion(f32[512,256]{1,0:T(8,128)S(1)} %collective-permute-done.1, f32[512,512]{1,0:T(8,128)} %bitcast.15, f32[512,256]{1,0:T(8,128)S(1)} %fusion.8), kind=kOutput, calls=%fused_computation.2 | convolution fusion | flops 402784256 | bytes 2621440 | tf_op jit(solution)/shard_map/dot_general | solution.py:26
  13.4 2.8 %collective-permute-start.2 = (f32[512,128]{1,0:T(8,128)S(1)}, f32[512,128]{1,0:T(8,128)S(1)}, u32[]{:S(2)}, u32[]{:S(2)}) collective-permute-start(f32[512,128]{1,0:T(8,128)S(1)} %constant_dynamic-slice_fusion), channel_id=1, source_target_pairs={{0,2},{2,0},{4,6},{6,4},{8,10},{10,8},{12,14},{14,12},{16,18},{18,... | collective-permute-start | bytes 786440 | tf_op jit(solution)/shard_map/ppermute | solution.py:22
  16.2 0.0 copy-done.5
  16.2 1.0 %fusion = f32[512,512]{1,0:T(8,128)S(1)} fusion(f32[512,1024]{1,0:T(8,128)S(1)} %copy-done.5, s32[]{:T(128)S(6)} %select_n.39, pred[]{:T(512)S(6)} %gt.4), kind=kOutput, calls=%fused_computation.5 | convolution fusion | flops 805568512 | bytes 3145733 | tf_op jit(solution)/shard_map/dot_general | solution.py:26
  17.2 5.7 %collective-permute-done.2 = f32[512,128]{1,0:T(8,128)S(1)} collective-permute-done((f32[512,128]{1,0:T(8,128)S(1)}, f32[512,128]{1,0:T(8,128)S(1)}, u32[]{:S(2)}, u32[]{:S(2)}) %collective-permute-start.2) | collective-permute-done | bytes 262176 | tf_op jit(solution)/shard_map/ppermute | solution.py:22
  22.9 0.0 copy-done.6
  22.9 0.6 %fusion.5 = f32[512,128]{1,0:T(8,128)S(1)} fusion(f32[512,1024]{1,0:T(8,128)S(1)} %copy-done.5, s32[]{:T(128)S(6)} %select_n.39, f32[512,128]{1,0:T(8,128)S(1)} %copy-done.6, f32[512,128]{1,0:T(8,128)S(1)} %collective-permute-done.2, f32[512,256]{1,0:T(8,128)S(1)} %convolution_add_fusion, s32[]{:T(128)S(6)} %select_n.46), kind=kOutput, calls=%fused_computation.10 | convolution fusion | flops 201457664 | bytes 2097160 | tf_op jit(solution)/shard_map/dot_general | solution.py:26
  23.5 0.1 collective-permute-start.3
  23.6 1.5 %collective-permute-done.3 = f32[512,128]{1,0:T(8,128)S(1)} collective-permute-done((f32[512,128]{1,0:T(8,128)S(1)}, f32[512,128]{1,0:T(8,128)S(1)}, u32[]{:S(2)}, u32[]{:S(2)}) %collective-permute-start.3) | collective-permute-done | bytes 262176 | tf_op jit(solution)/shard_map/ppermute | solution.py:77
  25.1 1.3 %convolution_subtract_fusion.1 = f32[512,128]{1,0:T(8,128)} fusion(f32[512,128]{1,0:T(8,128)S(1)} %fusion.5, f32[512,512]{1,0:T(8,128)S(1)} %fusion, f32[512,128]{1,0:T(8,128)S(1)} %collective-permute-done.3), kind=kOutput, calls=%fused_computation.4 | convolution fusion | flops 201392128 | bytes 1835008 | tf_op jit(solution)/shard_map/dot_general | solution.py:26
  (2 shorter events, 0.0 us)
Async XLA Ops:
  0.6 2.9 %copy-start = (f32[1024,512]{1,0:T(8,128)S(1)}, f32[1024,512]{1,0:T(8,128)}, u32[]{:S(2)}) copy-start(f32[1024,512]{1,0:T(8,128)} %param.8) | copy-start | bytes 6291460
  0.6 2.7 %copy-start.7 = (s32[1,8]{1,0:T(1,128)S(1)}, s32[1,8]{1,0:T(1,128)}, u32[]{:S(2)}) copy-start(s32[1,8]{1,0:T(1,128)} %param.9) | copy-start | bytes 100
  0.7 4.4 %copy-start.4 = (f32[512,256]{1,0:T(8,128)S(1)}, f32[512,256]{1,0:T(8,128)}, u32[]{:S(2)}) copy-start(f32[512,256]{1,0:T(8,128)} %param.7) | copy-start | bytes 1572868
  2.8 2.3 %collective-permute-start = (f32[512,256]{1,0:T(8,128)S(1)}, f32[512,256]{1,0:T(8,128)}, u32[]{:S(2)}, u32[]{:S(2)}) collective-permute-start(f32[512,256]{1,0:T(8,128)S(1)} %fusion.10), channel_id=1, source_target_pairs={{0,1},{1,0},{2,3},{3,2},{4,5},{5,4},{6,7},{7,6},{8,9},{9,8},{10,11... | collective-permute-start | bytes 1572872 | tf_op jit(solution)/shard_map/ppermute | solution.py:77
  5.1 2.1 %copy-start.1 = (f32[512,1024]{1,0:T(8,128)S(1)}, f32[512,1024]{1,0:T(8,128)}, u32[]{:S(2)}) copy-start(f32[512,1024]{1,0:T(8,128)} %param.6) | copy-start | bytes 6291460
  5.1 2.7 %copy-start.3 = (f32[4,128,512]{2,1,0:T(8,128)S(1)}, f32[4,128,512]{2,1,0:T(8,128)}, u32[]{:S(2)}) copy-start(f32[4,128,512]{2,1,0:T(8,128)} %gather_fusion.1) | copy-start | bytes 3145732
  7.8 3.6 %copy-start.2 = (f32[512,256]{1,0:T(8,128)}, f32[512,256]{1,0:T(8,128)S(1)}, u32[]{:S(2)}) copy-start(f32[512,256]{1,0:T(8,128)S(1)} %fusion.8) | copy-start | bytes 1572868
  9.2 2.1 %collective-permute-start.1 = (f32[512,256]{1,0:T(8,128)}, f32[512,256]{1,0:T(8,128)S(1)}, u32[]{:S(2)}, u32[]{:S(2)}) collective-permute-start(f32[512,256]{1,0:T(8,128)} %fusion.26), channel_id=1, source_target_pairs={{0,1},{1,0},{2,3},{3,2},{4,5},{5,4},{6,7},{7,6},{8,9},{9,8},{10,11... | collective-permute-start | bytes 1572872 | tf_op jit(solution)/shard_map/ppermute | solution.py:77
  11.1 5.1 %copy-start.5 = (f32[512,1024]{1,0:T(8,128)S(1)}, f32[512,1024]{1,0:T(8,128)}, u32[]{:S(2)}) copy-start(f32[512,1024]{1,0:T(8,128)} %param.10) | copy-start | bytes 6291460
  11.4 11.5 %copy-start.6 = (f32[512,128]{1,0:T(8,128)S(1)}, f32[512,128]{1,0:T(8,128)}, u32[]{:S(2)}) copy-start(f32[512,128]{1,0:T(8,128)} %param.11) | copy-start | bytes 786436
  13.4 9.5 %collective-permute-start.2 = (f32[512,128]{1,0:T(8,128)S(1)}, f32[512,128]{1,0:T(8,128)S(1)}, u32[]{:S(2)}, u32[]{:S(2)}) collective-permute-start(f32[512,128]{1,0:T(8,128)S(1)} %constant_dynamic-slice_fusion), channel_id=1, source_target_pairs={{0,2},{2,0},{4,6},{6,4},{8,10},{10,8},{12,14},{14,12},{16,18},{18,... | collective-permute-start | bytes 786440 | tf_op jit(solution)/shard_map/ppermute | solution.py:22
  23.5 1.6 %collective-permute-start.3 = (f32[512,128]{1,0:T(8,128)S(1)}, f32[512,128]{1,0:T(8,128)S(1)}, u32[]{:S(2)}, u32[]{:S(2)}) collective-permute-start(f32[512,128]{1,0:T(8,128)S(1)} %fusion.5), channel_id=1, source_target_pairs={{0,1},{1,0},{2,3},{3,2},{4,5},{5,4},{6,7},{7,6},{8,9},{9,8},{10,11... | collective-permute-start | bytes 786440 | tf_op jit(solution)/shard_map/ppermute | solution.py:77

commit v8 on v7

--- a/solution.py
+++ b/solution.py
@@ -2,6 +2,8 @@
 import jax.numpy as jnp
 from jax import lax
 from jax.sharding import PartitionSpec as P
+from jax.experimental import pallas as pl
+from jax.experimental.pallas import tpu as pltpu
 
 ROW_BLOCK = 128
 
@@ -73,6 +75,57 @@
     return (kept_half, sent_half)
 
 
+def split_bf16(values):
+    high = values.astype(jnp.bfloat16)
+    low = (values - high.astype(jnp.float32)).astype(jnp.bfloat16)
+    return high, low
+
+
+def dot_bf16x3(left, right):
+    left_high, left_low = split_bf16(left)
+    right_high, right_low = split_bf16(right)
+
+    def part(a, b):
+        return jnp.dot(a, b, preferred_element_type=jnp.float32)
+
+    return part(left_high, right_high) + (part(left_low, right_high) + part(left_high, right_low))
+
+
+def block_matmul_kernel(rows_ref, column_ref, keep_ref, left_ref, right_ref, *rest):
+    product = dot_bf16x3(left_ref[...], right_ref[...])
+    if len(rest) == 1:
+        rest[0][...] = product
+        return
+    extra_ref, out_ref = rest
+    out_ref[...] = extra_ref[...] - jnp.where(keep_ref[0] > 0, product, 0.0)
+
+
+def block_matmul(left, right, rows, column, block_rows, extra=None, keep=None):
+    inner, width = right.shape
+    steps = rows.shape[0]
+    if keep is None:
+        keep = jnp.ones((1,), jnp.int32)
+    in_specs = [
+        pl.BlockSpec((block_rows, inner), lambda i, r, c, k: (r[i], c[0])),
+        pl.BlockSpec((inner, width), lambda i, r, c, k: (0, 0)),
+    ]
+    operands = [left, right]
+    if extra is not None:
+        in_specs.append(pl.BlockSpec((block_rows, width), lambda i, r, c, k: (i, 0)))
+        operands.append(extra)
+    grid_spec = pltpu.PrefetchScalarGridSpec(
+        num_scalar_prefetch=3,
+        grid=(steps,),
+        in_specs=in_specs,
+        out_specs=pl.BlockSpec((block_rows, width), lambda i, r, c, k: (i, 0)),
+    )
+    return pl.pallas_call(
+        block_matmul_kernel,
+        grid_spec=grid_spec,
+        out_shape=jax.ShapeDtypeStruct((steps * block_rows, width), jnp.float32),
+    )(rows.astype(jnp.int32), jnp.reshape(column, (1,)).astype(jnp.int32), jnp.reshape(keep, (1,)).astype(jnp.int32), *operands)
+
+
 def pair_swap(block, axis):
     return lax.ppermute(block, axis, [(0, 1), (1, 0)])
 
@@ -83,13 +136,13 @@
     return matmul(diagonal, below, precision)
 
 
-def two_section_leaf(factor, right_side, section, precision):
+def two_section_leaf(factor, right_side, section):
     tile_rows = right_side.shape[0]
-    diagonal = lax.dynamic_slice_in_dim(factor, section * tile_rows, tile_rows, 1)
-    first = matmul(diagonal, right_side, precision)
+    steps = jnp.arange(tile_rows // ROW_BLOCK)
+    first = block_matmul(factor, right_side, steps, section, ROW_BLOCK)
     arrived = pair_swap(first, "rows")
-    below = jnp.where(section > 0, factor[:, :tile_rows], jnp.zeros_like(diagonal))
-    return matmul(diagonal, right_side - matmul(below, arrived, precision), precision)
+    target = block_matmul(factor, arrived, steps, 0, ROW_BLOCK, extra=right_side, keep=section)
+    return block_matmul(factor, target, steps, section, ROW_BLOCK)
 
 
 def inverse_order(update_blocks):
@@ -102,19 +155,14 @@
 def two_section_shards(leaf_factor, leaf_rhs, update_panel, update_blocks, parent_factor, parent_rhs):
     section = lax.axis_index("rows")
     precision = lax.Precision.HIGH
-    leaf_solution = two_section_leaf(leaf_factor, leaf_rhs, section, precision)
-    blocks = update_panel.reshape(-1, ROW_BLOCK, update_panel.shape[1])
+    leaf_solution = two_section_leaf(leaf_factor, leaf_rhs, section)
     order = inverse_order(update_blocks)
-    per_section = blocks.shape[0] // 2
-
-    def section_panel(rows_of):
-        chosen = lax.dynamic_slice_in_dim(order, rows_of * per_section, per_section)
-        taken = jnp.take(blocks, chosen, axis=0, mode="clip")
-        return taken.reshape(-1, update_panel.shape[1])
-
-    other_rows = matmul(section_panel(1 - section), leaf_solution, precision)
+    per_section = order.shape[0] // 2
+    other_blocks = lax.dynamic_slice_in_dim(order, (1 - section) * per_section, per_section)
+    own_blocks = lax.dynamic_slice_in_dim(order, section * per_section, per_section)
+    other_rows = block_matmul(update_panel, leaf_solution, other_blocks, 0, ROW_BLOCK)
     arrived_rows = pair_swap(other_rows, "rows")
-    chip_sum = matmul(section_panel(section), leaf_solution, precision) + arrived_rows
+    chip_sum = block_matmul(update_panel, leaf_solution, own_blocks, 0, ROW_BLOCK) + arrived_rows
     column_half = parent_rhs.shape[1]
     sibling = lax.axis_index("leaf") % 2
     kept = lax.dynamic_slice_in_dim(chip_sum, sibling * column_half, column_half, 1)
@@ -127,7 +175,8 @@
     pending = parent_rhs - (kept + arrived)
     first = matmul(diagonal, pending, precision)
     arrived = pair_swap(first, "rows")
-    parent_solution = first - matmul(coupling, arrived, precision)
+    steps = jnp.arange(tile_rows // ROW_BLOCK)
+    parent_solution = block_matmul(coupling, arrived, steps, 0, ROW_BLOCK, extra=first)
     return (leaf_solution, parent_solution)
 
 

time: 26.5 us -> 47.3 us (1.78)
  Pallas kernels: 0 us -> 28 us
  matrix products: 11.1 us -> 2.57 us
  other arithmetic: 0.09 us -> 1.24 us
    pallas_call x0 -> x6, Pallas kernels: none -> 28 us  [block_matmul(): pl.pallas_call(block_matmul_kernel, grid_spec=grid_spec, out_shape=jax.Sh...]
    dot_general x8 -> x2, matrix products: 11.1 us -> 2.57 us  [matmul(): jnp.dot(left, right, precision=precision, preferred_element_type=jnp.floa...]
    gather x2 -> x0, local copies, waits for them, and re-layouts: 3.17 us -> none  [section_panel(): taken = jnp.take(blocks, chosen, axis=0, mode='clip')]
    iota x0 -> x4, local copies, waits for them, and re-layouts: none -> 2.17 us  [the longest x3 1.57 us: two_section_leaf(): steps = jnp.arange(tile_rows // ROW_BLOCK)]
    add x0 -> x1, other arithmetic: none -> 1.15 us  [two_section_shards(): block_matmul(update_panel, leaf_solution, own_blocks, 0, ROW_BLOCK)]
    ppermute x1, waiting for transfers between devices: 5.68 us -> 4.85 us  [swapped(): return lax.ppermute(block, axis, route)]
    ppermute x3, waiting for transfers between devices: 1.79 us -> 2.57 us  [pair_swap(): return lax.ppermute(block, axis, [(0, 1), (1, 0)])]
    dynamic_slice x1, local copies, waits for them, and re-layouts: 0.08 us -> 0.61 us  [two_section_shards(): lax.dynamic_slice_in_dim(order, (1 - section) * per_section, per_section)]
  transfers between devices with their start and end apart: 4 -> 4, of which waited for: 3 -> 3; matrix products, arithmetic and copies ran while one was open for 16% -> 6% of each run, Pallas kernels for 0% -> 10%
where the time goes in v8:
time: 47.3 us; the launch traced here: 46.7 us
  Pallas kernels  28 us (59%)
  waiting for transfers between devices  7.42 us (16%)
  starting transfers between devices  3.6 us (8%)
  local copies, waits for them, and re-layouts  3.19 us (7%)
  matrix products  2.57 us (5%)
  other arithmetic  1.24 us (3%)
  between operations  0.69 us (1%)
    pallas_call x6, Pallas kernels, block_matmul(): pl.pallas_call(block_matmul_kernel, grid_spec=grid_spec, out_shape=jax.Sh...  28 us
    ppermute x1, waiting for transfers between devices, swapped(): return lax.ppermute(block, axis, route)  4.85 us
    ppermute x1, starting transfers between devices, swapped(): return lax.ppermute(block, axis, route)  2.7 us
    ppermute x3, waiting for transfers between devices, pair_swap(): return lax.ppermute(block, axis, [(0, 1), (1, 0)])  2.57 us
    dot_general x2, matrix products, matmul(): jnp.dot(left, right, precision=precision, preferred_element_type=jnp.floa...  2.57 us
    iota x3, local copies, waits for them, and re-layouts, two_section_leaf(): steps = jnp.arange(tile_rows // ROW_BLOCK)  1.57 us
    add x1, other arithmetic, two_section_shards(): block_matmul(update_panel, leaf_solution, own_blocks, 0, ROW_BLOCK)  1.15 us
  transfers between devices with their start and end apart: 4, of which 3 were waited for; matrix products, arithmetic and copies ran while one was open for 6% of the time, Pallas kernels for 10%

profile of v8, /device:TPU:0, one launch (start us, length us, event | category | flops | bytes accessed | tf_op | source)
XLA Modules:
  0.0 46.7 jit_solution(6082668306494902012)
XLA Ops:
  0.6 0.0 copy-start.5
  0.6 0.5 %iota.20.rows_ref = s32[4]{0:T(128)} iota(), iota_dimension=0 | iota | bytes 16 | tf_op jit(solution)/shard_map/iota | solution.py:141
  1.2 4.7 %shard_map.77 = f32[512,256]{1,0:T(8,128)} custom-call(s32[4]{0:T(128)} %iota.20.rows_ref, s32[1]{0:T(128)} %bitcast.column_ref.keep_ref, s32[1]{0:T(128)} %constant.15.clone.1.keep_ref, f32[512,1024]{1,0:T(8,128)} %left_ref.7, f32[512,256]{1,0:T(8,128)} %rest_0_.1), custom_call_target="tpu_custom_call" | custom-call | tf_op jit(solution)/shard_map/pallas_call | solution.py:122
  5.8 0.5 collective-permute-start
  6.3 0.0 copy-done.5
  6.3 0.1 select_reduce_fusion
  6.4 0.6 %fusion.14 = (s32[4]{0:T(128)}, s32[4]{0:T(128)}) fusion(s32[8]{0:T(128)S(1)} %select_reduce_fusion, s32[]{:T(128)S(6)} %select_n.36, s32[]{:T(128)S(6)} %select_n.35), kind=kLoop, calls=%fused_computation.17 | loop fusion | bytes 72 | tf_op jit(solution)/shard_map/dynamic_slice | solution.py:161
  7.0 1.0 %collective-permute-done.right_ref = f32[512,256]{1,0:T(8,128)S(1)} collective-permute-done((f32[512,256]{1,0:T(8,128)}, f32[512,256]{1,0:T(8,128)S(1)}, u32[]{:S(2)}, u32[]{:S(2)}) %collective-permute-start) | collective-permute-done | bytes 524320 | tf_op jit(solution)/shard_map/ppermute | solution.py:130
  8.0 0.0 copy-start.2
  8.0 0.5 %iota.19.rows_ref = s32[4]{0:T(128)} iota(), iota_dimension=0 | iota | bytes 16 | tf_op jit(solution)/shard_map/iota | solution.py:141
  8.6 0.3 copy-done.2
  8.8 4.8 %shard_map.78.right_ref = f32[512,256]{1,0:T(8,128)} custom-call(s32[4]{0:T(128)} %iota.19.rows_ref, s32[1]{0:T(128)} %constant.16.clone.1.column_ref, s32[1]{0:T(128)} %bitcast.column_ref.keep_ref, f32[512,1024]{1,0:T(8,128)} %left_ref.7, f32[512,256]{1,0:T(8,128)} %copy-done.2, f32[512,256]{1,0:T(8,128)} %rest_0_.1), custom_call_target="tpu_custom_call" | custom-call | tf_op jit(solution)/shard_map/pallas_call | solution.py:122
  13.6 0.5 %iota.18.rows_ref = s32[4]{0:T(128)} iota(), iota_dimension=0 | iota | bytes 16 | tf_op jit(solution)/shard_map/iota | solution.py:141
  14.1 4.7 %shard_map.79.right_ref = f32[512,256]{1,0:T(8,128)} custom-call(s32[4]{0:T(128)} %iota.18.rows_ref, s32[1]{0:T(128)} %bitcast.column_ref.keep_ref, s32[1]{0:T(128)} %constant.15.clone.1.keep_ref, f32[512,1024]{1,0:T(8,128)} %left_ref.7, f32[512,256]{1,0:T(8,128)} %shard_map.78.right_ref), custom_call_target="tpu_custom_call" | custom-call | tf_op jit(solution)/shard_map/pallas_call | solution.py:122
  18.8 4.6 %shard_map.81 = f32[512,256]{1,0:T(8,128)} custom-call(s32[4]{0:T(128)} %get-tuple-element.6.rows_ref, s32[1]{0:T(128)} %constant.16.clone.1.column_ref, s32[1]{0:T(128)} %constant.15.clone.1.keep_ref, f32[1024,512]{1,0:T(8,128)} %left_ref.9, f32[512,256]{1,0:T(8,128)} %shard_map.79.right_ref), custom_call_target="tpu_custom_call" | custom-call | tf_op jit(solution)/shard_map/pallas_call | solution.py:122
  23.4 0.4 collective-permute-start.1
  23.8 0.0 copy-start
  23.8 4.8 %shard_map.80 = f32[512,256]{1,0:T(8,128)} custom-call(s32[4]{0:T(128)} %get-tuple-element.7.rows_ref, s32[1]{0:T(128)} %constant.16.clone.1.column_ref, s32[1]{0:T(128)} %constant.15.clone.1.keep_ref, f32[1024,512]{1,0:T(8,128)} %left_ref.9, f32[512,256]{1,0:T(8,128)} %shard_map.79.right_ref), custom_call_target="tpu_custom_call" | custom-call | tf_op jit(solution)/shard_map/pallas_call | solution.py:122
  28.6 0.0 copy-start.3
  28.6 0.0 collective-permute-done.1
  28.6 1.2 %add.27 = f32[512,256]{1,0:T(8,128)S(1)} add(f32[512,256]{1,0:T(8,128)} %shard_map.80, f32[512,256]{1,0:T(8,128)S(1)} %collective-permute-done.1) | non-fusion elementwise | flops 131072 | bytes 1572864 | tf_op jit(solution)/shard_map/add | solution.py:165
  29.8 2.7 %collective-permute-start.2 = (f32[512,128]{1,0:T(8,128)S(1)}, f32[512,128]{1,0:T(8,128)S(1)}, u32[]{:S(2)}, u32[]{:S(2)}) collective-permute-start(f32[512,128]{1,0:T(8,128)S(1)} %constant_dynamic-slice_fusion), channel_id=1, source_target_pairs={{0,2},{2,0},{4,6},{6,4},{8,10},{10,8},{12,14},{14,12},{16,18},{18,... | collective-permute-start | bytes 786440 | tf_op jit(solution)/shard_map/ppermute | solution.py:24
  32.5 0.0 copy-done
  32.5 2.0 %fusion.left_ref = f32[512,512]{1,0:T(8,128)} fusion(f32[512,1024]{1,0:T(8,128)S(1)} %copy-done, s32[]{:T(128)S(6)} %select_n.39, pred[]{:T(512)S(6)} %gt.3), kind=kOutput, calls=%fused_computation | convolution fusion | flops 805568512 | bytes 3145733 | tf_op jit(solution)/shard_map/dot_general | solution.py:28
  34.4 4.8 %collective-permute-done.2 = f32[512,128]{1,0:T(8,128)S(1)} collective-permute-done((f32[512,128]{1,0:T(8,128)S(1)}, f32[512,128]{1,0:T(8,128)S(1)}, u32[]{:S(2)}, u32[]{:S(2)}) %collective-permute-start.2) | collective-permute-done | bytes 262176 | tf_op jit(solution)/shard_map/ppermute | solution.py:24
  39.3 0.0 copy-done.3
  39.3 0.6 %fusion.3.rest_0_ = f32[512,128]{1,0:T(8,128)S(1)} fusion(f32[512,1024]{1,0:T(8,128)S(1)} %copy-done, s32[]{:T(128)S(6)} %select_n.39, f32[512,128]{1,0:T(8,128)S(1)} %copy-done.3, f32[512,128]{1,0:T(8,128)S(1)} %collective-permute-done.2, f32[512,256]{1,0:T(8,128)S(1)} %add.27, s32[]{:T(128)S(6)} %select_n.42), kind=kOutput, calls=%fused_computation.3 | convolution fusion | flops 201457664 | bytes 2097160 | tf_op jit(solution)/shard_map/dot_general | solution.py:28
  39.9 0.0 copy-start.1
  39.9 0.1 collective-permute-start.3
  40.0 1.5 %collective-permute-done.3.right_ref = f32[512,128]{1,0:T(8,128)S(1)} collective-permute-done((f32[512,128]{1,0:T(8,128)S(1)}, f32[512,128]{1,0:T(8,128)S(1)}, u32[]{:S(2)}, u32[]{:S(2)}) %collective-permute-start.3) | collective-permute-done | bytes 262176 | tf_op jit(solution)/shard_map/ppermute | solution.py:130
  41.5 0.0 copy-start.4
  41.5 0.6 %iota.21.rows_ref = s32[4]{0:T(128)} iota(), iota_dimension=0 | iota | bytes 16 | tf_op jit(solution)/shard_map/iota | solution.py:178
  42.1 0.0 copy-done.1
  42.1 0.1 copy-done.4
  42.2 4.5 %shard_map.82 = f32[512,128]{1,0:T(8,128)} custom-call(s32[4]{0:T(128)} %iota.21.rows_ref, s32[1]{0:T(128)} %constant.16.clone.1.column_ref, s32[1]{0:T(128)} %constant.15.clone.1.keep_ref, f32[512,512]{1,0:T(8,128)} %fusion.left_ref, f32[512,128]{1,0:T(8,128)} %copy-done.4, f32[512,128]{1,0:T(8,128)} %copy-done.1), custom_call_target="tpu_custom_call" | custom-call | tf_op jit(solution)/shard_map/pallas_call | solution.py:122
  (1 shorter events, 0.0 us)
Async XLA Ops:
  0.6 5.6 %copy-start.5 = (s32[1,8]{1,0:T(1,128)S(1)}, s32[1,8]{1,0:T(1,128)}, u32[]{:S(2)}) copy-start(s32[1,8]{1,0:T(1,128)} %param.9) | copy-start | bytes 100
  5.8 2.2 %collective-permute-start = (f32[512,256]{1,0:T(8,128)}, f32[512,256]{1,0:T(8,128)S(1)}, u32[]{:S(2)}, u32[]{:S(2)}) collective-permute-start(f32[512,256]{1,0:T(8,128)} %shard_map.77), channel_id=1, source_target_pairs={{0,1},{1,0},{2,3},{3,2},{4,5},{5,4},{6,7},{7,6},{8,9},{9,8},{10,11... | collective-permute-start | bytes 1572872 | tf_op jit(solution)/shard_map/ppermute | solution.py:130
  8.0 0.8 %copy-start.2 = (f32[512,256]{1,0:T(8,128)}, f32[512,256]{1,0:T(8,128)S(1)}, u32[]{:S(2)}) copy-start(f32[512,256]{1,0:T(8,128)S(1)} %collective-permute-done.right_ref) | copy-start | bytes 1572868
  23.4 5.2 %collective-permute-start.1 = (f32[512,256]{1,0:T(8,128)}, f32[512,256]{1,0:T(8,128)S(1)}, u32[]{:S(2)}, u32[]{:S(2)}) collective-permute-start(f32[512,256]{1,0:T(8,128)} %shard_map.81), channel_id=1, source_target_pairs={{0,1},{1,0},{2,3},{3,2},{4,5},{5,4},{6,7},{7,6},{8,9},{9,8},{10,11... | collective-permute-start | bytes 1572872 | tf_op jit(solution)/shard_map/ppermute | solution.py:130
  23.8 8.7 %copy-start = (f32[512,1024]{1,0:T(8,128)S(1)}, f32[512,1024]{1,0:T(8,128)}, u32[]{:S(2)}) copy-start(f32[512,1024]{1,0:T(8,128)} %param.10) | copy-start | bytes 6291460
  28.6 10.7 %copy-start.3 = (f32[512,128]{1,0:T(8,128)S(1)}, f32[512,128]{1,0:T(8,128)}, u32[]{:S(2)}) copy-start(f32[512,128]{1,0:T(8,128)} %param.11) | copy-start | bytes 786436
  29.8 9.5 %collective-permute-start.2 = (f32[512,128]{1,0:T(8,128)S(1)}, f32[512,128]{1,0:T(8,128)S(1)}, u32[]{:S(2)}, u32[]{:S(2)}) collective-permute-start(f32[512,128]{1,0:T(8,128)S(1)} %constant_dynamic-slice_fusion), channel_id=1, source_target_pairs={{0,2},{2,0},{4,6},{6,4},{8,10},{10,8},{12,14},{14,12},{16,18},{18,... | collective-permute-start | bytes 786440 | tf_op jit(solution)/shard_map/ppermute | solution.py:24
  39.9 2.2 %copy-start.1 = (f32[512,128]{1,0:T(8,128)}, f32[512,128]{1,0:T(8,128)S(1)}, u32[]{:S(2)}) copy-start(f32[512,128]{1,0:T(8,128)S(1)} %fusion.3.rest_0_) | copy-start | bytes 786436
  39.9 1.6 %collective-permute-start.3 = (f32[512,128]{1,0:T(8,128)S(1)}, f32[512,128]{1,0:T(8,128)S(1)}, u32[]{:S(2)}, u32[]{:S(2)}) collective-permute-start(f32[512,128]{1,0:T(8,128)S(1)} %fusion.3.rest_0_), channel_id=1, source_target_pairs={{0,1},{1,0},{2,3},{3,2},{4,5},{5,4},{6,7},{7,6},{8,9},{9,8},{10,11... | collective-permute-start | bytes 786440 | tf_op jit(solution)/shard_map/ppermute | solution.py:130
  41.5 0.7 %copy-start.4 = (f32[512,128]{1,0:T(8,128)}, f32[512,128]{1,0:T(8,128)S(1)}, u32[]{:S(2)}) copy-start(f32[512,128]{1,0:T(8,128)S(1)} %collective-permute-done.3.right_ref) | copy-start | bytes 786436

commit v9 on v7

--- a/solution.py
+++ b/solution.py
@@ -86,9 +86,11 @@
 def two_section_leaf(factor, right_side, section, precision):
     tile_rows = right_side.shape[0]
     diagonal = lax.dynamic_slice_in_dim(factor, section * tile_rows, tile_rows, 1)
+    diagonal = lax.optimization_barrier(diagonal)
     first = matmul(diagonal, right_side, precision)
     arrived = pair_swap(first, "rows")
     below = jnp.where(section > 0, factor[:, :tile_rows], jnp.zeros_like(diagonal))
+    below, first = lax.optimization_barrier((below, first))
     return matmul(diagonal, right_side - matmul(below, arrived, precision), precision)
 
 

time: 26.5 us -> 29.6 us (1.12)
  other arithmetic: 0.09 us -> 3.03 us
  local copies, waits for them, and re-layouts: 3.31 us -> 4.13 us
  matrix products: 11.1 us -> 10.4 us
    select_n x0 -> x1, other arithmetic: none -> 2.94 us  [two_section_leaf(): jnp.where(section > 0, factor[:, :tile_rows], jnp.zeros_like(diagonal))]
    unnamed x16, local copies, waits for them, and re-layouts: 0.04 us -> 0.82 us
    dot_general x8, matrix products: 11.1 us -> 10.4 us  [matmul(): jnp.dot(left, right, precision=precision, preferred_element_type=jnp.floa...]
  transfers between devices with their start and end apart: 4 -> 4, of which waited for: 3 -> 4; matrix products, arithmetic and copies ran while one was open for 16% -> 15% of each run, Pallas kernels for 0% -> 0%
where the time goes in v9:
time: 29.6 us; the launch traced here: 29.5 us
  matrix products  10.4 us (35%)
  waiting for transfers between devices  7.47 us (25%)
  local copies, waits for them, and re-layouts  4.13 us (14%)
  starting transfers between devices  3.7 us (12%)
  other arithmetic  3.03 us (10%)
  between operations  0.73 us (2%)
    dot_general x8, matrix products, matmul(): jnp.dot(left, right, precision=precision, preferred_element_type=jnp.floa...  10.4 us
    ppermute x1, waiting for transfers between devices, swapped(): return lax.ppermute(block, axis, route)  5.63 us
    gather x2, local copies, waits for them, and re-layouts, section_panel(): taken = jnp.take(blocks, chosen, axis=0, mode='clip')  3.2 us
    select_n x1, other arithmetic, two_section_leaf(): jnp.where(section > 0, factor[:, :tile_rows], jnp.zeros_like(diagonal))  2.94 us
    ppermute x1, starting transfers between devices, swapped(): return lax.ppermute(block, axis, route)  2.88 us
    ppermute x3, waiting for transfers between devices, pair_swap(): return lax.ppermute(block, axis, [(0, 1), (1, 0)])  1.83 us
    ppermute x3, starting transfers between devices, pair_swap(): return lax.ppermute(block, axis, [(0, 1), (1, 0)])  0.82 us
    unnamed x16, local copies, waits for them, and re-layouts  0.82 us
  transfers between devices with their start and end apart: 4, of which 4 were waited for; matrix products, arithmetic and copies ran while one was open for 15% of the time, Pallas kernels for 0%

profile of v9, /device:TPU:0, one launch (start us, length us, event | category | flops | bytes accessed | tf_op | source)
XLA Modules:
  0.0 29.5 jit_solution(10139480305322840461)
XLA Ops:
  0.6 0.0 copy-start
  0.7 0.0 copy-start.4
  0.7 2.9 %slice_select_fusion = (f32[512,512]{1,0:T(8,128)}, f32[512,512]{1,0:T(8,128)S(1)}) fusion(f32[512,1024]{1,0:T(8,128)} %param.6, pred[]{:T(512)S(6)} %gt.4, s32[]{:T(128)S(6)} %select_n.39), kind=kLoop, calls=%fused_computation.8 | loop fusion | flops 262144 | bytes 4194309 | tf_op jit(solution)/shard_map/jit(_where)/select_n | solution.py:92
  3.6 0.0 copy-start.7
  3.6 0.0 copy-done.4
  3.6 1.4 %fusion.15 = f32[512,256]{1,0:T(8,128)} fusion(f32[512,512]{1,0:T(8,128)S(1)} %get-tuple-element.9, f32[512,256]{1,0:T(8,128)S(1)} %copy-done.4), kind=kOutput, calls=%fused_computation.27 | convolution fusion | flops 402653184 | bytes 2097152 | tf_op jit(solution)/shard_map/dot_general | solution.py:26
  5.0 0.5 %collective-permute-start = (f32[512,256]{1,0:T(8,128)}, f32[512,256]{1,0:T(8,128)}, u32[]{:S(2)}, u32[]{:S(2)}) collective-permute-start(f32[512,256]{1,0:T(8,128)} %fusion.15), channel_id=1, source_target_pairs={{0,1},{1,0},{2,3},{3,2},{4,5},{5,4},{6,7},{7,6},{8,9},{9,8},{10,11... | collective-permute-start | bytes 1572872 | tf_op jit(solution)/shard_map/ppermute | solution.py:77
  5.5 0.0 copy-done.7
  5.5 0.1 select_reduce_fusion
  5.5 0.1 fusion.14
  5.6 0.0 copy-done
  5.6 1.6 %gather_fusion.1 = f32[4,128,512]{2,1,0:T(8,128)} fusion(f32[8,128,512]{2,1,0:T(8,128)S(1)} %bitcast.17, s32[1024]{0:T(1024)S(1)} %get-tuple-element.12), kind=kCustom, calls=%fused_computation.1 | custom fusion | bytes 2097168 | tf_op jit(solution)/shard_map/jit(_take)/gather | solution.py:114
  7.2 0.0 copy-start.3
  7.3 0.1 collective-permute-done
  7.3 2.2 %convolution_subtract_fusion = f32[512,256]{1,0:T(8,128)S(1)} fusion(f32[512,256]{1,0:T(8,128)} %param.7, f32[512,512]{1,0:T(8,128)} %get-tuple-element.5, f32[512,256]{1,0:T(8,128)} %collective-permute-done), kind=kOutput, calls=%fused_computation.3 | convolution fusion | flops 402784256 | bytes 2621440 | tf_op jit(solution)/shard_map/dot_general | solution.py:26
  9.5 0.6 %fusion.16 = f32[512,256]{1,0:T(8,128)S(1)} fusion(f32[512,512]{1,0:T(8,128)S(1)} %get-tuple-element.9, f32[512,256]{1,0:T(8,128)S(1)} %convolution_subtract_fusion), kind=kOutput, calls=%fused_computation.28 | convolution fusion | flops 402653184 | bytes 2097152 | tf_op jit(solution)/shard_map/dot_general | solution.py:26
  10.1 0.0 copy-start.1
  10.1 0.8 %copy-done.1 = f32[512,256]{1,0:T(8,128)} copy-done((f32[512,256]{1,0:T(8,128)}, f32[512,256]{1,0:T(8,128)S(1)}, u32[]{:S(2)}) %copy-start.1) | copy-done | bytes 524312
  10.9 0.0 copy-done.3
  10.9 1.4 %fusion.17 = f32[512,256]{1,0:T(8,128)} fusion(f32[512,512]{1,0:T(8,128)S(1)} %bitcast.19, f32[512,256]{1,0:T(8,128)S(1)} %fusion.16), kind=kOutput, calls=%fused_computation.29 | convolution fusion | flops 402653184 | bytes 2097152 | tf_op jit(solution)/shard_map/dot_general | solution.py:26
  12.3 0.0 copy-start.2
  12.3 0.3 %collective-permute-start.1 = (f32[512,256]{1,0:T(8,128)}, f32[512,256]{1,0:T(8,128)S(1)}, u32[]{:S(2)}, u32[]{:S(2)}) collective-permute-start(f32[512,256]{1,0:T(8,128)} %fusion.17), channel_id=1, source_target_pairs={{0,1},{1,0},{2,3},{3,2},{4,5},{5,4},{6,7},{7,6},{8,9},{9,8},{10,11... | collective-permute-start | bytes 1572872 | tf_op jit(solution)/shard_map/ppermute | solution.py:77
  12.6 1.6 %gather_fusion = f32[4,128,512]{2,1,0:T(8,128)} fusion(f32[8,128,512]{2,1,0:T(8,128)S(1)} %bitcast.16, s32[1024]{0:T(1024)S(1)} %get-tuple-element.13), kind=kCustom, calls=%fused_computation | custom fusion | bytes 2097168 | tf_op jit(solution)/shard_map/jit(_take)/gather | solution.py:114
  14.2 0.0 copy-start.5
  14.2 0.2 collective-permute-done.1
  14.4 0.0 copy-done.2
  14.4 0.0 copy-start.6
  14.4 1.9 %convolution_add_fusion = f32[512,256]{1,0:T(8,128)S(1)} fusion(f32[512,256]{1,0:T(8,128)S(1)} %collective-permute-done.1, f32[512,512]{1,0:T(8,128)} %bitcast.18, f32[512,256]{1,0:T(8,128)S(1)} %copy-done.2), kind=kOutput, calls=%fused_computation.2 | convolution fusion | flops 402784256 | bytes 2621440 | tf_op jit(solution)/shard_map/dot_general | solution.py:26
  16.4 2.9 %collective-permute-start.2 = (f32[512,128]{1,0:T(8,128)S(1)}, f32[512,128]{1,0:T(8,128)S(1)}, u32[]{:S(2)}, u32[]{:S(2)}) collective-permute-start(f32[512,128]{1,0:T(8,128)S(1)} %constant_dynamic-slice_fusion), channel_id=1, source_target_pairs={{0,2},{2,0},{4,6},{6,4},{8,10},{10,8},{12,14},{14,12},{16,18},{18,... | collective-permute-start | bytes 786440 | tf_op jit(solution)/shard_map/ppermute | solution.py:22
  19.3 0.0 copy-done.5
  19.3 1.0 %fusion = f32[512,512]{1,0:T(8,128)S(1)} fusion(f32[512,1024]{1,0:T(8,128)S(1)} %copy-done.5, s32[]{:T(128)S(6)} %select_n.39, pred[]{:T(512)S(6)} %gt.4), kind=kOutput, calls=%fused_computation.5 | convolution fusion | flops 805568512 | bytes 3145733 | tf_op jit(solution)/shard_map/dot_general | solution.py:26
  20.3 5.6 %collective-permute-done.2 = f32[512,128]{1,0:T(8,128)S(1)} collective-permute-done((f32[512,128]{1,0:T(8,128)S(1)}, f32[512,128]{1,0:T(8,128)S(1)}, u32[]{:S(2)}, u32[]{:S(2)}) %collective-permute-start.2) | collective-permute-done | bytes 262176 | tf_op jit(solution)/shard_map/ppermute | solution.py:22
  26.0 0.0 copy-done.6
  26.0 0.6 %fusion.3 = f32[512,128]{1,0:T(8,128)S(1)} fusion(f32[512,1024]{1,0:T(8,128)S(1)} %copy-done.5, s32[]{:T(128)S(6)} %select_n.39, f32[512,128]{1,0:T(8,128)S(1)} %copy-done.6, f32[512,128]{1,0:T(8,128)S(1)} %collective-permute-done.2, f32[512,256]{1,0:T(8,128)S(1)} %convolution_add_fusion, s32[]{:T(128)S(6)} %select_n.46), kind=kOutput, calls=%fused_computation.9 | convolution fusion | flops 201457664 | bytes 2097160 | tf_op jit(solution)/shard_map/dot_general | solution.py:26
  26.6 0.1 collective-permute-start.3
  26.6 1.5 %collective-permute-done.3 = f32[512,128]{1,0:T(8,128)S(1)} collective-permute-done((f32[512,128]{1,0:T(8,128)S(1)}, f32[512,128]{1,0:T(8,128)S(1)}, u32[]{:S(2)}, u32[]{:S(2)}) %collective-permute-start.3) | collective-permute-done | bytes 262176 | tf_op jit(solution)/shard_map/ppermute | solution.py:77
  28.2 1.3 %convolution_subtract_fusion.1 = f32[512,128]{1,0:T(8,128)} fusion(f32[512,128]{1,0:T(8,128)S(1)} %fusion.3, f32[512,512]{1,0:T(8,128)S(1)} %fusion, f32[512,128]{1,0:T(8,128)S(1)} %collective-permute-done.3), kind=kOutput, calls=%fused_computation.4 | convolution fusion | flops 201392128 | bytes 1835008 | tf_op jit(solution)/shard_map/dot_general | solution.py:26
  (2 shorter events, 0.0 us)
Async XLA Ops:
  0.6 5.0 %copy-start = (f32[1024,512]{1,0:T(8,128)S(1)}, f32[1024,512]{1,0:T(8,128)}, u32[]{:S(2)}) copy-start(f32[1024,512]{1,0:T(8,128)} %param.8) | copy-start | bytes 6291460
  0.7 3.0 %copy-start.4 = (f32[512,256]{1,0:T(8,128)S(1)}, f32[512,256]{1,0:T(8,128)}, u32[]{:S(2)}) copy-start(f32[512,256]{1,0:T(8,128)} %param.7) | copy-start | bytes 1572868
  3.6 1.9 %copy-start.7 = (s32[1,8]{1,0:T(1,128)S(1)}, s32[1,8]{1,0:T(1,128)}, u32[]{:S(2)}) copy-start(s32[1,8]{1,0:T(1,128)} %param.9) | copy-start | bytes 100
  5.0 2.3 %collective-permute-start = (f32[512,256]{1,0:T(8,128)}, f32[512,256]{1,0:T(8,128)}, u32[]{:S(2)}, u32[]{:S(2)}) collective-permute-start(f32[512,256]{1,0:T(8,128)} %fusion.15), channel_id=1, source_target_pairs={{0,1},{1,0},{2,3},{3,2},{4,5},{5,4},{6,7},{7,6},{8,9},{9,8},{10,11... | collective-permute-start | bytes 1572872 | tf_op jit(solution)/shard_map/ppermute | solution.py:77
  7.2 3.7 %copy-start.3 = (f32[4,128,512]{2,1,0:T(8,128)S(1)}, f32[4,128,512]{2,1,0:T(8,128)}, u32[]{:S(2)}) copy-start(f32[4,128,512]{2,1,0:T(8,128)} %gather_fusion.1) | copy-start | bytes 3145732
  10.1 0.8 %copy-start.1 = (f32[512,256]{1,0:T(8,128)}, f32[512,256]{1,0:T(8,128)S(1)}, u32[]{:S(2)}) copy-start(f32[512,256]{1,0:T(8,128)S(1)} %fusion.16) | copy-start | bytes 1572868
  12.3 2.1 %copy-start.2 = (f32[512,256]{1,0:T(8,128)S(1)}, f32[512,256]{1,0:T(8,128)}, u32[]{:S(2)}) copy-start(f32[512,256]{1,0:T(8,128)} %copy-done.1) | copy-start | bytes 1572868
  12.3 2.1 %collective-permute-start.1 = (f32[512,256]{1,0:T(8,128)}, f32[512,256]{1,0:T(8,128)S(1)}, u32[]{:S(2)}, u32[]{:S(2)}) collective-permute-start(f32[512,256]{1,0:T(8,128)} %fusion.17), channel_id=1, source_target_pairs={{0,1},{1,0},{2,3},{3,2},{4,5},{5,4},{6,7},{7,6},{8,9},{9,8},{10,11... | collective-permute-start | bytes 1572872 | tf_op jit(solution)/shard_map/ppermute | solution.py:77
  14.2 5.1 %copy-start.5 = (f32[512,1024]{1,0:T(8,128)S(1)}, f32[512,1024]{1,0:T(8,128)}, u32[]{:S(2)}) copy-start(f32[512,1024]{1,0:T(8,128)} %param.10) | copy-start | bytes 6291460
  14.4 11.5 %copy-start.6 = (f32[512,128]{1,0:T(8,128)S(1)}, f32[512,128]{1,0:T(8,128)}, u32[]{:S(2)}) copy-start(f32[512,128]{1,0:T(8,128)} %param.11) | copy-start | bytes 786436
  16.4 9.5 %collective-permute-start.2 = (f32[512,128]{1,0:T(8,128)S(1)}, f32[512,128]{1,0:T(8,128)S(1)}, u32[]{:S(2)}, u32[]{:S(2)}) collective-permute-start(f32[512,128]{1,0:T(8,128)S(1)} %constant_dynamic-slice_fusion), channel_id=1, source_target_pairs={{0,2},{2,0},{4,6},{6,4},{8,10},{10,8},{12,14},{14,12},{16,18},{18,... | collective-permute-start | bytes 786440 | tf_op jit(solution)/shard_map/ppermute | solution.py:22
  26.6 1.6 %collective-permute-start.3 = (f32[512,128]{1,0:T(8,128)S(1)}, f32[512,128]{1,0:T(8,128)S(1)}, u32[]{:S(2)}, u32[]{:S(2)}) collective-permute-start(f32[512,128]{1,0:T(8,128)S(1)} %fusion.3), channel_id=1, source_target_pairs={{0,1},{1,0},{2,3},{3,2},{4,5},{5,4},{6,7},{7,6},{8,9},{9,8},{10,11... | collective-permute-start | bytes 786440 | tf_op jit(solution)/shard_map/ppermute | solution.py:77

commit v10 on v7

--- a/solution.py
+++ b/solution.py
@@ -114,7 +114,9 @@
 
     other_rows = matmul(section_panel(1 - section), leaf_solution, precision)
     arrived_rows = pair_swap(other_rows, "rows")
-    chip_sum = matmul(section_panel(section), leaf_solution, precision) + arrived_rows
+    own_rows = matmul(section_panel(section), leaf_solution, precision)
+    own_rows, arrived_rows = lax.optimization_barrier((own_rows, arrived_rows))
+    chip_sum = own_rows + arrived_rows
     column_half = parent_rhs.shape[1]
     sibling = lax.axis_index("leaf") % 2
     kept = lax.dynamic_slice_in_dim(chip_sum, sibling * column_half, column_half, 1)

time: 26.5 us -> 26.4 us (level)
    ppermute x3, waiting for transfers between devices: 1.79 us -> 1.53 us  [pair_swap(): return lax.ppermute(block, axis, [(0, 1), (1, 0)])]
  transfers between devices with their start and end apart: 4 -> 4, of which waited for: 3 -> 2; matrix products, arithmetic and copies ran while one was open for 16% -> 24% of each run, Pallas kernels for 0% -> 0%
where the time goes in v10:
time: 26.4 us; the launch traced here: 26.2 us
  matrix products  11.1 us (42%)
  waiting for transfers between devices  7.26 us (28%)
  starting transfers between devices  3.66 us (14%)
  local copies, waits for them, and re-layouts  3.31 us (13%)
  between operations  0.78 us (3%)
    dot_general x8, matrix products, matmul(): jnp.dot(left, right, precision=precision, preferred_element_type=jnp.floa...  11.1 us
    ppermute x1, waiting for transfers between devices, swapped(): return lax.ppermute(block, axis, route)  5.73 us
    gather x2, local copies, waits for them, and re-layouts, section_panel(): taken = jnp.take(blocks, chosen, axis=0, mode='clip')  3.17 us
    ppermute x1, starting transfers between devices, swapped(): return lax.ppermute(block, axis, route)  2.79 us
    ppermute x3, waiting for transfers between devices, pair_swap(): return lax.ppermute(block, axis, [(0, 1), (1, 0)])  1.53 us
    ppermute x3, starting transfers between devices, pair_swap(): return lax.ppermute(block, axis, [(0, 1), (1, 0)])  0.86 us
  transfers between devices with their start and end apart: 4, of which 2 were waited for; matrix products, arithmetic and copies ran while one was open for 24% of the time, Pallas kernels for 0%

profile of v10, /device:TPU:0, one launch (start us, length us, event | category | flops | bytes accessed | tf_op | source)
XLA Modules:
  0.0 26.2 jit_solution(18059090540183969263)
XLA Ops:
  0.6 0.0 copy-start
  0.6 0.0 copy-start.7
  0.7 0.0 copy-start.4
  0.7 2.1 %fusion.10 = f32[512,256]{1,0:T(8,128)S(1)} fusion(f32[512,256]{1,0:T(8,128)} %param.7, f32[512,1024]{1,0:T(8,128)} %param.6, s32[]{:T(128)S(6)} %select_n.39), kind=kOutput, calls=%fused_computation.14 | convolution fusion | flops 402653184 | bytes 2097156 | tf_op jit(solution)/shard_map/dot_general | solution.py:26
  2.8 0.5 %collective-permute-start = (f32[512,256]{1,0:T(8,128)S(1)}, f32[512,256]{1,0:T(8,128)}, u32[]{:S(2)}, u32[]{:S(2)}) collective-permute-start(f32[512,256]{1,0:T(8,128)S(1)} %fusion.10), channel_id=1, source_target_pairs={{0,1},{1,0},{2,3},{3,2},{4,5},{5,4},{6,7},{7,6},{8,9},{9,8},{10,11... | collective-permute-start | bytes 1572872 | tf_op jit(solution)/shard_map/ppermute | solution.py:77
  3.3 0.0 copy-done.7
  3.3 0.1 select_reduce_fusion
  3.4 0.1 fusion.25
  3.5 0.0 copy-done
  3.5 1.6 %gather_fusion.1 = f32[4,128,512]{2,1,0:T(8,128)} fusion(f32[8,128,512]{2,1,0:T(8,128)S(1)} %bitcast.14, s32[1024]{0:T(1024)S(1)} %get-tuple-element.12), kind=kCustom, calls=%fused_computation.1 | custom fusion | bytes 2097168 | tf_op jit(solution)/shard_map/jit(_take)/gather | solution.py:112
  5.1 0.0 copy-start.1
  5.1 0.0 copy-start.3
  5.1 0.0 collective-permute-done
  5.1 0.0 copy-done.4
  5.1 2.1 %convolution_subtract_fusion = f32[512,256]{1,0:T(8,128)S(1)} fusion(f32[512,256]{1,0:T(8,128)S(1)} %copy-done.4, f32[512,256]{1,0:T(8,128)} %collective-permute-done, f32[512,1024]{1,0:T(8,128)} %param.6, pred[]{:T(512)S(6)} %gt.4), kind=kOutput, calls=%fused_computation.2 | convolution fusion | flops 403046400 | bytes 2621441 | tf_op jit(solution)/shard_map/dot_general | solution.py:26
  7.2 0.0 copy-done.1
  7.2 0.6 %fusion.8 = f32[512,256]{1,0:T(8,128)S(1)} fusion(f32[512,256]{1,0:T(8,128)S(1)} %convolution_subtract_fusion, f32[512,1024]{1,0:T(8,128)S(1)} %copy-done.1, s32[]{:T(128)S(6)} %select_n.39), kind=kOutput, calls=%fused_computation.12 | convolution fusion | flops 402653184 | bytes 2097156 | tf_op jit(solution)/shard_map/dot_general | solution.py:26
  7.8 0.0 copy-start.2
  7.8 0.0 copy-done.3
  7.8 1.4 %fusion.27 = f32[512,256]{1,0:T(8,128)} fusion(f32[512,512]{1,0:T(8,128)S(1)} %bitcast.15, f32[512,256]{1,0:T(8,128)S(1)} %fusion.8), kind=kOutput, calls=%fused_computation.36 | convolution fusion | flops 402653184 | bytes 2097152 | tf_op jit(solution)/shard_map/dot_general | solution.py:26
  9.2 0.3 %collective-permute-start.1 = (f32[512,256]{1,0:T(8,128)}, f32[512,256]{1,0:T(8,128)S(1)}, u32[]{:S(2)}, u32[]{:S(2)}) collective-permute-start(f32[512,256]{1,0:T(8,128)} %fusion.27), channel_id=1, source_target_pairs={{0,1},{1,0},{2,3},{3,2},{4,5},{5,4},{6,7},{7,6},{8,9},{9,8},{10,11... | collective-permute-start | bytes 1572872 | tf_op jit(solution)/shard_map/ppermute | solution.py:77
  9.5 1.6 %gather_fusion = f32[4,128,512]{2,1,0:T(8,128)} fusion(f32[8,128,512]{2,1,0:T(8,128)S(1)} %bitcast.13, s32[1024]{0:T(1024)S(1)} %get-tuple-element.13), kind=kCustom, calls=%fused_computation | custom fusion | bytes 2097168 | tf_op jit(solution)/shard_map/jit(_take)/gather | solution.py:112
  11.1 0.0 copy-done.2
  11.1 0.0 copy-start.5
  11.1 2.0 %fusion.26 = f32[512,256]{1,0:T(8,128)S(1)} fusion(f32[512,512]{1,0:T(8,128)} %bitcast.16, f32[512,256]{1,0:T(8,128)S(1)} %fusion.8), kind=kOutput, calls=%fused_computation.35 | convolution fusion | flops 402653184 | bytes 2097152 | tf_op jit(solution)/shard_map/dot_general | solution.py:26
  13.1 0.0 copy-start.6
  13.1 0.0 collective-permute-done.1
  13.1 0.1 add.29
  13.2 2.8 %collective-permute-start.2 = (f32[512,128]{1,0:T(8,128)S(1)}, f32[512,128]{1,0:T(8,128)S(1)}, u32[]{:S(2)}, u32[]{:S(2)}) collective-permute-start(f32[512,128]{1,0:T(8,128)S(1)} %constant_dynamic-slice_fusion), channel_id=1, source_target_pairs={{0,2},{2,0},{4,6},{6,4},{8,10},{10,8},{12,14},{14,12},{16,18},{18,... | collective-permute-start | bytes 786440 | tf_op jit(solution)/shard_map/ppermute | solution.py:22
  16.0 0.0 copy-done.5
  16.0 1.0 %fusion = f32[512,512]{1,0:T(8,128)S(1)} fusion(f32[512,1024]{1,0:T(8,128)S(1)} %copy-done.5, s32[]{:T(128)S(6)} %select_n.39, pred[]{:T(512)S(6)} %gt.4), kind=kOutput, calls=%fused_computation.4 | convolution fusion | flops 805568512 | bytes 3145733 | tf_op jit(solution)/shard_map/dot_general | solution.py:26
  17.0 5.7 %collective-permute-done.2 = f32[512,128]{1,0:T(8,128)S(1)} collective-permute-done((f32[512,128]{1,0:T(8,128)S(1)}, f32[512,128]{1,0:T(8,128)S(1)}, u32[]{:S(2)}, u32[]{:S(2)}) %collective-permute-start.2) | collective-permute-done | bytes 262176 | tf_op jit(solution)/shard_map/ppermute | solution.py:22
  22.7 0.0 copy-done.6
  22.7 0.6 %fusion.5 = f32[512,128]{1,0:T(8,128)S(1)} fusion(f32[512,1024]{1,0:T(8,128)S(1)} %copy-done.5, s32[]{:T(128)S(6)} %select_n.39, f32[512,128]{1,0:T(8,128)S(1)} %copy-done.6, f32[512,128]{1,0:T(8,128)S(1)} %collective-permute-done.2, f32[512,256]{1,0:T(8,128)S(1)} %add.29, s32[]{:T(128)S(6)} %select_n.46), kind=kOutput, calls=%fused_computation.9 | convolution fusion | flops 201457664 | bytes 2097160 | tf_op jit(solution)/shard_map/dot_general | solution.py:26
  23.3 0.1 collective-permute-start.3
  23.4 1.5 %collective-permute-done.3 = f32[512,128]{1,0:T(8,128)S(1)} collective-permute-done((f32[512,128]{1,0:T(8,128)S(1)}, f32[512,128]{1,0:T(8,128)S(1)}, u32[]{:S(2)}, u32[]{:S(2)}) %collective-permute-start.3) | collective-permute-done | bytes 262176 | tf_op jit(solution)/shard_map/ppermute | solution.py:77
  24.9 1.3 %convolution_subtract_fusion.1 = f32[512,128]{1,0:T(8,128)} fusion(f32[512,128]{1,0:T(8,128)S(1)} %fusion.5, f32[512,512]{1,0:T(8,128)S(1)} %fusion, f32[512,128]{1,0:T(8,128)S(1)} %collective-permute-done.3), kind=kOutput, calls=%fused_computation.3 | convolution fusion | flops 201392128 | bytes 1835008 | tf_op jit(solution)/shard_map/dot_general | solution.py:26
  (2 shorter events, 0.0 us)
Async XLA Ops:
  0.6 2.9 %copy-start = (f32[1024,512]{1,0:T(8,128)S(1)}, f32[1024,512]{1,0:T(8,128)}, u32[]{:S(2)}) copy-start(f32[1024,512]{1,0:T(8,128)} %param.8) | copy-start | bytes 6291460
  0.6 2.7 %copy-start.7 = (s32[1,8]{1,0:T(1,128)S(1)}, s32[1,8]{1,0:T(1,128)}, u32[]{:S(2)}) copy-start(s32[1,8]{1,0:T(1,128)} %param.9) | copy-start | bytes 100
  0.7 4.4 %copy-start.4 = (f32[512,256]{1,0:T(8,128)S(1)}, f32[512,256]{1,0:T(8,128)}, u32[]{:S(2)}) copy-start(f32[512,256]{1,0:T(8,128)} %param.7) | copy-start | bytes 1572868
  2.8 2.3 %collective-permute-start = (f32[512,256]{1,0:T(8,128)S(1)}, f32[512,256]{1,0:T(8,128)}, u32[]{:S(2)}, u32[]{:S(2)}) collective-permute-start(f32[512,256]{1,0:T(8,128)S(1)} %fusion.10), channel_id=1, source_target_pairs={{0,1},{1,0},{2,3},{3,2},{4,5},{5,4},{6,7},{7,6},{8,9},{9,8},{10,11... | collective-permute-start | bytes 1572872 | tf_op jit(solution)/shard_map/ppermute | solution.py:77
  5.1 2.1 %copy-start.1 = (f32[512,1024]{1,0:T(8,128)S(1)}, f32[512,1024]{1,0:T(8,128)}, u32[]{:S(2)}) copy-start(f32[512,1024]{1,0:T(8,128)} %param.6) | copy-start | bytes 6291460
  5.1 2.7 %copy-start.3 = (f32[4,128,512]{2,1,0:T(8,128)S(1)}, f32[4,128,512]{2,1,0:T(8,128)}, u32[]{:S(2)}) copy-start(f32[4,128,512]{2,1,0:T(8,128)} %gather_fusion.1) | copy-start | bytes 3145732
  7.8 3.3 %copy-start.2 = (f32[512,256]{1,0:T(8,128)}, f32[512,256]{1,0:T(8,128)S(1)}, u32[]{:S(2)}) copy-start(f32[512,256]{1,0:T(8,128)S(1)} %fusion.8) | copy-start | bytes 1572868
  9.2 3.8 %collective-permute-start.1 = (f32[512,256]{1,0:T(8,128)}, f32[512,256]{1,0:T(8,128)S(1)}, u32[]{:S(2)}, u32[]{:S(2)}) collective-permute-start(f32[512,256]{1,0:T(8,128)} %fusion.27), channel_id=1, source_target_pairs={{0,1},{1,0},{2,3},{3,2},{4,5},{5,4},{6,7},{7,6},{8,9},{9,8},{10,11... | collective-permute-start | bytes 1572872 | tf_op jit(solution)/shard_map/ppermute | solution.py:77
  11.1 4.9 %copy-start.5 = (f32[512,1024]{1,0:T(8,128)S(1)}, f32[512,1024]{1,0:T(8,128)}, u32[]{:S(2)}) copy-start(f32[512,1024]{1,0:T(8,128)} %param.10) | copy-start | bytes 6291460
  13.1 9.7 %copy-start.6 = (f32[512,128]{1,0:T(8,128)S(1)}, f32[512,128]{1,0:T(8,128)}, u32[]{:S(2)}) copy-start(f32[512,128]{1,0:T(8,128)} %param.11) | copy-start | bytes 786436
  13.2 9.5 %collective-permute-start.2 = (f32[512,128]{1,0:T(8,128)S(1)}, f32[512,128]{1,0:T(8,128)S(1)}, u32[]{:S(2)}, u32[]{:S(2)}) collective-permute-start(f32[512,128]{1,0:T(8,128)S(1)} %constant_dynamic-slice_fusion), channel_id=1, source_target_pairs={{0,2},{2,0},{4,6},{6,4},{8,10},{10,8},{12,14},{14,12},{16,18},{18,... | collective-permute-start | bytes 786440 | tf_op jit(solution)/shard_map/ppermute | solution.py:22
  23.3 1.6 %collective-permute-start.3 = (f32[512,128]{1,0:T(8,128)S(1)}, f32[512,128]{1,0:T(8,128)S(1)}, u32[]{:S(2)}, u32[]{:S(2)}) collective-permute-start(f32[512,128]{1,0:T(8,128)S(1)} %fusion.5), channel_id=1, source_target_pairs={{0,1},{1,0},{2,3},{3,2},{4,5},{5,4},{6,7},{7,6},{8,9},{9,8},{10,11... | collective-permute-start | bytes 786440 | tf_op jit(solution)/shard_map/ppermute | solution.py:77

commit v11 on v10

--- a/solution.py
+++ b/solution.py
@@ -109,7 +109,10 @@
 
     def section_panel(rows_of):
         chosen = lax.dynamic_slice_in_dim(order, rows_of * per_section, per_section)
-        taken = jnp.take(blocks, chosen, axis=0, mode="clip")
+        taken = jnp.zeros((per_section,) + blocks.shape[1:], blocks.dtype)
+        for candidate in range(blocks.shape[0]):
+            hit = (chosen == candidate)[:, None, None]
+            taken = jnp.where(hit, blocks[candidate][None], taken)
         return taken.reshape(-1, update_panel.shape[1])
 
     other_rows = matmul(section_panel(1 - section), leaf_solution, precision)

time: 26.4 us -> 28.5 us (1.080)
  other arithmetic: 0.16 us -> 4.69 us
  local copies, waits for them, and re-layouts: 3.31 us -> 2.12 us
  matrix products: 11.1 us -> 10 us
    select_n x0 -> x2, other arithmetic: none -> 3.36 us  [section_panel(): taken = jnp.where(hit, blocks[candidate][None], taken)]
    gather x2 -> x0, local copies, waits for them, and re-layouts: 3.17 us -> none  [section_panel(): taken = jnp.take(blocks, chosen, axis=0, mode='clip')]
    broadcast_in_dim x0 -> x15, local copies, waits for them, and re-layouts: none -> 1.09 us  [section_panel(): taken = jnp.where(hit, blocks[candidate][None], taken)]
    add x1, other arithmetic: 0.07 us -> 1.15 us  [two_section_shards(): chip_sum = own_rows + arrived_rows]
    dot_general x8, matrix products: 11.1 us -> 10 us  [matmul(): jnp.dot(left, right, precision=precision, preferred_element_type=jnp.floa...]
    slice x0 -> x1, local copies, waits for them, and re-layouts: none -> 0.95 us  [section_panel(): taken = jnp.where(hit, blocks[candidate][None], taken)]
  transfers between devices with their start and end apart: 4 -> 4, of which waited for: 2 -> 2; matrix products, arithmetic and copies ran while one was open for 24% -> 25% of each run, Pallas kernels for 0% -> 0%
where the time goes in v11:
time: 28.5 us; the launch traced here: 28.2 us
  matrix products  10 us (35%)
  waiting for transfers between devices  6.98 us (24%)
  other arithmetic  4.69 us (16%)
  starting transfers between devices  3.59 us (13%)
  local copies, waits for them, and re-layouts  2.12 us (7%)
  between operations  0.84 us (3%)
    dot_general x8, matrix products, matmul(): jnp.dot(left, right, precision=precision, preferred_element_type=jnp.floa...  10 us
    ppermute x1, waiting for transfers between devices, swapped(): return lax.ppermute(block, axis, route)  5.45 us
    select_n x2, other arithmetic, section_panel(): taken = jnp.where(hit, blocks[candidate][None], taken)  3.36 us
    ppermute x1, starting transfers between devices, swapped(): return lax.ppermute(block, axis, route)  3 us
    ppermute x3, waiting for transfers between devices, pair_swap(): return lax.ppermute(block, axis, [(0, 1), (1, 0)])  1.53 us
    add x1, other arithmetic, two_section_shards(): chip_sum = own_rows + arrived_rows  1.15 us
    broadcast_in_dim x15, local copies, waits for them, and re-layouts, section_panel(): taken = jnp.where(hit, blocks[candidate][None], taken)  1.09 us
    slice x1, local copies, waits for them, and re-layouts, section_panel(): taken = jnp.where(hit, blocks[candidate][None], taken)  0.95 us
  transfers between devices with their start and end apart: 4, of which 2 were waited for; matrix products, arithmetic and copies ran while one was open for 25% of the time, Pallas kernels for 0%

profile of v11, /device:TPU:0, one launch (start us, length us, event | category | flops | bytes accessed | tf_op | source)
XLA Modules:
  0.0 28.2 jit_solution(3756703907734523553)
XLA Ops:
  0.6 0.0 copy-start.8
  0.6 2.9 %fusion.10 = f32[512,256]{1,0:T(8,128)} fusion(f32[512,256]{1,0:T(8,128)} %param.7, f32[512,1024]{1,0:T(8,128)} %param.6, s32[]{:T(128)S(6)} %select_n.104), kind=kOutput, calls=%fused_computation.28 | convolution fusion | flops 402653184 | bytes 2097156 | tf_op jit(solution)/shard_map/dot_general | solution.py:26
  3.5 0.5 %collective-permute-start = (f32[512,256]{1,0:T(8,128)}, f32[512,256]{1,0:T(8,128)}, u32[]{:S(2)}, u32[]{:S(2)}) collective-permute-start(f32[512,256]{1,0:T(8,128)} %fusion.10), channel_id=1, source_target_pairs={{0,1},{1,0},{2,3},{3,2},{4,5},{5,4},{6,7},{7,6},{8,9},{9,8},{10,11... | collective-permute-start | bytes 1572872 | tf_op jit(solution)/shard_map/ppermute | solution.py:77
  4.0 0.0 copy-done.8
  4.0 0.0 copy-start.12
  4.0 0.9 %fusion.25 = (f32[128,512]{1,0:T(8,128)S(1)}, f32[128,512]{1,0:T(8,128)S(1)}, f32[128,512]{1,0:T(8,128)S(1)}, f32[128,512]{1,0:T(8,128)S(1)}, f32[128,512]{1,0:T...) fusion(f32[1024,512]{1,0:T(8,128)S(1)} %copy-done.8), kind=kLoop, calls=%fused_computation.78 | loop fusion | bytes 4194304 | tf_op jit(solution)/shard_map/slice | solution.py:115
  4.9 0.0 copy-start.2
  4.9 0.0 copy-start.4
  4.9 0.0 copy-start
  4.9 0.0 copy-done.12
  5.0 0.1 select_reduce_fusion
  5.0 0.1 broadcast_compare_fusion.14
  5.1 0.1 broadcast_bitcast_fusion.8
  5.2 0.1 broadcast_bitcast_fusion.9
  5.3 0.1 broadcast_bitcast_fusion.10
  5.4 0.1 broadcast_bitcast_fusion
  5.4 0.1 broadcast_bitcast_fusion.1
  5.5 0.1 broadcast_bitcast_fusion.2
  5.6 0.1 broadcast_bitcast_fusion.3
  5.7 0.1 broadcast_bitcast_fusion.4
  5.7 0.1 broadcast_bitcast_fusion.5
  5.8 0.1 broadcast_bitcast_fusion.7
  5.9 0.1 broadcast_bitcast_fusion.6
  5.9 0.0 copy-start.9
  5.9 1.8 %bitcast_select_fusion.14 = f32[512,512]{1,0:T(8,128)S(1)} fusion(f32[128,512]{1,0:T(8,128)} %get-tuple-element.20, f32[128,512]{1,0:T(8,128)} %get-tuple-element.21, f32[128,512]{1,0:T(8,128)S(1)} %get-tuple-element.15, f32[128,512]{1,0:T(8,128)S(1)} %get-tuple-element.16, f32[128,512]{1,0:T(8,128)S(1)} %get-tuple-element.17, ...), kind=kLoop, calls=%fused_computation.14 | loop fusion | flops 2097152 | bytes 3149824 | tf_op jit(solution)/shard_map/jit(_where)/select_n | solution.py:115
  7.7 0.1 broadcast_bitcast_fusion.11
  7.8 0.1 broadcast_bitcast_fusion.12
  7.9 0.0 collective-permute-done
  7.9 0.0 copy-done.2
  7.9 0.0 copy-done.4
  7.9 0.0 copy-done
  7.9 0.0 copy-done.9
  7.9 1.6 %convolution_subtract_fusion = f32[512,256]{1,0:T(8,128)S(1)} fusion(f32[512,256]{1,0:T(8,128)S(1)} %copy-done.9, f32[512,256]{1,0:T(8,128)} %collective-permute-done, f32[512,1024]{1,0:T(8,128)S(1)} %copy-done, pred[]{:T(512)S(6)} %gt.4), kind=kOutput, calls=%fused_computation.16 | convolution fusion | flops 403046400 | bytes 2621441 | tf_op jit(solution)/shard_map/dot_general | solution.py:26
  9.6 0.6 %fusion.8 = f32[512,256]{1,0:T(8,128)S(1)} fusion(f32[512,256]{1,0:T(8,128)S(1)} %convolution_subtract_fusion, f32[512,1024]{1,0:T(8,128)S(1)} %copy-done, s32[]{:T(128)S(6)} %select_n.104), kind=kOutput, calls=%fused_computation.26 | convolution fusion | flops 402653184 | bytes 2097156 | tf_op jit(solution)/shard_map/dot_general | solution.py:26
  10.2 0.0 copy-start.1
  10.2 0.0 copy-start.3
  10.2 0.0 copy-start.5
  10.2 0.0 copy-start.6
  10.2 0.0 copy-start.7
  10.2 1.4 %fusion.27 = f32[512,256]{1,0:T(8,128)} fusion(f32[512,512]{1,0:T(8,128)S(1)} %bitcast_select_fusion.14, f32[512,256]{1,0:T(8,128)S(1)} %fusion.8), kind=kOutput, calls=%fused_computation.80 | convolution fusion | flops 402653184 | bytes 2097152 | tf_op jit(solution)/shard_map/dot_general | solution.py:26
  11.6 0.1 collective-permute-start.1
  11.7 0.1 broadcast_bitcast_fusion.13
  11.7 0.1 broadcast_bitcast_fusion.14
  11.8 0.0 copy-done.3
  11.8 0.0 copy-done.5
  11.8 0.0 copy-done.6
  11.8 0.0 copy-done.7
  11.8 1.6 %bitcast_select_fusion.15 = f32[512,512]{1,0:T(8,128)S(1)} fusion(f32[128,512]{1,0:T(8,128)S(1)} %copy-done.7, f32[128,512]{1,0:T(8,128)} %get-tuple-element.21, f32[128,512]{1,0:T(8,128)S(1)} %get-tuple-element.15, f32[128,512]{1,0:T(8,128)S(1)} %get-tuple-element.16, f32[128,512]{1,0:T(8,128)S(1)} %copy-done.3, f32[128,512]{1,0:T(8,128)S(1)} %copy-done.5, ...), kind=kLoop, calls=%fused_computation.15 | loop fusion | flops 2097152 | bytes 3149824 | tf_op jit(solution)/shard_map/jit(_where)/select_n | solution.py:115
  13.4 0.0 copy-done.1
  13.4 0.0 copy-start.10
  13.4 0.6 %fusion.26 = f32[512,256]{1,0:T(8,128)S(1)} fusion(f32[512,512]{1,0:T(8,128)S(1)} %bitcast_select_fusion.15, f32[512,256]{1,0:T(8,128)S(1)} %fusion.8), kind=kOutput, calls=%fused_computation.79 | convolution fusion | flops 402653184 | bytes 2097152 | tf_op jit(solution)/shard_map/dot_general | solution.py:26
  14.0 0.0 copy-start.11
  14.1 0.0 collective-permute-done.1
  14.1 1.2 %add.29 = f32[512,256]{1,0:T(8,128)S(1)} add(f32[512,256]{1,0:T(8,128)S(1)} %fusion.26, f32[512,256]{1,0:T(8,128)} %collective-permute-done.1) | non-fusion elementwise | flops 131072 | bytes 1572864 | tf_op jit(solution)/shard_map/add | solution.py:122
  15.3 3.0 %collective-permute-start.2 = (f32[512,128]{1,0:T(8,128)S(1)}, f32[512,128]{1,0:T(8,128)S(1)}, u32[]{:S(2)}, u32[]{:S(2)}) collective-permute-start(f32[512,128]{1,0:T(8,128)S(1)} %constant_dynamic-slice_fusion), channel_id=1, source_target_pairs={{0,2},{2,0},{4,6},{6,4},{8,10},{10,8},{12,14},{14,12},{16,18},{18,... | collective-permute-start | bytes 786440 | tf_op jit(solution)/shard_map/ppermute | solution.py:22
  18.3 0.0 copy-done.10
  18.3 1.0 %fusion = f32[512,512]{1,0:T(8,128)S(1)} fusion(f32[512,1024]{1,0:T(8,128)S(1)} %copy-done.10, s32[]{:T(128)S(6)} %select_n.104, pred[]{:T(512)S(6)} %gt.4), kind=kOutput, calls=%fused_computation.18 | convolution fusion | flops 805568512 | bytes 3145733 | tf_op jit(solution)/shard_map/dot_general | solution.py:26
  19.3 5.5 %collective-permute-done.2 = f32[512,128]{1,0:T(8,128)S(1)} collective-permute-done((f32[512,128]{1,0:T(8,128)S(1)}, f32[512,128]{1,0:T(8,128)S(1)}, u32[]{:S(2)}, u32[]{:S(2)}) %collective-permute-start.2) | collective-permute-done | bytes 262176 | tf_op jit(solution)/shard_map/ppermute | solution.py:22
  24.7 0.0 copy-done.11
  24.7 0.6 %fusion.5 = f32[512,128]{1,0:T(8,128)S(1)} fusion(f32[512,1024]{1,0:T(8,128)S(1)} %copy-done.10, s32[]{:T(128)S(6)} %select_n.104, f32[512,128]{1,0:T(8,128)S(1)} %copy-done.11, f32[512,128]{1,0:T(8,128)S(1)} %collective-permute-done.2, f32[512,256]{1,0:T(8,128)S(1)} %add.29, s32[]{:T(128)S(6)} %select_n.127), kind=kOutput, calls=%fused_computation.23 | convolution fusion | flops 201457664 | bytes 2097160 | tf_op jit(solution)/shard_map/dot_general | solution.py:26
  25.3 0.1 collective-permute-start.3
  25.4 1.5 %collective-permute-done.3 = f32[512,128]{1,0:T(8,128)S(1)} collective-permute-done((f32[512,128]{1,0:T(8,128)S(1)}, f32[512,128]{1,0:T(8,128)S(1)}, u32[]{:S(2)}, u32[]{:S(2)}) %collective-permute-start.3) | collective-permute-done | bytes 262176 | tf_op jit(solution)/shard_map/ppermute | solution.py:77
  26.9 1.3 %convolution_subtract_fusion.1 = f32[512,128]{1,0:T(8,128)} fusion(f32[512,128]{1,0:T(8,128)S(1)} %fusion.5, f32[512,512]{1,0:T(8,128)S(1)} %fusion, f32[512,128]{1,0:T(8,128)S(1)} %collective-permute-done.3), kind=kOutput, calls=%fused_computation.17 | convolution fusion | flops 201392128 | bytes 1835008 | tf_op jit(solution)/shard_map/dot_general | solution.py:26
  (2 shorter events, 0.0 us)
Async XLA Ops:
  0.6 3.4 %copy-start.8 = (f32[1024,512]{1,0:T(8,128)S(1)}, f32[1024,512]{1,0:T(8,128)}, u32[]{:S(2)}) copy-start(f32[1024,512]{1,0:T(8,128)} %param.8) | copy-start | bytes 6291460
  3.5 4.3 %collective-permute-start = (f32[512,256]{1,0:T(8,128)}, f32[512,256]{1,0:T(8,128)}, u32[]{:S(2)}, u32[]{:S(2)}) collective-permute-start(f32[512,256]{1,0:T(8,128)} %fusion.10), channel_id=1, source_target_pairs={{0,1},{1,0},{2,3},{3,2},{4,5},{5,4},{6,7},{7,6},{8,9},{9,8},{10,11... | collective-permute-start | bytes 1572872 | tf_op jit(solution)/shard_map/ppermute | solution.py:77
  4.0 1.0 %copy-start.12 = (s32[1,8]{1,0:T(1,128)S(1)}, s32[1,8]{1,0:T(1,128)}, u32[]{:S(2)}) copy-start(s32[1,8]{1,0:T(1,128)} %param.9) | copy-start | bytes 100
  4.9 2.9 %copy-start.2 = (f32[128,512]{1,0:T(8,128)}, f32[128,512]{1,0:T(8,128)S(1)}, u32[]{:S(2)}) copy-start(f32[128,512]{1,0:T(8,128)S(1)} %get-tuple-element.17) | copy-start | bytes 786436
  4.9 2.9 %copy-start.4 = (f32[128,512]{1,0:T(8,128)}, f32[128,512]{1,0:T(8,128)S(1)}, u32[]{:S(2)}) copy-start(f32[128,512]{1,0:T(8,128)S(1)} %get-tuple-element.18) | copy-start | bytes 786436
  4.9 3.0 %copy-start = (f32[512,1024]{1,0:T(8,128)S(1)}, f32[512,1024]{1,0:T(8,128)}, u32[]{:S(2)}) copy-start(f32[512,1024]{1,0:T(8,128)} %param.6) | copy-start | bytes 6291460
  5.9 2.0 %copy-start.9 = (f32[512,256]{1,0:T(8,128)S(1)}, f32[512,256]{1,0:T(8,128)}, u32[]{:S(2)}) copy-start(f32[512,256]{1,0:T(8,128)} %param.7) | copy-start | bytes 1572868
  10.2 3.3 %copy-start.1 = (f32[512,256]{1,0:T(8,128)}, f32[512,256]{1,0:T(8,128)S(1)}, u32[]{:S(2)}) copy-start(f32[512,256]{1,0:T(8,128)S(1)} %fusion.8) | copy-start | bytes 1572868
  10.2 1.6 %copy-start.3 = (f32[128,512]{1,0:T(8,128)S(1)}, f32[128,512]{1,0:T(8,128)}, u32[]{:S(2)}) copy-start(f32[128,512]{1,0:T(8,128)} %copy-done.2) | copy-start | bytes 786436
  10.2 1.6 %copy-start.5 = (f32[128,512]{1,0:T(8,128)S(1)}, f32[128,512]{1,0:T(8,128)}, u32[]{:S(2)}) copy-start(f32[128,512]{1,0:T(8,128)} %copy-done.4) | copy-start | bytes 786436
  10.2 1.6 %copy-start.6 = (f32[128,512]{1,0:T(8,128)S(1)}, f32[128,512]{1,0:T(8,128)}, u32[]{:S(2)}) copy-start(f32[128,512]{1,0:T(8,128)} %get-tuple-element.19) | copy-start | bytes 786436
  10.2 1.6 %copy-start.7 = (f32[128,512]{1,0:T(8,128)S(1)}, f32[128,512]{1,0:T(8,128)}, u32[]{:S(2)}) copy-start(f32[128,512]{1,0:T(8,128)} %get-tuple-element.20) | copy-start | bytes 786436
  11.6 2.4 %collective-permute-start.1 = (f32[512,256]{1,0:T(8,128)}, f32[512,256]{1,0:T(8,128)}, u32[]{:S(2)}, u32[]{:S(2)}) collective-permute-start(f32[512,256]{1,0:T(8,128)} %fusion.27), channel_id=1, source_target_pairs={{0,1},{1,0},{2,3},{3,2},{4,5},{5,4},{6,7},{7,6},{8,9},{9,8},{10,11... | collective-permute-start | bytes 1572872 | tf_op jit(solution)/shard_map/ppermute | solution.py:77
  13.4 4.8 %copy-start.10 = (f32[512,1024]{1,0:T(8,128)S(1)}, f32[512,1024]{1,0:T(8,128)}, u32[]{:S(2)}) copy-start(f32[512,1024]{1,0:T(8,128)} %param.10) | copy-start | bytes 6291460
  14.0 10.7 %copy-start.11 = (f32[512,128]{1,0:T(8,128)S(1)}, f32[512,128]{1,0:T(8,128)}, u32[]{:S(2)}) copy-start(f32[512,128]{1,0:T(8,128)} %param.11) | copy-start | bytes 786436
  15.3 9.5 %collective-permute-start.2 = (f32[512,128]{1,0:T(8,128)S(1)}, f32[512,128]{1,0:T(8,128)S(1)}, u32[]{:S(2)}, u32[]{:S(2)}) collective-permute-start(f32[512,128]{1,0:T(8,128)S(1)} %constant_dynamic-slice_fusion), channel_id=1, source_target_pairs={{0,2},{2,0},{4,6},{6,4},{8,10},{10,8},{12,14},{14,12},{16,18},{18,... | collective-permute-start | bytes 786440 | tf_op jit(solution)/shard_map/ppermute | solution.py:22
  25.3 1.6 %collective-permute-start.3 = (f32[512,128]{1,0:T(8,128)S(1)}, f32[512,128]{1,0:T(8,128)S(1)}, u32[]{:S(2)}, u32[]{:S(2)}) collective-permute-start(f32[512,128]{1,0:T(8,128)S(1)} %fusion.5), channel_id=1, source_target_pairs={{0,1},{1,0},{2,3},{3,2},{4,5},{5,4},{6,7},{7,6},{8,9},{9,8},{10,11... | collective-permute-start | bytes 786440 | tf_op jit(solution)/shard_map/ppermute | solution.py:77

commit v12 on v7

--- a/solution.py
+++ b/solution.py
@@ -112,18 +112,26 @@
         taken = jnp.take(blocks, chosen, axis=0, mode="clip")
         return taken.reshape(-1, update_panel.shape[1])
 
-    other_rows = matmul(section_panel(1 - section), leaf_solution, precision)
-    arrived_rows = pair_swap(other_rows, "rows")
-    chip_sum = matmul(section_panel(section), leaf_solution, precision) + arrived_rows
     column_half = parent_rhs.shape[1]
     sibling = lax.axis_index("leaf") % 2
-    kept = lax.dynamic_slice_in_dim(chip_sum, sibling * column_half, column_half, 1)
-    sent = lax.dynamic_slice_in_dim(chip_sum, (1 - sibling) * column_half, column_half, 1)
+    solution_kept = lax.dynamic_slice_in_dim(leaf_solution, sibling * column_half, column_half, 1)
+    solution_sent = lax.dynamic_slice_in_dim(leaf_solution, (1 - sibling) * column_half, column_half, 1)
+    panel_other = section_panel(1 - section)
+    panel_own = section_panel(section)
+    other_sent = matmul(panel_other, solution_sent, precision)
+    arrived_sent = pair_swap(other_sent, "rows")
+    own_sent = matmul(panel_own, solution_sent, precision)
+    own_sent, arrived_sent = lax.optimization_barrier((own_sent, arrived_sent))
+    sent = own_sent + arrived_sent
+    sent, solution_kept = lax.optimization_barrier((sent, solution_kept))
+    other_kept = matmul(panel_other, solution_kept, precision)
+    arrived_kept = pair_swap(other_kept, "rows")
+    kept = matmul(panel_own, solution_kept, precision) + arrived_kept
     tile_rows = parent_rhs.shape[0]
     diagonal = lax.dynamic_slice_in_dim(parent_factor, section * tile_rows, tile_rows, 1)
     coupling = lower_coupling(parent_factor, diagonal, section, precision)
     arrived = swapped(sent, "leaf", 0)
-    arrived, coupling = lax.optimization_barrier((arrived, coupling))
+    arrived, coupling, kept = lax.optimization_barrier((arrived, coupling, kept))
     pending = parent_rhs - (kept + arrived)
     first = matmul(diagonal, pending, precision)
     arrived = pair_swap(first, "rows")

time: 26.5 us -> 27.8 us (1.049)
  matrix products: 11.1 us -> 12.2 us
  local copies, waits for them, and re-layouts: 3.31 us -> 2.34 us
  waiting for transfers between devices: 7.47 us -> 8.38 us
    dot_general x8 -> x10, matrix products: 11.1 us -> 12.2 us  [matmul(): jnp.dot(left, right, precision=precision, preferred_element_type=jnp.floa...]
    gather x2, local copies, waits for them, and re-layouts: 3.17 us -> 2.2 us  [section_panel(): taken = jnp.take(blocks, chosen, axis=0, mode='clip')]
    ppermute x3 -> x4, waiting for transfers between devices: 1.79 us -> 2.37 us  [pair_swap(): return lax.ppermute(block, axis, [(0, 1), (1, 0)])]
    ppermute x1, waiting for transfers between devices: 5.68 us -> 6.01 us  [swapped(): return lax.ppermute(block, axis, route)]
    ppermute x3 -> x4, starting transfers between devices: 0.86 us -> 0.86 us  [pair_swap(): return lax.ppermute(block, axis, [(0, 1), (1, 0)])]
  transfers between devices with their start and end apart: 4 -> 5, of which waited for: 3 -> 3; matrix products, arithmetic and copies ran while one was open for 16% -> 17% of each run, Pallas kernels for 0% -> 0%
where the time goes in v12:
time: 27.8 us; the launch traced here: 27.6 us
  matrix products  12.2 us (44%)
  waiting for transfers between devices  8.38 us (30%)
  starting transfers between devices  3.78 us (14%)
  local copies, waits for them, and re-layouts  2.34 us (8%)
  between operations  0.8 us (3%)
    dot_general x10, matrix products, matmul(): jnp.dot(left, right, precision=precision, preferred_element_type=jnp.floa...  12.2 us
    ppermute x1, waiting for transfers between devices, swapped(): return lax.ppermute(block, axis, route)  6.01 us
    ppermute x1, starting transfers between devices, swapped(): return lax.ppermute(block, axis, route)  2.92 us
    ppermute x4, waiting for transfers between devices, pair_swap(): return lax.ppermute(block, axis, [(0, 1), (1, 0)])  2.37 us
    gather x2, local copies, waits for them, and re-layouts, section_panel(): taken = jnp.take(blocks, chosen, axis=0, mode='clip')  2.2 us
    ppermute x4, starting transfers between devices, pair_swap(): return lax.ppermute(block, axis, [(0, 1), (1, 0)])  0.86 us
  transfers between devices with their start and end apart: 5, of which 3 were waited for; matrix products, arithmetic and copies ran while one was open for 17% of the time, Pallas kernels for 0%

profile of v12, /device:TPU:0, one launch (start us, length us, event | category | flops | bytes accessed | tf_op | source)
XLA Modules:
  0.0 27.6 jit_solution(3822545602975799444)
XLA Ops:
  0.6 0.0 copy-start
  0.6 0.0 copy-start.5
  0.7 2.9 %fusion.10 = f32[512,256]{1,0:T(8,128)} fusion(f32[512,256]{1,0:T(8,128)} %param.7, f32[512,1024]{1,0:T(8,128)} %param.6, s32[]{:T(128)S(6)} %select_n.39), kind=kOutput, calls=%fused_computation.15 | convolution fusion | flops 402653184 | bytes 2097156 | tf_op jit(solution)/shard_map/dot_general | solution.py:26
  3.6 0.5 %collective-permute-start = (f32[512,256]{1,0:T(8,128)}, f32[512,256]{1,0:T(8,128)}, u32[]{:S(2)}, u32[]{:S(2)}) collective-permute-start(f32[512,256]{1,0:T(8,128)} %fusion.10), channel_id=1, source_target_pairs={{0,1},{1,0},{2,3},{3,2},{4,5},{5,4},{6,7},{7,6},{8,9},{9,8},{10,11... | collective-permute-start | bytes 1572872 | tf_op jit(solution)/shard_map/ppermute | solution.py:77
  4.0 0.0 copy-done.5
  4.0 0.1 select_reduce_fusion
  4.1 0.1 fusion.30
  4.2 0.0 copy-done
  4.2 1.6 %gather_fusion.1 = f32[4,128,512]{2,1,0:T(8,128)} fusion(f32[8,128,512]{2,1,0:T(8,128)S(1)} %bitcast.16, s32[1024]{0:T(1024)S(1)} %get-tuple-element.18), kind=kCustom, calls=%fused_computation.1 | custom fusion | bytes 2097168 | tf_op jit(solution)/shard_map/jit(_take)/gather | solution.py:112
  5.8 0.6 %gather_fusion = f32[4,128,512]{2,1,0:T(8,128)S(1)} fusion(f32[8,128,512]{2,1,0:T(8,128)S(1)} %bitcast.15, s32[1024]{0:T(1024)S(1)} %get-tuple-element.19), kind=kCustom, calls=%fused_computation | custom fusion | bytes 2097168 | tf_op jit(solution)/shard_map/jit(_take)/gather | solution.py:112
  6.4 0.0 copy-start.1
  6.4 0.0 collective-permute-done
  6.4 2.2 %convolution_subtract_fusion = f32[512,256]{1,0:T(8,128)S(1)} fusion(f32[512,256]{1,0:T(8,128)} %param.7, f32[512,256]{1,0:T(8,128)} %collective-permute-done, f32[512,1024]{1,0:T(8,128)} %param.6, pred[]{:T(512)S(6)} %gt.4), kind=kOutput, calls=%fused_computation.2 | convolution fusion | flops 403046400 | bytes 2621441 | tf_op jit(solution)/shard_map/dot_general | solution.py:26
  8.6 1.8 %fusion.8 = f32[512,256]{1,0:T(8,128)S(1)} fusion(f32[512,256]{1,0:T(8,128)S(1)} %convolution_subtract_fusion, f32[512,1024]{1,0:T(8,128)} %param.6, s32[]{:T(128)S(6)} %select_n.39), kind=kOutput, calls=%fused_computation.13 | convolution fusion | flops 402653184 | bytes 2097156 | tf_op jit(solution)/shard_map/dot_general | solution.py:26
  10.5 0.0 copy-start.2
  10.5 0.0 copy-done.1
  10.5 0.6 %fusion.18 = f32[512,128]{1,0:T(8,128)S(1)} fusion(f32[512,512]{1,0:T(8,128)S(1)} %bitcast.19, f32[512,256]{1,0:T(8,128)S(1)} %fusion.8, s32[]{:T(128)S(6)} %select_n.45), kind=kOutput, calls=%fused_computation.23 | convolution fusion | flops 201326592 | bytes 1572868 | tf_op jit(solution)/shard_map/dot_general | solution.py:26
  11.1 0.1 collective-permute-start.1
  11.2 0.0 copy-start.3
  11.2 0.6 %fusion.20 = f32[512,128]{1,0:T(8,128)S(1)} fusion(f32[512,512]{1,0:T(8,128)S(1)} %bitcast.17, f32[512,256]{1,0:T(8,128)S(1)} %fusion.8, s32[]{:T(128)S(6)} %select_n.45), kind=kOutput, calls=%fused_computation.25 | convolution fusion | flops 201326592 | bytes 1572868 | tf_op jit(solution)/shard_map/dot_general | solution.py:26
  11.8 0.8 %collective-permute-done.1 = f32[512,128]{1,0:T(8,128)S(1)} collective-permute-done((f32[512,128]{1,0:T(8,128)S(1)}, f32[512,128]{1,0:T(8,128)S(1)}, u32[]{:S(2)}, u32[]{:S(2)}) %collective-permute-start.1) | collective-permute-done | bytes 262176 | tf_op jit(solution)/shard_map/ppermute | solution.py:77
  12.7 0.0 copy-done.2
  12.7 0.6 %fusion.31 = f32[512,128]{1,0:T(8,128)S(1)} fusion(f32[512,512]{1,0:T(8,128)S(1)} %bitcast.20, f32[512,128]{1,0:T(8,128)S(1)} %constant_dynamic-slice_fusion), kind=kOutput, calls=%fused_computation.41 | convolution fusion | flops 201326592 | bytes 1572864 | tf_op jit(solution)/shard_map/dot_general | solution.py:26
  13.3 0.0 copy-start.4
  13.3 0.2 collective-permute-start.3
  13.5 0.0 copy-done.3
  13.5 1.0 %fusion = f32[512,512]{1,0:T(8,128)S(1)} fusion(f32[512,1024]{1,0:T(8,128)S(1)} %copy-done.3, s32[]{:T(128)S(6)} %select_n.39, pred[]{:T(512)S(6)} %gt.4), kind=kOutput, calls=%fused_computation.5 | convolution fusion | flops 805568512 | bytes 3145733 | tf_op jit(solution)/shard_map/dot_general | solution.py:26
  14.6 2.9 %collective-permute-start.2 = (f32[512,128]{1,0:T(8,128)S(1)}, f32[512,128]{1,0:T(8,128)S(1)}, u32[]{:S(2)}, u32[]{:S(2)}) collective-permute-start(f32[512,128]{1,0:T(8,128)S(1)} %add.34), channel_id=1, source_target_pairs={{0,2},{2,0},{4,6},{6,4},{8,10},{10,8},{12,14},{14,12},{16,18},{18,... | collective-permute-start | bytes 786440 | tf_op jit(solution)/shard_map/ppermute | solution.py:22
  17.5 0.0 collective-permute-done.3
  17.5 0.6 %convolution_add_fusion = f32[512,128]{1,0:T(8,128)S(1)} fusion(f32[512,128]{1,0:T(8,128)S(1)} %collective-permute-done.3, f32[512,512]{1,0:T(8,128)S(1)} %bitcast.18, f32[512,128]{1,0:T(8,128)S(1)} %constant_dynamic-slice_fusion), kind=kOutput, calls=%fused_computation.4 | convolution fusion | flops 201392128 | bytes 1835008 | tf_op jit(solution)/shard_map/dot_general | solution.py:26
  18.1 6.0 %collective-permute-done.2 = f32[512,128]{1,0:T(8,128)S(1)} collective-permute-done((f32[512,128]{1,0:T(8,128)S(1)}, f32[512,128]{1,0:T(8,128)S(1)}, u32[]{:S(2)}, u32[]{:S(2)}) %collective-permute-start.2) | collective-permute-done | bytes 262176 | tf_op jit(solution)/shard_map/ppermute | solution.py:22
  24.1 0.0 copy-done.4
  24.1 0.6 %fusion.5 = f32[512,128]{1,0:T(8,128)S(1)} fusion(f32[512,1024]{1,0:T(8,128)S(1)} %copy-done.3, s32[]{:T(128)S(6)} %select_n.39, f32[512,128]{1,0:T(8,128)S(1)} %copy-done.4, f32[512,128]{1,0:T(8,128)S(1)} %convolution_add_fusion, f32[512,128]{1,0:T(8,128)S(1)} %collective-permute-done.2), kind=kOutput, calls=%fused_computation.10 | convolution fusion | flops 201457664 | bytes 2097156 | tf_op jit(solution)/shard_map/dot_general | solution.py:26
  24.7 0.1 collective-permute-start.4
  24.8 1.5 %collective-permute-done.4 = f32[512,128]{1,0:T(8,128)S(1)} collective-permute-done((f32[512,128]{1,0:T(8,128)S(1)}, f32[512,128]{1,0:T(8,128)S(1)}, u32[]{:S(2)}, u32[]{:S(2)}) %collective-permute-start.4) | collective-permute-done | bytes 262176 | tf_op jit(solution)/shard_map/ppermute | solution.py:77
  26.3 1.3 %convolution_subtract_fusion.1 = f32[512,128]{1,0:T(8,128)} fusion(f32[512,128]{1,0:T(8,128)S(1)} %fusion.5, f32[512,512]{1,0:T(8,128)S(1)} %fusion, f32[512,128]{1,0:T(8,128)S(1)} %collective-permute-done.4), kind=kOutput, calls=%fused_computation.3 | convolution fusion | flops 201392128 | bytes 1835008 | tf_op jit(solution)/shard_map/dot_general | solution.py:26
  (3 shorter events, 0.1 us)
Async XLA Ops:
  0.6 3.6 %copy-start = (f32[1024,512]{1,0:T(8,128)S(1)}, f32[1024,512]{1,0:T(8,128)}, u32[]{:S(2)}) copy-start(f32[1024,512]{1,0:T(8,128)} %param.8) | copy-start | bytes 6291460
  0.6 3.4 %copy-start.5 = (s32[1,8]{1,0:T(1,128)S(1)}, s32[1,8]{1,0:T(1,128)}, u32[]{:S(2)}) copy-start(s32[1,8]{1,0:T(1,128)} %param.9) | copy-start | bytes 100
  3.6 2.9 %collective-permute-start = (f32[512,256]{1,0:T(8,128)}, f32[512,256]{1,0:T(8,128)}, u32[]{:S(2)}, u32[]{:S(2)}) collective-permute-start(f32[512,256]{1,0:T(8,128)} %fusion.10), channel_id=1, source_target_pairs={{0,1},{1,0},{2,3},{3,2},{4,5},{5,4},{6,7},{7,6},{8,9},{9,8},{10,11... | collective-permute-start | bytes 1572872 | tf_op jit(solution)/shard_map/ppermute | solution.py:77
  6.4 4.1 %copy-start.1 = (f32[4,128,512]{2,1,0:T(8,128)S(1)}, f32[4,128,512]{2,1,0:T(8,128)}, u32[]{:S(2)}) copy-start(f32[4,128,512]{2,1,0:T(8,128)} %gather_fusion.1) | copy-start | bytes 3145732
  10.5 2.3 %copy-start.2 = (f32[512,256]{1,0:T(8,128)}, f32[512,256]{1,0:T(8,128)S(1)}, u32[]{:S(2)}) copy-start(f32[512,256]{1,0:T(8,128)S(1)} %fusion.8) | copy-start | bytes 1572868
  11.1 1.6 %collective-permute-start.1 = (f32[512,128]{1,0:T(8,128)S(1)}, f32[512,128]{1,0:T(8,128)S(1)}, u32[]{:S(2)}, u32[]{:S(2)}) collective-permute-start(f32[512,128]{1,0:T(8,128)S(1)} %fusion.18), channel_id=1, source_target_pairs={{0,1},{1,0},{2,3},{3,2},{4,5},{5,4},{6,7},{7,6},{8,9},{9,8},{10,11... | collective-permute-start | bytes 786440 | tf_op jit(solution)/shard_map/ppermute | solution.py:77
  11.2 2.3 %copy-start.3 = (f32[512,1024]{1,0:T(8,128)S(1)}, f32[512,1024]{1,0:T(8,128)}, u32[]{:S(2)}) copy-start(f32[512,1024]{1,0:T(8,128)} %param.10) | copy-start | bytes 6291460
  13.3 10.8 %copy-start.4 = (f32[512,128]{1,0:T(8,128)S(1)}, f32[512,128]{1,0:T(8,128)}, u32[]{:S(2)}) copy-start(f32[512,128]{1,0:T(8,128)} %param.11) | copy-start | bytes 786436
  13.3 4.2 %collective-permute-start.3 = (f32[512,128]{1,0:T(8,128)S(1)}, f32[512,128]{1,0:T(8,128)S(1)}, u32[]{:S(2)}, u32[]{:S(2)}) collective-permute-start(f32[512,128]{1,0:T(8,128)S(1)} %fusion.31), channel_id=1, source_target_pairs={{0,1},{1,0},{2,3},{3,2},{4,5},{5,4},{6,7},{7,6},{8,9},{9,8},{10,11... | collective-permute-start | bytes 786440 | tf_op jit(solution)/shard_map/ppermute | solution.py:77
  14.6 9.5 %collective-permute-start.2 = (f32[512,128]{1,0:T(8,128)S(1)}, f32[512,128]{1,0:T(8,128)S(1)}, u32[]{:S(2)}, u32[]{:S(2)}) collective-permute-start(f32[512,128]{1,0:T(8,128)S(1)} %add.34), channel_id=1, source_target_pairs={{0,2},{2,0},{4,6},{6,4},{8,10},{10,8},{12,14},{14,12},{16,18},{18,... | collective-permute-start | bytes 786440 | tf_op jit(solution)/shard_map/ppermute | solution.py:22
  24.7 1.6 %collective-permute-start.4 = (f32[512,128]{1,0:T(8,128)S(1)}, f32[512,128]{1,0:T(8,128)S(1)}, u32[]{:S(2)}, u32[]{:S(2)}) collective-permute-start(f32[512,128]{1,0:T(8,128)S(1)} %fusion.5), channel_id=1, source_target_pairs={{0,1},{1,0},{2,3},{3,2},{4,5},{5,4},{6,7},{7,6},{8,9},{9,8},{10,11... | collective-permute-start | bytes 786440 | tf_op jit(solution)/shard_map/ppermute | solution.py:77

commit v13 on v10

--- a/solution.py
+++ b/solution.py
@@ -83,13 +83,14 @@
     return matmul(diagonal, below, precision)
 
 
-def two_section_leaf(factor, right_side, section, precision):
+def two_section_leaf(factor, right_side, section, precision, early=()):
     tile_rows = right_side.shape[0]
     diagonal = lax.dynamic_slice_in_dim(factor, section * tile_rows, tile_rows, 1)
     first = matmul(diagonal, right_side, precision)
     arrived = pair_swap(first, "rows")
+    arrived, early = lax.optimization_barrier((arrived, early))
     below = jnp.where(section > 0, factor[:, :tile_rows], jnp.zeros_like(diagonal))
-    return matmul(diagonal, right_side - matmul(below, arrived, precision), precision)
+    return matmul(diagonal, right_side - matmul(below, arrived, precision), precision), early
 
 
 def inverse_order(update_blocks):
@@ -102,7 +103,6 @@
 def two_section_shards(leaf_factor, leaf_rhs, update_panel, update_blocks, parent_factor, parent_rhs):
     section = lax.axis_index("rows")
     precision = lax.Precision.HIGH
-    leaf_solution = two_section_leaf(leaf_factor, leaf_rhs, section, precision)
     blocks = update_panel.reshape(-1, ROW_BLOCK, update_panel.shape[1])
     order = inverse_order(update_blocks)
     per_section = blocks.shape[0] // 2
@@ -112,9 +112,11 @@
         taken = jnp.take(blocks, chosen, axis=0, mode="clip")
         return taken.reshape(-1, update_panel.shape[1])
 
-    other_rows = matmul(section_panel(1 - section), leaf_solution, precision)
+    panels = (section_panel(1 - section), section_panel(section))
+    leaf_solution, (panel_other, panel_own) = two_section_leaf(leaf_factor, leaf_rhs, section, precision, panels)
+    other_rows = matmul(panel_other, leaf_solution, precision)
     arrived_rows = pair_swap(other_rows, "rows")
-    own_rows = matmul(section_panel(section), leaf_solution, precision)
+    own_rows = matmul(panel_own, leaf_solution, precision)
     own_rows, arrived_rows = lax.optimization_barrier((own_rows, arrived_rows))
     chip_sum = own_rows + arrived_rows
     column_half = parent_rhs.shape[1]

time: 26.4 us -> 26.3 us (level)
  transfers between devices with their start and end apart: 4 -> 4, of which waited for: 2 -> 3; matrix products, arithmetic and copies ran while one was open for 24% -> 24% of each run, Pallas kernels for 0% -> 0%
where the time goes in v13:
time: 26.3 us; the launch traced here: 26.1 us
  matrix products  11.1 us (42%)
  waiting for transfers between devices  7.15 us (27%)
  starting transfers between devices  3.59 us (14%)
  local copies, waits for them, and re-layouts  3.35 us (13%)
  between operations  0.79 us (3%)
    dot_general x8, matrix products, matmul(): jnp.dot(left, right, precision=precision, preferred_element_type=jnp.floa...  11.1 us
    ppermute x1, waiting for transfers between devices, swapped(): return lax.ppermute(block, axis, route)  5.55 us
    gather x2, local copies, waits for them, and re-layouts, section_panel(): taken = jnp.take(blocks, chosen, axis=0, mode='clip')  3.2 us
    ppermute x1, starting transfers between devices, swapped(): return lax.ppermute(block, axis, route)  2.95 us
    ppermute x3, waiting for transfers between devices, pair_swap(): return lax.ppermute(block, axis, [(0, 1), (1, 0)])  1.59 us
    ppermute x3, starting transfers between devices, pair_swap(): return lax.ppermute(block, axis, [(0, 1), (1, 0)])  0.64 us
  transfers between devices with their start and end apart: 4, of which 3 were waited for; matrix products, arithmetic and copies ran while one was open for 24% of the time, Pallas kernels for 0%

profile of v13, /device:TPU:0, one launch (start us, length us, event | category | flops | bytes accessed | tf_op | source)
XLA Modules:
  0.0 26.1 jit_solution(1014949869792386917)
XLA Ops:
  0.6 0.0 copy-start
  0.6 0.0 copy-start.7
  0.7 2.1 %fusion.10 = f32[512,256]{1,0:T(8,128)S(1)} fusion(f32[512,256]{1,0:T(8,128)} %param.7, f32[512,1024]{1,0:T(8,128)} %param.6, s32[]{:T(128)S(6)} %select_n.39), kind=kOutput, calls=%fused_computation.14 | convolution fusion | flops 402653184 | bytes 2097156 | tf_op jit(solution)/shard_map/dot_general | solution.py:26
  2.8 0.5 %collective-permute-start = (f32[512,256]{1,0:T(8,128)S(1)}, f32[512,256]{1,0:T(8,128)}, u32[]{:S(2)}, u32[]{:S(2)}) collective-permute-start(f32[512,256]{1,0:T(8,128)S(1)} %fusion.10), channel_id=1, source_target_pairs={{0,1},{1,0},{2,3},{3,2},{4,5},{5,4},{6,7},{7,6},{8,9},{9,8},{10,11... | collective-permute-start | bytes 1572872 | tf_op jit(solution)/shard_map/ppermute | solution.py:77
  3.3 0.0 copy-done.7
  3.3 0.1 select_reduce_fusion
  3.4 0.1 fusion.25
  3.5 0.0 copy-done
  3.5 0.0 copy-start.4
  3.5 1.6 %gather_fusion = f32[4,128,512]{2,1,0:T(8,128)} fusion(f32[8,128,512]{2,1,0:T(8,128)S(1)} %bitcast.13, s32[1024]{0:T(1024)S(1)} %get-tuple-element.19), kind=kCustom, calls=%fused_computation | custom fusion | bytes 2097168 | tf_op jit(solution)/shard_map/jit(_take)/gather | solution.py:112
  5.1 1.6 %gather_fusion.1 = f32[4,128,512]{2,1,0:T(8,128)} fusion(f32[8,128,512]{2,1,0:T(8,128)S(1)} %bitcast.14, s32[1024]{0:T(1024)S(1)} %get-tuple-element.18), kind=kCustom, calls=%fused_computation.1 | custom fusion | bytes 2097168 | tf_op jit(solution)/shard_map/jit(_take)/gather | solution.py:112
  6.7 0.0 copy-start.1
  6.7 0.0 collective-permute-done
  6.7 0.0 copy-done.4
  6.7 0.0 copy-start.3
  6.7 2.1 %convolution_subtract_fusion = f32[512,256]{1,0:T(8,128)S(1)} fusion(f32[512,256]{1,0:T(8,128)S(1)} %copy-done.4, f32[512,256]{1,0:T(8,128)} %collective-permute-done, f32[512,1024]{1,0:T(8,128)} %param.6, pred[]{:T(512)S(6)} %gt.4), kind=kOutput, calls=%fused_computation.2 | convolution fusion | flops 403046400 | bytes 2621441 | tf_op jit(solution)/shard_map/dot_general | solution.py:26
  8.8 0.0 copy-done.1
  8.8 0.6 %fusion.8 = f32[512,256]{1,0:T(8,128)S(1)} fusion(f32[512,256]{1,0:T(8,128)S(1)} %convolution_subtract_fusion, f32[512,1024]{1,0:T(8,128)S(1)} %copy-done.1, s32[]{:T(128)S(6)} %select_n.39), kind=kOutput, calls=%fused_computation.12 | convolution fusion | flops 402653184 | bytes 2097156 | tf_op jit(solution)/shard_map/dot_general | solution.py:26
  9.4 0.0 copy-done.3
  9.4 0.0 copy-start.2
  9.4 1.4 %fusion.27 = f32[512,256]{1,0:T(8,128)} fusion(f32[512,512]{1,0:T(8,128)S(1)} %bitcast.16, f32[512,256]{1,0:T(8,128)S(1)} %fusion.8), kind=kOutput, calls=%fused_computation.36 | convolution fusion | flops 402653184 | bytes 2097152 | tf_op jit(solution)/shard_map/dot_general | solution.py:26
  10.9 0.1 collective-permute-start.1
  10.9 0.0 copy-start.5
  10.9 2.0 %fusion.26 = f32[512,256]{1,0:T(8,128)S(1)} fusion(f32[512,512]{1,0:T(8,128)} %bitcast.15, f32[512,256]{1,0:T(8,128)S(1)} %fusion.8), kind=kOutput, calls=%fused_computation.35 | convolution fusion | flops 402653184 | bytes 2097152 | tf_op jit(solution)/shard_map/dot_general | solution.py:26
  12.9 0.0 copy-done.2
  12.9 0.0 copy-start.6
  12.9 0.1 collective-permute-done.1
  13.0 0.1 add.29
  13.1 2.9 %collective-permute-start.2 = (f32[512,128]{1,0:T(8,128)S(1)}, f32[512,128]{1,0:T(8,128)S(1)}, u32[]{:S(2)}, u32[]{:S(2)}) collective-permute-start(f32[512,128]{1,0:T(8,128)S(1)} %constant_dynamic-slice_fusion), channel_id=1, source_target_pairs={{0,2},{2,0},{4,6},{6,4},{8,10},{10,8},{12,14},{14,12},{16,18},{18,... | collective-permute-start | bytes 786440 | tf_op jit(solution)/shard_map/ppermute | solution.py:22
  16.0 0.0 copy-done.5
  16.0 1.0 %fusion = f32[512,512]{1,0:T(8,128)S(1)} fusion(f32[512,1024]{1,0:T(8,128)S(1)} %copy-done.5, s32[]{:T(128)S(6)} %select_n.39, pred[]{:T(512)S(6)} %gt.4), kind=kOutput, calls=%fused_computation.4 | convolution fusion | flops 805568512 | bytes 3145733 | tf_op jit(solution)/shard_map/dot_general | solution.py:26
  17.1 5.6 %collective-permute-done.2 = f32[512,128]{1,0:T(8,128)S(1)} collective-permute-done((f32[512,128]{1,0:T(8,128)S(1)}, f32[512,128]{1,0:T(8,128)S(1)}, u32[]{:S(2)}, u32[]{:S(2)}) %collective-permute-start.2) | collective-permute-done | bytes 262176 | tf_op jit(solution)/shard_map/ppermute | solution.py:22
  22.6 0.0 copy-done.6
  22.6 0.6 %fusion.5 = f32[512,128]{1,0:T(8,128)S(1)} fusion(f32[512,1024]{1,0:T(8,128)S(1)} %copy-done.5, s32[]{:T(128)S(6)} %select_n.39, f32[512,128]{1,0:T(8,128)S(1)} %copy-done.6, f32[512,128]{1,0:T(8,128)S(1)} %collective-permute-done.2, f32[512,256]{1,0:T(8,128)S(1)} %add.29, s32[]{:T(128)S(6)} %select_n.46), kind=kOutput, calls=%fused_computation.9 | convolution fusion | flops 201457664 | bytes 2097160 | tf_op jit(solution)/shard_map/dot_general | solution.py:26
  23.2 0.1 collective-permute-start.3
  23.3 1.5 %collective-permute-done.3 = f32[512,128]{1,0:T(8,128)S(1)} collective-permute-done((f32[512,128]{1,0:T(8,128)S(1)}, f32[512,128]{1,0:T(8,128)S(1)}, u32[]{:S(2)}, u32[]{:S(2)}) %collective-permute-start.3) | collective-permute-done | bytes 262176 | tf_op jit(solution)/shard_map/ppermute | solution.py:77
  24.8 1.3 %convolution_subtract_fusion.1 = f32[512,128]{1,0:T(8,128)} fusion(f32[512,128]{1,0:T(8,128)S(1)} %fusion.5, f32[512,512]{1,0:T(8,128)S(1)} %fusion, f32[512,128]{1,0:T(8,128)S(1)} %collective-permute-done.3), kind=kOutput, calls=%fused_computation.3 | convolution fusion | flops 201392128 | bytes 1835008 | tf_op jit(solution)/shard_map/dot_general | solution.py:26
  (2 shorter events, 0.0 us)
Async XLA Ops:
  0.6 2.8 %copy-start = (f32[1024,512]{1,0:T(8,128)S(1)}, f32[1024,512]{1,0:T(8,128)}, u32[]{:S(2)}) copy-start(f32[1024,512]{1,0:T(8,128)} %param.8) | copy-start | bytes 6291460
  0.6 2.6 %copy-start.7 = (s32[1,8]{1,0:T(1,128)S(1)}, s32[1,8]{1,0:T(1,128)}, u32[]{:S(2)}) copy-start(s32[1,8]{1,0:T(1,128)} %param.9) | copy-start | bytes 100
  2.8 3.9 %collective-permute-start = (f32[512,256]{1,0:T(8,128)S(1)}, f32[512,256]{1,0:T(8,128)}, u32[]{:S(2)}, u32[]{:S(2)}) collective-permute-start(f32[512,256]{1,0:T(8,128)S(1)} %fusion.10), channel_id=1, source_target_pairs={{0,1},{1,0},{2,3},{3,2},{4,5},{5,4},{6,7},{7,6},{8,9},{9,8},{10,11... | collective-permute-start | bytes 1572872 | tf_op jit(solution)/shard_map/ppermute | solution.py:77
  3.5 3.2 %copy-start.4 = (f32[512,256]{1,0:T(8,128)S(1)}, f32[512,256]{1,0:T(8,128)}, u32[]{:S(2)}) copy-start(f32[512,256]{1,0:T(8,128)} %param.7) | copy-start | bytes 1572868
  6.7 2.1 %copy-start.1 = (f32[512,1024]{1,0:T(8,128)S(1)}, f32[512,1024]{1,0:T(8,128)}, u32[]{:S(2)}) copy-start(f32[512,1024]{1,0:T(8,128)} %param.6) | copy-start | bytes 6291460
  6.7 2.7 %copy-start.3 = (f32[4,128,512]{2,1,0:T(8,128)S(1)}, f32[4,128,512]{2,1,0:T(8,128)}, u32[]{:S(2)}) copy-start(f32[4,128,512]{2,1,0:T(8,128)} %gather_fusion) | copy-start | bytes 3145732
  9.4 3.5 %copy-start.2 = (f32[512,256]{1,0:T(8,128)}, f32[512,256]{1,0:T(8,128)S(1)}, u32[]{:S(2)}) copy-start(f32[512,256]{1,0:T(8,128)S(1)} %fusion.8) | copy-start | bytes 1572868
  10.9 2.1 %collective-permute-start.1 = (f32[512,256]{1,0:T(8,128)}, f32[512,256]{1,0:T(8,128)S(1)}, u32[]{:S(2)}, u32[]{:S(2)}) collective-permute-start(f32[512,256]{1,0:T(8,128)} %fusion.27), channel_id=1, source_target_pairs={{0,1},{1,0},{2,3},{3,2},{4,5},{5,4},{6,7},{7,6},{8,9},{9,8},{10,11... | collective-permute-start | bytes 1572872 | tf_op jit(solution)/shard_map/ppermute | solution.py:77
  10.9 5.1 %copy-start.5 = (f32[512,1024]{1,0:T(8,128)S(1)}, f32[512,1024]{1,0:T(8,128)}, u32[]{:S(2)}) copy-start(f32[512,1024]{1,0:T(8,128)} %param.10) | copy-start | bytes 6291460
  12.9 9.7 %copy-start.6 = (f32[512,128]{1,0:T(8,128)S(1)}, f32[512,128]{1,0:T(8,128)}, u32[]{:S(2)}) copy-start(f32[512,128]{1,0:T(8,128)} %param.11) | copy-start | bytes 786436
  13.1 9.5 %collective-permute-start.2 = (f32[512,128]{1,0:T(8,128)S(1)}, f32[512,128]{1,0:T(8,128)S(1)}, u32[]{:S(2)}, u32[]{:S(2)}) collective-permute-start(f32[512,128]{1,0:T(8,128)S(1)} %constant_dynamic-slice_fusion), channel_id=1, source_target_pairs={{0,2},{2,0},{4,6},{6,4},{8,10},{10,8},{12,14},{14,12},{16,18},{18,... | collective-permute-start | bytes 786440 | tf_op jit(solution)/shard_map/ppermute | solution.py:22
  23.2 1.6 %collective-permute-start.3 = (f32[512,128]{1,0:T(8,128)S(1)}, f32[512,128]{1,0:T(8,128)S(1)}, u32[]{:S(2)}, u32[]{:S(2)}) collective-permute-start(f32[512,128]{1,0:T(8,128)S(1)} %fusion.5), channel_id=1, source_target_pairs={{0,1},{1,0},{2,3},{3,2},{4,5},{5,4},{6,7},{7,6},{8,9},{9,8},{10,11... | collective-permute-start | bytes 786440 | tf_op jit(solution)/shard_map/ppermute | solution.py:77

commit v14 on v13

--- a/solution.py
+++ b/solution.py
@@ -105,15 +105,13 @@
     precision = lax.Precision.HIGH
     blocks = update_panel.reshape(-1, ROW_BLOCK, update_panel.shape[1])
     order = inverse_order(update_blocks)
-    per_section = blocks.shape[0] // 2
 
-    def section_panel(rows_of):
-        chosen = lax.dynamic_slice_in_dim(order, rows_of * per_section, per_section)
-        taken = jnp.take(blocks, chosen, axis=0, mode="clip")
-        return taken.reshape(-1, update_panel.shape[1])
-
-    panels = (section_panel(1 - section), section_panel(section))
-    leaf_solution, (panel_other, panel_own) = two_section_leaf(leaf_factor, leaf_rhs, section, precision, panels)
+    placed_panel = jnp.take(blocks, order, axis=0, mode="clip").reshape(update_panel.shape)
+    placed_panel = two_section_leaf(leaf_factor, leaf_rhs, section, precision, placed_panel)
+    leaf_solution, placed_panel = placed_panel
+    rows_half = placed_panel.shape[0] // 2
+    panel_other = lax.dynamic_slice_in_dim(placed_panel, (1 - section) * rows_half, rows_half, 0)
+    panel_own = lax.dynamic_slice_in_dim(placed_panel, section * rows_half, rows_half, 0)
     other_rows = matmul(panel_other, leaf_solution, precision)
     arrived_rows = pair_swap(other_rows, "rows")
     own_rows = matmul(panel_own, leaf_solution, precision)

time: 26.3 us -> 25.3 us (0.962)
  local copies, waits for them, and re-layouts: 3.35 us -> 2.09 us
  other arithmetic: 0.16 us -> 1.24 us
  matrix products: 11.1 us -> 10.3 us
    gather x2 -> x1, local copies, waits for them, and re-layouts: 3.2 us -> 2.02 us  [two_section_shards(): jnp.take(blocks, order, axis=0, mode='clip').reshape(update_panel.shape)]
    add x1, other arithmetic: 0.07 us -> 1.15 us  [two_section_shards(): chip_sum = own_rows + arrived_rows]
    dot_general x8, matrix products: 11.1 us -> 10.3 us  [matmul(): jnp.dot(left, right, precision=precision, preferred_element_type=jnp.floa...]
  transfers between devices with their start and end apart: 4 -> 4, of which waited for: 3 -> 2; matrix products, arithmetic and copies ran while one was open for 24% -> 20% of each run, Pallas kernels for 0% -> 0%
where the time goes in v14:
time: 25.3 us; the launch traced here: 25.1 us
  matrix products  10.3 us (41%)
  waiting for transfers between devices  7.01 us (28%)
  starting transfers between devices  3.72 us (15%)
  local copies, waits for them, and re-layouts  2.09 us (8%)
  other arithmetic  1.24 us (5%)
  between operations  0.8 us (3%)
    dot_general x8, matrix products, matmul(): jnp.dot(left, right, precision=precision, preferred_element_type=jnp.floa...  10.3 us
    ppermute x1, waiting for transfers between devices, swapped(): return lax.ppermute(block, axis, route)  5.49 us
    ppermute x1, starting transfers between devices, swapped(): return lax.ppermute(block, axis, route)  3 us
    gather x1, local copies, waits for them, and re-layouts, two_section_shards(): jnp.take(blocks, order, axis=0, mode='clip').reshape(update_panel.shape)  2.02 us
    ppermute x3, waiting for transfers between devices, pair_swap(): return lax.ppermute(block, axis, [(0, 1), (1, 0)])  1.53 us
    add x1, other arithmetic, two_section_shards(): chip_sum = own_rows + arrived_rows  1.15 us
    ppermute x3, starting transfers between devices, pair_swap(): return lax.ppermute(block, axis, [(0, 1), (1, 0)])  0.71 us
  transfers between devices with their start and end apart: 4, of which 2 were waited for; matrix products, arithmetic and copies ran while one was open for 20% of the time, Pallas kernels for 0%

profile of v14, /device:TPU:0, one launch (start us, length us, event | category | flops | bytes accessed | tf_op | source)
XLA Modules:
  0.0 25.1 jit_solution(15141505903392772007)
XLA Ops:
  0.6 0.0 copy-start
  0.6 0.0 copy-start.7
  0.7 2.1 %fusion.14 = f32[512,256]{1,0:T(8,128)S(1)} fusion(f32[512,256]{1,0:T(8,128)} %param.7, f32[512,1024]{1,0:T(8,128)} %param.6, s32[]{:T(128)S(6)} %select_n.37), kind=kOutput, calls=%fused_computation.17 | convolution fusion | flops 402653184 | bytes 2097156 | tf_op jit(solution)/shard_map/dot_general | solution.py:26
  2.8 0.5 %collective-permute-start = (f32[512,256]{1,0:T(8,128)S(1)}, f32[512,256]{1,0:T(8,128)}, u32[]{:S(2)}, u32[]{:S(2)}) collective-permute-start(f32[512,256]{1,0:T(8,128)S(1)} %fusion.14), channel_id=1, source_target_pairs={{0,1},{1,0},{2,3},{3,2},{4,5},{5,4},{6,7},{7,6},{8,9},{9,8},{10,11... | collective-permute-start | bytes 1572872 | tf_op jit(solution)/shard_map/ppermute | solution.py:77
  3.3 0.0 copy-done.7
  3.3 0.1 select_reduce_fusion
  3.4 0.0 copy-done
  3.4 0.0 copy-start.4
  3.4 2.0 %gather_fusion = f32[8,128,512]{2,1,0:T(8,128)} fusion(f32[8,128,512]{2,1,0:T(8,128)S(1)} %bitcast.10, s32[1024]{0:T(1024)S(1)} %pad_clamp_fusion), kind=kCustom, calls=%fused_computation | custom fusion | bytes 4194336 | tf_op jit(solution)/shard_map/jit(_take)/gather | solution.py:109
  5.4 0.0 copy-start.3
  5.4 0.0 collective-permute-done
  5.4 0.0 copy-done.4
  5.4 0.0 copy-start.1
  5.4 2.1 %convolution_subtract_fusion = f32[512,256]{1,0:T(8,128)S(1)} fusion(f32[512,256]{1,0:T(8,128)S(1)} %copy-done.4, f32[512,256]{1,0:T(8,128)} %collective-permute-done, f32[512,1024]{1,0:T(8,128)} %param.6, pred[]{:T(512)S(6)} %gt.4), kind=kOutput, calls=%fused_computation.1 | convolution fusion | flops 403046400 | bytes 2621441 | tf_op jit(solution)/shard_map/dot_general | solution.py:26
  7.6 0.0 copy-done.3
  7.6 0.6 %fusion.12 = f32[512,256]{1,0:T(8,128)S(1)} fusion(f32[512,256]{1,0:T(8,128)S(1)} %convolution_subtract_fusion, f32[512,1024]{1,0:T(8,128)S(1)} %copy-done.3, s32[]{:T(128)S(6)} %select_n.37), kind=kOutput, calls=%fused_computation.15 | convolution fusion | flops 402653184 | bytes 2097156 | tf_op jit(solution)/shard_map/dot_general | solution.py:26
  8.2 0.0 copy-done.1
  8.2 0.0 copy-start.2
  8.2 0.6 %fusion.3 = f32[512,256]{1,0:T(8,128)S(1)} fusion(f32[512,256]{1,0:T(8,128)S(1)} %fusion.12, f32[1024,512]{1,0:T(8,128)S(1)} %bitcast.12, s32[]{:T(128)S(6)} %select_n.41), kind=kOutput, calls=%fused_computation.6 | convolution fusion | flops 402653184 | bytes 2097156 | tf_op jit(solution)/shard_map/dot_general | solution.py:26
  8.8 0.1 collective-permute-start.1
  8.9 0.0 copy-start.5
  8.9 2.0 %fusion.5 = f32[512,256]{1,0:T(8,128)S(1)} fusion(f32[512,256]{1,0:T(8,128)S(1)} %fusion.12, f32[1024,512]{1,0:T(8,128)} %bitcast.11, s32[]{:T(128)S(6)} %select_n.37), kind=kOutput, calls=%fused_computation.8 | convolution fusion | flops 402653184 | bytes 2097156 | tf_op jit(solution)/shard_map/dot_general | solution.py:26
  10.9 0.0 copy-done.2
  10.9 0.0 copy-start.6
  10.9 0.0 collective-permute-done.1
  10.9 1.1 %add.26 = f32[512,256]{1,0:T(8,128)S(1)} add(f32[512,256]{1,0:T(8,128)S(1)} %fusion.5, f32[512,256]{1,0:T(8,128)} %collective-permute-done.1) | non-fusion elementwise | flops 131072 | bytes 1572864 | tf_op jit(solution)/shard_map/add | solution.py:119
  12.1 3.0 %collective-permute-start.2 = (f32[512,128]{1,0:T(8,128)S(1)}, f32[512,128]{1,0:T(8,128)S(1)}, u32[]{:S(2)}, u32[]{:S(2)}) collective-permute-start(f32[512,128]{1,0:T(8,128)S(1)} %constant_dynamic-slice_fusion), channel_id=1, source_target_pairs={{0,2},{2,0},{4,6},{6,4},{8,10},{10,8},{12,14},{14,12},{16,18},{18,... | collective-permute-start | bytes 786440 | tf_op jit(solution)/shard_map/ppermute | solution.py:22
  15.1 0.0 copy-done.5
  15.1 1.0 %fusion = f32[512,512]{1,0:T(8,128)S(1)} fusion(f32[512,1024]{1,0:T(8,128)S(1)} %copy-done.5, s32[]{:T(128)S(6)} %select_n.37, pred[]{:T(512)S(6)} %gt.4), kind=kOutput, calls=%fused_computation.3 | convolution fusion | flops 805568512 | bytes 3145733 | tf_op jit(solution)/shard_map/dot_general | solution.py:26
  16.1 5.5 %collective-permute-done.2 = f32[512,128]{1,0:T(8,128)S(1)} collective-permute-done((f32[512,128]{1,0:T(8,128)S(1)}, f32[512,128]{1,0:T(8,128)S(1)}, u32[]{:S(2)}, u32[]{:S(2)}) %collective-permute-start.2) | collective-permute-done | bytes 262176 | tf_op jit(solution)/shard_map/ppermute | solution.py:22
  21.6 0.0 copy-done.6
  21.6 0.6 %fusion.9 = f32[512,128]{1,0:T(8,128)S(1)} fusion(f32[512,1024]{1,0:T(8,128)S(1)} %copy-done.5, s32[]{:T(128)S(6)} %select_n.37, f32[512,128]{1,0:T(8,128)S(1)} %copy-done.6, f32[512,128]{1,0:T(8,128)S(1)} %collective-permute-done.2, f32[512,256]{1,0:T(8,128)S(1)} %add.26, s32[]{:T(128)S(6)} %select_n.43), kind=kOutput, calls=%fused_computation.12 | convolution fusion | flops 201457664 | bytes 2097160 | tf_op jit(solution)/shard_map/dot_general | solution.py:26
  22.2 0.1 collective-permute-start.3
  22.3 1.5 %collective-permute-done.3 = f32[512,128]{1,0:T(8,128)S(1)} collective-permute-done((f32[512,128]{1,0:T(8,128)S(1)}, f32[512,128]{1,0:T(8,128)S(1)}, u32[]{:S(2)}, u32[]{:S(2)}) %collective-permute-start.3) | collective-permute-done | bytes 262176 | tf_op jit(solution)/shard_map/ppermute | solution.py:77
  23.8 1.3 %convolution_subtract_fusion.1 = f32[512,128]{1,0:T(8,128)} fusion(f32[512,128]{1,0:T(8,128)S(1)} %fusion.9, f32[512,512]{1,0:T(8,128)S(1)} %fusion, f32[512,128]{1,0:T(8,128)S(1)} %collective-permute-done.3), kind=kOutput, calls=%fused_computation.2 | convolution fusion | flops 201392128 | bytes 1835008 | tf_op jit(solution)/shard_map/dot_general | solution.py:26
  (2 shorter events, 0.0 us)
Async XLA Ops:
  0.6 2.8 %copy-start = (f32[1024,512]{1,0:T(8,128)S(1)}, f32[1024,512]{1,0:T(8,128)}, u32[]{:S(2)}) copy-start(f32[1024,512]{1,0:T(8,128)} %param.8) | copy-start | bytes 6291460
  0.6 2.6 %copy-start.7 = (s32[1,8]{1,0:T(1,128)S(1)}, s32[1,8]{1,0:T(1,128)}, u32[]{:S(2)}) copy-start(s32[1,8]{1,0:T(1,128)} %param.9) | copy-start | bytes 100
  2.8 2.7 %collective-permute-start = (f32[512,256]{1,0:T(8,128)S(1)}, f32[512,256]{1,0:T(8,128)}, u32[]{:S(2)}, u32[]{:S(2)}) collective-permute-start(f32[512,256]{1,0:T(8,128)S(1)} %fusion.14), channel_id=1, source_target_pairs={{0,1},{1,0},{2,3},{3,2},{4,5},{5,4},{6,7},{7,6},{8,9},{9,8},{10,11... | collective-permute-start | bytes 1572872 | tf_op jit(solution)/shard_map/ppermute | solution.py:77
  3.4 2.0 %copy-start.4 = (f32[512,256]{1,0:T(8,128)S(1)}, f32[512,256]{1,0:T(8,128)}, u32[]{:S(2)}) copy-start(f32[512,256]{1,0:T(8,128)} %param.7) | copy-start | bytes 1572868
  5.4 2.1 %copy-start.3 = (f32[512,1024]{1,0:T(8,128)S(1)}, f32[512,1024]{1,0:T(8,128)}, u32[]{:S(2)}) copy-start(f32[512,1024]{1,0:T(8,128)} %param.6) | copy-start | bytes 6291460
  5.4 2.7 %copy-start.1 = (f32[8,128,512]{2,1,0:T(8,128)S(1)}, f32[8,128,512]{2,1,0:T(8,128)}, u32[]{:S(2)}) copy-start(f32[8,128,512]{2,1,0:T(8,128)} %gather_fusion) | copy-start | bytes 6291460
  8.2 2.7 %copy-start.2 = (f32[512,256]{1,0:T(8,128)}, f32[512,256]{1,0:T(8,128)S(1)}, u32[]{:S(2)}) copy-start(f32[512,256]{1,0:T(8,128)S(1)} %fusion.12) | copy-start | bytes 1572868
  8.8 2.1 %collective-permute-start.1 = (f32[512,256]{1,0:T(8,128)S(1)}, f32[512,256]{1,0:T(8,128)}, u32[]{:S(2)}, u32[]{:S(2)}) collective-permute-start(f32[512,256]{1,0:T(8,128)S(1)} %fusion.3), channel_id=1, source_target_pairs={{0,1},{1,0},{2,3},{3,2},{4,5},{5,4},{6,7},{7,6},{8,9},{9,8},{10,11... | collective-permute-start | bytes 1572872 | tf_op jit(solution)/shard_map/ppermute | solution.py:77
  8.9 6.2 %copy-start.5 = (f32[512,1024]{1,0:T(8,128)S(1)}, f32[512,1024]{1,0:T(8,128)}, u32[]{:S(2)}) copy-start(f32[512,1024]{1,0:T(8,128)} %param.10) | copy-start | bytes 6291460
  10.9 10.7 %copy-start.6 = (f32[512,128]{1,0:T(8,128)S(1)}, f32[512,128]{1,0:T(8,128)}, u32[]{:S(2)}) copy-start(f32[512,128]{1,0:T(8,128)} %param.11) | copy-start | bytes 786436
  12.1 9.5 %collective-permute-start.2 = (f32[512,128]{1,0:T(8,128)S(1)}, f32[512,128]{1,0:T(8,128)S(1)}, u32[]{:S(2)}, u32[]{:S(2)}) collective-permute-start(f32[512,128]{1,0:T(8,128)S(1)} %constant_dynamic-slice_fusion), channel_id=1, source_target_pairs={{0,2},{2,0},{4,6},{6,4},{8,10},{10,8},{12,14},{14,12},{16,18},{18,... | collective-permute-start | bytes 786440 | tf_op jit(solution)/shard_map/ppermute | solution.py:22
  22.2 1.6 %collective-permute-start.3 = (f32[512,128]{1,0:T(8,128)S(1)}, f32[512,128]{1,0:T(8,128)S(1)}, u32[]{:S(2)}, u32[]{:S(2)}) collective-permute-start(f32[512,128]{1,0:T(8,128)S(1)} %fusion.9), channel_id=1, source_target_pairs={{0,1},{1,0},{2,3},{3,2},{4,5},{5,4},{6,7},{7,6},{8,9},{9,8},{10,11... | collective-permute-start | bytes 786440 | tf_op jit(solution)/shard_map/ppermute | solution.py:77

commit v15 on v14

--- a/solution.py
+++ b/solution.py
@@ -116,16 +116,22 @@
     arrived_rows = pair_swap(other_rows, "rows")
     own_rows = matmul(panel_own, leaf_solution, precision)
     own_rows, arrived_rows = lax.optimization_barrier((own_rows, arrived_rows))
-    chip_sum = own_rows + arrived_rows
     column_half = parent_rhs.shape[1]
     sibling = lax.axis_index("leaf") % 2
-    kept = lax.dynamic_slice_in_dim(chip_sum, sibling * column_half, column_half, 1)
-    sent = lax.dynamic_slice_in_dim(chip_sum, (1 - sibling) * column_half, column_half, 1)
+
+    def column_sum(half):
+        own_part = lax.dynamic_slice_in_dim(own_rows, half * column_half, column_half, 1)
+        arrived_part = lax.dynamic_slice_in_dim(arrived_rows, half * column_half, column_half, 1)
+        return own_part + arrived_part
+
+    sent = column_sum(1 - sibling)
+    sent, own_rows, arrived_rows = lax.optimization_barrier((sent, own_rows, arrived_rows))
+    kept = column_sum(sibling)
     tile_rows = parent_rhs.shape[0]
     diagonal = lax.dynamic_slice_in_dim(parent_factor, section * tile_rows, tile_rows, 1)
     coupling = lower_coupling(parent_factor, diagonal, section, precision)
     arrived = swapped(sent, "leaf", 0)
-    arrived, coupling = lax.optimization_barrier((arrived, coupling))
+    arrived, coupling, kept = lax.optimization_barrier((arrived, coupling, kept))
     pending = parent_rhs - (kept + arrived)
     first = matmul(diagonal, pending, precision)
     arrived = pair_swap(first, "rows")

time: 25.3 us -> 25.1 us (level)
  waiting for transfers between devices: 7.01 us -> 6.02 us
  other arithmetic: 1.24 us -> 2.12 us
    ppermute x1, waiting for transfers between devices: 5.49 us -> 4.5 us  [swapped(): return lax.ppermute(block, axis, route)]
    add x1 -> x2, other arithmetic: 1.15 us -> 2.02 us  [column_sum(): return own_part + arrived_part]
  transfers between devices with their start and end apart: 4 -> 4, of which waited for: 2 -> 2; matrix products, arithmetic and copies ran while one was open for 20% -> 24% of each run, Pallas kernels for 0% -> 0%
where the time goes in v15:
time: 25.1 us; the launch traced here: 25 us
  matrix products  10.3 us (41%)
  waiting for transfers between devices  6.02 us (24%)
  starting transfers between devices  3.71 us (15%)
  other arithmetic  2.12 us (8%)
  local copies, waits for them, and re-layouts  2.07 us (8%)
  between operations  0.79 us (3%)
    dot_general x8, matrix products, matmul(): jnp.dot(left, right, precision=precision, preferred_element_type=jnp.floa...  10.3 us
    ppermute x1, waiting for transfers between devices, swapped(): return lax.ppermute(block, axis, route)  4.5 us
    ppermute x1, starting transfers between devices, swapped(): return lax.ppermute(block, axis, route)  2.99 us
    add x2, other arithmetic, column_sum(): return own_part + arrived_part  2.02 us
    gather x1, local copies, waits for them, and re-layouts, two_section_shards(): jnp.take(blocks, order, axis=0, mode='clip').reshape(update_panel.shape)  2.02 us
    ppermute x3, waiting for transfers between devices, pair_swap(): return lax.ppermute(block, axis, [(0, 1), (1, 0)])  1.53 us
    ppermute x3, starting transfers between devices, pair_swap(): return lax.ppermute(block, axis, [(0, 1), (1, 0)])  0.71 us
  transfers between devices with their start and end apart: 4, of which 2 were waited for; matrix products, arithmetic and copies ran while one was open for 24% of the time, Pallas kernels for 0%

profile of v15, /device:TPU:0, one launch (start us, length us, event | category | flops | bytes accessed | tf_op | source)
XLA Modules:
  0.0 25.0 jit_solution(4098816301101205218)
XLA Ops:
  0.6 0.0 copy-start
  0.6 0.0 copy-start.7
  0.7 2.1 %fusion.14 = f32[512,256]{1,0:T(8,128)S(1)} fusion(f32[512,256]{1,0:T(8,128)} %param.7, f32[512,1024]{1,0:T(8,128)} %param.6, s32[]{:T(128)S(6)} %select_n.39), kind=kOutput, calls=%fused_computation.17 | convolution fusion | flops 402653184 | bytes 2097156 | tf_op jit(solution)/shard_map/dot_general | solution.py:26
  2.8 0.5 %collective-permute-start = (f32[512,256]{1,0:T(8,128)S(1)}, f32[512,256]{1,0:T(8,128)}, u32[]{:S(2)}, u32[]{:S(2)}) collective-permute-start(f32[512,256]{1,0:T(8,128)S(1)} %fusion.14), channel_id=1, source_target_pairs={{0,1},{1,0},{2,3},{3,2},{4,5},{5,4},{6,7},{7,6},{8,9},{9,8},{10,11... | collective-permute-start | bytes 1572872 | tf_op jit(solution)/shard_map/ppermute | solution.py:77
  3.3 0.0 copy-done.7
  3.3 0.1 select_reduce_fusion
  3.4 0.0 copy-done
  3.4 0.0 copy-start.5
  3.4 2.0 %gather_fusion = f32[8,128,512]{2,1,0:T(8,128)} fusion(f32[8,128,512]{2,1,0:T(8,128)S(1)} %bitcast.10, s32[1024]{0:T(1024)S(1)} %pad_clamp_fusion), kind=kCustom, calls=%fused_computation | custom fusion | bytes 4194336 | tf_op jit(solution)/shard_map/jit(_take)/gather | solution.py:109
  5.4 0.0 copy-start.3
  5.4 0.0 collective-permute-done
  5.4 0.0 copy-done.5
  5.4 0.0 copy-start.1
  5.4 2.1 %convolution_subtract_fusion = f32[512,256]{1,0:T(8,128)S(1)} fusion(f32[512,256]{1,0:T(8,128)S(1)} %copy-done.5, f32[512,256]{1,0:T(8,128)} %collective-permute-done, f32[512,1024]{1,0:T(8,128)} %param.6, pred[]{:T(512)S(6)} %gt.4), kind=kOutput, calls=%fused_computation.1 | convolution fusion | flops 403046400 | bytes 2621441 | tf_op jit(solution)/shard_map/dot_general | solution.py:26
  7.6 0.0 copy-done.3
  7.6 0.6 %fusion.12 = f32[512,256]{1,0:T(8,128)S(1)} fusion(f32[512,256]{1,0:T(8,128)S(1)} %convolution_subtract_fusion, f32[512,1024]{1,0:T(8,128)S(1)} %copy-done.3, s32[]{:T(128)S(6)} %select_n.39), kind=kOutput, calls=%fused_computation.15 | convolution fusion | flops 402653184 | bytes 2097156 | tf_op jit(solution)/shard_map/dot_general | solution.py:26
  8.2 0.0 copy-done.1
  8.2 0.0 copy-start.2
  8.2 0.6 %fusion.3 = f32[512,256]{1,0:T(8,128)S(1)} fusion(f32[512,256]{1,0:T(8,128)S(1)} %fusion.12, f32[1024,512]{1,0:T(8,128)S(1)} %bitcast.12, s32[]{:T(128)S(6)} %select_n.43), kind=kOutput, calls=%fused_computation.6 | convolution fusion | flops 402653184 | bytes 2097156 | tf_op jit(solution)/shard_map/dot_general | solution.py:26
  8.8 0.1 collective-permute-start.1
  8.9 0.0 copy-start.4
  8.9 2.0 %fusion.5 = f32[512,256]{1,0:T(8,128)S(1)} fusion(f32[512,256]{1,0:T(8,128)S(1)} %fusion.12, f32[1024,512]{1,0:T(8,128)} %bitcast.11, s32[]{:T(128)S(6)} %select_n.39), kind=kOutput, calls=%fused_computation.8 | convolution fusion | flops 402653184 | bytes 2097156 | tf_op jit(solution)/shard_map/dot_general | solution.py:26
  10.9 0.0 copy-done.2
  10.9 0.0 copy-start.6
  10.9 0.0 collective-permute-done.1
  10.9 1.0 %dynamic-slice_add_fusion.1 = f32[512,128]{1,0:T(8,128)S(1)} fusion(f32[512,256]{1,0:T(8,128)} %collective-permute-done.1, s32[]{:T(128)S(6)} %select_n.45, f32[512,256]{1,0:T(8,128)S(1)} %fusion.5), kind=kLoop, calls=%fused_computation.26 | loop fusion | flops 65536 | bytes 786436 | tf_op jit(solution)/shard_map/add | solution.py:125
  11.9 3.0 %collective-permute-start.2 = (f32[512,128]{1,0:T(8,128)S(1)}, f32[512,128]{1,0:T(8,128)S(1)}, u32[]{:S(2)}, u32[]{:S(2)}) collective-permute-start(f32[512,128]{1,0:T(8,128)S(1)} %dynamic-slice_add_fusion.1), channel_id=1, source_target_pairs={{0,2},{2,0},{4,6},{6,4},{8,10},{10,8},{12,14},{14,12},{16,18},{18,... | collective-permute-start | bytes 786440 | tf_op jit(solution)/shard_map/ppermute | solution.py:22
  14.9 0.0 copy-done.4
  14.9 1.0 %fusion = f32[512,512]{1,0:T(8,128)S(1)} fusion(f32[512,1024]{1,0:T(8,128)S(1)} %copy-done.4, s32[]{:T(128)S(6)} %select_n.39, pred[]{:T(512)S(6)} %gt.4), kind=kOutput, calls=%fused_computation.3 | convolution fusion | flops 805568512 | bytes 3145733 | tf_op jit(solution)/shard_map/dot_general | solution.py:26
  16.0 1.0 %dynamic-slice_add_fusion = f32[512,128]{1,0:T(8,128)S(1)} fusion(f32[512,256]{1,0:T(8,128)} %collective-permute-done.1, s32[]{:T(128)S(6)} %select_n.47, f32[512,256]{1,0:T(8,128)S(1)} %fusion.5), kind=kLoop, calls=%fused_computation.25 | loop fusion | flops 65536 | bytes 786436 | tf_op jit(solution)/shard_map/add | solution.py:125
  17.0 4.5 %collective-permute-done.2 = f32[512,128]{1,0:T(8,128)S(1)} collective-permute-done((f32[512,128]{1,0:T(8,128)S(1)}, f32[512,128]{1,0:T(8,128)S(1)}, u32[]{:S(2)}, u32[]{:S(2)}) %collective-permute-start.2) | collective-permute-done | bytes 262176 | tf_op jit(solution)/shard_map/ppermute | solution.py:22
  21.5 0.0 copy-done.6
  21.5 0.6 %fusion.9 = f32[512,128]{1,0:T(8,128)S(1)} fusion(f32[512,1024]{1,0:T(8,128)S(1)} %copy-done.4, s32[]{:T(128)S(6)} %select_n.39, f32[512,128]{1,0:T(8,128)S(1)} %copy-done.6, f32[512,128]{1,0:T(8,128)S(1)} %dynamic-slice_add_fusion, f32[512,128]{1,0:T(8,128)S(1)} %collective-permute-done.2), kind=kOutput, calls=%fused_computation.12 | convolution fusion | flops 201457664 | bytes 2097156 | tf_op jit(solution)/shard_map/dot_general | solution.py:26
  22.1 0.1 collective-permute-start.3
  22.1 1.5 %collective-permute-done.3 = f32[512,128]{1,0:T(8,128)S(1)} collective-permute-done((f32[512,128]{1,0:T(8,128)S(1)}, f32[512,128]{1,0:T(8,128)S(1)}, u32[]{:S(2)}, u32[]{:S(2)}) %collective-permute-start.3) | collective-permute-done | bytes 262176 | tf_op jit(solution)/shard_map/ppermute | solution.py:77
  23.7 1.3 %convolution_subtract_fusion.1 = f32[512,128]{1,0:T(8,128)} fusion(f32[512,128]{1,0:T(8,128)S(1)} %fusion.9, f32[512,512]{1,0:T(8,128)S(1)} %fusion, f32[512,128]{1,0:T(8,128)S(1)} %collective-permute-done.3), kind=kOutput, calls=%fused_computation.2 | convolution fusion | flops 201392128 | bytes 1835008 | tf_op jit(solution)/shard_map/dot_general | solution.py:26
  (1 shorter events, 0.0 us)
Async XLA Ops:
  0.6 2.8 %copy-start = (f32[1024,512]{1,0:T(8,128)S(1)}, f32[1024,512]{1,0:T(8,128)}, u32[]{:S(2)}) copy-start(f32[1024,512]{1,0:T(8,128)} %param.8) | copy-start | bytes 6291460
  0.6 2.6 %copy-start.7 = (s32[1,8]{1,0:T(1,128)S(1)}, s32[1,8]{1,0:T(1,128)}, u32[]{:S(2)}) copy-start(s32[1,8]{1,0:T(1,128)} %param.9) | copy-start | bytes 100
  2.8 2.7 %collective-permute-start = (f32[512,256]{1,0:T(8,128)S(1)}, f32[512,256]{1,0:T(8,128)}, u32[]{:S(2)}, u32[]{:S(2)}) collective-permute-start(f32[512,256]{1,0:T(8,128)S(1)} %fusion.14), channel_id=1, source_target_pairs={{0,1},{1,0},{2,3},{3,2},{4,5},{5,4},{6,7},{7,6},{8,9},{9,8},{10,11... | collective-permute-start | bytes 1572872 | tf_op jit(solution)/shard_map/ppermute | solution.py:77
  3.4 2.0 %copy-start.5 = (f32[512,256]{1,0:T(8,128)S(1)}, f32[512,256]{1,0:T(8,128)}, u32[]{:S(2)}) copy-start(f32[512,256]{1,0:T(8,128)} %param.7) | copy-start | bytes 1572868
  5.4 2.1 %copy-start.3 = (f32[512,1024]{1,0:T(8,128)S(1)}, f32[512,1024]{1,0:T(8,128)}, u32[]{:S(2)}) copy-start(f32[512,1024]{1,0:T(8,128)} %param.6) | copy-start | bytes 6291460
  5.4 2.7 %copy-start.1 = (f32[8,128,512]{2,1,0:T(8,128)S(1)}, f32[8,128,512]{2,1,0:T(8,128)}, u32[]{:S(2)}) copy-start(f32[8,128,512]{2,1,0:T(8,128)} %gather_fusion) | copy-start | bytes 6291460
  8.2 2.7 %copy-start.2 = (f32[512,256]{1,0:T(8,128)}, f32[512,256]{1,0:T(8,128)S(1)}, u32[]{:S(2)}) copy-start(f32[512,256]{1,0:T(8,128)S(1)} %fusion.12) | copy-start | bytes 1572868
  8.8 2.1 %collective-permute-start.1 = (f32[512,256]{1,0:T(8,128)S(1)}, f32[512,256]{1,0:T(8,128)}, u32[]{:S(2)}, u32[]{:S(2)}) collective-permute-start(f32[512,256]{1,0:T(8,128)S(1)} %fusion.3), channel_id=1, source_target_pairs={{0,1},{1,0},{2,3},{3,2},{4,5},{5,4},{6,7},{7,6},{8,9},{9,8},{10,11... | collective-permute-start | bytes 1572872 | tf_op jit(solution)/shard_map/ppermute | solution.py:77
  8.9 6.0 %copy-start.4 = (f32[512,1024]{1,0:T(8,128)S(1)}, f32[512,1024]{1,0:T(8,128)}, u32[]{:S(2)}) copy-start(f32[512,1024]{1,0:T(8,128)} %param.10) | copy-start | bytes 6291460
  10.9 10.6 %copy-start.6 = (f32[512,128]{1,0:T(8,128)S(1)}, f32[512,128]{1,0:T(8,128)}, u32[]{:S(2)}) copy-start(f32[512,128]{1,0:T(8,128)} %param.11) | copy-start | bytes 786436
  11.9 9.5 %collective-permute-start.2 = (f32[512,128]{1,0:T(8,128)S(1)}, f32[512,128]{1,0:T(8,128)S(1)}, u32[]{:S(2)}, u32[]{:S(2)}) collective-permute-start(f32[512,128]{1,0:T(8,128)S(1)} %dynamic-slice_add_fusion.1), channel_id=1, source_target_pairs={{0,2},{2,0},{4,6},{6,4},{8,10},{10,8},{12,14},{14,12},{16,18},{18,... | collective-permute-start | bytes 786440 | tf_op jit(solution)/shard_map/ppermute | solution.py:22
  22.1 1.6 %collective-permute-start.3 = (f32[512,128]{1,0:T(8,128)S(1)}, f32[512,128]{1,0:T(8,128)S(1)}, u32[]{:S(2)}, u32[]{:S(2)}) collective-permute-start(f32[512,128]{1,0:T(8,128)S(1)} %fusion.9), channel_id=1, source_target_pairs={{0,1},{1,0},{2,3},{3,2},{4,5},{5,4},{6,7},{7,6},{8,9},{9,8},{10,11... | collective-permute-start | bytes 786440 | tf_op jit(solution)/shard_map/ppermute | solution.py:77

commit v16 on v15

--- a/solution.py
+++ b/solution.py
@@ -135,7 +135,8 @@
     pending = parent_rhs - (kept + arrived)
     first = matmul(diagonal, pending, precision)
     arrived = pair_swap(first, "rows")
-    parent_solution = first - matmul(coupling, arrived, precision)
+    correction = lax.optimization_barrier(matmul(coupling, arrived, precision))
+    parent_solution = first - correction
     return (leaf_solution, parent_solution)
 
 

time: 25.1 us -> 25.2 us (level)
  matrix products: 10.3 us -> 9.56 us
  other arithmetic: 2.12 us -> 2.85 us
    sub x0 -> x1, other arithmetic: none -> 0.73 us  [two_section_shards(): parent_solution = first - correction]
    dot_general x8, matrix products: 10.3 us -> 9.56 us  [matmul(): jnp.dot(left, right, precision=precision, preferred_element_type=jnp.floa...]
where the time goes in v16:
time: 25.2 us; the launch traced here: 25 us
  matrix products  9.56 us (38%)
  waiting for transfers between devices  6.02 us (24%)
  starting transfers between devices  3.71 us (15%)
  other arithmetic  2.85 us (11%)
  local copies, waits for them, and re-layouts  2.07 us (8%)
  between operations  0.8 us (3%)
    dot_general x8, matrix products, matmul(): jnp.dot(left, right, precision=precision, preferred_element_type=jnp.floa...  9.56 us
    ppermute x1, waiting for transfers between devices, swapped(): return lax.ppermute(block, axis, route)  4.5 us
    ppermute x1, starting transfers between devices, swapped(): return lax.ppermute(block, axis, route)  2.99 us
    add x2, other arithmetic, column_sum(): return own_part + arrived_part  2.02 us
    gather x1, local copies, waits for them, and re-layouts, two_section_shards(): jnp.take(blocks, order, axis=0, mode='clip').reshape(update_panel.shape)  2.02 us
    ppermute x3, waiting for transfers between devices, pair_swap(): return lax.ppermute(block, axis, [(0, 1), (1, 0)])  1.53 us
    sub x1, other arithmetic, two_section_shards(): parent_solution = first - correction  0.73 us
    ppermute x3, starting transfers between devices, pair_swap(): return lax.ppermute(block, axis, [(0, 1), (1, 0)])  0.71 us
  transfers between devices with their start and end apart: 4, of which 2 were waited for; matrix products, arithmetic and copies ran while one was open for 24% of the time, Pallas kernels for 0%

profile of v16, /device:TPU:0, one launch (start us, length us, event | category | flops | bytes accessed | tf_op | source)
XLA Modules:
  0.0 25.0 jit_solution(13273608023558799352)
XLA Ops:
  0.6 0.0 copy-start
  0.6 0.0 copy-start.7
  0.7 2.1 %fusion.14 = f32[512,256]{1,0:T(8,128)S(1)} fusion(f32[512,256]{1,0:T(8,128)} %param.7, f32[512,1024]{1,0:T(8,128)} %param.6, s32[]{:T(128)S(6)} %select_n.39), kind=kOutput, calls=%fused_computation.16 | convolution fusion | flops 402653184 | bytes 2097156 | tf_op jit(solution)/shard_map/dot_general | solution.py:26
  2.8 0.5 %collective-permute-start = (f32[512,256]{1,0:T(8,128)S(1)}, f32[512,256]{1,0:T(8,128)}, u32[]{:S(2)}, u32[]{:S(2)}) collective-permute-start(f32[512,256]{1,0:T(8,128)S(1)} %fusion.14), channel_id=1, source_target_pairs={{0,1},{1,0},{2,3},{3,2},{4,5},{5,4},{6,7},{7,6},{8,9},{9,8},{10,11... | collective-permute-start | bytes 1572872 | tf_op jit(solution)/shard_map/ppermute | solution.py:77
  3.3 0.0 copy-done.7
  3.3 0.1 select_reduce_fusion
  3.4 0.0 copy-done
  3.4 0.0 copy-start.5
  3.4 2.0 %gather_fusion = f32[8,128,512]{2,1,0:T(8,128)} fusion(f32[8,128,512]{2,1,0:T(8,128)S(1)} %bitcast.10, s32[1024]{0:T(1024)S(1)} %pad_clamp_fusion), kind=kCustom, calls=%fused_computation | custom fusion | bytes 4194336 | tf_op jit(solution)/shard_map/jit(_take)/gather | solution.py:109
  5.4 0.0 copy-start.3
  5.4 0.0 collective-permute-done
  5.4 0.0 copy-done.5
  5.4 0.0 copy-start.1
  5.4 2.1 %convolution_subtract_fusion = f32[512,256]{1,0:T(8,128)S(1)} fusion(f32[512,256]{1,0:T(8,128)S(1)} %copy-done.5, f32[512,256]{1,0:T(8,128)} %collective-permute-done, f32[512,1024]{1,0:T(8,128)} %param.6, pred[]{:T(512)S(6)} %gt.4), kind=kOutput, calls=%fused_computation.1 | convolution fusion | flops 403046400 | bytes 2621441 | tf_op jit(solution)/shard_map/dot_general | solution.py:26
  7.6 0.0 copy-done.3
  7.6 0.6 %fusion.12 = f32[512,256]{1,0:T(8,128)S(1)} fusion(f32[512,256]{1,0:T(8,128)S(1)} %convolution_subtract_fusion, f32[512,1024]{1,0:T(8,128)S(1)} %copy-done.3, s32[]{:T(128)S(6)} %select_n.39), kind=kOutput, calls=%fused_computation.14 | convolution fusion | flops 402653184 | bytes 2097156 | tf_op jit(solution)/shard_map/dot_general | solution.py:26
  8.2 0.0 copy-done.1
  8.2 0.0 copy-start.2
  8.2 0.6 %fusion.3 = f32[512,256]{1,0:T(8,128)S(1)} fusion(f32[512,256]{1,0:T(8,128)S(1)} %fusion.12, f32[1024,512]{1,0:T(8,128)S(1)} %bitcast.12, s32[]{:T(128)S(6)} %select_n.43), kind=kOutput, calls=%fused_computation.5 | convolution fusion | flops 402653184 | bytes 2097156 | tf_op jit(solution)/shard_map/dot_general | solution.py:26
  8.8 0.1 collective-permute-start.1
  8.9 0.0 copy-start.4
  8.9 2.0 %fusion.5 = f32[512,256]{1,0:T(8,128)S(1)} fusion(f32[512,256]{1,0:T(8,128)S(1)} %fusion.12, f32[1024,512]{1,0:T(8,128)} %bitcast.11, s32[]{:T(128)S(6)} %select_n.39), kind=kOutput, calls=%fused_computation.7 | convolution fusion | flops 402653184 | bytes 2097156 | tf_op jit(solution)/shard_map/dot_general | solution.py:26
  10.9 0.0 copy-done.2
  10.9 0.0 copy-start.6
  10.9 0.0 collective-permute-done.1
  10.9 1.0 %dynamic-slice_add_fusion.1 = f32[512,128]{1,0:T(8,128)S(1)} fusion(f32[512,256]{1,0:T(8,128)} %collective-permute-done.1, s32[]{:T(128)S(6)} %select_n.45, f32[512,256]{1,0:T(8,128)S(1)} %fusion.5), kind=kLoop, calls=%fused_computation.25 | loop fusion | flops 65536 | bytes 786436 | tf_op jit(solution)/shard_map/add | solution.py:125
  11.9 3.0 %collective-permute-start.2 = (f32[512,128]{1,0:T(8,128)S(1)}, f32[512,128]{1,0:T(8,128)S(1)}, u32[]{:S(2)}, u32[]{:S(2)}) collective-permute-start(f32[512,128]{1,0:T(8,128)S(1)} %dynamic-slice_add_fusion.1), channel_id=1, source_target_pairs={{0,2},{2,0},{4,6},{6,4},{8,10},{10,8},{12,14},{14,12},{16,18},{18,... | collective-permute-start | bytes 786440 | tf_op jit(solution)/shard_map/ppermute | solution.py:22
  14.9 0.0 copy-done.4
  14.9 1.0 %fusion = f32[512,512]{1,0:T(8,128)S(1)} fusion(f32[512,1024]{1,0:T(8,128)S(1)} %copy-done.4, s32[]{:T(128)S(6)} %select_n.39, pred[]{:T(512)S(6)} %gt.4), kind=kOutput, calls=%fused_computation.2 | convolution fusion | flops 805568512 | bytes 3145733 | tf_op jit(solution)/shard_map/dot_general | solution.py:26
  16.0 1.0 %dynamic-slice_add_fusion = f32[512,128]{1,0:T(8,128)S(1)} fusion(f32[512,256]{1,0:T(8,128)} %collective-permute-done.1, s32[]{:T(128)S(6)} %select_n.47, f32[512,256]{1,0:T(8,128)S(1)} %fusion.5), kind=kLoop, calls=%fused_computation.24 | loop fusion | flops 65536 | bytes 786436 | tf_op jit(solution)/shard_map/add | solution.py:125
  17.0 4.5 %collective-permute-done.2 = f32[512,128]{1,0:T(8,128)S(1)} collective-permute-done((f32[512,128]{1,0:T(8,128)S(1)}, f32[512,128]{1,0:T(8,128)S(1)}, u32[]{:S(2)}, u32[]{:S(2)}) %collective-permute-start.2) | collective-permute-done | bytes 262176 | tf_op jit(solution)/shard_map/ppermute | solution.py:22
  21.5 0.0 copy-done.6
  21.5 0.6 %fusion.9 = f32[512,128]{1,0:T(8,128)S(1)} fusion(f32[512,1024]{1,0:T(8,128)S(1)} %copy-done.4, s32[]{:T(128)S(6)} %select_n.39, f32[512,128]{1,0:T(8,128)S(1)} %copy-done.6, f32[512,128]{1,0:T(8,128)S(1)} %dynamic-slice_add_fusion, f32[512,128]{1,0:T(8,128)S(1)} %collective-permute-done.2), kind=kOutput, calls=%fused_computation.11 | convolution fusion | flops 201457664 | bytes 2097156 | tf_op jit(solution)/shard_map/dot_general | solution.py:26
  22.1 0.1 collective-permute-start.3
  22.1 1.5 %collective-permute-done.3 = f32[512,128]{1,0:T(8,128)S(1)} collective-permute-done((f32[512,128]{1,0:T(8,128)S(1)}, f32[512,128]{1,0:T(8,128)S(1)}, u32[]{:S(2)}, u32[]{:S(2)}) %collective-permute-start.3) | collective-permute-done | bytes 262176 | tf_op jit(solution)/shard_map/ppermute | solution.py:77
  23.7 0.6 %fusion.30 = f32[512,128]{1,0:T(8,128)S(1)} fusion(f32[512,512]{1,0:T(8,128)S(1)} %fusion, f32[512,128]{1,0:T(8,128)S(1)} %collective-permute-done.3), kind=kOutput, calls=%fused_computation.37 | convolution fusion | flops 201326592 | bytes 1572864 | tf_op jit(solution)/shard_map/dot_general | solution.py:26
  24.3 0.7 %sub.19 = f32[512,128]{1,0:T(8,128)} subtract(f32[512,128]{1,0:T(8,128)S(1)} %fusion.9, f32[512,128]{1,0:T(8,128)S(1)} %fusion.30) | non-fusion elementwise | flops 65536 | bytes 786432 | tf_op jit(solution)/shard_map/sub | solution.py:139
  (1 shorter events, 0.0 us)
Async XLA Ops:
  0.6 2.8 %copy-start = (f32[1024,512]{1,0:T(8,128)S(1)}, f32[1024,512]{1,0:T(8,128)}, u32[]{:S(2)}) copy-start(f32[1024,512]{1,0:T(8,128)} %param.8) | copy-start | bytes 6291460
  0.6 2.6 %copy-start.7 = (s32[1,8]{1,0:T(1,128)S(1)}, s32[1,8]{1,0:T(1,128)}, u32[]{:S(2)}) copy-start(s32[1,8]{1,0:T(1,128)} %param.9) | copy-start | bytes 100
  2.8 2.7 %collective-permute-start = (f32[512,256]{1,0:T(8,128)S(1)}, f32[512,256]{1,0:T(8,128)}, u32[]{:S(2)}, u32[]{:S(2)}) collective-permute-start(f32[512,256]{1,0:T(8,128)S(1)} %fusion.14), channel_id=1, source_target_pairs={{0,1},{1,0},{2,3},{3,2},{4,5},{5,4},{6,7},{7,6},{8,9},{9,8},{10,11... | collective-permute-start | bytes 1572872 | tf_op jit(solution)/shard_map/ppermute | solution.py:77
  3.4 2.0 %copy-start.5 = (f32[512,256]{1,0:T(8,128)S(1)}, f32[512,256]{1,0:T(8,128)}, u32[]{:S(2)}) copy-start(f32[512,256]{1,0:T(8,128)} %param.7) | copy-start | bytes 1572868
  5.4 2.1 %copy-start.3 = (f32[512,1024]{1,0:T(8,128)S(1)}, f32[512,1024]{1,0:T(8,128)}, u32[]{:S(2)}) copy-start(f32[512,1024]{1,0:T(8,128)} %param.6) | copy-start | bytes 6291460
  5.4 2.7 %copy-start.1 = (f32[8,128,512]{2,1,0:T(8,128)S(1)}, f32[8,128,512]{2,1,0:T(8,128)}, u32[]{:S(2)}) copy-start(f32[8,128,512]{2,1,0:T(8,128)} %gather_fusion) | copy-start | bytes 6291460
  8.2 2.7 %copy-start.2 = (f32[512,256]{1,0:T(8,128)}, f32[512,256]{1,0:T(8,128)S(1)}, u32[]{:S(2)}) copy-start(f32[512,256]{1,0:T(8,128)S(1)} %fusion.12) | copy-start | bytes 1572868
  8.8 2.1 %collective-permute-start.1 = (f32[512,256]{1,0:T(8,128)S(1)}, f32[512,256]{1,0:T(8,128)}, u32[]{:S(2)}, u32[]{:S(2)}) collective-permute-start(f32[512,256]{1,0:T(8,128)S(1)} %fusion.3), channel_id=1, source_target_pairs={{0,1},{1,0},{2,3},{3,2},{4,5},{5,4},{6,7},{7,6},{8,9},{9,8},{10,11... | collective-permute-start | bytes 1572872 | tf_op jit(solution)/shard_map/ppermute | solution.py:77
  8.9 6.0 %copy-start.4 = (f32[512,1024]{1,0:T(8,128)S(1)}, f32[512,1024]{1,0:T(8,128)}, u32[]{:S(2)}) copy-start(f32[512,1024]{1,0:T(8,128)} %param.10) | copy-start | bytes 6291460
  10.9 10.6 %copy-start.6 = (f32[512,128]{1,0:T(8,128)S(1)}, f32[512,128]{1,0:T(8,128)}, u32[]{:S(2)}) copy-start(f32[512,128]{1,0:T(8,128)} %param.11) | copy-start | bytes 786436
  11.9 9.5 %collective-permute-start.2 = (f32[512,128]{1,0:T(8,128)S(1)}, f32[512,128]{1,0:T(8,128)S(1)}, u32[]{:S(2)}, u32[]{:S(2)}) collective-permute-start(f32[512,128]{1,0:T(8,128)S(1)} %dynamic-slice_add_fusion.1), channel_id=1, source_target_pairs={{0,2},{2,0},{4,6},{6,4},{8,10},{10,8},{12,14},{14,12},{16,18},{18,... | collective-permute-start | bytes 786440 | tf_op jit(solution)/shard_map/ppermute | solution.py:22
  22.1 1.6 %collective-permute-start.3 = (f32[512,128]{1,0:T(8,128)S(1)}, f32[512,128]{1,0:T(8,128)S(1)}, u32[]{:S(2)}, u32[]{:S(2)}) collective-permute-start(f32[512,128]{1,0:T(8,128)S(1)} %fusion.9), channel_id=1, source_target_pairs={{0,1},{1,0},{2,3},{3,2},{4,5},{5,4},{6,7},{7,6},{8,9},{9,8},{10,11... | collective-permute-start | bytes 786440 | tf_op jit(solution)/shard_map/ppermute | solution.py:77

commit v17 on v15

--- a/solution.py
+++ b/solution.py
@@ -88,8 +88,8 @@
     diagonal = lax.dynamic_slice_in_dim(factor, section * tile_rows, tile_rows, 1)
     first = matmul(diagonal, right_side, precision)
     arrived = pair_swap(first, "rows")
-    arrived, early = lax.optimization_barrier((arrived, early))
     below = jnp.where(section > 0, factor[:, :tile_rows], jnp.zeros_like(diagonal))
+    arrived, below, early = lax.optimization_barrier((arrived, below, early))
     return matmul(diagonal, right_side - matmul(below, arrived, precision), precision), early
 
 

time: 25.1 us -> 26.3 us (1.048)
  other arithmetic: 2.12 us -> 3.58 us
  matrix products: 10.3 us -> 9.54 us
  local copies, waits for them, and re-layouts: 2.07 us -> 2.58 us
    select_n x0 -> x1, other arithmetic: none -> 1.46 us  [two_section_leaf(): jnp.where(section > 0, factor[:, :tile_rows], jnp.zeros_like(diagonal))]
    dot_general x8, matrix products: 10.3 us -> 9.54 us  [matmul(): jnp.dot(left, right, precision=precision, preferred_element_type=jnp.floa...]
    unnamed x16, local copies, waits for them, and re-layouts: 0.04 us -> 0.56 us
  transfers between devices with their start and end apart: 4 -> 4, of which waited for: 2 -> 2; matrix products, arithmetic and copies ran while one was open for 24% -> 29% of each run, Pallas kernels for 0% -> 0%
where the time goes in v17:
time: 26.3 us; the launch traced here: 26.1 us
  matrix products  9.54 us (36%)
  waiting for transfers between devices  6.03 us (23%)
  starting transfers between devices  3.64 us (14%)
  other arithmetic  3.58 us (14%)
  local copies, waits for them, and re-layouts  2.58 us (10%)
  between operations  0.78 us (3%)
    dot_general x8, matrix products, matmul(): jnp.dot(left, right, precision=precision, preferred_element_type=jnp.floa...  9.54 us
    ppermute x1, waiting for transfers between devices, swapped(): return lax.ppermute(block, axis, route)  4.5 us
    ppermute x1, starting transfers between devices, swapped(): return lax.ppermute(block, axis, route)  2.99 us
    add x2, other arithmetic, column_sum(): return own_part + arrived_part  2.02 us
    gather x1, local copies, waits for them, and re-layouts, two_section_shards(): jnp.take(blocks, order, axis=0, mode='clip').reshape(update_panel.shape)  2.02 us
    ppermute x3, waiting for transfers between devices, pair_swap(): return lax.ppermute(block, axis, [(0, 1), (1, 0)])  1.53 us
    select_n x1, other arithmetic, two_section_leaf(): jnp.where(section > 0, factor[:, :tile_rows], jnp.zeros_like(diagonal))  1.46 us
    ppermute x3, starting transfers between devices, pair_swap(): return lax.ppermute(block, axis, [(0, 1), (1, 0)])  0.64 us
  transfers between devices with their start and end apart: 4, of which 2 were waited for; matrix products, arithmetic and copies ran while one was open for 29% of the time, Pallas kernels for 0%

profile of v17, /device:TPU:0, one launch (start us, length us, event | category | flops | bytes accessed | tf_op | source)
XLA Modules:
  0.0 26.1 jit_solution(16086871609914069320)
XLA Ops:
  0.6 0.0 copy-start
  0.6 0.0 copy-start.7
  0.7 2.9 %fusion.12 = f32[512,256]{1,0:T(8,128)} fusion(f32[512,256]{1,0:T(8,128)} %param.7, f32[512,1024]{1,0:T(8,128)} %param.6, s32[]{:T(128)S(6)} %select_n.39), kind=kOutput, calls=%fused_computation.16 | convolution fusion | flops 402653184 | bytes 2097156 | tf_op jit(solution)/shard_map/dot_general | solution.py:26
  3.6 0.5 %collective-permute-start = (f32[512,256]{1,0:T(8,128)}, f32[512,256]{1,0:T(8,128)S(1)}, u32[]{:S(2)}, u32[]{:S(2)}) collective-permute-start(f32[512,256]{1,0:T(8,128)} %fusion.12), channel_id=1, source_target_pairs={{0,1},{1,0},{2,3},{3,2},{4,5},{5,4},{6,7},{7,6},{8,9},{9,8},{10,11... | collective-permute-start | bytes 1572872 | tf_op jit(solution)/shard_map/ppermute | solution.py:77
  4.0 0.0 copy-done.7
  4.0 0.1 select_reduce_fusion
  4.1 0.0 copy-done
  4.1 2.0 %gather_fusion = f32[8,128,512]{2,1,0:T(8,128)} fusion(f32[8,128,512]{2,1,0:T(8,128)S(1)} %bitcast.11, s32[1024]{0:T(1024)S(1)} %pad_clamp_fusion), kind=kCustom, calls=%fused_computation | custom fusion | bytes 4194336 | tf_op jit(solution)/shard_map/jit(_take)/gather | solution.py:109
  6.1 0.0 copy-start.4
  6.1 0.0 copy-start.3
  6.1 1.5 %slice_select_fusion = f32[512,512]{1,0:T(8,128)S(1)} fusion(f32[512,1024]{1,0:T(8,128)} %param.6, pred[]{:T(512)S(6)} %gt.4), kind=kLoop, calls=%fused_computation.10 | loop fusion | flops 262144 | bytes 2097153 | tf_op jit(solution)/shard_map/jit(_where)/select_n | solution.py:91
  7.6 0.0 collective-permute-done
  7.6 0.0 copy-done.4
  7.6 0.0 copy-start.1
  7.6 0.6 %convolution_subtract_fusion = f32[512,256]{1,0:T(8,128)S(1)} fusion(f32[512,256]{1,0:T(8,128)S(1)} %copy-done.4, f32[512,512]{1,0:T(8,128)S(1)} %slice_select_fusion, f32[512,256]{1,0:T(8,128)S(1)} %collective-permute-done), kind=kOutput, calls=%fused_computation.1 | convolution fusion | flops 402784256 | bytes 2621440 | tf_op jit(solution)/shard_map/dot_general | solution.py:26
  8.2 0.0 copy-done.3
  8.2 0.6 %fusion.10 = f32[512,256]{1,0:T(8,128)S(1)} fusion(f32[512,256]{1,0:T(8,128)S(1)} %convolution_subtract_fusion, f32[512,1024]{1,0:T(8,128)S(1)} %copy-done.3, s32[]{:T(128)S(6)} %select_n.39), kind=kOutput, calls=%fused_computation.14 | convolution fusion | flops 402653184 | bytes 2097156 | tf_op jit(solution)/shard_map/dot_general | solution.py:26
  8.8 0.5 %copy-done.1 = f32[8,128,512]{2,1,0:T(8,128)S(1)} copy-done((f32[8,128,512]{2,1,0:T(8,128)S(1)}, f32[8,128,512]{2,1,0:T(8,128)}, u32[]{:S(2)}) %copy-start.1) | copy-done | bytes 2097176
  9.4 0.0 copy-start.2
  9.4 0.6 %fusion.3 = f32[512,256]{1,0:T(8,128)S(1)} fusion(f32[512,256]{1,0:T(8,128)S(1)} %fusion.10, f32[1024,512]{1,0:T(8,128)S(1)} %bitcast.13, s32[]{:T(128)S(6)} %select_n.43), kind=kOutput, calls=%fused_computation.6 | convolution fusion | flops 402653184 | bytes 2097156 | tf_op jit(solution)/shard_map/dot_general | solution.py:26
  10.0 0.1 collective-permute-start.1
  10.1 0.0 copy-start.5
  10.1 2.0 %fusion.5 = f32[512,256]{1,0:T(8,128)S(1)} fusion(f32[512,256]{1,0:T(8,128)S(1)} %fusion.10, f32[1024,512]{1,0:T(8,128)} %bitcast.12, s32[]{:T(128)S(6)} %select_n.39), kind=kOutput, calls=%fused_computation.8 | convolution fusion | flops 402653184 | bytes 2097156 | tf_op jit(solution)/shard_map/dot_general | solution.py:26
  12.1 0.0 copy-done.2
  12.1 0.0 copy-start.6
  12.1 0.0 collective-permute-done.1
  12.1 1.0 %dynamic-slice_add_fusion.1 = f32[512,128]{1,0:T(8,128)S(1)} fusion(f32[512,256]{1,0:T(8,128)} %collective-permute-done.1, s32[]{:T(128)S(6)} %select_n.45, f32[512,256]{1,0:T(8,128)S(1)} %fusion.5), kind=kLoop, calls=%fused_computation.23 | loop fusion | flops 65536 | bytes 786436 | tf_op jit(solution)/shard_map/add | solution.py:125
  13.1 3.0 %collective-permute-start.2 = (f32[512,128]{1,0:T(8,128)S(1)}, f32[512,128]{1,0:T(8,128)S(1)}, u32[]{:S(2)}, u32[]{:S(2)}) collective-permute-start(f32[512,128]{1,0:T(8,128)S(1)} %dynamic-slice_add_fusion.1), channel_id=1, source_target_pairs={{0,2},{2,0},{4,6},{6,4},{8,10},{10,8},{12,14},{14,12},{16,18},{18,... | collective-permute-start | bytes 786440 | tf_op jit(solution)/shard_map/ppermute | solution.py:22
  16.1 0.0 copy-done.5
  16.1 1.0 %fusion = f32[512,512]{1,0:T(8,128)S(1)} fusion(f32[512,1024]{1,0:T(8,128)S(1)} %copy-done.5, s32[]{:T(128)S(6)} %select_n.39, pred[]{:T(512)S(6)} %gt.4), kind=kOutput, calls=%fused_computation.3 | convolution fusion | flops 805568512 | bytes 3145733 | tf_op jit(solution)/shard_map/dot_general | solution.py:26
  17.2 1.0 %dynamic-slice_add_fusion = f32[512,128]{1,0:T(8,128)S(1)} fusion(f32[512,256]{1,0:T(8,128)} %collective-permute-done.1, s32[]{:T(128)S(6)} %select_n.47, f32[512,256]{1,0:T(8,128)S(1)} %fusion.5), kind=kLoop, calls=%fused_computation.22 | loop fusion | flops 65536 | bytes 786436 | tf_op jit(solution)/shard_map/add | solution.py:125
  18.1 4.5 %collective-permute-done.2 = f32[512,128]{1,0:T(8,128)S(1)} collective-permute-done((f32[512,128]{1,0:T(8,128)S(1)}, f32[512,128]{1,0:T(8,128)S(1)}, u32[]{:S(2)}, u32[]{:S(2)}) %collective-permute-start.2) | collective-permute-done | bytes 262176 | tf_op jit(solution)/shard_map/ppermute | solution.py:22
  22.6 0.0 copy-done.6
  22.6 0.6 %fusion.7 = f32[512,128]{1,0:T(8,128)S(1)} fusion(f32[512,1024]{1,0:T(8,128)S(1)} %copy-done.5, s32[]{:T(128)S(6)} %select_n.39, f32[512,128]{1,0:T(8,128)S(1)} %copy-done.6, f32[512,128]{1,0:T(8,128)S(1)} %dynamic-slice_add_fusion, f32[512,128]{1,0:T(8,128)S(1)} %collective-permute-done.2), kind=kOutput, calls=%fused_computation.11 | convolution fusion | flops 201457664 | bytes 2097156 | tf_op jit(solution)/shard_map/dot_general | solution.py:26
  23.2 0.1 collective-permute-start.3
  23.3 1.5 %collective-permute-done.3 = f32[512,128]{1,0:T(8,128)S(1)} collective-permute-done((f32[512,128]{1,0:T(8,128)S(1)}, f32[512,128]{1,0:T(8,128)S(1)}, u32[]{:S(2)}, u32[]{:S(2)}) %collective-permute-start.3) | collective-permute-done | bytes 262176 | tf_op jit(solution)/shard_map/ppermute | solution.py:77
  24.8 1.3 %convolution_subtract_fusion.1 = f32[512,128]{1,0:T(8,128)} fusion(f32[512,128]{1,0:T(8,128)S(1)} %fusion.7, f32[512,512]{1,0:T(8,128)S(1)} %fusion, f32[512,128]{1,0:T(8,128)S(1)} %collective-permute-done.3), kind=kOutput, calls=%fused_computation.2 | convolution fusion | flops 201392128 | bytes 1835008 | tf_op jit(solution)/shard_map/dot_general | solution.py:26
  (1 shorter events, 0.0 us)
Async XLA Ops:
  0.6 3.5 %copy-start = (f32[1024,512]{1,0:T(8,128)S(1)}, f32[1024,512]{1,0:T(8,128)}, u32[]{:S(2)}) copy-start(f32[1024,512]{1,0:T(8,128)} %param.8) | copy-start | bytes 6291460
  0.6 3.4 %copy-start.7 = (s32[1,8]{1,0:T(1,128)S(1)}, s32[1,8]{1,0:T(1,128)}, u32[]{:S(2)}) copy-start(s32[1,8]{1,0:T(1,128)} %param.9) | copy-start | bytes 100
  3.6 4.0 %collective-permute-start = (f32[512,256]{1,0:T(8,128)}, f32[512,256]{1,0:T(8,128)S(1)}, u32[]{:S(2)}, u32[]{:S(2)}) collective-permute-start(f32[512,256]{1,0:T(8,128)} %fusion.12), channel_id=1, source_target_pairs={{0,1},{1,0},{2,3},{3,2},{4,5},{5,4},{6,7},{7,6},{8,9},{9,8},{10,11... | collective-permute-start | bytes 1572872 | tf_op jit(solution)/shard_map/ppermute | solution.py:77
  6.1 1.5 %copy-start.4 = (f32[512,256]{1,0:T(8,128)S(1)}, f32[512,256]{1,0:T(8,128)}, u32[]{:S(2)}) copy-start(f32[512,256]{1,0:T(8,128)} %param.7) | copy-start | bytes 1572868
  6.1 2.1 %copy-start.3 = (f32[512,1024]{1,0:T(8,128)S(1)}, f32[512,1024]{1,0:T(8,128)}, u32[]{:S(2)}) copy-start(f32[512,1024]{1,0:T(8,128)} %param.6) | copy-start | bytes 6291460
  7.6 1.7 %copy-start.1 = (f32[8,128,512]{2,1,0:T(8,128)S(1)}, f32[8,128,512]{2,1,0:T(8,128)}, u32[]{:S(2)}) copy-start(f32[8,128,512]{2,1,0:T(8,128)} %gather_fusion) | copy-start | bytes 6291460
  9.4 2.7 %copy-start.2 = (f32[512,256]{1,0:T(8,128)}, f32[512,256]{1,0:T(8,128)S(1)}, u32[]{:S(2)}) copy-start(f32[512,256]{1,0:T(8,128)S(1)} %fusion.10) | copy-start | bytes 1572868
  10.0 2.1 %collective-permute-start.1 = (f32[512,256]{1,0:T(8,128)S(1)}, f32[512,256]{1,0:T(8,128)}, u32[]{:S(2)}, u32[]{:S(2)}) collective-permute-start(f32[512,256]{1,0:T(8,128)S(1)} %fusion.3), channel_id=1, source_target_pairs={{0,1},{1,0},{2,3},{3,2},{4,5},{5,4},{6,7},{7,6},{8,9},{9,8},{10,11... | collective-permute-start | bytes 1572872 | tf_op jit(solution)/shard_map/ppermute | solution.py:77
  10.1 6.0 %copy-start.5 = (f32[512,1024]{1,0:T(8,128)S(1)}, f32[512,1024]{1,0:T(8,128)}, u32[]{:S(2)}) copy-start(f32[512,1024]{1,0:T(8,128)} %param.10) | copy-start | bytes 6291460
  12.1 10.6 %copy-start.6 = (f32[512,128]{1,0:T(8,128)S(1)}, f32[512,128]{1,0:T(8,128)}, u32[]{:S(2)}) copy-start(f32[512,128]{1,0:T(8,128)} %param.11) | copy-start | bytes 786436
  13.1 9.5 %collective-permute-start.2 = (f32[512,128]{1,0:T(8,128)S(1)}, f32[512,128]{1,0:T(8,128)S(1)}, u32[]{:S(2)}, u32[]{:S(2)}) collective-permute-start(f32[512,128]{1,0:T(8,128)S(1)} %dynamic-slice_add_fusion.1), channel_id=1, source_target_pairs={{0,2},{2,0},{4,6},{6,4},{8,10},{10,8},{12,14},{14,12},{16,18},{18,... | collective-permute-start | bytes 786440 | tf_op jit(solution)/shard_map/ppermute | solution.py:22
  23.2 1.6 %collective-permute-start.3 = (f32[512,128]{1,0:T(8,128)S(1)}, f32[512,128]{1,0:T(8,128)S(1)}, u32[]{:S(2)}, u32[]{:S(2)}) collective-permute-start(f32[512,128]{1,0:T(8,128)S(1)} %fusion.7), channel_id=1, source_target_pairs={{0,1},{1,0},{2,3},{3,2},{4,5},{5,4},{6,7},{7,6},{8,9},{9,8},{10,11... | collective-permute-start | bytes 786440 | tf_op jit(solution)/shard_map/ppermute | solution.py:77

commit v18 on v14

--- a/solution.py
+++ b/solution.py
@@ -112,23 +112,28 @@
     rows_half = placed_panel.shape[0] // 2
     panel_other = lax.dynamic_slice_in_dim(placed_panel, (1 - section) * rows_half, rows_half, 0)
     panel_own = lax.dynamic_slice_in_dim(placed_panel, section * rows_half, rows_half, 0)
-    other_rows = matmul(panel_other, leaf_solution, precision)
-    arrived_rows = pair_swap(other_rows, "rows")
-    own_rows = matmul(panel_own, leaf_solution, precision)
-    own_rows, arrived_rows = lax.optimization_barrier((own_rows, arrived_rows))
-    chip_sum = own_rows + arrived_rows
     column_half = parent_rhs.shape[1]
     sibling = lax.axis_index("leaf") % 2
-    kept = lax.dynamic_slice_in_dim(chip_sum, sibling * column_half, column_half, 1)
-    sent = lax.dynamic_slice_in_dim(chip_sum, (1 - sibling) * column_half, column_half, 1)
+    solution_kept = lax.dynamic_slice_in_dim(leaf_solution, sibling * column_half, column_half, 1)
+    solution_sent = lax.dynamic_slice_in_dim(leaf_solution, (1 - sibling) * column_half, column_half, 1)
+    other_sent = matmul(panel_other, solution_sent, precision)
+    arrived_sent = pair_swap(other_sent, "rows")
+    own_sent = matmul(panel_own, solution_sent, precision)
+    own_sent, arrived_sent = lax.optimization_barrier((own_sent, arrived_sent))
+    sent = own_sent + arrived_sent
+    sent, solution_kept = lax.optimization_barrier((sent, solution_kept))
+    other_kept = matmul(panel_other, solution_kept, precision)
+    arrived_kept = pair_swap(other_kept, "rows")
+    kept = matmul(panel_own, solution_kept, precision) + arrived_kept
     tile_rows = parent_rhs.shape[0]
     diagonal = lax.dynamic_slice_in_dim(parent_factor, section * tile_rows, tile_rows, 1)
     coupling = lower_coupling(parent_factor, diagonal, section, precision)
     arrived = swapped(sent, "leaf", 0)
-    arrived, coupling = lax.optimization_barrier((arrived, coupling))
+    arrived, kept = lax.optimization_barrier((arrived, kept))
     pending = parent_rhs - (kept + arrived)
     first = matmul(diagonal, pending, precision)
     arrived = pair_swap(first, "rows")
+    arrived, coupling = lax.optimization_barrier((arrived, coupling))
     parent_solution = first - matmul(coupling, arrived, precision)
     return (leaf_solution, parent_solution)
 

time: 25.3 us -> 25.2 us (level)
  other arithmetic: 1.24 us -> 0.12 us
  matrix products: 10.3 us -> 11.4 us
    dot_general x8 -> x10, matrix products: 10.3 us -> 11.4 us  [matmul(): jnp.dot(left, right, precision=precision, preferred_element_type=jnp.floa...]
    add x1, other arithmetic: 1.15 us -> 0.03 us  [two_section_shards(): sent = own_sent + arrived_sent]
    ppermute x3 -> x4, waiting for transfers between devices: 1.53 us -> 0.51 us  [pair_swap(): return lax.ppermute(block, axis, [(0, 1), (1, 0)])]
    ppermute x1, waiting for transfers between devices: 5.49 us -> 6.3 us  [swapped(): return lax.ppermute(block, axis, route)]
    ppermute x3 -> x4, starting transfers between devices: 0.71 us -> 1.22 us  [pair_swap(): return lax.ppermute(block, axis, [(0, 1), (1, 0)])]
    ppermute x1, starting transfers between devices: 3 us -> 2.57 us  [swapped(): return lax.ppermute(block, axis, route)]
  transfers between devices with their start and end apart: 4 -> 5, of which waited for: 2 -> 2; matrix products, arithmetic and copies ran while one was open for 20% -> 23% of each run, Pallas kernels for 0% -> 0%
where the time goes in v18:
time: 25.2 us; the launch traced here: 25.1 us
  matrix products  11.4 us (45%)
  waiting for transfers between devices  6.81 us (27%)
  starting transfers between devices  3.79 us (15%)
  local copies, waits for them, and re-layouts  2.09 us (8%)
  between operations  0.83 us (3%)
    dot_general x10, matrix products, matmul(): jnp.dot(left, right, precision=precision, preferred_element_type=jnp.floa...  11.4 us
    ppermute x1, waiting for transfers between devices, swapped(): return lax.ppermute(block, axis, route)  6.3 us
    ppermute x1, starting transfers between devices, swapped(): return lax.ppermute(block, axis, route)  2.57 us
    gather x1, local copies, waits for them, and re-layouts, two_section_shards(): jnp.take(blocks, order, axis=0, mode='clip').reshape(update_panel.shape)  2.01 us
    ppermute x4, starting transfers between devices, pair_swap(): return lax.ppermute(block, axis, [(0, 1), (1, 0)])  1.22 us
    ppermute x4, waiting for transfers between devices, pair_swap(): return lax.ppermute(block, axis, [(0, 1), (1, 0)])  0.51 us
  transfers between devices with their start and end apart: 5, of which 2 were waited for; matrix products, arithmetic and copies ran while one was open for 23% of the time, Pallas kernels for 0%

profile of v18, /device:TPU:0, one launch (start us, length us, event | category | flops | bytes accessed | tf_op | source)
XLA Modules:
  0.0 25.1 jit_solution(4580900493455002971)
XLA Ops:
  0.6 0.0 copy-start
  0.6 0.0 copy-start.8
  0.7 2.1 %fusion.17 = f32[512,256]{1,0:T(8,128)S(1)} fusion(f32[512,256]{1,0:T(8,128)} %param.7, f32[512,1024]{1,0:T(8,128)} %param.6, s32[]{:T(128)S(6)} %select_n.37), kind=kOutput, calls=%fused_computation.21 | convolution fusion | flops 402653184 | bytes 2097156 | tf_op jit(solution)/shard_map/dot_general | solution.py:26
  2.8 0.5 %collective-permute-start = (f32[512,256]{1,0:T(8,128)S(1)}, f32[512,256]{1,0:T(8,128)}, u32[]{:S(2)}, u32[]{:S(2)}) collective-permute-start(f32[512,256]{1,0:T(8,128)S(1)} %fusion.17), channel_id=1, source_target_pairs={{0,1},{1,0},{2,3},{3,2},{4,5},{5,4},{6,7},{7,6},{8,9},{9,8},{10,11... | collective-permute-start | bytes 1572872 | tf_op jit(solution)/shard_map/ppermute | solution.py:77
  3.3 0.0 copy-done.8
  3.3 0.1 select_reduce_fusion
  3.4 0.0 copy-done
  3.4 0.0 copy-start.6
  3.4 2.0 %gather_fusion = f32[8,128,512]{2,1,0:T(8,128)} fusion(f32[8,128,512]{2,1,0:T(8,128)S(1)} %bitcast.10, s32[1024]{0:T(1024)S(1)} %pad_clamp_fusion), kind=kCustom, calls=%fused_computation | custom fusion | bytes 4194336 | tf_op jit(solution)/shard_map/jit(_take)/gather | solution.py:109
  5.4 0.0 copy-start.3
  5.4 0.0 collective-permute-done
  5.4 0.0 copy-done.6
  5.4 0.0 copy-start.1
  5.4 2.1 %convolution_subtract_fusion = f32[512,256]{1,0:T(8,128)S(1)} fusion(f32[512,256]{1,0:T(8,128)S(1)} %copy-done.6, f32[512,256]{1,0:T(8,128)} %collective-permute-done, f32[512,1024]{1,0:T(8,128)} %param.6, pred[]{:T(512)S(6)} %gt.4), kind=kOutput, calls=%fused_computation.1 | convolution fusion | flops 403046400 | bytes 2621441 | tf_op jit(solution)/shard_map/dot_general | solution.py:26
  7.5 0.0 copy-done.3
  7.6 0.6 %fusion.15 = f32[512,256]{1,0:T(8,128)S(1)} fusion(f32[512,256]{1,0:T(8,128)S(1)} %convolution_subtract_fusion, f32[512,1024]{1,0:T(8,128)S(1)} %copy-done.3, s32[]{:T(128)S(6)} %select_n.37), kind=kOutput, calls=%fused_computation.19 | convolution fusion | flops 402653184 | bytes 2097156 | tf_op jit(solution)/shard_map/dot_general | solution.py:26
  8.2 0.0 copy-done.1
  8.2 0.0 copy-start.4
  8.2 0.6 %fusion.7 = f32[512,128]{1,0:T(8,128)S(1)} fusion(f32[1024,512]{1,0:T(8,128)S(1)} %bitcast.12, s32[]{:T(128)S(6)} %select_n.43, f32[512,256]{1,0:T(8,128)S(1)} %fusion.15, s32[]{:T(128)S(6)} %select_n.42), kind=kOutput, calls=%fused_computation.11 | convolution fusion | flops 201326592 | bytes 1572872 | tf_op jit(solution)/shard_map/dot_general | solution.py:26
  8.8 0.1 collective-permute-start.1
  8.9 0.0 copy-start.2
  8.9 2.0 %fusion.10 = f32[512,128]{1,0:T(8,128)S(1)} fusion(f32[1024,512]{1,0:T(8,128)} %bitcast.11, s32[]{:T(128)S(6)} %select_n.37, f32[512,256]{1,0:T(8,128)S(1)} %fusion.15, s32[]{:T(128)S(6)} %select_n.42), kind=kOutput, calls=%fused_computation.14 | convolution fusion | flops 201326592 | bytes 1572872 | tf_op jit(solution)/shard_map/dot_general | solution.py:26
  10.9 0.0 copy-start.5
  10.9 0.0 copy-start.7
  10.9 0.0 collective-permute-done.1
  11.0 0.0 copy-done.4
  11.0 0.0 copy-done.2
  11.0 0.6 %fusion.5 = f32[512,128]{1,0:T(8,128)S(1)} fusion(f32[512,128]{1,0:T(8,128)S(1)} %constant_dynamic-slice_fusion, f32[1024,512]{1,0:T(8,128)S(1)} %bitcast.13, s32[]{:T(128)S(6)} %select_n.43), kind=kOutput, calls=%fused_computation.9 | convolution fusion | flops 201326592 | bytes 1572868 | tf_op jit(solution)/shard_map/dot_general | solution.py:26
  11.6 0.5 %collective-permute-start.3 = (f32[512,128]{1,0:T(8,128)S(1)}, f32[512,128]{1,0:T(8,128)S(1)}, u32[]{:S(2)}, u32[]{:S(2)}) collective-permute-start(f32[512,128]{1,0:T(8,128)S(1)} %fusion.5), channel_id=1, source_target_pairs={{0,1},{1,0},{2,3},{3,2},{4,5},{5,4},{6,7},{7,6},{8,9},{9,8},{10,11... | collective-permute-start | bytes 786440 | tf_op jit(solution)/shard_map/ppermute | solution.py:77
  12.1 2.6 %collective-permute-start.2 = (f32[512,128]{1,0:T(8,128)S(1)}, f32[512,128]{1,0:T(8,128)S(1)}, u32[]{:S(2)}, u32[]{:S(2)}) collective-permute-start(f32[512,128]{1,0:T(8,128)S(1)} %add.31), channel_id=1, source_target_pairs={{0,2},{2,0},{4,6},{6,4},{8,10},{10,8},{12,14},{14,12},{16,18},{18,... | collective-permute-start | bytes 786440 | tf_op jit(solution)/shard_map/ppermute | solution.py:22
  14.7 0.0 collective-permute-done.3
  14.7 0.6 %convolution_add_fusion = f32[512,128]{1,0:T(8,128)S(1)} fusion(f32[512,128]{1,0:T(8,128)S(1)} %collective-permute-done.3, f32[512,128]{1,0:T(8,128)S(1)} %constant_dynamic-slice_fusion, f32[1024,512]{1,0:T(8,128)S(1)} %bitcast.14, s32[]{:T(128)S(6)} %select_n.37), kind=kOutput, calls=%fused_computation.3 | convolution fusion | flops 201392128 | bytes 1835012 | tf_op jit(solution)/shard_map/dot_general | solution.py:26
  15.3 6.3 %collective-permute-done.2 = f32[512,128]{1,0:T(8,128)S(1)} collective-permute-done((f32[512,128]{1,0:T(8,128)S(1)}, f32[512,128]{1,0:T(8,128)S(1)}, u32[]{:S(2)}, u32[]{:S(2)}) %collective-permute-start.2) | collective-permute-done | bytes 262176 | tf_op jit(solution)/shard_map/ppermute | solution.py:22
  21.6 0.0 copy-done.5
  21.6 0.0 copy-done.7
  21.6 0.6 %fusion.13 = f32[512,128]{1,0:T(8,128)S(1)} fusion(f32[512,1024]{1,0:T(8,128)S(1)} %copy-done.5, s32[]{:T(128)S(6)} %select_n.37, f32[512,128]{1,0:T(8,128)S(1)} %copy-done.7, f32[512,128]{1,0:T(8,128)S(1)} %convolution_add_fusion, f32[512,128]{1,0:T(8,128)S(1)} %collective-permute-done.2), kind=kOutput, calls=%fused_computation.17 | convolution fusion | flops 201457664 | bytes 2097156 | tf_op jit(solution)/shard_map/dot_general | solution.py:26
  22.2 0.1 collective-permute-start.4
  22.3 1.0 %fusion = f32[512,512]{1,0:T(8,128)S(1)} fusion(f32[512,1024]{1,0:T(8,128)S(1)} %copy-done.5, s32[]{:T(128)S(6)} %select_n.37, pred[]{:T(512)S(6)} %gt.4), kind=kOutput, calls=%fused_computation.4 | convolution fusion | flops 805568512 | bytes 3145733 | tf_op jit(solution)/shard_map/dot_general | solution.py:26
  23.3 0.5 %collective-permute-done.4 = f32[512,128]{1,0:T(8,128)S(1)} collective-permute-done((f32[512,128]{1,0:T(8,128)S(1)}, f32[512,128]{1,0:T(8,128)S(1)}, u32[]{:S(2)}, u32[]{:S(2)}) %collective-permute-start.4) | collective-permute-done | bytes 262176 | tf_op jit(solution)/shard_map/ppermute | solution.py:77
  23.8 1.3 %convolution_subtract_fusion.1 = f32[512,128]{1,0:T(8,128)} fusion(f32[512,128]{1,0:T(8,128)S(1)} %fusion.13, f32[512,512]{1,0:T(8,128)S(1)} %fusion, f32[512,128]{1,0:T(8,128)S(1)} %collective-permute-done.4), kind=kOutput, calls=%fused_computation.2 | convolution fusion | flops 201392128 | bytes 1835008 | tf_op jit(solution)/shard_map/dot_general | solution.py:26
  (3 shorter events, 0.1 us)
Async XLA Ops:
  0.6 2.8 %copy-start = (f32[1024,512]{1,0:T(8,128)S(1)}, f32[1024,512]{1,0:T(8,128)}, u32[]{:S(2)}) copy-start(f32[1024,512]{1,0:T(8,128)} %param.8) | copy-start | bytes 6291460
  0.6 2.6 %copy-start.8 = (s32[1,8]{1,0:T(1,128)S(1)}, s32[1,8]{1,0:T(1,128)}, u32[]{:S(2)}) copy-start(s32[1,8]{1,0:T(1,128)} %param.9) | copy-start | bytes 100
  2.8 2.6 %collective-permute-start = (f32[512,256]{1,0:T(8,128)S(1)}, f32[512,256]{1,0:T(8,128)}, u32[]{:S(2)}, u32[]{:S(2)}) collective-permute-start(f32[512,256]{1,0:T(8,128)S(1)} %fusion.17), channel_id=1, source_target_pairs={{0,1},{1,0},{2,3},{3,2},{4,5},{5,4},{6,7},{7,6},{8,9},{9,8},{10,11... | collective-permute-start | bytes 1572872 | tf_op jit(solution)/shard_map/ppermute | solution.py:77
  3.4 2.0 %copy-start.6 = (f32[512,256]{1,0:T(8,128)S(1)}, f32[512,256]{1,0:T(8,128)}, u32[]{:S(2)}) copy-start(f32[512,256]{1,0:T(8,128)} %param.7) | copy-start | bytes 1572868
  5.4 2.1 %copy-start.3 = (f32[512,1024]{1,0:T(8,128)S(1)}, f32[512,1024]{1,0:T(8,128)}, u32[]{:S(2)}) copy-start(f32[512,1024]{1,0:T(8,128)} %param.6) | copy-start | bytes 6291460
  5.4 2.7 %copy-start.1 = (f32[8,128,512]{2,1,0:T(8,128)S(1)}, f32[8,128,512]{2,1,0:T(8,128)}, u32[]{:S(2)}) copy-start(f32[8,128,512]{2,1,0:T(8,128)} %gather_fusion) | copy-start | bytes 6291460
  8.2 2.8 %copy-start.4 = (f32[512,256]{1,0:T(8,128)}, f32[512,256]{1,0:T(8,128)S(1)}, u32[]{:S(2)}) copy-start(f32[512,256]{1,0:T(8,128)S(1)} %fusion.15) | copy-start | bytes 1572868
  8.8 2.2 %collective-permute-start.1 = (f32[512,128]{1,0:T(8,128)S(1)}, f32[512,128]{1,0:T(8,128)S(1)}, u32[]{:S(2)}, u32[]{:S(2)}) collective-permute-start(f32[512,128]{1,0:T(8,128)S(1)} %fusion.7), channel_id=1, source_target_pairs={{0,1},{1,0},{2,3},{3,2},{4,5},{5,4},{6,7},{7,6},{8,9},{9,8},{10,11... | collective-permute-start | bytes 786440 | tf_op jit(solution)/shard_map/ppermute | solution.py:77
  8.9 2.1 %copy-start.2 = (f32[8,128,512]{2,1,0:T(8,128)S(1)}, f32[8,128,512]{2,1,0:T(8,128)}, u32[]{:S(2)}) copy-start(f32[8,128,512]{2,1,0:T(8,128)} %gather_fusion) | copy-start | bytes 6291460
  10.9 10.7 %copy-start.5 = (f32[512,1024]{1,0:T(8,128)S(1)}, f32[512,1024]{1,0:T(8,128)}, u32[]{:S(2)}) copy-start(f32[512,1024]{1,0:T(8,128)} %param.10) | copy-start | bytes 6291460
  10.9 10.7 %copy-start.7 = (f32[512,128]{1,0:T(8,128)S(1)}, f32[512,128]{1,0:T(8,128)}, u32[]{:S(2)}) copy-start(f32[512,128]{1,0:T(8,128)} %param.11) | copy-start | bytes 786436
  11.6 3.1 %collective-permute-start.3 = (f32[512,128]{1,0:T(8,128)S(1)}, f32[512,128]{1,0:T(8,128)S(1)}, u32[]{:S(2)}, u32[]{:S(2)}) collective-permute-start(f32[512,128]{1,0:T(8,128)S(1)} %fusion.5), channel_id=1, source_target_pairs={{0,1},{1,0},{2,3},{3,2},{4,5},{5,4},{6,7},{7,6},{8,9},{9,8},{10,11... | collective-permute-start | bytes 786440 | tf_op jit(solution)/shard_map/ppermute | solution.py:77
  12.1 9.5 %collective-permute-start.2 = (f32[512,128]{1,0:T(8,128)S(1)}, f32[512,128]{1,0:T(8,128)S(1)}, u32[]{:S(2)}, u32[]{:S(2)}) collective-permute-start(f32[512,128]{1,0:T(8,128)S(1)} %add.31), channel_id=1, source_target_pairs={{0,2},{2,0},{4,6},{6,4},{8,10},{10,8},{12,14},{14,12},{16,18},{18,... | collective-permute-start | bytes 786440 | tf_op jit(solution)/shard_map/ppermute | solution.py:22
  22.2 1.6 %collective-permute-start.4 = (f32[512,128]{1,0:T(8,128)S(1)}, f32[512,128]{1,0:T(8,128)S(1)}, u32[]{:S(2)}, u32[]{:S(2)}) collective-permute-start(f32[512,128]{1,0:T(8,128)S(1)} %fusion.13), channel_id=1, source_target_pairs={{0,1},{1,0},{2,3},{3,2},{4,5},{5,4},{6,7},{7,6},{8,9},{9,8},{10,11... | collective-permute-start | bytes 786440 | tf_op jit(solution)/shard_map/ppermute | solution.py:77

commit v19 on v15

--- a/solution.py
+++ b/solution.py
@@ -131,10 +131,11 @@
     diagonal = lax.dynamic_slice_in_dim(parent_factor, section * tile_rows, tile_rows, 1)
     coupling = lower_coupling(parent_factor, diagonal, section, precision)
     arrived = swapped(sent, "leaf", 0)
-    arrived, coupling, kept = lax.optimization_barrier((arrived, coupling, kept))
+    arrived, kept = lax.optimization_barrier((arrived, kept))
     pending = parent_rhs - (kept + arrived)
     first = matmul(diagonal, pending, precision)
     arrived = pair_swap(first, "rows")
+    arrived, coupling = lax.optimization_barrier((arrived, coupling))
     parent_solution = first - matmul(coupling, arrived, precision)
     return (leaf_solution, parent_solution)
 

time: 25.1 us -> 27.3 us (1.088)
  matrix products: 10.3 us -> 12.2 us
  waiting for transfers between devices: 6.02 us -> 6.52 us
  starting transfers between devices: 3.71 us -> 3.33 us
    dot_general x8, matrix products: 10.3 us -> 12.2 us  [matmul(): jnp.dot(left, right, precision=precision, preferred_element_type=jnp.floa...]
    ppermute x1, waiting for transfers between devices: 4.5 us -> 5.7 us  [swapped(): return lax.ppermute(block, axis, route)]
    ppermute x3, waiting for transfers between devices: 1.53 us -> 0.83 us  [pair_swap(): return lax.ppermute(block, axis, [(0, 1), (1, 0)])]
    ppermute x1, starting transfers between devices: 2.99 us -> 2.69 us  [swapped(): return lax.ppermute(block, axis, route)]
  transfers between devices with their start and end apart: 4 -> 4, of which waited for: 2 -> 3; matrix products, arithmetic and copies ran while one was open for 24% -> 23% of each run, Pallas kernels for 0% -> 0%
where the time goes in v19:
time: 27.3 us; the launch traced here: 27.1 us
  matrix products  12.2 us (45%)
  waiting for transfers between devices  6.52 us (24%)
  starting transfers between devices  3.33 us (12%)
  other arithmetic  2.21 us (8%)
  local copies, waits for them, and re-layouts  2.06 us (8%)
  between operations  0.78 us (3%)
    dot_general x8, matrix products, matmul(): jnp.dot(left, right, precision=precision, preferred_element_type=jnp.floa...  12.2 us
    ppermute x1, waiting for transfers between devices, swapped(): return lax.ppermute(block, axis, route)  5.7 us
    ppermute x1, starting transfers between devices, swapped(): return lax.ppermute(block, axis, route)  2.69 us
    add x2, other arithmetic, column_sum(): return own_part + arrived_part  2.12 us
    gather x1, local copies, waits for them, and re-layouts, two_section_shards(): jnp.take(blocks, order, axis=0, mode='clip').reshape(update_panel.shape)  2.02 us
    ppermute x3, waiting for transfers between devices, pair_swap(): return lax.ppermute(block, axis, [(0, 1), (1, 0)])  0.83 us
    ppermute x3, starting transfers between devices, pair_swap(): return lax.ppermute(block, axis, [(0, 1), (1, 0)])  0.64 us
  transfers between devices with their start and end apart: 4, of which 3 were waited for; matrix products, arithmetic and copies ran while one was open for 23% of the time, Pallas kernels for 0%

profile of v19, /device:TPU:0, one launch (start us, length us, event | category | flops | bytes accessed | tf_op | source)
XLA Modules:
  0.0 27.1 jit_solution(8437106659487340909)
XLA Ops:
  0.6 0.0 copy-start
  0.6 0.0 copy-start.7
  0.7 2.1 %fusion.14 = f32[512,256]{1,0:T(8,128)S(1)} fusion(f32[512,256]{1,0:T(8,128)} %param.7, f32[512,1024]{1,0:T(8,128)} %param.6, s32[]{:T(128)S(6)} %select_n.39), kind=kOutput, calls=%fused_computation.17 | convolution fusion | flops 402653184 | bytes 2097156 | tf_op jit(solution)/shard_map/dot_general | solution.py:26
  2.8 0.5 %collective-permute-start = (f32[512,256]{1,0:T(8,128)S(1)}, f32[512,256]{1,0:T(8,128)}, u32[]{:S(2)}, u32[]{:S(2)}) collective-permute-start(f32[512,256]{1,0:T(8,128)S(1)} %fusion.14), channel_id=1, source_target_pairs={{0,1},{1,0},{2,3},{3,2},{4,5},{5,4},{6,7},{7,6},{8,9},{9,8},{10,11... | collective-permute-start | bytes 1572872 | tf_op jit(solution)/shard_map/ppermute | solution.py:77
  3.3 0.0 copy-done.7
  3.3 0.1 select_reduce_fusion
  3.4 0.0 copy-done
  3.4 0.0 copy-start.5
  3.4 2.0 %gather_fusion = f32[8,128,512]{2,1,0:T(8,128)} fusion(f32[8,128,512]{2,1,0:T(8,128)S(1)} %bitcast.10, s32[1024]{0:T(1024)S(1)} %pad_clamp_fusion), kind=kCustom, calls=%fused_computation | custom fusion | bytes 4194336 | tf_op jit(solution)/shard_map/jit(_take)/gather | solution.py:109
  5.4 0.0 copy-start.3
  5.4 0.0 collective-permute-done
  5.4 0.0 copy-done.5
  5.4 0.0 copy-start.1
  5.4 2.1 %convolution_subtract_fusion = f32[512,256]{1,0:T(8,128)S(1)} fusion(f32[512,256]{1,0:T(8,128)S(1)} %copy-done.5, f32[512,256]{1,0:T(8,128)} %collective-permute-done, f32[512,1024]{1,0:T(8,128)} %param.6, pred[]{:T(512)S(6)} %gt.4), kind=kOutput, calls=%fused_computation.1 | convolution fusion | flops 403046400 | bytes 2621441 | tf_op jit(solution)/shard_map/dot_general | solution.py:26
  7.6 0.0 copy-done.3
  7.6 0.6 %fusion.12 = f32[512,256]{1,0:T(8,128)S(1)} fusion(f32[512,256]{1,0:T(8,128)S(1)} %convolution_subtract_fusion, f32[512,1024]{1,0:T(8,128)S(1)} %copy-done.3, s32[]{:T(128)S(6)} %select_n.39), kind=kOutput, calls=%fused_computation.15 | convolution fusion | flops 402653184 | bytes 2097156 | tf_op jit(solution)/shard_map/dot_general | solution.py:26
  8.2 0.0 copy-done.1
  8.2 0.0 copy-start.2
  8.2 1.4 %fusion.3 = f32[512,256]{1,0:T(8,128)} fusion(f32[512,256]{1,0:T(8,128)S(1)} %fusion.12, f32[1024,512]{1,0:T(8,128)S(1)} %bitcast.12, s32[]{:T(128)S(6)} %select_n.43), kind=kOutput, calls=%fused_computation.6 | convolution fusion | flops 402653184 | bytes 2097156 | tf_op jit(solution)/shard_map/dot_general | solution.py:26
  9.6 0.0 copy-start.6
  9.6 0.1 collective-permute-start.1
  9.7 1.8 %fusion.5 = f32[512,256]{1,0:T(8,128)S(1)} fusion(f32[512,256]{1,0:T(8,128)S(1)} %fusion.12, f32[1024,512]{1,0:T(8,128)} %bitcast.11, s32[]{:T(128)S(6)} %select_n.39), kind=kOutput, calls=%fused_computation.8 | convolution fusion | flops 402653184 | bytes 2097156 | tf_op jit(solution)/shard_map/dot_general | solution.py:26
  11.5 0.0 copy-done.2
  11.5 0.3 %collective-permute-done.1 = f32[512,256]{1,0:T(8,128)} collective-permute-done((f32[512,256]{1,0:T(8,128)}, f32[512,256]{1,0:T(8,128)}, u32[]{:S(2)}, u32[]{:S(2)}) %collective-permute-start.1) | collective-permute-done | bytes 524320 | tf_op jit(solution)/shard_map/ppermute | solution.py:77
  11.9 1.0 %dynamic-slice_add_fusion.1 = f32[512,128]{1,0:T(8,128)S(1)} fusion(f32[512,256]{1,0:T(8,128)} %collective-permute-done.1, s32[]{:T(128)S(6)} %select_n.45, f32[512,256]{1,0:T(8,128)S(1)} %fusion.5), kind=kLoop, calls=%fused_computation.26 | loop fusion | flops 65536 | bytes 786436 | tf_op jit(solution)/shard_map/add | solution.py:125
  12.8 2.7 %collective-permute-start.2 = (f32[512,128]{1,0:T(8,128)S(1)}, f32[512,128]{1,0:T(8,128)S(1)}, u32[]{:S(2)}, u32[]{:S(2)}) collective-permute-start(f32[512,128]{1,0:T(8,128)S(1)} %dynamic-slice_add_fusion.1), channel_id=1, source_target_pairs={{0,2},{2,0},{4,6},{6,4},{8,10},{10,8},{12,14},{14,12},{16,18},{18,... | collective-permute-start | bytes 786440 | tf_op jit(solution)/shard_map/ppermute | solution.py:22
  15.5 0.0 copy-start.4
  15.5 1.1 %dynamic-slice_add_fusion = f32[512,128]{1,0:T(8,128)S(1)} fusion(f32[512,256]{1,0:T(8,128)} %collective-permute-done.1, s32[]{:T(128)S(6)} %select_n.46, f32[512,256]{1,0:T(8,128)S(1)} %fusion.5), kind=kLoop, calls=%fused_computation.25 | loop fusion | flops 65536 | bytes 786436 | tf_op jit(solution)/shard_map/add | solution.py:125
  16.7 5.7 %collective-permute-done.2 = f32[512,128]{1,0:T(8,128)S(1)} collective-permute-done((f32[512,128]{1,0:T(8,128)S(1)}, f32[512,128]{1,0:T(8,128)S(1)}, u32[]{:S(2)}, u32[]{:S(2)}) %collective-permute-start.2) | collective-permute-done | bytes 262176 | tf_op jit(solution)/shard_map/ppermute | solution.py:22
  22.4 0.0 copy-done.6
  22.4 1.8 %fusion.10 = f32[512,128]{1,0:T(8,128)S(1)} fusion(f32[512,1024]{1,0:T(8,128)} %param.10, s32[]{:T(128)S(6)} %select_n.39, f32[512,128]{1,0:T(8,128)S(1)} %copy-done.6, f32[512,128]{1,0:T(8,128)S(1)} %dynamic-slice_add_fusion, f32[512,128]{1,0:T(8,128)S(1)} %collective-permute-done.2), kind=kOutput, calls=%fused_computation.13 | convolution fusion | flops 201457664 | bytes 2097156 | tf_op jit(solution)/shard_map/dot_general | solution.py:26
  24.2 0.1 collective-permute-start.3
  24.3 0.0 copy-done.4
  24.3 1.0 %fusion = f32[512,512]{1,0:T(8,128)S(1)} fusion(f32[512,1024]{1,0:T(8,128)S(1)} %copy-done.4, s32[]{:T(128)S(6)} %select_n.39, pred[]{:T(512)S(6)} %gt.4), kind=kOutput, calls=%fused_computation.3 | convolution fusion | flops 805568512 | bytes 3145733 | tf_op jit(solution)/shard_map/dot_general | solution.py:26
  25.3 0.5 %collective-permute-done.3 = f32[512,128]{1,0:T(8,128)S(1)} collective-permute-done((f32[512,128]{1,0:T(8,128)S(1)}, f32[512,128]{1,0:T(8,128)S(1)}, u32[]{:S(2)}, u32[]{:S(2)}) %collective-permute-start.3) | collective-permute-done | bytes 262176 | tf_op jit(solution)/shard_map/ppermute | solution.py:77
  25.8 1.3 %convolution_subtract_fusion.1 = f32[512,128]{1,0:T(8,128)} fusion(f32[512,128]{1,0:T(8,128)S(1)} %fusion.10, f32[512,512]{1,0:T(8,128)S(1)} %fusion, f32[512,128]{1,0:T(8,128)S(1)} %collective-permute-done.3), kind=kOutput, calls=%fused_computation.2 | convolution fusion | flops 201392128 | bytes 1835008 | tf_op jit(solution)/shard_map/dot_general | solution.py:26
  (1 shorter events, 0.0 us)
Async XLA Ops:
  0.6 2.8 %copy-start = (f32[1024,512]{1,0:T(8,128)S(1)}, f32[1024,512]{1,0:T(8,128)}, u32[]{:S(2)}) copy-start(f32[1024,512]{1,0:T(8,128)} %param.8) | copy-start | bytes 6291460
  0.6 2.6 %copy-start.7 = (s32[1,8]{1,0:T(1,128)S(1)}, s32[1,8]{1,0:T(1,128)}, u32[]{:S(2)}) copy-start(s32[1,8]{1,0:T(1,128)} %param.9) | copy-start | bytes 100
  2.8 2.7 %collective-permute-start = (f32[512,256]{1,0:T(8,128)S(1)}, f32[512,256]{1,0:T(8,128)}, u32[]{:S(2)}, u32[]{:S(2)}) collective-permute-start(f32[512,256]{1,0:T(8,128)S(1)} %fusion.14), channel_id=1, source_target_pairs={{0,1},{1,0},{2,3},{3,2},{4,5},{5,4},{6,7},{7,6},{8,9},{9,8},{10,11... | collective-permute-start | bytes 1572872 | tf_op jit(solution)/shard_map/ppermute | solution.py:77
  3.4 2.0 %copy-start.5 = (f32[512,256]{1,0:T(8,128)S(1)}, f32[512,256]{1,0:T(8,128)}, u32[]{:S(2)}) copy-start(f32[512,256]{1,0:T(8,128)} %param.7) | copy-start | bytes 1572868
  5.4 2.1 %copy-start.3 = (f32[512,1024]{1,0:T(8,128)S(1)}, f32[512,1024]{1,0:T(8,128)}, u32[]{:S(2)}) copy-start(f32[512,1024]{1,0:T(8,128)} %param.6) | copy-start | bytes 6291460
  5.4 2.7 %copy-start.1 = (f32[8,128,512]{2,1,0:T(8,128)S(1)}, f32[8,128,512]{2,1,0:T(8,128)}, u32[]{:S(2)}) copy-start(f32[8,128,512]{2,1,0:T(8,128)} %gather_fusion) | copy-start | bytes 6291460
  8.2 3.3 %copy-start.2 = (f32[512,256]{1,0:T(8,128)}, f32[512,256]{1,0:T(8,128)S(1)}, u32[]{:S(2)}) copy-start(f32[512,256]{1,0:T(8,128)S(1)} %fusion.12) | copy-start | bytes 1572868
  9.6 12.8 %copy-start.6 = (f32[512,128]{1,0:T(8,128)S(1)}, f32[512,128]{1,0:T(8,128)}, u32[]{:S(2)}) copy-start(f32[512,128]{1,0:T(8,128)} %param.11) | copy-start | bytes 786436
  9.6 2.3 %collective-permute-start.1 = (f32[512,256]{1,0:T(8,128)}, f32[512,256]{1,0:T(8,128)}, u32[]{:S(2)}, u32[]{:S(2)}) collective-permute-start(f32[512,256]{1,0:T(8,128)} %fusion.3), channel_id=1, source_target_pairs={{0,1},{1,0},{2,3},{3,2},{4,5},{5,4},{6,7},{7,6},{8,9},{9,8},{10,11... | collective-permute-start | bytes 1572872 | tf_op jit(solution)/shard_map/ppermute | solution.py:77
  12.8 9.5 %collective-permute-start.2 = (f32[512,128]{1,0:T(8,128)S(1)}, f32[512,128]{1,0:T(8,128)S(1)}, u32[]{:S(2)}, u32[]{:S(2)}) collective-permute-start(f32[512,128]{1,0:T(8,128)S(1)} %dynamic-slice_add_fusion.1), channel_id=1, source_target_pairs={{0,2},{2,0},{4,6},{6,4},{8,10},{10,8},{12,14},{14,12},{16,18},{18,... | collective-permute-start | bytes 786440 | tf_op jit(solution)/shard_map/ppermute | solution.py:22
  15.5 8.7 %copy-start.4 = (f32[512,1024]{1,0:T(8,128)S(1)}, f32[512,1024]{1,0:T(8,128)}, u32[]{:S(2)}) copy-start(f32[512,1024]{1,0:T(8,128)} %param.10) | copy-start | bytes 6291460
  24.2 1.6 %collective-permute-start.3 = (f32[512,128]{1,0:T(8,128)S(1)}, f32[512,128]{1,0:T(8,128)S(1)}, u32[]{:S(2)}, u32[]{:S(2)}) collective-permute-start(f32[512,128]{1,0:T(8,128)S(1)} %fusion.10), channel_id=1, source_target_pairs={{0,1},{1,0},{2,3},{3,2},{4,5},{5,4},{6,7},{7,6},{8,9},{9,8},{10,11... | collective-permute-start | bytes 786440 | tf_op jit(solution)/shard_map/ppermute | solution.py:77

commit v20 on v18

--- a/solution.py
+++ b/solution.py
@@ -118,12 +118,13 @@
     solution_sent = lax.dynamic_slice_in_dim(leaf_solution, (1 - sibling) * column_half, column_half, 1)
     other_sent = matmul(panel_other, solution_sent, precision)
     arrived_sent = pair_swap(other_sent, "rows")
+    other_kept = matmul(panel_other, solution_kept, precision)
+    solution_sent, other_kept = lax.optimization_barrier((solution_sent, other_kept))
+    arrived_kept = pair_swap(other_kept, "rows")
     own_sent = matmul(panel_own, solution_sent, precision)
     own_sent, arrived_sent = lax.optimization_barrier((own_sent, arrived_sent))
     sent = own_sent + arrived_sent
     sent, solution_kept = lax.optimization_barrier((sent, solution_kept))
-    other_kept = matmul(panel_other, solution_kept, precision)
-    arrived_kept = pair_swap(other_kept, "rows")
     kept = matmul(panel_own, solution_kept, precision) + arrived_kept
     tile_rows = parent_rhs.shape[0]
     diagonal = lax.dynamic_slice_in_dim(parent_factor, section * tile_rows, tile_rows, 1)

time: 25.2 us -> 24.8 us (0.984)
  matrix products: 11.4 us -> 10 us
  local copies, waits for them, and re-layouts: 2.09 us -> 3.02 us
    dot_general x10, matrix products: 11.4 us -> 10 us  [matmul(): jnp.dot(left, right, precision=precision, preferred_element_type=jnp.floa...]
    unnamed x18 -> x16, local copies, waits for them, and re-layouts: 0.05 us -> 0.96 us
  transfers between devices with their start and end apart: 5 -> 5, of which waited for: 2 -> 2; matrix products, arithmetic and copies ran while one was open for 23% -> 20% of each run, Pallas kernels for 0% -> 0%
where the time goes in v20:
time: 24.8 us; the launch traced here: 24.7 us
  matrix products  10 us (40%)
  waiting for transfers between devices  6.84 us (28%)
  starting transfers between devices  3.84 us (15%)
  local copies, waits for them, and re-layouts  3.02 us (12%)
  between operations  0.82 us (3%)
    dot_general x10, matrix products, matmul(): jnp.dot(left, right, precision=precision, preferred_element_type=jnp.floa...  10 us
    ppermute x1, waiting for transfers between devices, swapped(): return lax.ppermute(block, axis, route)  6.34 us
    ppermute x1, starting transfers between devices, swapped(): return lax.ppermute(block, axis, route)  2.61 us
    gather x1, local copies, waits for them, and re-layouts, two_section_shards(): jnp.take(blocks, order, axis=0, mode='clip').reshape(update_panel.shape)  2.01 us
    ppermute x4, starting transfers between devices, pair_swap(): return lax.ppermute(block, axis, [(0, 1), (1, 0)])  1.23 us
    unnamed x16, local copies, waits for them, and re-layouts  0.96 us
    ppermute x4, waiting for transfers between devices, pair_swap(): return lax.ppermute(block, axis, [(0, 1), (1, 0)])  0.5 us
  transfers between devices with their start and end apart: 5, of which 2 were waited for; matrix products, arithmetic and copies ran while one was open for 20% of the time, Pallas kernels for 0%

profile of v20, /device:TPU:0, one launch (start us, length us, event | category | flops | bytes accessed | tf_op | source)
XLA Modules:
  0.0 24.7 jit_solution(6964702305361953442)
XLA Ops:
  0.6 0.0 copy-start
  0.6 0.0 copy-start.7
  0.7 2.1 %fusion.17 = f32[512,256]{1,0:T(8,128)S(1)} fusion(f32[512,256]{1,0:T(8,128)} %param.7, f32[512,1024]{1,0:T(8,128)} %param.6, s32[]{:T(128)S(6)} %select_n.37), kind=kOutput, calls=%fused_computation.21 | convolution fusion | flops 402653184 | bytes 2097156 | tf_op jit(solution)/shard_map/dot_general | solution.py:26
  2.8 0.5 %collective-permute-start = (f32[512,256]{1,0:T(8,128)S(1)}, f32[512,256]{1,0:T(8,128)}, u32[]{:S(2)}, u32[]{:S(2)}) collective-permute-start(f32[512,256]{1,0:T(8,128)S(1)} %fusion.17), channel_id=1, source_target_pairs={{0,1},{1,0},{2,3},{3,2},{4,5},{5,4},{6,7},{7,6},{8,9},{9,8},{10,11... | collective-permute-start | bytes 1572872 | tf_op jit(solution)/shard_map/ppermute | solution.py:77
  3.3 0.0 copy-done.7
  3.3 0.1 select_reduce_fusion
  3.4 0.0 copy-done
  3.4 0.0 copy-start.5
  3.4 2.0 %gather_fusion = f32[8,128,512]{2,1,0:T(8,128)} fusion(f32[8,128,512]{2,1,0:T(8,128)S(1)} %bitcast.12, s32[1024]{0:T(1024)S(1)} %pad_clamp_fusion), kind=kCustom, calls=%fused_computation | custom fusion | bytes 4194336 | tf_op jit(solution)/shard_map/jit(_take)/gather | solution.py:109
  5.4 0.0 copy-start.2
  5.4 0.0 collective-permute-done
  5.4 0.0 copy-done.5
  5.4 2.1 %convolution_subtract_fusion = f32[512,256]{1,0:T(8,128)S(1)} fusion(f32[512,256]{1,0:T(8,128)S(1)} %copy-done.5, f32[512,256]{1,0:T(8,128)} %collective-permute-done, f32[512,1024]{1,0:T(8,128)} %param.6, pred[]{:T(512)S(6)} %gt.4), kind=kOutput, calls=%fused_computation.1 | convolution fusion | flops 403046400 | bytes 2621441 | tf_op jit(solution)/shard_map/dot_general | solution.py:26
  7.5 0.0 copy-done.2
  7.5 0.0 copy-start.1
  7.5 0.6 %fusion.15 = f32[512,256]{1,0:T(8,128)S(1)} fusion(f32[512,256]{1,0:T(8,128)S(1)} %convolution_subtract_fusion, f32[512,1024]{1,0:T(8,128)S(1)} %copy-done.2, s32[]{:T(128)S(6)} %select_n.37), kind=kOutput, calls=%fused_computation.19 | convolution fusion | flops 402653184 | bytes 2097156 | tf_op jit(solution)/shard_map/dot_general | solution.py:26
  8.1 0.0 copy-start.3
  8.2 0.9 %copy-done.1 = f32[8,128,512]{2,1,0:T(8,128)S(1)} copy-done((f32[8,128,512]{2,1,0:T(8,128)S(1)}, f32[8,128,512]{2,1,0:T(8,128)}, u32[]{:S(2)}) %copy-start.1) | copy-done | bytes 2097176
  9.1 0.6 %fusion.5 = f32[512,128]{1,0:T(8,128)S(1)} fusion(f32[512,128]{1,0:T(8,128)S(1)} %get-tuple-element.16, f32[1024,512]{1,0:T(8,128)S(1)} %bitcast.13, s32[]{:T(128)S(6)} %select_n.43), kind=kOutput, calls=%fused_computation.9 | convolution fusion | flops 201326592 | bytes 1572868 | tf_op jit(solution)/shard_map/dot_general | solution.py:26
  9.7 0.1 collective-permute-start.1
  9.8 0.6 %fusion.7 = f32[512,128]{1,0:T(8,128)S(1)} fusion(f32[512,128]{1,0:T(8,128)S(1)} %get-tuple-element.20, f32[1024,512]{1,0:T(8,128)S(1)} %bitcast.14, s32[]{:T(128)S(6)} %select_n.43), kind=kOutput, calls=%fused_computation.11 | convolution fusion | flops 201326592 | bytes 1572868 | tf_op jit(solution)/shard_map/dot_general | solution.py:26
  10.4 0.0 copy-done.3
  10.4 0.0 copy-start.4
  10.5 0.0 copy-start.6
  10.5 0.5 %collective-permute-start.3 = (f32[512,128]{1,0:T(8,128)S(1)}, f32[512,128]{1,0:T(8,128)S(1)}, u32[]{:S(2)}, u32[]{:S(2)}) collective-permute-start(f32[512,128]{1,0:T(8,128)S(1)} %fusion.7), channel_id=1, source_target_pairs={{0,1},{1,0},{2,3},{3,2},{4,5},{5,4},{6,7},{7,6},{8,9},{9,8},{10,11... | collective-permute-start | bytes 786440 | tf_op jit(solution)/shard_map/ppermute | solution.py:77
  11.0 0.6 %fusion.10 = f32[512,128]{1,0:T(8,128)S(1)} fusion(f32[512,128]{1,0:T(8,128)S(1)} %get-tuple-element.16, f32[1024,512]{1,0:T(8,128)S(1)} %bitcast.15, s32[]{:T(128)S(6)} %select_n.37), kind=kOutput, calls=%fused_computation.14 | convolution fusion | flops 201326592 | bytes 1572868 | tf_op jit(solution)/shard_map/dot_general | solution.py:26
  11.6 0.0 collective-permute-done.1
  11.6 2.6 %collective-permute-start.2 = (f32[512,128]{1,0:T(8,128)S(1)}, f32[512,128]{1,0:T(8,128)S(1)}, u32[]{:S(2)}, u32[]{:S(2)}) collective-permute-start(f32[512,128]{1,0:T(8,128)S(1)} %add.32), channel_id=1, source_target_pairs={{0,2},{2,0},{4,6},{6,4},{8,10},{10,8},{12,14},{14,12},{16,18},{18,... | collective-permute-start | bytes 786440 | tf_op jit(solution)/shard_map/ppermute | solution.py:22
  14.2 0.0 collective-permute-done.3
  14.2 0.6 %convolution_add_fusion = f32[512,128]{1,0:T(8,128)S(1)} fusion(f32[512,128]{1,0:T(8,128)S(1)} %collective-permute-done.3, f32[512,128]{1,0:T(8,128)S(1)} %get-tuple-element.20, f32[1024,512]{1,0:T(8,128)S(1)} %bitcast.16, s32[]{:T(128)S(6)} %select_n.37), kind=kOutput, calls=%fused_computation.3 | convolution fusion | flops 201392128 | bytes 1835012 | tf_op jit(solution)/shard_map/dot_general | solution.py:26
  14.8 6.3 %collective-permute-done.2 = f32[512,128]{1,0:T(8,128)S(1)} collective-permute-done((f32[512,128]{1,0:T(8,128)S(1)}, f32[512,128]{1,0:T(8,128)S(1)}, u32[]{:S(2)}, u32[]{:S(2)}) %collective-permute-start.2) | collective-permute-done | bytes 262176 | tf_op jit(solution)/shard_map/ppermute | solution.py:22
  21.2 0.0 copy-done.4
  21.2 0.0 copy-done.6
  21.2 0.6 %fusion.13 = f32[512,128]{1,0:T(8,128)S(1)} fusion(f32[512,1024]{1,0:T(8,128)S(1)} %copy-done.4, s32[]{:T(128)S(6)} %select_n.37, f32[512,128]{1,0:T(8,128)S(1)} %copy-done.6, f32[512,128]{1,0:T(8,128)S(1)} %convolution_add_fusion, f32[512,128]{1,0:T(8,128)S(1)} %collective-permute-done.2), kind=kOutput, calls=%fused_computation.17 | convolution fusion | flops 201457664 | bytes 2097156 | tf_op jit(solution)/shard_map/dot_general | solution.py:26
  21.8 0.1 collective-permute-start.4
  21.8 1.0 %fusion = f32[512,512]{1,0:T(8,128)S(1)} fusion(f32[512,1024]{1,0:T(8,128)S(1)} %copy-done.4, s32[]{:T(128)S(6)} %select_n.37, pred[]{:T(512)S(6)} %gt.4), kind=kOutput, calls=%fused_computation.4 | convolution fusion | flops 805568512 | bytes 3145733 | tf_op jit(solution)/shard_map/dot_general | solution.py:26
  22.9 0.5 %collective-permute-done.4 = f32[512,128]{1,0:T(8,128)S(1)} collective-permute-done((f32[512,128]{1,0:T(8,128)S(1)}, f32[512,128]{1,0:T(8,128)S(1)}, u32[]{:S(2)}, u32[]{:S(2)}) %collective-permute-start.4) | collective-permute-done | bytes 262176 | tf_op jit(solution)/shard_map/ppermute | solution.py:77
  23.4 1.3 %convolution_subtract_fusion.1 = f32[512,128]{1,0:T(8,128)} fusion(f32[512,128]{1,0:T(8,128)S(1)} %fusion.13, f32[512,512]{1,0:T(8,128)S(1)} %fusion, f32[512,128]{1,0:T(8,128)S(1)} %collective-permute-done.4), kind=kOutput, calls=%fused_computation.2 | convolution fusion | flops 201392128 | bytes 1835008 | tf_op jit(solution)/shard_map/dot_general | solution.py:26
  (3 shorter events, 0.1 us)
Async XLA Ops:
  0.6 2.8 %copy-start = (f32[1024,512]{1,0:T(8,128)S(1)}, f32[1024,512]{1,0:T(8,128)}, u32[]{:S(2)}) copy-start(f32[1024,512]{1,0:T(8,128)} %param.8) | copy-start | bytes 6291460
  0.6 2.6 %copy-start.7 = (s32[1,8]{1,0:T(1,128)S(1)}, s32[1,8]{1,0:T(1,128)}, u32[]{:S(2)}) copy-start(s32[1,8]{1,0:T(1,128)} %param.9) | copy-start | bytes 100
  2.8 2.6 %collective-permute-start = (f32[512,256]{1,0:T(8,128)S(1)}, f32[512,256]{1,0:T(8,128)}, u32[]{:S(2)}, u32[]{:S(2)}) collective-permute-start(f32[512,256]{1,0:T(8,128)S(1)} %fusion.17), channel_id=1, source_target_pairs={{0,1},{1,0},{2,3},{3,2},{4,5},{5,4},{6,7},{7,6},{8,9},{9,8},{10,11... | collective-permute-start | bytes 1572872 | tf_op jit(solution)/shard_map/ppermute | solution.py:77
  3.4 2.0 %copy-start.5 = (f32[512,256]{1,0:T(8,128)S(1)}, f32[512,256]{1,0:T(8,128)}, u32[]{:S(2)}) copy-start(f32[512,256]{1,0:T(8,128)} %param.7) | copy-start | bytes 1572868
  5.4 2.1 %copy-start.2 = (f32[512,1024]{1,0:T(8,128)S(1)}, f32[512,1024]{1,0:T(8,128)}, u32[]{:S(2)}) copy-start(f32[512,1024]{1,0:T(8,128)} %param.6) | copy-start | bytes 6291460
  7.5 1.6 %copy-start.1 = (f32[8,128,512]{2,1,0:T(8,128)S(1)}, f32[8,128,512]{2,1,0:T(8,128)}, u32[]{:S(2)}) copy-start(f32[8,128,512]{2,1,0:T(8,128)} %gather_fusion) | copy-start | bytes 6291460
  8.1 2.3 %copy-start.3 = (f32[512,256]{1,0:T(8,128)}, f32[512,256]{1,0:T(8,128)S(1)}, u32[]{:S(2)}) copy-start(f32[512,256]{1,0:T(8,128)S(1)} %fusion.15) | copy-start | bytes 1572868
  9.7 1.9 %collective-permute-start.1 = (f32[512,128]{1,0:T(8,128)S(1)}, f32[512,128]{1,0:T(8,128)S(1)}, u32[]{:S(2)}, u32[]{:S(2)}) collective-permute-start(f32[512,128]{1,0:T(8,128)S(1)} %fusion.5), channel_id=1, source_target_pairs={{0,1},{1,0},{2,3},{3,2},{4,5},{5,4},{6,7},{7,6},{8,9},{9,8},{10,11... | collective-permute-start | bytes 786440 | tf_op jit(solution)/shard_map/ppermute | solution.py:77
  10.4 10.7 %copy-start.4 = (f32[512,1024]{1,0:T(8,128)S(1)}, f32[512,1024]{1,0:T(8,128)}, u32[]{:S(2)}) copy-start(f32[512,1024]{1,0:T(8,128)} %param.10) | copy-start | bytes 6291460
  10.5 10.7 %copy-start.6 = (f32[512,128]{1,0:T(8,128)S(1)}, f32[512,128]{1,0:T(8,128)}, u32[]{:S(2)}) copy-start(f32[512,128]{1,0:T(8,128)} %param.11) | copy-start | bytes 786436
  10.5 3.8 %collective-permute-start.3 = (f32[512,128]{1,0:T(8,128)S(1)}, f32[512,128]{1,0:T(8,128)S(1)}, u32[]{:S(2)}, u32[]{:S(2)}) collective-permute-start(f32[512,128]{1,0:T(8,128)S(1)} %fusion.7), channel_id=1, source_target_pairs={{0,1},{1,0},{2,3},{3,2},{4,5},{5,4},{6,7},{7,6},{8,9},{9,8},{10,11... | collective-permute-start | bytes 786440 | tf_op jit(solution)/shard_map/ppermute | solution.py:77
  11.6 9.5 %collective-permute-start.2 = (f32[512,128]{1,0:T(8,128)S(1)}, f32[512,128]{1,0:T(8,128)S(1)}, u32[]{:S(2)}, u32[]{:S(2)}) collective-permute-start(f32[512,128]{1,0:T(8,128)S(1)} %add.32), channel_id=1, source_target_pairs={{0,2},{2,0},{4,6},{6,4},{8,10},{10,8},{12,14},{14,12},{16,18},{18,... | collective-permute-start | bytes 786440 | tf_op jit(solution)/shard_map/ppermute | solution.py:22
  21.8 1.6 %collective-permute-start.4 = (f32[512,128]{1,0:T(8,128)S(1)}, f32[512,128]{1,0:T(8,128)S(1)}, u32[]{:S(2)}, u32[]{:S(2)}) collective-permute-start(f32[512,128]{1,0:T(8,128)S(1)} %fusion.13), channel_id=1, source_target_pairs={{0,1},{1,0},{2,3},{3,2},{4,5},{5,4},{6,7},{7,6},{8,9},{9,8},{10,11... | collective-permute-start | bytes 786440 | tf_op jit(solution)/shard_map/ppermute | solution.py:77

commit v21 on v20

--- a/solution.py
+++ b/solution.py
@@ -124,7 +124,7 @@
     own_sent = matmul(panel_own, solution_sent, precision)
     own_sent, arrived_sent = lax.optimization_barrier((own_sent, arrived_sent))
     sent = own_sent + arrived_sent
-    sent, solution_kept = lax.optimization_barrier((sent, solution_kept))
+    sent, solution_kept, arrived_kept = lax.optimization_barrier((sent, solution_kept, arrived_kept))
     kept = matmul(panel_own, solution_kept, precision) + arrived_kept
     tile_rows = parent_rhs.shape[0]
     diagonal = lax.dynamic_slice_in_dim(parent_factor, section * tile_rows, tile_rows, 1)

time: 24.8 us -> 25.3 us (1.020)
    ppermute x4, waiting for transfers between devices: 0.5 us -> 1.03 us  [pair_swap(): return lax.ppermute(block, axis, [(0, 1), (1, 0)])]
    ppermute x1, waiting for transfers between devices: 6.34 us -> 6.01 us  [swapped(): return lax.ppermute(block, axis, route)]
    ppermute x1, starting transfers between devices: 2.61 us -> 2.86 us  [swapped(): return lax.ppermute(block, axis, route)]
  transfers between devices with their start and end apart: 5 -> 5, of which waited for: 2 -> 3; matrix products, arithmetic and copies ran while one was open for 20% -> 20% of each run, Pallas kernels for 0% -> 0%
where the time goes in v21:
time: 25.3 us; the launch traced here: 25.1 us
  matrix products  10 us (40%)
  waiting for transfers between devices  7.04 us (28%)
  starting transfers between devices  4.09 us (16%)
  local copies, waits for them, and re-layouts  3.02 us (12%)
  between operations  0.82 us (3%)
    dot_general x10, matrix products, matmul(): jnp.dot(left, right, precision=precision, preferred_element_type=jnp.floa...  10 us
    ppermute x1, waiting for transfers between devices, swapped(): return lax.ppermute(block, axis, route)  6.01 us
    ppermute x1, starting transfers between devices, swapped(): return lax.ppermute(block, axis, route)  2.86 us
    gather x1, local copies, waits for them, and re-layouts, two_section_shards(): jnp.take(blocks, order, axis=0, mode='clip').reshape(update_panel.shape)  2.01 us
    ppermute x4, starting transfers between devices, pair_swap(): return lax.ppermute(block, axis, [(0, 1), (1, 0)])  1.23 us
    ppermute x4, waiting for transfers between devices, pair_swap(): return lax.ppermute(block, axis, [(0, 1), (1, 0)])  1.03 us
    unnamed x16, local copies, waits for them, and re-layouts  0.96 us
  transfers between devices with their start and end apart: 5, of which 3 were waited for; matrix products, arithmetic and copies ran while one was open for 20% of the time, Pallas kernels for 0%

profile of v21, /device:TPU:0, one launch (start us, length us, event | category | flops | bytes accessed | tf_op | source)
XLA Modules:
  0.0 25.1 jit_solution(11944835734572764612)
XLA Ops:
  0.6 0.0 copy-start
  0.6 0.0 copy-start.7
  0.7 2.1 %fusion.17 = f32[512,256]{1,0:T(8,128)S(1)} fusion(f32[512,256]{1,0:T(8,128)} %param.7, f32[512,1024]{1,0:T(8,128)} %param.6, s32[]{:T(128)S(6)} %select_n.37), kind=kOutput, calls=%fused_computation.21 | convolution fusion | flops 402653184 | bytes 2097156 | tf_op jit(solution)/shard_map/dot_general | solution.py:26
  2.8 0.5 %collective-permute-start = (f32[512,256]{1,0:T(8,128)S(1)}, f32[512,256]{1,0:T(8,128)}, u32[]{:S(2)}, u32[]{:S(2)}) collective-permute-start(f32[512,256]{1,0:T(8,128)S(1)} %fusion.17), channel_id=1, source_target_pairs={{0,1},{1,0},{2,3},{3,2},{4,5},{5,4},{6,7},{7,6},{8,9},{9,8},{10,11... | collective-permute-start | bytes 1572872 | tf_op jit(solution)/shard_map/ppermute | solution.py:77
  3.3 0.0 copy-done.7
  3.3 0.1 select_reduce_fusion
  3.4 0.0 copy-done
  3.4 0.0 copy-start.5
  3.4 2.0 %gather_fusion = f32[8,128,512]{2,1,0:T(8,128)} fusion(f32[8,128,512]{2,1,0:T(8,128)S(1)} %bitcast.12, s32[1024]{0:T(1024)S(1)} %pad_clamp_fusion), kind=kCustom, calls=%fused_computation | custom fusion | bytes 4194336 | tf_op jit(solution)/shard_map/jit(_take)/gather | solution.py:109
  5.4 0.0 copy-start.2
  5.4 0.0 collective-permute-done
  5.4 0.0 copy-done.5
  5.4 2.1 %convolution_subtract_fusion = f32[512,256]{1,0:T(8,128)S(1)} fusion(f32[512,256]{1,0:T(8,128)S(1)} %copy-done.5, f32[512,256]{1,0:T(8,128)} %collective-permute-done, f32[512,1024]{1,0:T(8,128)} %param.6, pred[]{:T(512)S(6)} %gt.4), kind=kOutput, calls=%fused_computation.1 | convolution fusion | flops 403046400 | bytes 2621441 | tf_op jit(solution)/shard_map/dot_general | solution.py:26
  7.5 0.0 copy-done.2
  7.5 0.0 copy-start.1
  7.5 0.6 %fusion.15 = f32[512,256]{1,0:T(8,128)S(1)} fusion(f32[512,256]{1,0:T(8,128)S(1)} %convolution_subtract_fusion, f32[512,1024]{1,0:T(8,128)S(1)} %copy-done.2, s32[]{:T(128)S(6)} %select_n.37), kind=kOutput, calls=%fused_computation.19 | convolution fusion | flops 402653184 | bytes 2097156 | tf_op jit(solution)/shard_map/dot_general | solution.py:26
  8.1 0.0 copy-start.3
  8.2 0.9 %copy-done.1 = f32[8,128,512]{2,1,0:T(8,128)S(1)} copy-done((f32[8,128,512]{2,1,0:T(8,128)S(1)}, f32[8,128,512]{2,1,0:T(8,128)}, u32[]{:S(2)}) %copy-start.1) | copy-done | bytes 2097176
  9.1 0.6 %fusion.5 = f32[512,128]{1,0:T(8,128)S(1)} fusion(f32[512,128]{1,0:T(8,128)S(1)} %get-tuple-element.17, f32[1024,512]{1,0:T(8,128)S(1)} %bitcast.13, s32[]{:T(128)S(6)} %select_n.43), kind=kOutput, calls=%fused_computation.9 | convolution fusion | flops 201326592 | bytes 1572868 | tf_op jit(solution)/shard_map/dot_general | solution.py:26
  9.7 0.1 collective-permute-start.1
  9.8 0.6 %fusion.7 = f32[512,128]{1,0:T(8,128)S(1)} fusion(f32[512,128]{1,0:T(8,128)S(1)} %get-tuple-element.22, f32[1024,512]{1,0:T(8,128)S(1)} %bitcast.14, s32[]{:T(128)S(6)} %select_n.43), kind=kOutput, calls=%fused_computation.11 | convolution fusion | flops 201326592 | bytes 1572868 | tf_op jit(solution)/shard_map/dot_general | solution.py:26
  10.4 0.0 copy-done.3
  10.4 0.0 copy-start.4
  10.5 0.0 copy-start.6
  10.5 0.5 %collective-permute-start.2 = (f32[512,128]{1,0:T(8,128)S(1)}, f32[512,128]{1,0:T(8,128)S(1)}, u32[]{:S(2)}, u32[]{:S(2)}) collective-permute-start(f32[512,128]{1,0:T(8,128)S(1)} %fusion.7), channel_id=1, source_target_pairs={{0,1},{1,0},{2,3},{3,2},{4,5},{5,4},{6,7},{7,6},{8,9},{9,8},{10,11... | collective-permute-start | bytes 786440 | tf_op jit(solution)/shard_map/ppermute | solution.py:77
  11.0 0.6 %fusion.10 = f32[512,128]{1,0:T(8,128)S(1)} fusion(f32[512,128]{1,0:T(8,128)S(1)} %get-tuple-element.17, f32[1024,512]{1,0:T(8,128)S(1)} %bitcast.15, s32[]{:T(128)S(6)} %select_n.37), kind=kOutput, calls=%fused_computation.14 | convolution fusion | flops 201326592 | bytes 1572868 | tf_op jit(solution)/shard_map/dot_general | solution.py:26
  11.6 0.0 collective-permute-done.1
  11.6 0.5 %collective-permute-done.2 = f32[512,128]{1,0:T(8,128)S(1)} collective-permute-done((f32[512,128]{1,0:T(8,128)S(1)}, f32[512,128]{1,0:T(8,128)S(1)}, u32[]{:S(2)}, u32[]{:S(2)}) %collective-permute-start.2) | collective-permute-done | bytes 262176 | tf_op jit(solution)/shard_map/ppermute | solution.py:77
  12.1 2.9 %collective-permute-start.3 = (f32[512,128]{1,0:T(8,128)S(1)}, f32[512,128]{1,0:T(8,128)S(1)}, u32[]{:S(2)}, u32[]{:S(2)}) collective-permute-start(f32[512,128]{1,0:T(8,128)S(1)} %add.32), channel_id=1, source_target_pairs={{0,2},{2,0},{4,6},{6,4},{8,10},{10,8},{12,14},{14,12},{16,18},{18,... | collective-permute-start | bytes 786440 | tf_op jit(solution)/shard_map/ppermute | solution.py:22
  15.0 0.6 %convolution_add_fusion = f32[512,128]{1,0:T(8,128)S(1)} fusion(f32[512,128]{1,0:T(8,128)S(1)} %collective-permute-done.2, f32[512,128]{1,0:T(8,128)S(1)} %get-tuple-element.22, f32[1024,512]{1,0:T(8,128)S(1)} %bitcast.16, s32[]{:T(128)S(6)} %select_n.37), kind=kOutput, calls=%fused_computation.3 | convolution fusion | flops 201392128 | bytes 1835012 | tf_op jit(solution)/shard_map/dot_general | solution.py:26
  15.6 6.0 %collective-permute-done.3 = f32[512,128]{1,0:T(8,128)S(1)} collective-permute-done((f32[512,128]{1,0:T(8,128)S(1)}, f32[512,128]{1,0:T(8,128)S(1)}, u32[]{:S(2)}, u32[]{:S(2)}) %collective-permute-start.3) | collective-permute-done | bytes 262176 | tf_op jit(solution)/shard_map/ppermute | solution.py:22
  21.6 0.0 copy-done.4
  21.6 0.0 copy-done.6
  21.6 0.6 %fusion.13 = f32[512,128]{1,0:T(8,128)S(1)} fusion(f32[512,1024]{1,0:T(8,128)S(1)} %copy-done.4, s32[]{:T(128)S(6)} %select_n.37, f32[512,128]{1,0:T(8,128)S(1)} %copy-done.6, f32[512,128]{1,0:T(8,128)S(1)} %convolution_add_fusion, f32[512,128]{1,0:T(8,128)S(1)} %collective-permute-done.3), kind=kOutput, calls=%fused_computation.17 | convolution fusion | flops 201457664 | bytes 2097156 | tf_op jit(solution)/shard_map/dot_general | solution.py:26
  22.2 0.1 collective-permute-start.4
  22.3 1.0 %fusion = f32[512,512]{1,0:T(8,128)S(1)} fusion(f32[512,1024]{1,0:T(8,128)S(1)} %copy-done.4, s32[]{:T(128)S(6)} %select_n.37, pred[]{:T(512)S(6)} %gt.4), kind=kOutput, calls=%fused_computation.4 | convolution fusion | flops 805568512 | bytes 3145733 | tf_op jit(solution)/shard_map/dot_general | solution.py:26
  23.3 0.5 %collective-permute-done.4 = f32[512,128]{1,0:T(8,128)S(1)} collective-permute-done((f32[512,128]{1,0:T(8,128)S(1)}, f32[512,128]{1,0:T(8,128)S(1)}, u32[]{:S(2)}, u32[]{:S(2)}) %collective-permute-start.4) | collective-permute-done | bytes 262176 | tf_op jit(solution)/shard_map/ppermute | solution.py:77
  23.8 1.3 %convolution_subtract_fusion.1 = f32[512,128]{1,0:T(8,128)} fusion(f32[512,128]{1,0:T(8,128)S(1)} %fusion.13, f32[512,512]{1,0:T(8,128)S(1)} %fusion, f32[512,128]{1,0:T(8,128)S(1)} %collective-permute-done.4), kind=kOutput, calls=%fused_computation.2 | convolution fusion | flops 201392128 | bytes 1835008 | tf_op jit(solution)/shard_map/dot_general | solution.py:26
  (3 shorter events, 0.1 us)
Async XLA Ops:
  0.6 2.8 %copy-start = (f32[1024,512]{1,0:T(8,128)S(1)}, f32[1024,512]{1,0:T(8,128)}, u32[]{:S(2)}) copy-start(f32[1024,512]{1,0:T(8,128)} %param.8) | copy-start | bytes 6291460
  0.6 2.6 %copy-start.7 = (s32[1,8]{1,0:T(1,128)S(1)}, s32[1,8]{1,0:T(1,128)}, u32[]{:S(2)}) copy-start(s32[1,8]{1,0:T(1,128)} %param.9) | copy-start | bytes 100
  2.8 2.6 %collective-permute-start = (f32[512,256]{1,0:T(8,128)S(1)}, f32[512,256]{1,0:T(8,128)}, u32[]{:S(2)}, u32[]{:S(2)}) collective-permute-start(f32[512,256]{1,0:T(8,128)S(1)} %fusion.17), channel_id=1, source_target_pairs={{0,1},{1,0},{2,3},{3,2},{4,5},{5,4},{6,7},{7,6},{8,9},{9,8},{10,11... | collective-permute-start | bytes 1572872 | tf_op jit(solution)/shard_map/ppermute | solution.py:77
  3.4 2.0 %copy-start.5 = (f32[512,256]{1,0:T(8,128)S(1)}, f32[512,256]{1,0:T(8,128)}, u32[]{:S(2)}) copy-start(f32[512,256]{1,0:T(8,128)} %param.7) | copy-start | bytes 1572868
  5.4 2.1 %copy-start.2 = (f32[512,1024]{1,0:T(8,128)S(1)}, f32[512,1024]{1,0:T(8,128)}, u32[]{:S(2)}) copy-start(f32[512,1024]{1,0:T(8,128)} %param.6) | copy-start | bytes 6291460
  7.5 1.6 %copy-start.1 = (f32[8,128,512]{2,1,0:T(8,128)S(1)}, f32[8,128,512]{2,1,0:T(8,128)}, u32[]{:S(2)}) copy-start(f32[8,128,512]{2,1,0:T(8,128)} %gather_fusion) | copy-start | bytes 6291460
  8.1 2.3 %copy-start.3 = (f32[512,256]{1,0:T(8,128)}, f32[512,256]{1,0:T(8,128)S(1)}, u32[]{:S(2)}) copy-start(f32[512,256]{1,0:T(8,128)S(1)} %fusion.15) | copy-start | bytes 1572868
  9.7 1.9 %collective-permute-start.1 = (f32[512,128]{1,0:T(8,128)S(1)}, f32[512,128]{1,0:T(8,128)S(1)}, u32[]{:S(2)}, u32[]{:S(2)}) collective-permute-start(f32[512,128]{1,0:T(8,128)S(1)} %fusion.5), channel_id=1, source_target_pairs={{0,1},{1,0},{2,3},{3,2},{4,5},{5,4},{6,7},{7,6},{8,9},{9,8},{10,11... | collective-permute-start | bytes 786440 | tf_op jit(solution)/shard_map/ppermute | solution.py:77
  10.4 11.2 %copy-start.4 = (f32[512,1024]{1,0:T(8,128)S(1)}, f32[512,1024]{1,0:T(8,128)}, u32[]{:S(2)}) copy-start(f32[512,1024]{1,0:T(8,128)} %param.10) | copy-start | bytes 6291460
  10.5 11.2 %copy-start.6 = (f32[512,128]{1,0:T(8,128)S(1)}, f32[512,128]{1,0:T(8,128)}, u32[]{:S(2)}) copy-start(f32[512,128]{1,0:T(8,128)} %param.11) | copy-start | bytes 786436
  10.5 1.7 %collective-permute-start.2 = (f32[512,128]{1,0:T(8,128)S(1)}, f32[512,128]{1,0:T(8,128)S(1)}, u32[]{:S(2)}, u32[]{:S(2)}) collective-permute-start(f32[512,128]{1,0:T(8,128)S(1)} %fusion.7), channel_id=1, source_target_pairs={{0,1},{1,0},{2,3},{3,2},{4,5},{5,4},{6,7},{7,6},{8,9},{9,8},{10,11... | collective-permute-start | bytes 786440 | tf_op jit(solution)/shard_map/ppermute | solution.py:77
  12.1 9.5 %collective-permute-start.3 = (f32[512,128]{1,0:T(8,128)S(1)}, f32[512,128]{1,0:T(8,128)S(1)}, u32[]{:S(2)}, u32[]{:S(2)}) collective-permute-start(f32[512,128]{1,0:T(8,128)S(1)} %add.32), channel_id=1, source_target_pairs={{0,2},{2,0},{4,6},{6,4},{8,10},{10,8},{12,14},{14,12},{16,18},{18,... | collective-permute-start | bytes 786440 | tf_op jit(solution)/shard_map/ppermute | solution.py:22
  22.2 1.6 %collective-permute-start.4 = (f32[512,128]{1,0:T(8,128)S(1)}, f32[512,128]{1,0:T(8,128)S(1)}, u32[]{:S(2)}, u32[]{:S(2)}) collective-permute-start(f32[512,128]{1,0:T(8,128)S(1)} %fusion.13), channel_id=1, source_target_pairs={{0,1},{1,0},{2,3},{3,2},{4,5},{5,4},{6,7},{7,6},{8,9},{9,8},{10,11... | collective-permute-start | bytes 786440 | tf_op jit(solution)/shard_map/ppermute | solution.py:77

commit v22 on v18

--- a/solution.py
+++ b/solution.py
@@ -104,27 +104,39 @@
     section = lax.axis_index("rows")
     precision = lax.Precision.HIGH
     blocks = update_panel.reshape(-1, ROW_BLOCK, update_panel.shape[1])
-    order = inverse_order(update_blocks)
+    placed_panel = jnp.take(blocks, inverse_order(update_blocks), axis=0, mode="clip").reshape(update_panel.shape)
+    tile_rows = leaf_rhs.shape[0]
+    leaf_diagonal = lax.dynamic_slice_in_dim(leaf_factor, section * tile_rows, tile_rows, 1)
+    leaf_first = matmul(leaf_diagonal, leaf_rhs, precision)
+    leaf_arrived = pair_swap(leaf_first, "rows")
+    leaf_arrived, placed_panel = lax.optimization_barrier((leaf_arrived, placed_panel))
+    below = jnp.where(section > 0, leaf_factor[:, :tile_rows], jnp.zeros_like(leaf_diagonal))
+    column_half = parent_rhs.shape[1]
+    sibling = lax.axis_index("leaf") % 2
 
-    placed_panel = jnp.take(blocks, order, axis=0, mode="clip").reshape(update_panel.shape)
-    placed_panel = two_section_leaf(leaf_factor, leaf_rhs, section, precision, placed_panel)
-    leaf_solution, placed_panel = placed_panel
+    def leaf_columns(half, arrived_all):
+        rhs_part = lax.dynamic_slice_in_dim(leaf_rhs, half * column_half, column_half, 1)
+        arrived_part = lax.dynamic_slice_in_dim(arrived_all, half * column_half, column_half, 1)
+        target = rhs_part - matmul(below, arrived_part, precision)
+        return matmul(leaf_diagonal, target, precision)
+
     rows_half = placed_panel.shape[0] // 2
     panel_other = lax.dynamic_slice_in_dim(placed_panel, (1 - section) * rows_half, rows_half, 0)
     panel_own = lax.dynamic_slice_in_dim(placed_panel, section * rows_half, rows_half, 0)
-    column_half = parent_rhs.shape[1]
-    sibling = lax.axis_index("leaf") % 2
-    solution_kept = lax.dynamic_slice_in_dim(leaf_solution, sibling * column_half, column_half, 1)
-    solution_sent = lax.dynamic_slice_in_dim(leaf_solution, (1 - sibling) * column_half, column_half, 1)
+    solution_sent = leaf_columns(1 - sibling, leaf_arrived)
     other_sent = matmul(panel_other, solution_sent, precision)
     arrived_sent = pair_swap(other_sent, "rows")
     own_sent = matmul(panel_own, solution_sent, precision)
     own_sent, arrived_sent = lax.optimization_barrier((own_sent, arrived_sent))
     sent = own_sent + arrived_sent
-    sent, solution_kept = lax.optimization_barrier((sent, solution_kept))
+    sent, leaf_arrived = lax.optimization_barrier((sent, leaf_arrived))
+    solution_kept = leaf_columns(sibling, leaf_arrived)
     other_kept = matmul(panel_other, solution_kept, precision)
     arrived_kept = pair_swap(other_kept, "rows")
     kept = matmul(panel_own, solution_kept, precision) + arrived_kept
+    leaf_solution = jnp.zeros_like(leaf_rhs)
+    leaf_solution = lax.dynamic_update_slice_in_dim(leaf_solution, solution_kept, sibling * column_half, 1)
+    leaf_solution = lax.dynamic_update_slice_in_dim(leaf_solution, solution_sent, (1 - sibling) * column_half, 1)
     tile_rows = parent_rhs.shape[0]
     diagonal = lax.dynamic_slice_in_dim(parent_factor, section * tile_rows, tile_rows, 1)
     coupling = lower_coupling(parent_factor, diagonal, section, precision)
@@ -140,7 +152,7 @@
 
 def shards(leaf_factor, leaf_rhs, update_panel, update_blocks, parent_factor, parent_rhs):
     sections = lax.axis_size("rows")
-    if sections == 2:
+    if sections == 2 and leaf_rhs.shape[1] == 2 * parent_rhs.shape[1]:
         return two_section_shards(leaf_factor, leaf_rhs, update_panel, update_blocks, parent_factor, parent_rhs)
     section = lax.axis_index("rows")
     leaf_solution = front_forward(leaf_factor, leaf_rhs, section, sections, leaf_pass)

time: 25.2 us -> 28.6 us (1.13)
  matrix products: 11.4 us -> 14.8 us
    dot_general x10 -> x12, matrix products: 11.4 us -> 14.8 us  [matmul(): jnp.dot(left, right, precision=precision, preferred_element_type=jnp.floa...]
  transfers between devices with their start and end apart: 5 -> 5, of which waited for: 2 -> 2; matrix products, arithmetic and copies ran while one was open for 23% -> 20% of each run, Pallas kernels for 0% -> 0%
where the time goes in v22:
time: 28.6 us; the launch traced here: 28.5 us
  matrix products  14.8 us (52%)
  waiting for transfers between devices  6.76 us (24%)
  starting transfers between devices  3.79 us (13%)
  local copies, waits for them, and re-layouts  2.12 us (7%)
  between operations  0.84 us (3%)
    dot_general x12, matrix products, matmul(): jnp.dot(left, right, precision=precision, preferred_element_type=jnp.floa...  14.8 us
    ppermute x1, waiting for transfers between devices, swapped(): return lax.ppermute(block, axis, route)  6.3 us
    ppermute x1, starting transfers between devices, swapped(): return lax.ppermute(block, axis, route)  2.56 us
    gather x1, local copies, waits for them, and re-layouts, two_section_shards(): jnp.take(blocks, inverse_order(update_blocks), axis=0, mode='clip')  2.01 us
    ppermute x4, starting transfers between devices, pair_swap(): return lax.ppermute(block, axis, [(0, 1), (1, 0)])  1.23 us
  transfers between devices with their start and end apart: 5, of which 2 were waited for; matrix products, arithmetic and copies ran while one was open for 20% of the time, Pallas kernels for 0%

profile of v22, /device:TPU:0, one launch (start us, length us, event | category | flops | bytes accessed | tf_op | source)
XLA Modules:
  0.0 28.5 jit_solution(10398504845292204873)
XLA Ops:
  0.6 0.0 copy-start
  0.6 0.0 copy-start.8
  0.7 2.1 %fusion.17 = f32[512,256]{1,0:T(8,128)S(1)} fusion(f32[512,256]{1,0:T(8,128)} %param.7, f32[512,1024]{1,0:T(8,128)} %param.6, s32[]{:T(128)S(6)} %select_n.41), kind=kOutput, calls=%fused_computation.23 | convolution fusion | flops 402653184 | bytes 2097156 | tf_op jit(solution)/shard_map/dot_general | solution.py:26
  2.8 0.5 %collective-permute-start = (f32[512,256]{1,0:T(8,128)S(1)}, f32[512,256]{1,0:T(8,128)}, u32[]{:S(2)}, u32[]{:S(2)}) collective-permute-start(f32[512,256]{1,0:T(8,128)S(1)} %fusion.17), channel_id=1, source_target_pairs={{0,1},{1,0},{2,3},{3,2},{4,5},{5,4},{6,7},{7,6},{8,9},{9,8},{10,11... | collective-permute-start | bytes 1572872 | tf_op jit(solution)/shard_map/ppermute | solution.py:77
  3.3 0.0 copy-done.8
  3.3 0.1 select_reduce_fusion
  3.4 0.0 copy-done
  3.4 0.0 copy-start.5
  3.4 2.0 %gather_fusion = f32[8,128,512]{2,1,0:T(8,128)} fusion(f32[8,128,512]{2,1,0:T(8,128)S(1)} %bitcast.12, s32[1024]{0:T(1024)S(1)} %pad_clamp_fusion), kind=kCustom, calls=%fused_computation | custom fusion | bytes 4194336 | tf_op jit(solution)/shard_map/jit(_take)/gather | solution.py:107
  5.4 0.0 copy-start.1
  5.4 0.0 collective-permute-done
  5.4 0.0 copy-done.5
  5.4 2.0 %convolution_subtract_fusion.2 = f32[512,128]{1,0:T(8,128)S(1)} fusion(f32[512,1024]{1,0:T(8,128)} %param.6, pred[]{:T(512)S(6)} %gt.4, f32[512,256]{1,0:T(8,128)} %collective-permute-done, s32[]{:T(128)S(6)} %select_n.47, f32[512,256]{1,0:T(8,128)S(1)} %copy-done.5), kind=kOutput, calls=%fused_computation.4 | convolution fusion | flops 201654272 | bytes 1836544 | tf_op jit(solution)/shard_map/dot_general | solution.py:26
  7.4 1.8 %fusion.15 = f32[512,128]{1,0:T(8,128)S(1)} fusion(f32[512,128]{1,0:T(8,128)S(1)} %convolution_subtract_fusion.2, f32[512,1024]{1,0:T(8,128)} %param.6, s32[]{:T(128)S(6)} %select_n.41), kind=kOutput, calls=%fused_computation.21 | convolution fusion | flops 201326592 | bytes 1572868 | tf_op jit(solution)/shard_map/dot_general | solution.py:26
  9.3 0.0 copy-done.1
  9.3 0.6 %fusion.8 = f32[512,128]{1,0:T(8,128)S(1)} fusion(f32[512,128]{1,0:T(8,128)S(1)} %fusion.15, f32[1024,512]{1,0:T(8,128)S(1)} %bitcast.14, s32[]{:T(128)S(6)} %select_n.48), kind=kOutput, calls=%fused_computation.14 | convolution fusion | flops 201326592 | bytes 1572868 | tf_op jit(solution)/shard_map/dot_general | solution.py:26
  9.9 0.1 collective-permute-start.1
  10.0 0.0 copy-start.3
  10.0 2.0 %fusion.11 = f32[512,128]{1,0:T(8,128)S(1)} fusion(f32[512,128]{1,0:T(8,128)S(1)} %fusion.15, f32[1024,512]{1,0:T(8,128)} %bitcast.13, s32[]{:T(128)S(6)} %select_n.41), kind=kOutput, calls=%fused_computation.17 | convolution fusion | flops 201326592 | bytes 1572868 | tf_op jit(solution)/shard_map/dot_general | solution.py:26
  11.9 0.0 collective-permute-done.1
  12.0 0.0 copy-done.3
  12.0 0.0 copy-start.2
  12.0 1.7 %convolution_subtract_fusion.1 = f32[512,128]{1,0:T(8,128)S(1)} fusion(f32[512,1024]{1,0:T(8,128)S(1)} %copy-done.3, pred[]{:T(512)S(6)} %gt.4, f32[512,256]{1,0:T(8,128)} %collective-permute-done, s32[]{:T(128)S(6)} %select_n.43, f32[512,256]{1,0:T(8,128)S(1)} %copy-done.5), kind=kOutput, calls=%fused_computation.3 | convolution fusion | flops 201654272 | bytes 1836544 | tf_op jit(solution)/shard_map/dot_general | solution.py:26
  13.7 0.6 %constant_dynamic-update-slice_fusion.1 = (f32[512,256]{1,0:T(8,128)S(1)}, f32[512,128]{1,0:T(8,128)S(1)}) fusion(f32[512,256]{1,0:T(8,128)S(1)} %broadcast_in_dim.21, s32[]{:T(128)S(6)} %select_n.43, f32[512,128]{1,0:T(8,128)S(1)} %convolution_subtract_fusion.1, f32[512,1024]{1,0:T(8,128)S(1)} %copy-done.3, s32[]{:T(128)S(6)} %select_n.41), kind=kOutput, calls=%fused_computation.43 | convolution fusion | flops 201326592 | bytes 1835016 | tf_op jit(solution)/shard_map/dot_general | solution.py:26
  14.3 0.0 copy-start.4
  14.3 0.0 copy-start.7
  14.4 0.0 copy-done.2
  14.4 0.6 %fusion.6 = f32[512,128]{1,0:T(8,128)S(1)} fusion(f32[512,128]{1,0:T(8,128)S(1)} %get-tuple-element.23, f32[1024,512]{1,0:T(8,128)S(1)} %bitcast.15, s32[]{:T(128)S(6)} %select_n.48), kind=kOutput, calls=%fused_computation.12 | convolution fusion | flops 201326592 | bytes 1572868 | tf_op jit(solution)/shard_map/dot_general | solution.py:26
  15.0 0.5 %collective-permute-start.3 = (f32[512,128]{1,0:T(8,128)S(1)}, f32[512,128]{1,0:T(8,128)S(1)}, u32[]{:S(2)}, u32[]{:S(2)}) collective-permute-start(f32[512,128]{1,0:T(8,128)S(1)} %fusion.6), channel_id=1, source_target_pairs={{0,1},{1,0},{2,3},{3,2},{4,5},{5,4},{6,7},{7,6},{8,9},{9,8},{10,11... | collective-permute-start | bytes 786440 | tf_op jit(solution)/shard_map/ppermute | solution.py:77
  15.5 2.6 %collective-permute-start.2 = (f32[512,128]{1,0:T(8,128)S(1)}, f32[512,128]{1,0:T(8,128)S(1)}, u32[]{:S(2)}, u32[]{:S(2)}) collective-permute-start(f32[512,128]{1,0:T(8,128)S(1)} %add.36), channel_id=1, source_target_pairs={{0,2},{2,0},{4,6},{6,4},{8,10},{10,8},{12,14},{14,12},{16,18},{18,... | collective-permute-start | bytes 786440 | tf_op jit(solution)/shard_map/ppermute | solution.py:22
  18.0 0.0 collective-permute-done.3
  18.0 0.6 %convolution_add_fusion = f32[512,128]{1,0:T(8,128)S(1)} fusion(f32[512,128]{1,0:T(8,128)S(1)} %collective-permute-done.3, f32[512,128]{1,0:T(8,128)S(1)} %get-tuple-element.23, f32[1024,512]{1,0:T(8,128)S(1)} %bitcast.16, s32[]{:T(128)S(6)} %select_n.41), kind=kOutput, calls=%fused_computation.2 | convolution fusion | flops 201392128 | bytes 1835012 | tf_op jit(solution)/shard_map/dot_general | solution.py:26
  18.6 6.3 %collective-permute-done.2 = f32[512,128]{1,0:T(8,128)S(1)} collective-permute-done((f32[512,128]{1,0:T(8,128)S(1)}, f32[512,128]{1,0:T(8,128)S(1)}, u32[]{:S(2)}, u32[]{:S(2)}) %collective-permute-start.2) | collective-permute-done | bytes 262176 | tf_op jit(solution)/shard_map/ppermute | solution.py:22
  24.9 0.0 copy-done.4
  24.9 0.0 copy-done.7
  25.0 0.6 %fusion.4 = f32[512,128]{1,0:T(8,128)S(1)} fusion(f32[512,1024]{1,0:T(8,128)S(1)} %copy-done.4, s32[]{:T(128)S(6)} %select_n.41, f32[512,128]{1,0:T(8,128)S(1)} %copy-done.7, f32[512,128]{1,0:T(8,128)S(1)} %convolution_add_fusion, f32[512,128]{1,0:T(8,128)S(1)} %collective-permute-done.2), kind=kOutput, calls=%fused_computation.10 | convolution fusion | flops 201457664 | bytes 2097156 | tf_op jit(solution)/shard_map/dot_general | solution.py:26
  25.6 0.1 collective-permute-start.4
  25.6 1.0 %fusion = f32[512,512]{1,0:T(8,128)S(1)} fusion(f32[512,1024]{1,0:T(8,128)S(1)} %copy-done.4, s32[]{:T(128)S(6)} %select_n.41, pred[]{:T(512)S(6)} %gt.4), kind=kOutput, calls=%fused_computation.5 | convolution fusion | flops 805568512 | bytes 3145733 | tf_op jit(solution)/shard_map/dot_general | solution.py:26
  26.7 0.0 copy-start.6
  26.7 0.5 %collective-permute-done.4 = f32[512,128]{1,0:T(8,128)S(1)} collective-permute-done((f32[512,128]{1,0:T(8,128)S(1)}, f32[512,128]{1,0:T(8,128)S(1)}, u32[]{:S(2)}, u32[]{:S(2)}) %collective-permute-start.4) | collective-permute-done | bytes 262176 | tf_op jit(solution)/shard_map/ppermute | solution.py:77
  27.2 1.3 %convolution_subtract_fusion = f32[512,128]{1,0:T(8,128)} fusion(f32[512,128]{1,0:T(8,128)S(1)} %fusion.4, f32[512,512]{1,0:T(8,128)S(1)} %fusion, f32[512,128]{1,0:T(8,128)S(1)} %collective-permute-done.4), kind=kOutput, calls=%fused_computation.1 | convolution fusion | flops 201392128 | bytes 1835008 | tf_op jit(solution)/shard_map/dot_general | solution.py:26
  28.5 0.0 copy-done.6
  (4 shorter events, 0.1 us)
Async XLA Ops:
  0.6 2.8 %copy-start = (f32[1024,512]{1,0:T(8,128)S(1)}, f32[1024,512]{1,0:T(8,128)}, u32[]{:S(2)}) copy-start(f32[1024,512]{1,0:T(8,128)} %param.8) | copy-start | bytes 6291460
  0.6 2.6 %copy-start.8 = (s32[1,8]{1,0:T(1,128)S(1)}, s32[1,8]{1,0:T(1,128)}, u32[]{:S(2)}) copy-start(s32[1,8]{1,0:T(1,128)} %param.9) | copy-start | bytes 100
  2.8 2.6 %collective-permute-start = (f32[512,256]{1,0:T(8,128)S(1)}, f32[512,256]{1,0:T(8,128)}, u32[]{:S(2)}, u32[]{:S(2)}) collective-permute-start(f32[512,256]{1,0:T(8,128)S(1)} %fusion.17), channel_id=1, source_target_pairs={{0,1},{1,0},{2,3},{3,2},{4,5},{5,4},{6,7},{7,6},{8,9},{9,8},{10,11... | collective-permute-start | bytes 1572872 | tf_op jit(solution)/shard_map/ppermute | solution.py:77
  3.4 2.0 %copy-start.5 = (f32[512,256]{1,0:T(8,128)S(1)}, f32[512,256]{1,0:T(8,128)}, u32[]{:S(2)}) copy-start(f32[512,256]{1,0:T(8,128)} %param.7) | copy-start | bytes 1572868
  5.4 3.8 %copy-start.1 = (f32[8,128,512]{2,1,0:T(8,128)S(1)}, f32[8,128,512]{2,1,0:T(8,128)}, u32[]{:S(2)}) copy-start(f32[8,128,512]{2,1,0:T(8,128)} %gather_fusion) | copy-start | bytes 6291460
  9.9 2.1 %collective-permute-start.1 = (f32[512,128]{1,0:T(8,128)S(1)}, f32[512,128]{1,0:T(8,128)S(1)}, u32[]{:S(2)}, u32[]{:S(2)}) collective-permute-start(f32[512,128]{1,0:T(8,128)S(1)} %fusion.8), channel_id=1, source_target_pairs={{0,1},{1,0},{2,3},{3,2},{4,5},{5,4},{6,7},{7,6},{8,9},{9,8},{10,11... | collective-permute-start | bytes 786440 | tf_op jit(solution)/shard_map/ppermute | solution.py:77
  10.0 2.0 %copy-start.3 = (f32[512,1024]{1,0:T(8,128)S(1)}, f32[512,1024]{1,0:T(8,128)}, u32[]{:S(2)}) copy-start(f32[512,1024]{1,0:T(8,128)} %param.6) | copy-start | bytes 6291460
  12.0 2.4 %copy-start.2 = (f32[8,128,512]{2,1,0:T(8,128)S(1)}, f32[8,128,512]{2,1,0:T(8,128)}, u32[]{:S(2)}) copy-start(f32[8,128,512]{2,1,0:T(8,128)} %gather_fusion) | copy-start | bytes 6291460
  14.3 10.6 %copy-start.4 = (f32[512,1024]{1,0:T(8,128)S(1)}, f32[512,1024]{1,0:T(8,128)}, u32[]{:S(2)}) copy-start(f32[512,1024]{1,0:T(8,128)} %param.10) | copy-start | bytes 6291460
  14.3 10.6 %copy-start.7 = (f32[512,128]{1,0:T(8,128)S(1)}, f32[512,128]{1,0:T(8,128)}, u32[]{:S(2)}) copy-start(f32[512,128]{1,0:T(8,128)} %param.11) | copy-start | bytes 786436
  15.0 3.1 %collective-permute-start.3 = (f32[512,128]{1,0:T(8,128)S(1)}, f32[512,128]{1,0:T(8,128)S(1)}, u32[]{:S(2)}, u32[]{:S(2)}) collective-permute-start(f32[512,128]{1,0:T(8,128)S(1)} %fusion.6), channel_id=1, source_target_pairs={{0,1},{1,0},{2,3},{3,2},{4,5},{5,4},{6,7},{7,6},{8,9},{9,8},{10,11... | collective-permute-start | bytes 786440 | tf_op jit(solution)/shard_map/ppermute | solution.py:77
  15.5 9.5 %collective-permute-start.2 = (f32[512,128]{1,0:T(8,128)S(1)}, f32[512,128]{1,0:T(8,128)S(1)}, u32[]{:S(2)}, u32[]{:S(2)}) collective-permute-start(f32[512,128]{1,0:T(8,128)S(1)} %add.36), channel_id=1, source_target_pairs={{0,2},{2,0},{4,6},{6,4},{8,10},{10,8},{12,14},{14,12},{16,18},{18,... | collective-permute-start | bytes 786440 | tf_op jit(solution)/shard_map/ppermute | solution.py:22
  25.6 1.6 %collective-permute-start.4 = (f32[512,128]{1,0:T(8,128)S(1)}, f32[512,128]{1,0:T(8,128)S(1)}, u32[]{:S(2)}, u32[]{:S(2)}) collective-permute-start(f32[512,128]{1,0:T(8,128)S(1)} %fusion.4), channel_id=1, source_target_pairs={{0,1},{1,0},{2,3},{3,2},{4,5},{5,4},{6,7},{7,6},{8,9},{9,8},{10,11... | collective-permute-start | bytes 786440 | tf_op jit(solution)/shard_map/ppermute | solution.py:77
  26.7 1.8 %copy-start.6 = (f32[512,256]{1,0:T(8,128)}, f32[512,256]{1,0:T(8,128)S(1)}, u32[]{:S(2)}) copy-start(f32[512,256]{1,0:T(8,128)S(1)} %constant_dynamic-update-slice_fusion) | copy-start | bytes 1572868

commit v23 on v20

--- a/solution.py
+++ b/solution.py
@@ -130,12 +130,16 @@
     diagonal = lax.dynamic_slice_in_dim(parent_factor, section * tile_rows, tile_rows, 1)
     coupling = lower_coupling(parent_factor, diagonal, section, precision)
     arrived = swapped(sent, "leaf", 0)
-    arrived, kept = lax.optimization_barrier((arrived, kept))
+    arrived, kept, coupling = lax.optimization_barrier((arrived, kept, coupling))
     pending = parent_rhs - (kept + arrived)
-    first = matmul(diagonal, pending, precision)
-    arrived = pair_swap(first, "rows")
-    arrived, coupling = lax.optimization_barrier((arrived, coupling))
-    parent_solution = first - matmul(coupling, arrived, precision)
+    half_rows = tile_rows // 2
+    first_top = matmul(diagonal[:half_rows], pending, precision)
+    arrived_top = pair_swap(first_top, "rows")
+    first_bottom = matmul(diagonal[half_rows:], pending, precision)
+    arrived_bottom = pair_swap(first_bottom, "rows")
+    correction = matmul(coupling[:, :half_rows], arrived_top, precision)
+    correction = correction + matmul(coupling[:, half_rows:], arrived_bottom, precision)
+    parent_solution = jnp.concatenate([first_top, first_bottom], axis=0) - correction
     return (leaf_solution, parent_solution)
 
 

time: 24.8 us -> 28.8 us (1.16)
  matrix products: 10 us -> 14.7 us
  waiting for transfers between devices: 6.84 us -> 4.9 us
  other arithmetic: 0.12 us -> 0.82 us
  starting transfers between devices: 3.84 us -> 4.25 us
    dot_general x10 -> x12, matrix products: 10 us -> 14.7 us  [matmul(): jnp.dot(left, right, precision=precision, preferred_element_type=jnp.floa...]
    ppermute x1, waiting for transfers between devices: 6.34 us -> 4.29 us  [swapped(): return lax.ppermute(block, axis, route)]
    add x1, other arithmetic: 0.03 us -> 0.73 us  [two_section_shards(): sent = own_sent + arrived_sent]
    ppermute x4 -> x5, starting transfers between devices: 1.23 us -> 1.7 us  [pair_swap(): return lax.ppermute(block, axis, [(0, 1), (1, 0)])]
    ppermute x4 -> x5, waiting for transfers between devices: 0.5 us -> 0.61 us  [pair_swap(): return lax.ppermute(block, axis, [(0, 1), (1, 0)])]
  transfers between devices with their start and end apart: 5 -> 6, of which waited for: 2 -> 2; matrix products, arithmetic and copies ran while one was open for 20% -> 33% of each run, Pallas kernels for 0% -> 0%
where the time goes in v23:
time: 28.8 us; the launch traced here: 28.5 us
  matrix products  14.7 us (51%)
  waiting for transfers between devices  4.9 us (17%)
  starting transfers between devices  4.25 us (15%)
  local copies, waits for them, and re-layouts  3.02 us (10%)
  between operations  0.83 us (3%)
  other arithmetic  0.82 us (3%)
    dot_general x12, matrix products, matmul(): jnp.dot(left, right, precision=precision, preferred_element_type=jnp.floa...  14.7 us
    ppermute x1, waiting for transfers between devices, swapped(): return lax.ppermute(block, axis, route)  4.29 us
    ppermute x1, starting transfers between devices, swapped(): return lax.ppermute(block, axis, route)  2.55 us
    gather x1, local copies, waits for them, and re-layouts, two_section_shards(): jnp.take(blocks, order, axis=0, mode='clip').reshape(update_panel.shape)  2.01 us
    ppermute x5, starting transfers between devices, pair_swap(): return lax.ppermute(block, axis, [(0, 1), (1, 0)])  1.7 us
    unnamed x16, local copies, waits for them, and re-layouts  0.96 us
    add x1, other arithmetic, two_section_shards(): sent = own_sent + arrived_sent  0.73 us
    ppermute x5, waiting for transfers between devices, pair_swap(): return lax.ppermute(block, axis, [(0, 1), (1, 0)])  0.61 us
  transfers between devices with their start and end apart: 6, of which 2 were waited for; matrix products, arithmetic and copies ran while one was open for 33% of the time, Pallas kernels for 0%

profile of v23, /device:TPU:0, one launch (start us, length us, event | category | flops | bytes accessed | tf_op | source)
XLA Modules:
  0.0 28.5 jit_solution(17355161537451366099)
XLA Ops:
  0.6 0.0 copy-start
  0.6 0.0 copy-start.7
  0.7 2.1 %fusion.16 = f32[512,256]{1,0:T(8,128)S(1)} fusion(f32[512,256]{1,0:T(8,128)} %param.7, f32[512,1024]{1,0:T(8,128)} %param.6, s32[]{:T(128)S(6)} %select_n.37), kind=kOutput, calls=%fused_computation.20 | convolution fusion | flops 402653184 | bytes 2097156 | tf_op jit(solution)/shard_map/dot_general | solution.py:26
  2.8 0.5 %collective-permute-start = (f32[512,256]{1,0:T(8,128)S(1)}, f32[512,256]{1,0:T(8,128)}, u32[]{:S(2)}, u32[]{:S(2)}) collective-permute-start(f32[512,256]{1,0:T(8,128)S(1)} %fusion.16), channel_id=1, source_target_pairs={{0,1},{1,0},{2,3},{3,2},{4,5},{5,4},{6,7},{7,6},{8,9},{9,8},{10,11... | collective-permute-start | bytes 1572872 | tf_op jit(solution)/shard_map/ppermute | solution.py:77
  3.3 0.0 copy-done.7
  3.3 0.1 select_reduce_fusion
  3.4 0.0 copy-done
  3.4 0.0 copy-start.5
  3.4 2.0 %gather_fusion = f32[8,128,512]{2,1,0:T(8,128)} fusion(f32[8,128,512]{2,1,0:T(8,128)S(1)} %bitcast.12, s32[1024]{0:T(1024)S(1)} %pad_clamp_fusion), kind=kCustom, calls=%fused_computation | custom fusion | bytes 4194336 | tf_op jit(solution)/shard_map/jit(_take)/gather | solution.py:109
  5.4 0.0 copy-start.2
  5.4 0.0 collective-permute-done
  5.4 0.0 copy-done.5
  5.4 2.1 %convolution_subtract_fusion = f32[512,256]{1,0:T(8,128)S(1)} fusion(f32[512,256]{1,0:T(8,128)S(1)} %copy-done.5, f32[512,256]{1,0:T(8,128)} %collective-permute-done, f32[512,1024]{1,0:T(8,128)} %param.6, pred[]{:T(512)S(6)} %gt.4), kind=kOutput, calls=%fused_computation.1 | convolution fusion | flops 403046400 | bytes 2621441 | tf_op jit(solution)/shard_map/dot_general | solution.py:26
  7.5 0.0 copy-done.2
  7.5 0.0 copy-start.1
  7.6 0.6 %fusion.14 = f32[512,256]{1,0:T(8,128)S(1)} fusion(f32[512,256]{1,0:T(8,128)S(1)} %convolution_subtract_fusion, f32[512,1024]{1,0:T(8,128)S(1)} %copy-done.2, s32[]{:T(128)S(6)} %select_n.37), kind=kOutput, calls=%fused_computation.18 | convolution fusion | flops 402653184 | bytes 2097156 | tf_op jit(solution)/shard_map/dot_general | solution.py:26
  8.2 0.0 copy-start.3
  8.2 0.9 %copy-done.1 = f32[8,128,512]{2,1,0:T(8,128)S(1)} copy-done((f32[8,128,512]{2,1,0:T(8,128)S(1)}, f32[8,128,512]{2,1,0:T(8,128)}, u32[]{:S(2)}) %copy-start.1) | copy-done | bytes 2097176
  9.1 0.6 %fusion.7 = f32[512,128]{1,0:T(8,128)S(1)} fusion(f32[512,128]{1,0:T(8,128)S(1)} %get-tuple-element.15, f32[1024,512]{1,0:T(8,128)S(1)} %bitcast.14, s32[]{:T(128)S(6)} %select_n.43), kind=kOutput, calls=%fused_computation.11 | convolution fusion | flops 201326592 | bytes 1572868 | tf_op jit(solution)/shard_map/dot_general | solution.py:26
  9.7 0.0 copy-start.4
  9.7 0.1 collective-permute-start.1
  9.9 1.3 %fusion.9 = f32[512,128]{1,0:T(8,128)} fusion(f32[512,128]{1,0:T(8,128)S(1)} %get-tuple-element.19, f32[1024,512]{1,0:T(8,128)S(1)} %bitcast.15, s32[]{:T(128)S(6)} %select_n.43), kind=kOutput, calls=%fused_computation.13 | convolution fusion | flops 201326592 | bytes 1572868 | tf_op jit(solution)/shard_map/dot_general | solution.py:26
  11.1 0.0 copy-done.3
  11.2 0.4 %collective-permute-start.3 = (f32[512,128]{1,0:T(8,128)}, f32[512,128]{1,0:T(8,128)}, u32[]{:S(2)}, u32[]{:S(2)}) collective-permute-start(f32[512,128]{1,0:T(8,128)} %fusion.9), channel_id=1, source_target_pairs={{0,1},{1,0},{2,3},{3,2},{4,5},{5,4},{6,7},{7,6},{8,9},{9,8},{10,11... | collective-permute-start | bytes 786440 | tf_op jit(solution)/shard_map/ppermute | solution.py:77
  11.6 0.6 %fusion.12 = f32[512,128]{1,0:T(8,128)S(1)} fusion(f32[512,128]{1,0:T(8,128)S(1)} %get-tuple-element.15, f32[1024,512]{1,0:T(8,128)S(1)} %bitcast.16, s32[]{:T(128)S(6)} %select_n.37), kind=kOutput, calls=%fused_computation.16 | convolution fusion | flops 201326592 | bytes 1572868 | tf_op jit(solution)/shard_map/dot_general | solution.py:26
  12.2 0.0 collective-permute-done.1
  12.2 0.7 %add.35 = f32[512,128]{1,0:T(8,128)} add(f32[512,128]{1,0:T(8,128)S(1)} %fusion.12, f32[512,128]{1,0:T(8,128)S(1)} %collective-permute-done.1) | non-fusion elementwise | flops 65536 | bytes 786432 | tf_op jit(solution)/shard_map/add | solution.py:126
  12.9 2.5 %collective-permute-start.2 = (f32[512,128]{1,0:T(8,128)}, f32[512,128]{1,0:T(8,128)}, u32[]{:S(2)}, u32[]{:S(2)}) collective-permute-start(f32[512,128]{1,0:T(8,128)} %add.35), channel_id=1, source_target_pairs={{0,2},{2,0},{4,6},{6,4},{8,10},{10,8},{12,14},{14,12},{16,18},{18,... | collective-permute-start | bytes 786440 | tf_op jit(solution)/shard_map/ppermute | solution.py:22
  15.5 0.0 copy-done.4
  15.5 1.0 %fusion.1 = f32[512,512]{1,0:T(8,128)S(1)} fusion(f32[512,1024]{1,0:T(8,128)S(1)} %copy-done.4, s32[]{:T(128)S(6)} %select_n.37, pred[]{:T(512)S(6)} %gt.4), kind=kOutput, calls=%fused_computation.5 | convolution fusion | flops 805568512 | bytes 3145733 | tf_op jit(solution)/shard_map/dot_general | solution.py:26
  16.5 0.0 copy-start.6
  16.5 0.0 collective-permute-done.3
  16.5 1.9 %convolution_add_fusion.1 = f32[512,128]{1,0:T(8,128)S(1)} fusion(f32[512,128]{1,0:T(8,128)} %collective-permute-done.3, f32[512,128]{1,0:T(8,128)S(1)} %get-tuple-element.19, f32[1024,512]{1,0:T(8,128)} %bitcast.13, s32[]{:T(128)S(6)} %select_n.37), kind=kOutput, calls=%fused_computation.4 | convolution fusion | flops 201392128 | bytes 1835012 | tf_op jit(solution)/shard_map/dot_general | solution.py:26
  18.4 4.3 %collective-permute-done.2 = f32[512,128]{1,0:T(8,128)} collective-permute-done((f32[512,128]{1,0:T(8,128)}, f32[512,128]{1,0:T(8,128)}, u32[]{:S(2)}, u32[]{:S(2)}) %collective-permute-start.2) | collective-permute-done | bytes 262176 | tf_op jit(solution)/shard_map/ppermute | solution.py:22
  22.7 1.6 %fusion.18 = f32[256,128]{1,0:T(8,128)S(1)} fusion(f32[512,1024]{1,0:T(8,128)} %param.10, s32[]{:T(128)S(6)} %add.39, s32[]{:T(128)S(6)} %select_n.37, f32[512,128]{1,0:T(8,128)} %param.11, f32[512,128]{1,0:T(8,128)S(1)} %convolution_add_fusion.1, f32[512,128]{1,0:T(8,128)} %collective-permute-done.2), kind=kOutput, calls=%fused_computation.22 | convolution fusion | flops 100794368 | bytes 1441800 | tf_op jit(solution)/shard_map/dot_general | solution.py:26
  24.3 0.1 collective-permute-start.5
  24.4 0.0 copy-done.6
  24.4 1.5 %fusion.20 = f32[256,128]{1,0:T(8,128)S(1)} fusion(f32[512,1024]{1,0:T(8,128)} %param.10, s32[]{:T(128)S(6)} %select_n.37, f32[512,128]{1,0:T(8,128)S(1)} %copy-done.6, f32[512,128]{1,0:T(8,128)S(1)} %convolution_add_fusion.1, f32[512,128]{1,0:T(8,128)} %collective-permute-done.2), kind=kOutput, calls=%fused_computation.24 | convolution fusion | flops 100794368 | bytes 1441796 | tf_op jit(solution)/shard_map/dot_general | solution.py:26
  25.9 0.5 %collective-permute-start.4 = (f32[256,128]{1,0:T(8,128)S(1)}, f32[256,128]{1,0:T(8,128)S(1)}, u32[]{:S(2)}, u32[]{:S(2)}) collective-permute-start(f32[256,128]{1,0:T(8,128)S(1)} %fusion.20), channel_id=1, source_target_pairs={{0,1},{1,0},{2,3},{3,2},{4,5},{5,4},{6,7},{7,6},{8,9},{9,8},{10,11... | collective-permute-start | bytes 393224 | tf_op jit(solution)/shard_map/ppermute | solution.py:77
  26.5 0.0 collective-permute-done.5
  26.5 0.4 %fusion.22 = f32[512,128]{1,0:T(8,128)S(1)} fusion(f32[256,128]{1,0:T(8,128)S(1)} %collective-permute-done.5, f32[512,512]{1,0:T(8,128)S(1)} %fusion.1), kind=kOutput, calls=%fused_computation.26 | convolution fusion | flops 100663296 | bytes 917504 | tf_op jit(solution)/shard_map/dot_general | solution.py:26
  26.9 0.6 %collective-permute-done.4 = f32[256,128]{1,0:T(8,128)S(1)} collective-permute-done((f32[256,128]{1,0:T(8,128)S(1)}, f32[256,128]{1,0:T(8,128)S(1)}, u32[]{:S(2)}, u32[]{:S(2)}) %collective-permute-start.4) | collective-permute-done | bytes 131104 | tf_op jit(solution)/shard_map/ppermute | solution.py:77
  27.5 1.1 %fusion = f32[512,128]{1,0:T(8,128)} fusion(f32[512,128]{1,0:T(8,128)S(1)} %fusion.22, f32[256,128]{1,0:T(8,128)S(1)} %collective-permute-done.4, f32[512,512]{1,0:T(8,128)S(1)} %fusion.1, f32[256,128]{1,0:T(8,128)S(1)} %fusion.18, f32[256,128]{1,0:T(8,128)S(1)} %fusion.20), kind=kOutput, calls=%fused_computation.3 | convolution fusion | flops 100859904 | bytes 1441792 | tf_op jit(solution)/shard_map/dot_general | solution.py:26
  (2 shorter events, 0.1 us)
Async XLA Ops:
  0.6 2.8 %copy-start = (f32[1024,512]{1,0:T(8,128)S(1)}, f32[1024,512]{1,0:T(8,128)}, u32[]{:S(2)}) copy-start(f32[1024,512]{1,0:T(8,128)} %param.8) | copy-start | bytes 6291460
  0.6 2.6 %copy-start.7 = (s32[1,8]{1,0:T(1,128)S(1)}, s32[1,8]{1,0:T(1,128)}, u32[]{:S(2)}) copy-start(s32[1,8]{1,0:T(1,128)} %param.9) | copy-start | bytes 100
  2.8 2.6 %collective-permute-start = (f32[512,256]{1,0:T(8,128)S(1)}, f32[512,256]{1,0:T(8,128)}, u32[]{:S(2)}, u32[]{:S(2)}) collective-permute-start(f32[512,256]{1,0:T(8,128)S(1)} %fusion.16), channel_id=1, source_target_pairs={{0,1},{1,0},{2,3},{3,2},{4,5},{5,4},{6,7},{7,6},{8,9},{9,8},{10,11... | collective-permute-start | bytes 1572872 | tf_op jit(solution)/shard_map/ppermute | solution.py:77
  3.4 2.0 %copy-start.5 = (f32[512,256]{1,0:T(8,128)S(1)}, f32[512,256]{1,0:T(8,128)}, u32[]{:S(2)}) copy-start(f32[512,256]{1,0:T(8,128)} %param.7) | copy-start | bytes 1572868
  5.4 2.1 %copy-start.2 = (f32[512,1024]{1,0:T(8,128)S(1)}, f32[512,1024]{1,0:T(8,128)}, u32[]{:S(2)}) copy-start(f32[512,1024]{1,0:T(8,128)} %param.6) | copy-start | bytes 6291460
  7.5 1.6 %copy-start.1 = (f32[8,128,512]{2,1,0:T(8,128)S(1)}, f32[8,128,512]{2,1,0:T(8,128)}, u32[]{:S(2)}) copy-start(f32[8,128,512]{2,1,0:T(8,128)} %gather_fusion) | copy-start | bytes 6291460
  8.2 3.0 %copy-start.3 = (f32[512,256]{1,0:T(8,128)}, f32[512,256]{1,0:T(8,128)S(1)}, u32[]{:S(2)}) copy-start(f32[512,256]{1,0:T(8,128)S(1)} %fusion.14) | copy-start | bytes 1572868
  9.7 5.8 %copy-start.4 = (f32[512,1024]{1,0:T(8,128)S(1)}, f32[512,1024]{1,0:T(8,128)}, u32[]{:S(2)}) copy-start(f32[512,1024]{1,0:T(8,128)} %param.10) | copy-start | bytes 6291460
  9.7 2.5 %collective-permute-start.1 = (f32[512,128]{1,0:T(8,128)S(1)}, f32[512,128]{1,0:T(8,128)S(1)}, u32[]{:S(2)}, u32[]{:S(2)}) collective-permute-start(f32[512,128]{1,0:T(8,128)S(1)} %fusion.7), channel_id=1, source_target_pairs={{0,1},{1,0},{2,3},{3,2},{4,5},{5,4},{6,7},{7,6},{8,9},{9,8},{10,11... | collective-permute-start | bytes 786440 | tf_op jit(solution)/shard_map/ppermute | solution.py:77
  11.2 5.4 %collective-permute-start.3 = (f32[512,128]{1,0:T(8,128)}, f32[512,128]{1,0:T(8,128)}, u32[]{:S(2)}, u32[]{:S(2)}) collective-permute-start(f32[512,128]{1,0:T(8,128)} %fusion.9), channel_id=1, source_target_pairs={{0,1},{1,0},{2,3},{3,2},{4,5},{5,4},{6,7},{7,6},{8,9},{9,8},{10,11... | collective-permute-start | bytes 786440 | tf_op jit(solution)/shard_map/ppermute | solution.py:77
  12.9 9.8 %collective-permute-start.2 = (f32[512,128]{1,0:T(8,128)}, f32[512,128]{1,0:T(8,128)}, u32[]{:S(2)}, u32[]{:S(2)}) collective-permute-start(f32[512,128]{1,0:T(8,128)} %add.35), channel_id=1, source_target_pairs={{0,2},{2,0},{4,6},{6,4},{8,10},{10,8},{12,14},{14,12},{16,18},{18,... | collective-permute-start | bytes 786440 | tf_op jit(solution)/shard_map/ppermute | solution.py:22
  16.5 7.9 %copy-start.6 = (f32[512,128]{1,0:T(8,128)S(1)}, f32[512,128]{1,0:T(8,128)}, u32[]{:S(2)}) copy-start(f32[512,128]{1,0:T(8,128)} %param.11) | copy-start | bytes 786436
  24.3 2.2 %collective-permute-start.5 = (f32[256,128]{1,0:T(8,128)S(1)}, f32[256,128]{1,0:T(8,128)S(1)}, u32[]{:S(2)}, u32[]{:S(2)}) collective-permute-start(f32[256,128]{1,0:T(8,128)S(1)} %fusion.18), channel_id=1, source_target_pairs={{0,1},{1,0},{2,3},{3,2},{4,5},{5,4},{6,7},{7,6},{8,9},{9,8},{10,11... | collective-permute-start | bytes 393224 | tf_op jit(solution)/shard_map/ppermute | solution.py:77
  25.9 1.5 %collective-permute-start.4 = (f32[256,128]{1,0:T(8,128)S(1)}, f32[256,128]{1,0:T(8,128)S(1)}, u32[]{:S(2)}, u32[]{:S(2)}) collective-permute-start(f32[256,128]{1,0:T(8,128)S(1)} %fusion.20), channel_id=1, source_target_pairs={{0,1},{1,0},{2,3},{3,2},{4,5},{5,4},{6,7},{7,6},{8,9},{9,8},{10,11... | collective-permute-start | bytes 393224 | tf_op jit(solution)/shard_map/ppermute | solution.py:77

commit v24 on v23

--- a/solution.py
+++ b/solution.py
@@ -130,13 +130,14 @@
     diagonal = lax.dynamic_slice_in_dim(parent_factor, section * tile_rows, tile_rows, 1)
     coupling = lower_coupling(parent_factor, diagonal, section, precision)
     arrived = swapped(sent, "leaf", 0)
-    arrived, kept, coupling = lax.optimization_barrier((arrived, kept, coupling))
+    arrived, kept = lax.optimization_barrier((arrived, kept))
     pending = parent_rhs - (kept + arrived)
     half_rows = tile_rows // 2
     first_top = matmul(diagonal[:half_rows], pending, precision)
     arrived_top = pair_swap(first_top, "rows")
     first_bottom = matmul(diagonal[half_rows:], pending, precision)
     arrived_bottom = pair_swap(first_bottom, "rows")
+    arrived_top, arrived_bottom, coupling = lax.optimization_barrier((arrived_top, arrived_bottom, coupling))
     correction = matmul(coupling[:, :half_rows], arrived_top, precision)
     correction = correction + matmul(coupling[:, half_rows:], arrived_bottom, precision)
     parent_solution = jnp.concatenate([first_top, first_bottom], axis=0) - correction

time: 28.8 us -> 26.9 us (0.934)
  matrix products: 14.7 us -> 13.5 us
  other arithmetic: 0.82 us -> 0.13 us
    dot_general x12, matrix products: 14.7 us -> 13.5 us  [matmul(): jnp.dot(left, right, precision=precision, preferred_element_type=jnp.floa...]
    add x1, other arithmetic: 0.73 us -> 0.04 us  [two_section_shards(): sent = own_sent + arrived_sent]
    ppermute x1, waiting for transfers between devices: 4.29 us -> 4.95 us  [swapped(): return lax.ppermute(block, axis, route)]
    ppermute x5, waiting for transfers between devices: 0.61 us -> 0.01 us  [pair_swap(): return lax.ppermute(block, axis, [(0, 1), (1, 0)])]
  transfers between devices with their start and end apart: 6 -> 6, of which waited for: 2 -> 1; matrix products, arithmetic and copies ran while one was open for 33% -> 26% of each run, Pallas kernels for 0% -> 0%
where the time goes in v24:
time: 26.9 us; the launch traced here: 26.7 us
  matrix products  13.5 us (50%)
  waiting for transfers between devices  4.96 us (18%)
  starting transfers between devices  4.27 us (16%)
  local copies, waits for them, and re-layouts  3.01 us (11%)
  between operations  0.82 us (3%)
    dot_general x12, matrix products, matmul(): jnp.dot(left, right, precision=precision, preferred_element_type=jnp.floa...  13.5 us
    ppermute x1, waiting for transfers between devices, swapped(): return lax.ppermute(block, axis, route)  4.95 us
    ppermute x1, starting transfers between devices, swapped(): return lax.ppermute(block, axis, route)  2.6 us
    gather x1, local copies, waits for them, and re-layouts, two_section_shards(): jnp.take(blocks, order, axis=0, mode='clip').reshape(update_panel.shape)  2.01 us
    ppermute x5, starting transfers between devices, pair_swap(): return lax.ppermute(block, axis, [(0, 1), (1, 0)])  1.67 us
    unnamed x16, local copies, waits for them, and re-layouts  0.95 us
  transfers between devices with their start and end apart: 6, of which 1 were waited for; matrix products, arithmetic and copies ran while one was open for 26% of the time, Pallas kernels for 0%

profile of v24, /device:TPU:0, one launch (start us, length us, event | category | flops | bytes accessed | tf_op | source)
XLA Modules:
  0.0 26.7 jit_solution(17349437986696971549)
XLA Ops:
  0.6 0.0 copy-start
  0.6 0.0 copy-start.7
  0.7 2.1 %fusion.16 = f32[512,256]{1,0:T(8,128)S(1)} fusion(f32[512,256]{1,0:T(8,128)} %param.7, f32[512,1024]{1,0:T(8,128)} %param.6, s32[]{:T(128)S(6)} %select_n.37), kind=kOutput, calls=%fused_computation.20 | convolution fusion | flops 402653184 | bytes 2097156 | tf_op jit(solution)/shard_map/dot_general | solution.py:26
  2.8 0.5 %collective-permute-start = (f32[512,256]{1,0:T(8,128)S(1)}, f32[512,256]{1,0:T(8,128)}, u32[]{:S(2)}, u32[]{:S(2)}) collective-permute-start(f32[512,256]{1,0:T(8,128)S(1)} %fusion.16), channel_id=1, source_target_pairs={{0,1},{1,0},{2,3},{3,2},{4,5},{5,4},{6,7},{7,6},{8,9},{9,8},{10,11... | collective-permute-start | bytes 1572872 | tf_op jit(solution)/shard_map/ppermute | solution.py:77
  3.3 0.0 copy-done.7
  3.3 0.1 select_reduce_fusion
  3.4 0.0 copy-done
  3.4 0.0 copy-start.5
  3.4 2.0 %gather_fusion = f32[8,128,512]{2,1,0:T(8,128)} fusion(f32[8,128,512]{2,1,0:T(8,128)S(1)} %bitcast.12, s32[1024]{0:T(1024)S(1)} %pad_clamp_fusion), kind=kCustom, calls=%fused_computation | custom fusion | bytes 4194336 | tf_op jit(solution)/shard_map/jit(_take)/gather | solution.py:109
  5.4 0.0 copy-start.2
  5.4 0.0 collective-permute-done
  5.4 0.0 copy-done.5
  5.4 2.1 %convolution_subtract_fusion = f32[512,256]{1,0:T(8,128)S(1)} fusion(f32[512,256]{1,0:T(8,128)S(1)} %copy-done.5, f32[512,256]{1,0:T(8,128)} %collective-permute-done, f32[512,1024]{1,0:T(8,128)} %param.6, pred[]{:T(512)S(6)} %gt.4), kind=kOutput, calls=%fused_computation.1 | convolution fusion | flops 403046400 | bytes 2621441 | tf_op jit(solution)/shard_map/dot_general | solution.py:26
  7.5 0.0 copy-done.2
  7.5 0.0 copy-start.1
  7.6 0.6 %fusion.14 = f32[512,256]{1,0:T(8,128)S(1)} fusion(f32[512,256]{1,0:T(8,128)S(1)} %convolution_subtract_fusion, f32[512,1024]{1,0:T(8,128)S(1)} %copy-done.2, s32[]{:T(128)S(6)} %select_n.37), kind=kOutput, calls=%fused_computation.18 | convolution fusion | flops 402653184 | bytes 2097156 | tf_op jit(solution)/shard_map/dot_general | solution.py:26
  8.2 0.0 copy-start.3
  8.2 0.9 %copy-done.1 = f32[8,128,512]{2,1,0:T(8,128)S(1)} copy-done((f32[8,128,512]{2,1,0:T(8,128)S(1)}, f32[8,128,512]{2,1,0:T(8,128)}, u32[]{:S(2)}) %copy-start.1) | copy-done | bytes 2097176
  9.1 0.6 %fusion.7 = f32[512,128]{1,0:T(8,128)S(1)} fusion(f32[512,128]{1,0:T(8,128)S(1)} %get-tuple-element.17, f32[1024,512]{1,0:T(8,128)S(1)} %bitcast.14, s32[]{:T(128)S(6)} %select_n.43), kind=kOutput, calls=%fused_computation.11 | convolution fusion | flops 201326592 | bytes 1572868 | tf_op jit(solution)/shard_map/dot_general | solution.py:26
  9.7 0.1 collective-permute-start.1
  9.8 1.3 %fusion.9 = f32[512,128]{1,0:T(8,128)} fusion(f32[512,128]{1,0:T(8,128)S(1)} %get-tuple-element.21, f32[1024,512]{1,0:T(8,128)S(1)} %bitcast.15, s32[]{:T(128)S(6)} %select_n.43), kind=kOutput, calls=%fused_computation.13 | convolution fusion | flops 201326592 | bytes 1572868 | tf_op jit(solution)/shard_map/dot_general | solution.py:26
  11.1 0.0 copy-done.3
  11.1 0.0 copy-start.6
  11.1 0.5 %collective-permute-start.3 = (f32[512,128]{1,0:T(8,128)}, f32[512,128]{1,0:T(8,128)S(1)}, u32[]{:S(2)}, u32[]{:S(2)}) collective-permute-start(f32[512,128]{1,0:T(8,128)} %fusion.9), channel_id=1, source_target_pairs={{0,1},{1,0},{2,3},{3,2},{4,5},{5,4},{6,7},{7,6},{8,9},{9,8},{10,11... | collective-permute-start | bytes 786440 | tf_op jit(solution)/shard_map/ppermute | solution.py:77
  11.6 0.6 %fusion.12 = f32[512,128]{1,0:T(8,128)S(1)} fusion(f32[512,128]{1,0:T(8,128)S(1)} %get-tuple-element.17, f32[1024,512]{1,0:T(8,128)S(1)} %bitcast.16, s32[]{:T(128)S(6)} %select_n.37), kind=kOutput, calls=%fused_computation.16 | convolution fusion | flops 201326592 | bytes 1572868 | tf_op jit(solution)/shard_map/dot_general | solution.py:26
  12.2 0.0 collective-permute-done.1
  12.2 2.6 %collective-permute-start.2 = (f32[512,128]{1,0:T(8,128)S(1)}, f32[512,128]{1,0:T(8,128)S(1)}, u32[]{:S(2)}, u32[]{:S(2)}) collective-permute-start(f32[512,128]{1,0:T(8,128)S(1)} %add.35), channel_id=1, source_target_pairs={{0,2},{2,0},{4,6},{6,4},{8,10},{10,8},{12,14},{14,12},{16,18},{18,... | collective-permute-start | bytes 786440 | tf_op jit(solution)/shard_map/ppermute | solution.py:22
  14.8 0.0 copy-start.4
  14.8 0.0 collective-permute-done.3
  14.8 2.0 %convolution_add_fusion.1 = f32[512,128]{1,0:T(8,128)S(1)} fusion(f32[512,128]{1,0:T(8,128)S(1)} %collective-permute-done.3, f32[512,128]{1,0:T(8,128)S(1)} %get-tuple-element.21, f32[1024,512]{1,0:T(8,128)} %bitcast.13, s32[]{:T(128)S(6)} %select_n.37), kind=kOutput, calls=%fused_computation.4 | convolution fusion | flops 201392128 | bytes 1835012 | tf_op jit(solution)/shard_map/dot_general | solution.py:26
  16.8 4.9 %collective-permute-done.2 = f32[512,128]{1,0:T(8,128)S(1)} collective-permute-done((f32[512,128]{1,0:T(8,128)S(1)}, f32[512,128]{1,0:T(8,128)S(1)}, u32[]{:S(2)}, u32[]{:S(2)}) %collective-permute-start.2) | collective-permute-done | bytes 262176 | tf_op jit(solution)/shard_map/ppermute | solution.py:22
  21.8 0.0 copy-done.6
  21.8 1.4 %fusion.20 = f32[256,128]{1,0:T(8,128)S(1)} fusion(f32[512,1024]{1,0:T(8,128)} %param.10, s32[]{:T(128)S(6)} %select_n.37, f32[512,128]{1,0:T(8,128)S(1)} %copy-done.6, f32[512,128]{1,0:T(8,128)S(1)} %convolution_add_fusion.1, f32[512,128]{1,0:T(8,128)S(1)} %collective-permute-done.2), kind=kOutput, calls=%fused_computation.24 | convolution fusion | flops 100794368 | bytes 1441796 | tf_op jit(solution)/shard_map/dot_general | solution.py:26
  23.2 0.0 copy-done.4
  23.2 0.4 %fusion.18 = f32[256,128]{1,0:T(8,128)S(1)} fusion(f32[512,1024]{1,0:T(8,128)S(1)} %copy-done.4, s32[]{:T(128)S(6)} %add.39, s32[]{:T(128)S(6)} %select_n.37, f32[512,128]{1,0:T(8,128)S(1)} %copy-done.6, f32[512,128]{1,0:T(8,128)S(1)} %convolution_add_fusion.1, f32[512,128]{1,0:T(8,128)S(1)} %collective-permute-done.2), kind=kOutput, calls=%fused_computation.22 | convolution fusion | flops 100794368 | bytes 1441800 | tf_op jit(solution)/shard_map/dot_general | solution.py:26
  23.6 0.1 collective-permute-start.5
  23.7 0.5 %collective-permute-start.4 = (f32[256,128]{1,0:T(8,128)S(1)}, f32[256,128]{1,0:T(8,128)S(1)}, u32[]{:S(2)}, u32[]{:S(2)}) collective-permute-start(f32[256,128]{1,0:T(8,128)S(1)} %fusion.20), channel_id=1, source_target_pairs={{0,1},{1,0},{2,3},{3,2},{4,5},{5,4},{6,7},{7,6},{8,9},{9,8},{10,11... | collective-permute-start | bytes 393224 | tf_op jit(solution)/shard_map/ppermute | solution.py:77
  24.2 1.0 %fusion.1 = f32[512,512]{1,0:T(8,128)S(1)} fusion(f32[512,1024]{1,0:T(8,128)S(1)} %copy-done.4, s32[]{:T(128)S(6)} %select_n.37, pred[]{:T(512)S(6)} %gt.4), kind=kOutput, calls=%fused_computation.5 | convolution fusion | flops 805568512 | bytes 3145733 | tf_op jit(solution)/shard_map/dot_general | solution.py:26
  25.2 0.0 collective-permute-done.5
  25.2 0.0 collective-permute-done.4
  25.3 0.4 %fusion.22 = f32[512,128]{1,0:T(8,128)S(1)} fusion(f32[256,128]{1,0:T(8,128)S(1)} %collective-permute-done.5, f32[512,512]{1,0:T(8,128)S(1)} %fusion.1), kind=kOutput, calls=%fused_computation.26 | convolution fusion | flops 100663296 | bytes 917504 | tf_op jit(solution)/shard_map/dot_general | solution.py:26
  25.6 1.1 %fusion = f32[512,128]{1,0:T(8,128)} fusion(f32[512,128]{1,0:T(8,128)S(1)} %fusion.22, f32[256,128]{1,0:T(8,128)S(1)} %collective-permute-done.4, f32[512,512]{1,0:T(8,128)S(1)} %fusion.1, f32[256,128]{1,0:T(8,128)S(1)} %fusion.18, f32[256,128]{1,0:T(8,128)S(1)} %fusion.20), kind=kOutput, calls=%fused_computation.3 | convolution fusion | flops 100859904 | bytes 1441792 | tf_op jit(solution)/shard_map/dot_general | solution.py:26
  (3 shorter events, 0.1 us)
Async XLA Ops:
  0.6 2.8 %copy-start = (f32[1024,512]{1,0:T(8,128)S(1)}, f32[1024,512]{1,0:T(8,128)}, u32[]{:S(2)}) copy-start(f32[1024,512]{1,0:T(8,128)} %param.8) | copy-start | bytes 6291460
  0.6 2.6 %copy-start.7 = (s32[1,8]{1,0:T(1,128)S(1)}, s32[1,8]{1,0:T(1,128)}, u32[]{:S(2)}) copy-start(s32[1,8]{1,0:T(1,128)} %param.9) | copy-start | bytes 100
  2.8 2.6 %collective-permute-start = (f32[512,256]{1,0:T(8,128)S(1)}, f32[512,256]{1,0:T(8,128)}, u32[]{:S(2)}, u32[]{:S(2)}) collective-permute-start(f32[512,256]{1,0:T(8,128)S(1)} %fusion.16), channel_id=1, source_target_pairs={{0,1},{1,0},{2,3},{3,2},{4,5},{5,4},{6,7},{7,6},{8,9},{9,8},{10,11... | collective-permute-start | bytes 1572872 | tf_op jit(solution)/shard_map/ppermute | solution.py:77
  3.4 2.0 %copy-start.5 = (f32[512,256]{1,0:T(8,128)S(1)}, f32[512,256]{1,0:T(8,128)}, u32[]{:S(2)}) copy-start(f32[512,256]{1,0:T(8,128)} %param.7) | copy-start | bytes 1572868
  5.4 2.1 %copy-start.2 = (f32[512,1024]{1,0:T(8,128)S(1)}, f32[512,1024]{1,0:T(8,128)}, u32[]{:S(2)}) copy-start(f32[512,1024]{1,0:T(8,128)} %param.6) | copy-start | bytes 6291460
  7.5 1.6 %copy-start.1 = (f32[8,128,512]{2,1,0:T(8,128)S(1)}, f32[8,128,512]{2,1,0:T(8,128)}, u32[]{:S(2)}) copy-start(f32[8,128,512]{2,1,0:T(8,128)} %gather_fusion) | copy-start | bytes 6291460
  8.2 3.0 %copy-start.3 = (f32[512,256]{1,0:T(8,128)}, f32[512,256]{1,0:T(8,128)S(1)}, u32[]{:S(2)}) copy-start(f32[512,256]{1,0:T(8,128)S(1)} %fusion.14) | copy-start | bytes 1572868
  9.7 2.5 %collective-permute-start.1 = (f32[512,128]{1,0:T(8,128)S(1)}, f32[512,128]{1,0:T(8,128)S(1)}, u32[]{:S(2)}, u32[]{:S(2)}) collective-permute-start(f32[512,128]{1,0:T(8,128)S(1)} %fusion.7), channel_id=1, source_target_pairs={{0,1},{1,0},{2,3},{3,2},{4,5},{5,4},{6,7},{7,6},{8,9},{9,8},{10,11... | collective-permute-start | bytes 786440 | tf_op jit(solution)/shard_map/ppermute | solution.py:77
  11.1 10.6 %copy-start.6 = (f32[512,128]{1,0:T(8,128)S(1)}, f32[512,128]{1,0:T(8,128)}, u32[]{:S(2)}) copy-start(f32[512,128]{1,0:T(8,128)} %param.11) | copy-start | bytes 786436
  11.1 3.7 %collective-permute-start.3 = (f32[512,128]{1,0:T(8,128)}, f32[512,128]{1,0:T(8,128)S(1)}, u32[]{:S(2)}, u32[]{:S(2)}) collective-permute-start(f32[512,128]{1,0:T(8,128)} %fusion.9), channel_id=1, source_target_pairs={{0,1},{1,0},{2,3},{3,2},{4,5},{5,4},{6,7},{7,6},{8,9},{9,8},{10,11... | collective-permute-start | bytes 786440 | tf_op jit(solution)/shard_map/ppermute | solution.py:77
  12.2 9.5 %collective-permute-start.2 = (f32[512,128]{1,0:T(8,128)S(1)}, f32[512,128]{1,0:T(8,128)S(1)}, u32[]{:S(2)}, u32[]{:S(2)}) collective-permute-start(f32[512,128]{1,0:T(8,128)S(1)} %add.35), channel_id=1, source_target_pairs={{0,2},{2,0},{4,6},{6,4},{8,10},{10,8},{12,14},{14,12},{16,18},{18,... | collective-permute-start | bytes 786440 | tf_op jit(solution)/shard_map/ppermute | solution.py:22
  14.8 8.4 %copy-start.4 = (f32[512,1024]{1,0:T(8,128)S(1)}, f32[512,1024]{1,0:T(8,128)}, u32[]{:S(2)}) copy-start(f32[512,1024]{1,0:T(8,128)} %param.10) | copy-start | bytes 6291460
  23.6 1.6 %collective-permute-start.5 = (f32[256,128]{1,0:T(8,128)S(1)}, f32[256,128]{1,0:T(8,128)S(1)}, u32[]{:S(2)}, u32[]{:S(2)}) collective-permute-start(f32[256,128]{1,0:T(8,128)S(1)} %fusion.18), channel_id=1, source_target_pairs={{0,1},{1,0},{2,3},{3,2},{4,5},{5,4},{6,7},{7,6},{8,9},{9,8},{10,11... | collective-permute-start | bytes 393224 | tf_op jit(solution)/shard_map/ppermute | solution.py:77
  23.7 1.5 %collective-permute-start.4 = (f32[256,128]{1,0:T(8,128)S(1)}, f32[256,128]{1,0:T(8,128)S(1)}, u32[]{:S(2)}, u32[]{:S(2)}) collective-permute-start(f32[256,128]{1,0:T(8,128)S(1)} %fusion.20), channel_id=1, source_target_pairs={{0,1},{1,0},{2,3},{3,2},{4,5},{5,4},{6,7},{7,6},{8,9},{9,8},{10,11... | collective-permute-start | bytes 393224 | tf_op jit(solution)/shard_map/ppermute | solution.py:77

commit v25 on v20

--- a/solution.py
+++ b/solution.py
@@ -89,8 +89,8 @@
     first = matmul(diagonal, right_side, precision)
     arrived = pair_swap(first, "rows")
     arrived, early = lax.optimization_barrier((arrived, early))
-    below = jnp.where(section > 0, factor[:, :tile_rows], jnp.zeros_like(diagonal))
-    return matmul(diagonal, right_side - matmul(below, arrived, precision), precision), early
+    arrived = jnp.where(section > 0, arrived, jnp.zeros_like(arrived))
+    return matmul(diagonal, right_side - matmul(factor[:, :tile_rows], arrived, precision), precision), early
 
 
 def inverse_order(update_blocks):

time: 24.8 us -> 24.9 us (level)
  no operation moved by 1% of the time
where the time goes in v25:
time: 24.9 us; the launch traced here: 24.7 us
  matrix products  9.92 us (40%)
  waiting for transfers between devices  6.87 us (28%)
  starting transfers between devices  3.96 us (16%)
  local copies, waits for them, and re-layouts  3.02 us (12%)
  between operations  0.82 us (3%)
    dot_general x10, matrix products, matmul(): jnp.dot(left, right, precision=precision, preferred_element_type=jnp.floa...  9.92 us
    ppermute x1, waiting for transfers between devices, swapped(): return lax.ppermute(block, axis, route)  6.37 us
    ppermute x1, starting transfers between devices, swapped(): return lax.ppermute(block, axis, route)  2.72 us
    gather x1, local copies, waits for them, and re-layouts, two_section_shards(): jnp.take(blocks, order, axis=0, mode='clip').reshape(update_panel.shape)  2.01 us
    ppermute x4, starting transfers between devices, pair_swap(): return lax.ppermute(block, axis, [(0, 1), (1, 0)])  1.23 us
    unnamed x16, local copies, waits for them, and re-layouts  0.96 us
    ppermute x4, waiting for transfers between devices, pair_swap(): return lax.ppermute(block, axis, [(0, 1), (1, 0)])  0.5 us
  transfers between devices with their start and end apart: 5, of which 2 were waited for; matrix products, arithmetic and copies ran while one was open for 20% of the time, Pallas kernels for 0%

profile of v25, /device:TPU:0, one launch (start us, length us, event | category | flops | bytes accessed | tf_op | source)
XLA Modules:
  0.0 24.7 jit_solution(14867239141469435429)
XLA Ops:
  0.6 0.0 copy-start
  0.6 0.0 copy-start.7
  0.7 2.1 %fusion.17 = f32[512,256]{1,0:T(8,128)S(1)} fusion(f32[512,256]{1,0:T(8,128)} %param.7, f32[512,1024]{1,0:T(8,128)} %param.6, s32[]{:T(128)S(6)} %select_n.41), kind=kOutput, calls=%fused_computation.21 | convolution fusion | flops 402653184 | bytes 2097156 | tf_op jit(solution)/shard_map/dot_general | solution.py:26
  2.8 0.5 %collective-permute-start = (f32[512,256]{1,0:T(8,128)S(1)}, f32[512,256]{1,0:T(8,128)}, u32[]{:S(2)}, u32[]{:S(2)}) collective-permute-start(f32[512,256]{1,0:T(8,128)S(1)} %fusion.17), channel_id=1, source_target_pairs={{0,1},{1,0},{2,3},{3,2},{4,5},{5,4},{6,7},{7,6},{8,9},{9,8},{10,11... | collective-permute-start | bytes 1572872 | tf_op jit(solution)/shard_map/ppermute | solution.py:77
  3.3 0.0 copy-done.7
  3.3 0.1 select_reduce_fusion
  3.4 0.0 copy-done
  3.4 0.0 copy-start.5
  3.4 2.0 %gather_fusion = f32[8,128,512]{2,1,0:T(8,128)} fusion(f32[8,128,512]{2,1,0:T(8,128)S(1)} %bitcast.15, s32[1024]{0:T(1024)S(1)} %pad_clamp_fusion), kind=kCustom, calls=%fused_computation | custom fusion | bytes 4194336 | tf_op jit(solution)/shard_map/jit(_take)/gather | solution.py:109
  5.4 0.0 copy-start.2
  5.4 0.0 collective-permute-done
  5.4 0.0 copy-done.5
  5.4 2.0 %fusion = f32[512,256]{1,0:T(8,128)S(1)} fusion(f32[512,256]{1,0:T(8,128)S(1)} %copy-done.5, f32[512,1024]{1,0:T(8,128)} %param.6, f32[512,256]{1,0:T(8,128)} %collective-permute-done, pred[]{:T(512)S(6)} %gt.4), kind=kOutput, calls=%fused_computation.2 | convolution fusion | flops 402915328 | bytes 2621441 | tf_op jit(solution)/shard_map/dot_general | solution.py:26
  7.4 0.0 copy-done.2
  7.4 0.0 copy-start.1
  7.4 0.6 %fusion.15 = f32[512,256]{1,0:T(8,128)S(1)} fusion(f32[512,256]{1,0:T(8,128)S(1)} %fusion, f32[512,1024]{1,0:T(8,128)S(1)} %copy-done.2, s32[]{:T(128)S(6)} %select_n.41), kind=kOutput, calls=%fused_computation.19 | convolution fusion | flops 402653184 | bytes 2097156 | tf_op jit(solution)/shard_map/dot_general | solution.py:26
  8.0 0.0 copy-start.3
  8.1 0.9 %copy-done.1 = f32[8,128,512]{2,1,0:T(8,128)S(1)} copy-done((f32[8,128,512]{2,1,0:T(8,128)S(1)}, f32[8,128,512]{2,1,0:T(8,128)}, u32[]{:S(2)}) %copy-start.1) | copy-done | bytes 2097176
  9.0 0.6 %fusion.5 = f32[512,128]{1,0:T(8,128)S(1)} fusion(f32[512,128]{1,0:T(8,128)S(1)} %get-tuple-element.16, f32[1024,512]{1,0:T(8,128)S(1)} %bitcast.16, s32[]{:T(128)S(6)} %select_n.47), kind=kOutput, calls=%fused_computation.9 | convolution fusion | flops 201326592 | bytes 1572868 | tf_op jit(solution)/shard_map/dot_general | solution.py:26
  9.6 0.3 %collective-permute-start.1 = (f32[512,128]{1,0:T(8,128)S(1)}, f32[512,128]{1,0:T(8,128)S(1)}, u32[]{:S(2)}, u32[]{:S(2)}) collective-permute-start(f32[512,128]{1,0:T(8,128)S(1)} %fusion.5), channel_id=1, source_target_pairs={{0,1},{1,0},{2,3},{3,2},{4,5},{5,4},{6,7},{7,6},{8,9},{9,8},{10,11... | collective-permute-start | bytes 786440 | tf_op jit(solution)/shard_map/ppermute | solution.py:77
  9.9 0.6 %fusion.7 = f32[512,128]{1,0:T(8,128)S(1)} fusion(f32[512,128]{1,0:T(8,128)S(1)} %get-tuple-element.20, f32[1024,512]{1,0:T(8,128)S(1)} %bitcast.17, s32[]{:T(128)S(6)} %select_n.47), kind=kOutput, calls=%fused_computation.11 | convolution fusion | flops 201326592 | bytes 1572868 | tf_op jit(solution)/shard_map/dot_general | solution.py:26
  10.5 0.0 copy-done.3
  10.5 0.0 copy-start.4
  10.5 0.0 copy-start.6
  10.5 0.4 %collective-permute-start.3 = (f32[512,128]{1,0:T(8,128)S(1)}, f32[512,128]{1,0:T(8,128)S(1)}, u32[]{:S(2)}, u32[]{:S(2)}) collective-permute-start(f32[512,128]{1,0:T(8,128)S(1)} %fusion.7), channel_id=1, source_target_pairs={{0,1},{1,0},{2,3},{3,2},{4,5},{5,4},{6,7},{7,6},{8,9},{9,8},{10,11... | collective-permute-start | bytes 786440 | tf_op jit(solution)/shard_map/ppermute | solution.py:77
  10.9 0.6 %fusion.10 = f32[512,128]{1,0:T(8,128)S(1)} fusion(f32[512,128]{1,0:T(8,128)S(1)} %get-tuple-element.16, f32[1024,512]{1,0:T(8,128)S(1)} %bitcast.18, s32[]{:T(128)S(6)} %select_n.41), kind=kOutput, calls=%fused_computation.14 | convolution fusion | flops 201326592 | bytes 1572868 | tf_op jit(solution)/shard_map/dot_general | solution.py:26
  11.5 0.0 collective-permute-done.1
  11.5 2.7 %collective-permute-start.2 = (f32[512,128]{1,0:T(8,128)S(1)}, f32[512,128]{1,0:T(8,128)S(1)}, u32[]{:S(2)}, u32[]{:S(2)}) collective-permute-start(f32[512,128]{1,0:T(8,128)S(1)} %add.32), channel_id=1, source_target_pairs={{0,2},{2,0},{4,6},{6,4},{8,10},{10,8},{12,14},{14,12},{16,18},{18,... | collective-permute-start | bytes 786440 | tf_op jit(solution)/shard_map/ppermute | solution.py:22
  14.2 0.0 collective-permute-done.3
  14.2 0.6 %convolution_add_fusion = f32[512,128]{1,0:T(8,128)S(1)} fusion(f32[512,128]{1,0:T(8,128)S(1)} %collective-permute-done.3, f32[512,128]{1,0:T(8,128)S(1)} %get-tuple-element.20, f32[1024,512]{1,0:T(8,128)S(1)} %bitcast.19, s32[]{:T(128)S(6)} %select_n.41), kind=kOutput, calls=%fused_computation.4 | convolution fusion | flops 201392128 | bytes 1835012 | tf_op jit(solution)/shard_map/dot_general | solution.py:26
  14.8 6.4 %collective-permute-done.2 = f32[512,128]{1,0:T(8,128)S(1)} collective-permute-done((f32[512,128]{1,0:T(8,128)S(1)}, f32[512,128]{1,0:T(8,128)S(1)}, u32[]{:S(2)}, u32[]{:S(2)}) %collective-permute-start.2) | collective-permute-done | bytes 262176 | tf_op jit(solution)/shard_map/ppermute | solution.py:22
  21.2 0.0 copy-done.4
  21.2 0.0 copy-done.6
  21.2 0.6 %fusion.13 = f32[512,128]{1,0:T(8,128)S(1)} fusion(f32[512,1024]{1,0:T(8,128)S(1)} %copy-done.4, s32[]{:T(128)S(6)} %select_n.41, f32[512,128]{1,0:T(8,128)S(1)} %copy-done.6, f32[512,128]{1,0:T(8,128)S(1)} %convolution_add_fusion, f32[512,128]{1,0:T(8,128)S(1)} %collective-permute-done.2), kind=kOutput, calls=%fused_computation.17 | convolution fusion | flops 201457664 | bytes 2097156 | tf_op jit(solution)/shard_map/dot_general | solution.py:26
  21.8 0.1 collective-permute-start.4
  21.9 1.0 %fusion.1 = f32[512,512]{1,0:T(8,128)S(1)} fusion(f32[512,1024]{1,0:T(8,128)S(1)} %copy-done.4, s32[]{:T(128)S(6)} %select_n.41, pred[]{:T(512)S(6)} %gt.4), kind=kOutput, calls=%fused_computation.5 | convolution fusion | flops 805568512 | bytes 3145733 | tf_op jit(solution)/shard_map/dot_general | solution.py:26
  22.9 0.5 %collective-permute-done.4 = f32[512,128]{1,0:T(8,128)S(1)} collective-permute-done((f32[512,128]{1,0:T(8,128)S(1)}, f32[512,128]{1,0:T(8,128)S(1)}, u32[]{:S(2)}, u32[]{:S(2)}) %collective-permute-start.4) | collective-permute-done | bytes 262176 | tf_op jit(solution)/shard_map/ppermute | solution.py:77
  23.4 1.3 %convolution_subtract_fusion = f32[512,128]{1,0:T(8,128)} fusion(f32[512,128]{1,0:T(8,128)S(1)} %fusion.13, f32[512,512]{1,0:T(8,128)S(1)} %fusion.1, f32[512,128]{1,0:T(8,128)S(1)} %collective-permute-done.4), kind=kOutput, calls=%fused_computation.3 | convolution fusion | flops 201392128 | bytes 1835008 | tf_op jit(solution)/shard_map/dot_general | solution.py:26
  (3 shorter events, 0.1 us)
Async XLA Ops:
  0.6 2.8 %copy-start = (f32[1024,512]{1,0:T(8,128)S(1)}, f32[1024,512]{1,0:T(8,128)}, u32[]{:S(2)}) copy-start(f32[1024,512]{1,0:T(8,128)} %param.8) | copy-start | bytes 6291460
  0.6 2.6 %copy-start.7 = (s32[1,8]{1,0:T(1,128)S(1)}, s32[1,8]{1,0:T(1,128)}, u32[]{:S(2)}) copy-start(s32[1,8]{1,0:T(1,128)} %param.9) | copy-start | bytes 100
  2.8 2.6 %collective-permute-start = (f32[512,256]{1,0:T(8,128)S(1)}, f32[512,256]{1,0:T(8,128)}, u32[]{:S(2)}, u32[]{:S(2)}) collective-permute-start(f32[512,256]{1,0:T(8,128)S(1)} %fusion.17), channel_id=1, source_target_pairs={{0,1},{1,0},{2,3},{3,2},{4,5},{5,4},{6,7},{7,6},{8,9},{9,8},{10,11... | collective-permute-start | bytes 1572872 | tf_op jit(solution)/shard_map/ppermute | solution.py:77
  3.4 2.0 %copy-start.5 = (f32[512,256]{1,0:T(8,128)S(1)}, f32[512,256]{1,0:T(8,128)}, u32[]{:S(2)}) copy-start(f32[512,256]{1,0:T(8,128)} %param.7) | copy-start | bytes 1572868
  5.4 2.0 %copy-start.2 = (f32[512,1024]{1,0:T(8,128)S(1)}, f32[512,1024]{1,0:T(8,128)}, u32[]{:S(2)}) copy-start(f32[512,1024]{1,0:T(8,128)} %param.6) | copy-start | bytes 6291460
  7.4 1.6 %copy-start.1 = (f32[8,128,512]{2,1,0:T(8,128)S(1)}, f32[8,128,512]{2,1,0:T(8,128)}, u32[]{:S(2)}) copy-start(f32[8,128,512]{2,1,0:T(8,128)} %gather_fusion) | copy-start | bytes 6291460
  8.0 2.4 %copy-start.3 = (f32[512,256]{1,0:T(8,128)}, f32[512,256]{1,0:T(8,128)S(1)}, u32[]{:S(2)}) copy-start(f32[512,256]{1,0:T(8,128)S(1)} %fusion.15) | copy-start | bytes 1572868
  9.6 1.9 %collective-permute-start.1 = (f32[512,128]{1,0:T(8,128)S(1)}, f32[512,128]{1,0:T(8,128)S(1)}, u32[]{:S(2)}, u32[]{:S(2)}) collective-permute-start(f32[512,128]{1,0:T(8,128)S(1)} %fusion.5), channel_id=1, source_target_pairs={{0,1},{1,0},{2,3},{3,2},{4,5},{5,4},{6,7},{7,6},{8,9},{9,8},{10,11... | collective-permute-start | bytes 786440 | tf_op jit(solution)/shard_map/ppermute | solution.py:77
  10.5 10.7 %copy-start.4 = (f32[512,1024]{1,0:T(8,128)S(1)}, f32[512,1024]{1,0:T(8,128)}, u32[]{:S(2)}) copy-start(f32[512,1024]{1,0:T(8,128)} %param.10) | copy-start | bytes 6291460
  10.5 10.7 %copy-start.6 = (f32[512,128]{1,0:T(8,128)S(1)}, f32[512,128]{1,0:T(8,128)}, u32[]{:S(2)}) copy-start(f32[512,128]{1,0:T(8,128)} %param.11) | copy-start | bytes 786436
  10.5 3.7 %collective-permute-start.3 = (f32[512,128]{1,0:T(8,128)S(1)}, f32[512,128]{1,0:T(8,128)S(1)}, u32[]{:S(2)}, u32[]{:S(2)}) collective-permute-start(f32[512,128]{1,0:T(8,128)S(1)} %fusion.7), channel_id=1, source_target_pairs={{0,1},{1,0},{2,3},{3,2},{4,5},{5,4},{6,7},{7,6},{8,9},{9,8},{10,11... | collective-permute-start | bytes 786440 | tf_op jit(solution)/shard_map/ppermute | solution.py:77
  11.5 9.7 %collective-permute-start.2 = (f32[512,128]{1,0:T(8,128)S(1)}, f32[512,128]{1,0:T(8,128)S(1)}, u32[]{:S(2)}, u32[]{:S(2)}) collective-permute-start(f32[512,128]{1,0:T(8,128)S(1)} %add.32), channel_id=1, source_target_pairs={{0,2},{2,0},{4,6},{6,4},{8,10},{10,8},{12,14},{14,12},{16,18},{18,... | collective-permute-start | bytes 786440 | tf_op jit(solution)/shard_map/ppermute | solution.py:22
  21.8 1.6 %collective-permute-start.4 = (f32[512,128]{1,0:T(8,128)S(1)}, f32[512,128]{1,0:T(8,128)S(1)}, u32[]{:S(2)}, u32[]{:S(2)}) collective-permute-start(f32[512,128]{1,0:T(8,128)S(1)} %fusion.13), channel_id=1, source_target_pairs={{0,1},{1,0},{2,3},{3,2},{4,5},{5,4},{6,7},{7,6},{8,9},{9,8},{10,11... | collective-permute-start | bytes 786440 | tf_op jit(solution)/shard_map/ppermute | solution.py:77

commit v26 on v18

--- a/solution.py
+++ b/solution.py
@@ -116,14 +116,15 @@
     sibling = lax.axis_index("leaf") % 2
     solution_kept = lax.dynamic_slice_in_dim(leaf_solution, sibling * column_half, column_half, 1)
     solution_sent = lax.dynamic_slice_in_dim(leaf_solution, (1 - sibling) * column_half, column_half, 1)
+    other_kept = matmul(panel_other, solution_kept, precision)
+    arrived_kept = pair_swap(other_kept, "rows")
+    solution_sent, other_kept = lax.optimization_barrier((solution_sent, other_kept))
     other_sent = matmul(panel_other, solution_sent, precision)
     arrived_sent = pair_swap(other_sent, "rows")
     own_sent = matmul(panel_own, solution_sent, precision)
     own_sent, arrived_sent = lax.optimization_barrier((own_sent, arrived_sent))
     sent = own_sent + arrived_sent
     sent, solution_kept = lax.optimization_barrier((sent, solution_kept))
-    other_kept = matmul(panel_other, solution_kept, precision)
-    arrived_kept = pair_swap(other_kept, "rows")
     kept = matmul(panel_own, solution_kept, precision) + arrived_kept
     tile_rows = parent_rhs.shape[0]
     diagonal = lax.dynamic_slice_in_dim(parent_factor, section * tile_rows, tile_rows, 1)

time: 25.2 us -> 25.2 us (level)
  matrix products: 11.4 us -> 10 us
  local copies, waits for them, and re-layouts: 2.09 us -> 3.02 us
  waiting for transfers between devices: 6.81 us -> 7.17 us
    dot_general x10, matrix products: 11.4 us -> 10 us  [matmul(): jnp.dot(left, right, precision=precision, preferred_element_type=jnp.floa...]
    unnamed x18 -> x16, local copies, waits for them, and re-layouts: 0.05 us -> 0.96 us
    ppermute x4, waiting for transfers between devices: 0.51 us -> 0.94 us  [pair_swap(): return lax.ppermute(block, axis, [(0, 1), (1, 0)])]
  transfers between devices with their start and end apart: 5 -> 5, of which waited for: 2 -> 3; matrix products, arithmetic and copies ran while one was open for 23% -> 17% of each run, Pallas kernels for 0% -> 0%
where the time goes in v26:
time: 25.2 us; the launch traced here: 25 us
  matrix products  10 us (40%)
  waiting for transfers between devices  7.17 us (28%)
  starting transfers between devices  3.87 us (15%)
  local copies, waits for them, and re-layouts  3.02 us (12%)
  between operations  0.8 us (3%)
    dot_general x10, matrix products, matmul(): jnp.dot(left, right, precision=precision, preferred_element_type=jnp.floa...  10 us
    ppermute x1, waiting for transfers between devices, swapped(): return lax.ppermute(block, axis, route)  6.23 us
    ppermute x1, starting transfers between devices, swapped(): return lax.ppermute(block, axis, route)  2.71 us
    gather x1, local copies, waits for them, and re-layouts, two_section_shards(): jnp.take(blocks, order, axis=0, mode='clip').reshape(update_panel.shape)  2.01 us
    ppermute x4, starting transfers between devices, pair_swap(): return lax.ppermute(block, axis, [(0, 1), (1, 0)])  1.16 us
    unnamed x16, local copies, waits for them, and re-layouts  0.96 us
    ppermute x4, waiting for transfers between devices, pair_swap(): return lax.ppermute(block, axis, [(0, 1), (1, 0)])  0.94 us
  transfers between devices with their start and end apart: 5, of which 3 were waited for; matrix products, arithmetic and copies ran while one was open for 17% of the time, Pallas kernels for 0%

profile of v26, /device:TPU:0, one launch (start us, length us, event | category | flops | bytes accessed | tf_op | source)
XLA Modules:
  0.0 25.0 jit_solution(7896830842997162506)
XLA Ops:
  0.6 0.0 copy-start
  0.6 0.0 copy-start.7
  0.7 2.1 %fusion.17 = f32[512,256]{1,0:T(8,128)S(1)} fusion(f32[512,256]{1,0:T(8,128)} %param.7, f32[512,1024]{1,0:T(8,128)} %param.6, s32[]{:T(128)S(6)} %select_n.37), kind=kOutput, calls=%fused_computation.21 | convolution fusion | flops 402653184 | bytes 2097156 | tf_op jit(solution)/shard_map/dot_general | solution.py:26
  2.8 0.5 %collective-permute-start = (f32[512,256]{1,0:T(8,128)S(1)}, f32[512,256]{1,0:T(8,128)}, u32[]{:S(2)}, u32[]{:S(2)}) collective-permute-start(f32[512,256]{1,0:T(8,128)S(1)} %fusion.17), channel_id=1, source_target_pairs={{0,1},{1,0},{2,3},{3,2},{4,5},{5,4},{6,7},{7,6},{8,9},{9,8},{10,11... | collective-permute-start | bytes 1572872 | tf_op jit(solution)/shard_map/ppermute | solution.py:77
  3.3 0.0 copy-done.7
  3.3 0.1 select_reduce_fusion
  3.4 0.0 copy-done
  3.4 0.0 copy-start.5
  3.4 2.0 %gather_fusion = f32[8,128,512]{2,1,0:T(8,128)} fusion(f32[8,128,512]{2,1,0:T(8,128)S(1)} %bitcast.12, s32[1024]{0:T(1024)S(1)} %pad_clamp_fusion), kind=kCustom, calls=%fused_computation | custom fusion | bytes 4194336 | tf_op jit(solution)/shard_map/jit(_take)/gather | solution.py:109
  5.4 0.0 copy-start.2
  5.4 0.0 collective-permute-done
  5.4 0.0 copy-done.5
  5.4 2.1 %convolution_subtract_fusion = f32[512,256]{1,0:T(8,128)S(1)} fusion(f32[512,256]{1,0:T(8,128)S(1)} %copy-done.5, f32[512,256]{1,0:T(8,128)} %collective-permute-done, f32[512,1024]{1,0:T(8,128)} %param.6, pred[]{:T(512)S(6)} %gt.4), kind=kOutput, calls=%fused_computation.1 | convolution fusion | flops 403046400 | bytes 2621441 | tf_op jit(solution)/shard_map/dot_general | solution.py:26
  7.5 0.0 copy-done.2
  7.5 0.0 copy-start.1
  7.5 0.6 %fusion.15 = f32[512,256]{1,0:T(8,128)S(1)} fusion(f32[512,256]{1,0:T(8,128)S(1)} %convolution_subtract_fusion, f32[512,1024]{1,0:T(8,128)S(1)} %copy-done.2, s32[]{:T(128)S(6)} %select_n.37), kind=kOutput, calls=%fused_computation.19 | convolution fusion | flops 402653184 | bytes 2097156 | tf_op jit(solution)/shard_map/dot_general | solution.py:26
  8.1 0.0 copy-start.3
  8.2 0.9 %copy-done.1 = f32[8,128,512]{2,1,0:T(8,128)S(1)} copy-done((f32[8,128,512]{2,1,0:T(8,128)S(1)}, f32[8,128,512]{2,1,0:T(8,128)}, u32[]{:S(2)}) %copy-start.1) | copy-done | bytes 2097176
  9.1 0.6 %fusion.7 = f32[512,128]{1,0:T(8,128)S(1)} fusion(f32[512,128]{1,0:T(8,128)S(1)} %get-tuple-element.19, f32[1024,512]{1,0:T(8,128)S(1)} %bitcast.13, s32[]{:T(128)S(6)} %select_n.43), kind=kOutput, calls=%fused_computation.11 | convolution fusion | flops 201326592 | bytes 1572868 | tf_op jit(solution)/shard_map/dot_general | solution.py:26
  9.7 0.6 %fusion.5 = f32[512,128]{1,0:T(8,128)S(1)} fusion(f32[512,128]{1,0:T(8,128)S(1)} %get-tuple-element.15, f32[1024,512]{1,0:T(8,128)S(1)} %bitcast.14, s32[]{:T(128)S(6)} %select_n.43), kind=kOutput, calls=%fused_computation.9 | convolution fusion | flops 201326592 | bytes 1572868 | tf_op jit(solution)/shard_map/dot_general | solution.py:26
  10.3 0.0 copy-done.3
  10.3 0.0 copy-start.4
  10.3 0.0 copy-start.6
  10.3 0.1 collective-permute-start.1
  10.5 0.4 %collective-permute-start.3 = (f32[512,128]{1,0:T(8,128)S(1)}, f32[512,128]{1,0:T(8,128)S(1)}, u32[]{:S(2)}, u32[]{:S(2)}) collective-permute-start(f32[512,128]{1,0:T(8,128)S(1)} %fusion.7), channel_id=1, source_target_pairs={{0,1},{1,0},{2,3},{3,2},{4,5},{5,4},{6,7},{7,6},{8,9},{9,8},{10,11... | collective-permute-start | bytes 786440 | tf_op jit(solution)/shard_map/ppermute | solution.py:77
  10.9 0.6 %fusion.10 = f32[512,128]{1,0:T(8,128)S(1)} fusion(f32[512,128]{1,0:T(8,128)S(1)} %get-tuple-element.15, f32[1024,512]{1,0:T(8,128)S(1)} %bitcast.15, s32[]{:T(128)S(6)} %select_n.37), kind=kOutput, calls=%fused_computation.14 | convolution fusion | flops 201326592 | bytes 1572868 | tf_op jit(solution)/shard_map/dot_general | solution.py:26
  11.5 0.4 %collective-permute-done.1 = f32[512,128]{1,0:T(8,128)S(1)} collective-permute-done((f32[512,128]{1,0:T(8,128)S(1)}, f32[512,128]{1,0:T(8,128)S(1)}, u32[]{:S(2)}, u32[]{:S(2)}) %collective-permute-start.1) | collective-permute-done | bytes 262176 | tf_op jit(solution)/shard_map/ppermute | solution.py:77
  12.0 2.7 %collective-permute-start.2 = (f32[512,128]{1,0:T(8,128)S(1)}, f32[512,128]{1,0:T(8,128)S(1)}, u32[]{:S(2)}, u32[]{:S(2)}) collective-permute-start(f32[512,128]{1,0:T(8,128)S(1)} %add.32), channel_id=1, source_target_pairs={{0,2},{2,0},{4,6},{6,4},{8,10},{10,8},{12,14},{14,12},{16,18},{18,... | collective-permute-start | bytes 786440 | tf_op jit(solution)/shard_map/ppermute | solution.py:22
  14.7 0.0 collective-permute-done.3
  14.7 0.6 %convolution_add_fusion = f32[512,128]{1,0:T(8,128)S(1)} fusion(f32[512,128]{1,0:T(8,128)S(1)} %collective-permute-done.3, f32[512,128]{1,0:T(8,128)S(1)} %get-tuple-element.19, f32[1024,512]{1,0:T(8,128)S(1)} %bitcast.16, s32[]{:T(128)S(6)} %select_n.37), kind=kOutput, calls=%fused_computation.3 | convolution fusion | flops 201392128 | bytes 1835012 | tf_op jit(solution)/shard_map/dot_general | solution.py:26
  15.3 6.2 %collective-permute-done.2 = f32[512,128]{1,0:T(8,128)S(1)} collective-permute-done((f32[512,128]{1,0:T(8,128)S(1)}, f32[512,128]{1,0:T(8,128)S(1)}, u32[]{:S(2)}, u32[]{:S(2)}) %collective-permute-start.2) | collective-permute-done | bytes 262176 | tf_op jit(solution)/shard_map/ppermute | solution.py:22
  21.5 0.0 copy-done.4
  21.5 0.0 copy-done.6
  21.5 0.6 %fusion.13 = f32[512,128]{1,0:T(8,128)S(1)} fusion(f32[512,1024]{1,0:T(8,128)S(1)} %copy-done.4, s32[]{:T(128)S(6)} %select_n.37, f32[512,128]{1,0:T(8,128)S(1)} %copy-done.6, f32[512,128]{1,0:T(8,128)S(1)} %convolution_add_fusion, f32[512,128]{1,0:T(8,128)S(1)} %collective-permute-done.2), kind=kOutput, calls=%fused_computation.17 | convolution fusion | flops 201457664 | bytes 2097156 | tf_op jit(solution)/shard_map/dot_general | solution.py:26
  22.1 0.1 collective-permute-start.4
  22.2 1.0 %fusion = f32[512,512]{1,0:T(8,128)S(1)} fusion(f32[512,1024]{1,0:T(8,128)S(1)} %copy-done.4, s32[]{:T(128)S(6)} %select_n.37, pred[]{:T(512)S(6)} %gt.4), kind=kOutput, calls=%fused_computation.4 | convolution fusion | flops 805568512 | bytes 3145733 | tf_op jit(solution)/shard_map/dot_general | solution.py:26
  23.2 0.5 %collective-permute-done.4 = f32[512,128]{1,0:T(8,128)S(1)} collective-permute-done((f32[512,128]{1,0:T(8,128)S(1)}, f32[512,128]{1,0:T(8,128)S(1)}, u32[]{:S(2)}, u32[]{:S(2)}) %collective-permute-start.4) | collective-permute-done | bytes 262176 | tf_op jit(solution)/shard_map/ppermute | solution.py:77
  23.7 1.3 %convolution_subtract_fusion.1 = f32[512,128]{1,0:T(8,128)} fusion(f32[512,128]{1,0:T(8,128)S(1)} %fusion.13, f32[512,512]{1,0:T(8,128)S(1)} %fusion, f32[512,128]{1,0:T(8,128)S(1)} %collective-permute-done.4), kind=kOutput, calls=%fused_computation.2 | convolution fusion | flops 201392128 | bytes 1835008 | tf_op jit(solution)/shard_map/dot_general | solution.py:26
  (3 shorter events, 0.1 us)
Async XLA Ops:
  0.6 2.8 %copy-start = (f32[1024,512]{1,0:T(8,128)S(1)}, f32[1024,512]{1,0:T(8,128)}, u32[]{:S(2)}) copy-start(f32[1024,512]{1,0:T(8,128)} %param.8) | copy-start | bytes 6291460
  0.6 2.6 %copy-start.7 = (s32[1,8]{1,0:T(1,128)S(1)}, s32[1,8]{1,0:T(1,128)}, u32[]{:S(2)}) copy-start(s32[1,8]{1,0:T(1,128)} %param.9) | copy-start | bytes 100
  2.8 2.6 %collective-permute-start = (f32[512,256]{1,0:T(8,128)S(1)}, f32[512,256]{1,0:T(8,128)}, u32[]{:S(2)}, u32[]{:S(2)}) collective-permute-start(f32[512,256]{1,0:T(8,128)S(1)} %fusion.17), channel_id=1, source_target_pairs={{0,1},{1,0},{2,3},{3,2},{4,5},{5,4},{6,7},{7,6},{8,9},{9,8},{10,11... | collective-permute-start | bytes 1572872 | tf_op jit(solution)/shard_map/ppermute | solution.py:77
  3.4 2.0 %copy-start.5 = (f32[512,256]{1,0:T(8,128)S(1)}, f32[512,256]{1,0:T(8,128)}, u32[]{:S(2)}) copy-start(f32[512,256]{1,0:T(8,128)} %param.7) | copy-start | bytes 1572868
  5.4 2.1 %copy-start.2 = (f32[512,1024]{1,0:T(8,128)S(1)}, f32[512,1024]{1,0:T(8,128)}, u32[]{:S(2)}) copy-start(f32[512,1024]{1,0:T(8,128)} %param.6) | copy-start | bytes 6291460
  7.5 1.6 %copy-start.1 = (f32[8,128,512]{2,1,0:T(8,128)S(1)}, f32[8,128,512]{2,1,0:T(8,128)}, u32[]{:S(2)}) copy-start(f32[8,128,512]{2,1,0:T(8,128)} %gather_fusion) | copy-start | bytes 6291460
  8.1 2.2 %copy-start.3 = (f32[512,256]{1,0:T(8,128)}, f32[512,256]{1,0:T(8,128)S(1)}, u32[]{:S(2)}) copy-start(f32[512,256]{1,0:T(8,128)S(1)} %fusion.15) | copy-start | bytes 1572868
  10.3 11.2 %copy-start.4 = (f32[512,1024]{1,0:T(8,128)S(1)}, f32[512,1024]{1,0:T(8,128)}, u32[]{:S(2)}) copy-start(f32[512,1024]{1,0:T(8,128)} %param.10) | copy-start | bytes 6291460
  10.3 11.2 %copy-start.6 = (f32[512,128]{1,0:T(8,128)S(1)}, f32[512,128]{1,0:T(8,128)}, u32[]{:S(2)}) copy-start(f32[512,128]{1,0:T(8,128)} %param.11) | copy-start | bytes 786436
  10.3 1.6 %collective-permute-start.1 = (f32[512,128]{1,0:T(8,128)S(1)}, f32[512,128]{1,0:T(8,128)S(1)}, u32[]{:S(2)}, u32[]{:S(2)}) collective-permute-start(f32[512,128]{1,0:T(8,128)S(1)} %fusion.5), channel_id=1, source_target_pairs={{0,1},{1,0},{2,3},{3,2},{4,5},{5,4},{6,7},{7,6},{8,9},{9,8},{10,11... | collective-permute-start | bytes 786440 | tf_op jit(solution)/shard_map/ppermute | solution.py:77
  10.5 4.2 %collective-permute-start.3 = (f32[512,128]{1,0:T(8,128)S(1)}, f32[512,128]{1,0:T(8,128)S(1)}, u32[]{:S(2)}, u32[]{:S(2)}) collective-permute-start(f32[512,128]{1,0:T(8,128)S(1)} %fusion.7), channel_id=1, source_target_pairs={{0,1},{1,0},{2,3},{3,2},{4,5},{5,4},{6,7},{7,6},{8,9},{9,8},{10,11... | collective-permute-start | bytes 786440 | tf_op jit(solution)/shard_map/ppermute | solution.py:77
  12.0 9.5 %collective-permute-start.2 = (f32[512,128]{1,0:T(8,128)S(1)}, f32[512,128]{1,0:T(8,128)S(1)}, u32[]{:S(2)}, u32[]{:S(2)}) collective-permute-start(f32[512,128]{1,0:T(8,128)S(1)} %add.32), channel_id=1, source_target_pairs={{0,2},{2,0},{4,6},{6,4},{8,10},{10,8},{12,14},{14,12},{16,18},{18,... | collective-permute-start | bytes 786440 | tf_op jit(solution)/shard_map/ppermute | solution.py:22
  22.1 1.6 %collective-permute-start.4 = (f32[512,128]{1,0:T(8,128)S(1)}, f32[512,128]{1,0:T(8,128)S(1)}, u32[]{:S(2)}, u32[]{:S(2)}) collective-permute-start(f32[512,128]{1,0:T(8,128)S(1)} %fusion.13), channel_id=1, source_target_pairs={{0,1},{1,0},{2,3},{3,2},{4,5},{5,4},{6,7},{7,6},{8,9},{9,8},{10,11... | collective-permute-start | bytes 786440 | tf_op jit(solution)/shard_map/ppermute | solution.py:77

commit v27 on v20

--- a/solution.py
+++ b/solution.py
@@ -106,7 +106,7 @@
     blocks = update_panel.reshape(-1, ROW_BLOCK, update_panel.shape[1])
     order = inverse_order(update_blocks)
 
-    placed_panel = jnp.take(blocks, order, axis=0, mode="clip").reshape(update_panel.shape)
+    placed_panel = blocks.at[order].get(mode="promise_in_bounds").reshape(update_panel.shape)
     placed_panel = two_section_leaf(leaf_factor, leaf_rhs, section, precision, placed_panel)
     leaf_solution, placed_panel = placed_panel
     rows_half = placed_panel.shape[0] // 2

time: 24.8 us -> 24.8 us (level)
  no operation moved by 1% of the time
where the time goes in v27:
time: 24.8 us; the launch traced here: 24.7 us
  matrix products  10 us (40%)
  waiting for transfers between devices  6.83 us (28%)
  starting transfers between devices  3.84 us (15%)
  local copies, waits for them, and re-layouts  3.02 us (12%)
  between operations  0.82 us (3%)
    dot_general x10, matrix products, matmul(): jnp.dot(left, right, precision=precision, preferred_element_type=jnp.floa...  10 us
    ppermute x1, waiting for transfers between devices, swapped(): return lax.ppermute(block, axis, route)  6.33 us
    ppermute x1, starting transfers between devices, swapped(): return lax.ppermute(block, axis, route)  2.6 us
    gather x1, local copies, waits for them, and re-layouts, two_section_shards(): blocks.at[order].get(mode='promise_in_bounds').reshape(update_panel.shape)  2.01 us
    ppermute x4, starting transfers between devices, pair_swap(): return lax.ppermute(block, axis, [(0, 1), (1, 0)])  1.23 us
    unnamed x16, local copies, waits for them, and re-layouts  0.96 us
    ppermute x4, waiting for transfers between devices, pair_swap(): return lax.ppermute(block, axis, [(0, 1), (1, 0)])  0.5 us
  transfers between devices with their start and end apart: 5, of which 2 were waited for; matrix products, arithmetic and copies ran while one was open for 20% of the time, Pallas kernels for 0%

profile of v27, /device:TPU:0, one launch (start us, length us, event | category | flops | bytes accessed | tf_op | source)
XLA Modules:
  0.0 24.7 jit_solution(11665822468487043813)
XLA Ops:
  0.6 0.0 copy-start
  0.6 0.0 copy-start.7
  0.7 2.1 %fusion.17 = f32[512,256]{1,0:T(8,128)S(1)} fusion(f32[512,256]{1,0:T(8,128)} %param.7, f32[512,1024]{1,0:T(8,128)} %param.6, s32[]{:T(128)S(6)} %select_n.47), kind=kOutput, calls=%fused_computation.21 | convolution fusion | flops 402653184 | bytes 2097156 | tf_op jit(solution)/shard_map/dot_general | solution.py:26
  2.8 0.5 %collective-permute-start = (f32[512,256]{1,0:T(8,128)S(1)}, f32[512,256]{1,0:T(8,128)}, u32[]{:S(2)}, u32[]{:S(2)}) collective-permute-start(f32[512,256]{1,0:T(8,128)S(1)} %fusion.17), channel_id=1, source_target_pairs={{0,1},{1,0},{2,3},{3,2},{4,5},{5,4},{6,7},{7,6},{8,9},{9,8},{10,11... | collective-permute-start | bytes 1572872 | tf_op jit(solution)/shard_map/ppermute | solution.py:77
  3.3 0.0 copy-done.7
  3.3 0.1 select_reduce_fusion
  3.4 0.0 copy-done
  3.4 0.0 copy-start.5
  3.4 2.0 %gather_fusion = f32[8,128,512]{2,1,0:T(8,128)} fusion(f32[8,128,512]{2,1,0:T(8,128)S(1)} %bitcast.16, s32[1024]{0:T(1024)S(1)} %pad_clamp_fusion), kind=kCustom, calls=%fused_computation | custom fusion | bytes 4194336 | tf_op jit(solution)/shard_map/gather | solution.py:109
  5.4 0.0 copy-start.2
  5.4 0.0 collective-permute-done
  5.4 0.0 copy-done.5
  5.4 2.1 %convolution_subtract_fusion = f32[512,256]{1,0:T(8,128)S(1)} fusion(f32[512,256]{1,0:T(8,128)S(1)} %copy-done.5, f32[512,256]{1,0:T(8,128)} %collective-permute-done, f32[512,1024]{1,0:T(8,128)} %param.6, pred[]{:T(512)S(6)} %gt.4), kind=kOutput, calls=%fused_computation.1 | convolution fusion | flops 403046400 | bytes 2621441 | tf_op jit(solution)/shard_map/dot_general | solution.py:26
  7.5 0.0 copy-done.2
  7.6 0.0 copy-start.1
  7.6 0.6 %fusion.15 = f32[512,256]{1,0:T(8,128)S(1)} fusion(f32[512,256]{1,0:T(8,128)S(1)} %convolution_subtract_fusion, f32[512,1024]{1,0:T(8,128)S(1)} %copy-done.2, s32[]{:T(128)S(6)} %select_n.47), kind=kOutput, calls=%fused_computation.19 | convolution fusion | flops 402653184 | bytes 2097156 | tf_op jit(solution)/shard_map/dot_general | solution.py:26
  8.2 0.0 copy-start.3
  8.2 0.9 %copy-done.1 = f32[8,128,512]{2,1,0:T(8,128)S(1)} copy-done((f32[8,128,512]{2,1,0:T(8,128)S(1)}, f32[8,128,512]{2,1,0:T(8,128)}, u32[]{:S(2)}) %copy-start.1) | copy-done | bytes 2097176
  9.1 0.6 %fusion.5 = f32[512,128]{1,0:T(8,128)S(1)} fusion(f32[512,128]{1,0:T(8,128)S(1)} %get-tuple-element.16, f32[1024,512]{1,0:T(8,128)S(1)} %bitcast.17, s32[]{:T(128)S(6)} %select_n.54), kind=kOutput, calls=%fused_computation.9 | convolution fusion | flops 201326592 | bytes 1572868 | tf_op jit(solution)/shard_map/dot_general | solution.py:26
  9.7 0.1 collective-permute-start.1
  9.9 0.6 %fusion.7 = f32[512,128]{1,0:T(8,128)S(1)} fusion(f32[512,128]{1,0:T(8,128)S(1)} %get-tuple-element.20, f32[1024,512]{1,0:T(8,128)S(1)} %bitcast.18, s32[]{:T(128)S(6)} %select_n.54), kind=kOutput, calls=%fused_computation.11 | convolution fusion | flops 201326592 | bytes 1572868 | tf_op jit(solution)/shard_map/dot_general | solution.py:26
  10.4 0.0 copy-done.3
  10.5 0.0 copy-start.4
  10.5 0.0 copy-start.6
  10.5 0.5 %collective-permute-start.3 = (f32[512,128]{1,0:T(8,128)S(1)}, f32[512,128]{1,0:T(8,128)S(1)}, u32[]{:S(2)}, u32[]{:S(2)}) collective-permute-start(f32[512,128]{1,0:T(8,128)S(1)} %fusion.7), channel_id=1, source_target_pairs={{0,1},{1,0},{2,3},{3,2},{4,5},{5,4},{6,7},{7,6},{8,9},{9,8},{10,11... | collective-permute-start | bytes 786440 | tf_op jit(solution)/shard_map/ppermute | solution.py:77
  11.0 0.6 %fusion.10 = f32[512,128]{1,0:T(8,128)S(1)} fusion(f32[512,128]{1,0:T(8,128)S(1)} %get-tuple-element.16, f32[1024,512]{1,0:T(8,128)S(1)} %bitcast.19, s32[]{:T(128)S(6)} %select_n.47), kind=kOutput, calls=%fused_computation.14 | convolution fusion | flops 201326592 | bytes 1572868 | tf_op jit(solution)/shard_map/dot_general | solution.py:26
  11.6 0.0 collective-permute-done.1
  11.6 2.6 %collective-permute-start.2 = (f32[512,128]{1,0:T(8,128)S(1)}, f32[512,128]{1,0:T(8,128)S(1)}, u32[]{:S(2)}, u32[]{:S(2)}) collective-permute-start(f32[512,128]{1,0:T(8,128)S(1)} %add.43), channel_id=1, source_target_pairs={{0,2},{2,0},{4,6},{6,4},{8,10},{10,8},{12,14},{14,12},{16,18},{18,... | collective-permute-start | bytes 786440 | tf_op jit(solution)/shard_map/ppermute | solution.py:22
  14.2 0.0 collective-permute-done.3
  14.2 0.6 %convolution_add_fusion = f32[512,128]{1,0:T(8,128)S(1)} fusion(f32[512,128]{1,0:T(8,128)S(1)} %collective-permute-done.3, f32[512,128]{1,0:T(8,128)S(1)} %get-tuple-element.20, f32[1024,512]{1,0:T(8,128)S(1)} %bitcast.20, s32[]{:T(128)S(6)} %select_n.47), kind=kOutput, calls=%fused_computation.3 | convolution fusion | flops 201392128 | bytes 1835012 | tf_op jit(solution)/shard_map/dot_general | solution.py:26
  14.8 6.3 %collective-permute-done.2 = f32[512,128]{1,0:T(8,128)S(1)} collective-permute-done((f32[512,128]{1,0:T(8,128)S(1)}, f32[512,128]{1,0:T(8,128)S(1)}, u32[]{:S(2)}, u32[]{:S(2)}) %collective-permute-start.2) | collective-permute-done | bytes 262176 | tf_op jit(solution)/shard_map/ppermute | solution.py:22
  21.2 0.0 copy-done.4
  21.2 0.0 copy-done.6
  21.2 0.6 %fusion.13 = f32[512,128]{1,0:T(8,128)S(1)} fusion(f32[512,1024]{1,0:T(8,128)S(1)} %copy-done.4, s32[]{:T(128)S(6)} %select_n.47, f32[512,128]{1,0:T(8,128)S(1)} %copy-done.6, f32[512,128]{1,0:T(8,128)S(1)} %convolution_add_fusion, f32[512,128]{1,0:T(8,128)S(1)} %collective-permute-done.2), kind=kOutput, calls=%fused_computation.17 | convolution fusion | flops 201457664 | bytes 2097156 | tf_op jit(solution)/shard_map/dot_general | solution.py:26
  21.8 0.1 collective-permute-start.4
  21.9 1.0 %fusion = f32[512,512]{1,0:T(8,128)S(1)} fusion(f32[512,1024]{1,0:T(8,128)S(1)} %copy-done.4, s32[]{:T(128)S(6)} %select_n.47, pred[]{:T(512)S(6)} %gt.4), kind=kOutput, calls=%fused_computation.4 | convolution fusion | flops 805568512 | bytes 3145733 | tf_op jit(solution)/shard_map/dot_general | solution.py:26
  22.9 0.5 %collective-permute-done.4 = f32[512,128]{1,0:T(8,128)S(1)} collective-permute-done((f32[512,128]{1,0:T(8,128)S(1)}, f32[512,128]{1,0:T(8,128)S(1)}, u32[]{:S(2)}, u32[]{:S(2)}) %collective-permute-start.4) | collective-permute-done | bytes 262176 | tf_op jit(solution)/shard_map/ppermute | solution.py:77
  23.4 1.3 %convolution_subtract_fusion.1 = f32[512,128]{1,0:T(8,128)} fusion(f32[512,128]{1,0:T(8,128)S(1)} %fusion.13, f32[512,512]{1,0:T(8,128)S(1)} %fusion, f32[512,128]{1,0:T(8,128)S(1)} %collective-permute-done.4), kind=kOutput, calls=%fused_computation.2 | convolution fusion | flops 201392128 | bytes 1835008 | tf_op jit(solution)/shard_map/dot_general | solution.py:26
  (4 shorter events, 0.1 us)
Async XLA Ops:
  0.6 2.8 %copy-start = (f32[1024,512]{1,0:T(8,128)S(1)}, f32[1024,512]{1,0:T(8,128)}, u32[]{:S(2)}) copy-start(f32[1024,512]{1,0:T(8,128)} %param.8) | copy-start | bytes 6291460
  0.6 2.6 %copy-start.7 = (s32[1,8]{1,0:T(1,128)S(1)}, s32[1,8]{1,0:T(1,128)}, u32[]{:S(2)}) copy-start(s32[1,8]{1,0:T(1,128)} %param.9) | copy-start | bytes 100
  2.8 2.7 %collective-permute-start = (f32[512,256]{1,0:T(8,128)S(1)}, f32[512,256]{1,0:T(8,128)}, u32[]{:S(2)}, u32[]{:S(2)}) collective-permute-start(f32[512,256]{1,0:T(8,128)S(1)} %fusion.17), channel_id=1, source_target_pairs={{0,1},{1,0},{2,3},{3,2},{4,5},{5,4},{6,7},{7,6},{8,9},{9,8},{10,11... | collective-permute-start | bytes 1572872 | tf_op jit(solution)/shard_map/ppermute | solution.py:77
  3.4 2.0 %copy-start.5 = (f32[512,256]{1,0:T(8,128)S(1)}, f32[512,256]{1,0:T(8,128)}, u32[]{:S(2)}) copy-start(f32[512,256]{1,0:T(8,128)} %param.7) | copy-start | bytes 1572868
  5.4 2.1 %copy-start.2 = (f32[512,1024]{1,0:T(8,128)S(1)}, f32[512,1024]{1,0:T(8,128)}, u32[]{:S(2)}) copy-start(f32[512,1024]{1,0:T(8,128)} %param.6) | copy-start | bytes 6291460
  7.6 1.6 %copy-start.1 = (f32[8,128,512]{2,1,0:T(8,128)S(1)}, f32[8,128,512]{2,1,0:T(8,128)}, u32[]{:S(2)}) copy-start(f32[8,128,512]{2,1,0:T(8,128)} %gather_fusion) | copy-start | bytes 6291460
  8.2 2.3 %copy-start.3 = (f32[512,256]{1,0:T(8,128)}, f32[512,256]{1,0:T(8,128)S(1)}, u32[]{:S(2)}) copy-start(f32[512,256]{1,0:T(8,128)S(1)} %fusion.15) | copy-start | bytes 1572868
  9.7 1.9 %collective-permute-start.1 = (f32[512,128]{1,0:T(8,128)S(1)}, f32[512,128]{1,0:T(8,128)S(1)}, u32[]{:S(2)}, u32[]{:S(2)}) collective-permute-start(f32[512,128]{1,0:T(8,128)S(1)} %fusion.5), channel_id=1, source_target_pairs={{0,1},{1,0},{2,3},{3,2},{4,5},{5,4},{6,7},{7,6},{8,9},{9,8},{10,11... | collective-permute-start | bytes 786440 | tf_op jit(solution)/shard_map/ppermute | solution.py:77
  10.5 10.7 %copy-start.4 = (f32[512,1024]{1,0:T(8,128)S(1)}, f32[512,1024]{1,0:T(8,128)}, u32[]{:S(2)}) copy-start(f32[512,1024]{1,0:T(8,128)} %param.10) | copy-start | bytes 6291460
  10.5 10.7 %copy-start.6 = (f32[512,128]{1,0:T(8,128)S(1)}, f32[512,128]{1,0:T(8,128)}, u32[]{:S(2)}) copy-start(f32[512,128]{1,0:T(8,128)} %param.11) | copy-start | bytes 786436
  10.5 3.8 %collective-permute-start.3 = (f32[512,128]{1,0:T(8,128)S(1)}, f32[512,128]{1,0:T(8,128)S(1)}, u32[]{:S(2)}, u32[]{:S(2)}) collective-permute-start(f32[512,128]{1,0:T(8,128)S(1)} %fusion.7), channel_id=1, source_target_pairs={{0,1},{1,0},{2,3},{3,2},{4,5},{5,4},{6,7},{7,6},{8,9},{9,8},{10,11... | collective-permute-start | bytes 786440 | tf_op jit(solution)/shard_map/ppermute | solution.py:77
  11.6 9.5 %collective-permute-start.2 = (f32[512,128]{1,0:T(8,128)S(1)}, f32[512,128]{1,0:T(8,128)S(1)}, u32[]{:S(2)}, u32[]{:S(2)}) collective-permute-start(f32[512,128]{1,0:T(8,128)S(1)} %add.43), channel_id=1, source_target_pairs={{0,2},{2,0},{4,6},{6,4},{8,10},{10,8},{12,14},{14,12},{16,18},{18,... | collective-permute-start | bytes 786440 | tf_op jit(solution)/shard_map/ppermute | solution.py:22
  21.8 1.6 %collective-permute-start.4 = (f32[512,128]{1,0:T(8,128)S(1)}, f32[512,128]{1,0:T(8,128)S(1)}, u32[]{:S(2)}, u32[]{:S(2)}) collective-permute-start(f32[512,128]{1,0:T(8,128)S(1)} %fusion.13), channel_id=1, source_target_pairs={{0,1},{1,0},{2,3},{3,2},{4,5},{5,4},{6,7},{7,6},{8,9},{9,8},{10,11... | collective-permute-start | bytes 786440 | tf_op jit(solution)/shard_map/ppermute | solution.py:77

commit v28 on v25

--- a/solution.py
+++ b/solution.py
@@ -106,7 +106,7 @@
     blocks = update_panel.reshape(-1, ROW_BLOCK, update_panel.shape[1])
     order = inverse_order(update_blocks)
 
-    placed_panel = jnp.take(blocks, order, axis=0, mode="clip").reshape(update_panel.shape)
+    placed_panel = blocks.at[order].get(mode="promise_in_bounds").reshape(update_panel.shape)
     placed_panel = two_section_leaf(leaf_factor, leaf_rhs, section, precision, placed_panel)
     leaf_solution, placed_panel = placed_panel
     rows_half = placed_panel.shape[0] // 2

time: 24.9 us -> 24.9 us (level)
  no operation moved by 1% of the time
where the time goes in v28:
time: 24.9 us; the launch traced here: 24.7 us
  matrix products  9.93 us (40%)
  waiting for transfers between devices  6.87 us (28%)
  starting transfers between devices  3.95 us (16%)
  local copies, waits for them, and re-layouts  3.02 us (12%)
  between operations  0.82 us (3%)
    dot_general x10, matrix products, matmul(): jnp.dot(left, right, precision=precision, preferred_element_type=jnp.floa...  9.93 us
    ppermute x1, waiting for transfers between devices, swapped(): return lax.ppermute(block, axis, route)  6.37 us
    ppermute x1, starting transfers between devices, swapped(): return lax.ppermute(block, axis, route)  2.72 us
    gather x1, local copies, waits for them, and re-layouts, two_section_shards(): blocks.at[order].get(mode='promise_in_bounds').reshape(update_panel.shape)  2.01 us
    ppermute x4, starting transfers between devices, pair_swap(): return lax.ppermute(block, axis, [(0, 1), (1, 0)])  1.23 us
    unnamed x16, local copies, waits for them, and re-layouts  0.96 us
    ppermute x4, waiting for transfers between devices, pair_swap(): return lax.ppermute(block, axis, [(0, 1), (1, 0)])  0.5 us
  transfers between devices with their start and end apart: 5, of which 2 were waited for; matrix products, arithmetic and copies ran while one was open for 20% of the time, Pallas kernels for 0%

profile of v28, /device:TPU:0, one launch (start us, length us, event | category | flops | bytes accessed | tf_op | source)
XLA Modules:
  0.0 24.7 jit_solution(8726621948794888649)
XLA Ops:
  0.6 0.0 copy-start
  0.6 0.0 copy-start.7
  0.7 2.1 %fusion.17 = f32[512,256]{1,0:T(8,128)S(1)} fusion(f32[512,256]{1,0:T(8,128)} %param.7, f32[512,1024]{1,0:T(8,128)} %param.6, s32[]{:T(128)S(6)} %select_n.51), kind=kOutput, calls=%fused_computation.21 | convolution fusion | flops 402653184 | bytes 2097156 | tf_op jit(solution)/shard_map/dot_general | solution.py:26
  2.8 0.5 %collective-permute-start = (f32[512,256]{1,0:T(8,128)S(1)}, f32[512,256]{1,0:T(8,128)}, u32[]{:S(2)}, u32[]{:S(2)}) collective-permute-start(f32[512,256]{1,0:T(8,128)S(1)} %fusion.17), channel_id=1, source_target_pairs={{0,1},{1,0},{2,3},{3,2},{4,5},{5,4},{6,7},{7,6},{8,9},{9,8},{10,11... | collective-permute-start | bytes 1572872 | tf_op jit(solution)/shard_map/ppermute | solution.py:77
  3.3 0.0 copy-done.7
  3.3 0.1 select_reduce_fusion
  3.4 0.0 copy-done
  3.4 0.0 copy-start.5
  3.4 2.0 %gather_fusion = f32[8,128,512]{2,1,0:T(8,128)} fusion(f32[8,128,512]{2,1,0:T(8,128)S(1)} %bitcast.19, s32[1024]{0:T(1024)S(1)} %pad_clamp_fusion), kind=kCustom, calls=%fused_computation | custom fusion | bytes 4194336 | tf_op jit(solution)/shard_map/gather | solution.py:109
  5.4 0.0 copy-start.2
  5.4 0.0 collective-permute-done
  5.4 0.0 copy-done.5
  5.4 2.0 %fusion = f32[512,256]{1,0:T(8,128)S(1)} fusion(f32[512,256]{1,0:T(8,128)S(1)} %copy-done.5, f32[512,1024]{1,0:T(8,128)} %param.6, f32[512,256]{1,0:T(8,128)} %collective-permute-done, pred[]{:T(512)S(6)} %gt.4), kind=kOutput, calls=%fused_computation.2 | convolution fusion | flops 402915328 | bytes 2621441 | tf_op jit(solution)/shard_map/dot_general | solution.py:26
  7.4 0.0 copy-done.2
  7.4 0.0 copy-start.1
  7.5 0.6 %fusion.15 = f32[512,256]{1,0:T(8,128)S(1)} fusion(f32[512,256]{1,0:T(8,128)S(1)} %fusion, f32[512,1024]{1,0:T(8,128)S(1)} %copy-done.2, s32[]{:T(128)S(6)} %select_n.51), kind=kOutput, calls=%fused_computation.19 | convolution fusion | flops 402653184 | bytes 2097156 | tf_op jit(solution)/shard_map/dot_general | solution.py:26
  8.1 0.0 copy-start.3
  8.1 0.9 %copy-done.1 = f32[8,128,512]{2,1,0:T(8,128)S(1)} copy-done((f32[8,128,512]{2,1,0:T(8,128)S(1)}, f32[8,128,512]{2,1,0:T(8,128)}, u32[]{:S(2)}) %copy-start.1) | copy-done | bytes 2097176
  9.0 0.6 %fusion.5 = f32[512,128]{1,0:T(8,128)S(1)} fusion(f32[512,128]{1,0:T(8,128)S(1)} %get-tuple-element.16, f32[1024,512]{1,0:T(8,128)S(1)} %bitcast.20, s32[]{:T(128)S(6)} %select_n.58), kind=kOutput, calls=%fused_computation.9 | convolution fusion | flops 201326592 | bytes 1572868 | tf_op jit(solution)/shard_map/dot_general | solution.py:26
  9.6 0.3 %collective-permute-start.1 = (f32[512,128]{1,0:T(8,128)S(1)}, f32[512,128]{1,0:T(8,128)S(1)}, u32[]{:S(2)}, u32[]{:S(2)}) collective-permute-start(f32[512,128]{1,0:T(8,128)S(1)} %fusion.5), channel_id=1, source_target_pairs={{0,1},{1,0},{2,3},{3,2},{4,5},{5,4},{6,7},{7,6},{8,9},{9,8},{10,11... | collective-permute-start | bytes 786440 | tf_op jit(solution)/shard_map/ppermute | solution.py:77
  9.9 0.6 %fusion.7 = f32[512,128]{1,0:T(8,128)S(1)} fusion(f32[512,128]{1,0:T(8,128)S(1)} %get-tuple-element.20, f32[1024,512]{1,0:T(8,128)S(1)} %bitcast.21, s32[]{:T(128)S(6)} %select_n.58), kind=kOutput, calls=%fused_computation.11 | convolution fusion | flops 201326592 | bytes 1572868 | tf_op jit(solution)/shard_map/dot_general | solution.py:26
  10.5 0.0 copy-done.3
  10.5 0.0 copy-start.4
  10.5 0.0 copy-start.6
  10.5 0.4 %collective-permute-start.3 = (f32[512,128]{1,0:T(8,128)S(1)}, f32[512,128]{1,0:T(8,128)S(1)}, u32[]{:S(2)}, u32[]{:S(2)}) collective-permute-start(f32[512,128]{1,0:T(8,128)S(1)} %fusion.7), channel_id=1, source_target_pairs={{0,1},{1,0},{2,3},{3,2},{4,5},{5,4},{6,7},{7,6},{8,9},{9,8},{10,11... | collective-permute-start | bytes 786440 | tf_op jit(solution)/shard_map/ppermute | solution.py:77
  10.9 0.6 %fusion.10 = f32[512,128]{1,0:T(8,128)S(1)} fusion(f32[512,128]{1,0:T(8,128)S(1)} %get-tuple-element.16, f32[1024,512]{1,0:T(8,128)S(1)} %bitcast.22, s32[]{:T(128)S(6)} %select_n.51), kind=kOutput, calls=%fused_computation.14 | convolution fusion | flops 201326592 | bytes 1572868 | tf_op jit(solution)/shard_map/dot_general | solution.py:26
  11.5 0.0 collective-permute-done.1
  11.5 2.7 %collective-permute-start.2 = (f32[512,128]{1,0:T(8,128)S(1)}, f32[512,128]{1,0:T(8,128)S(1)}, u32[]{:S(2)}, u32[]{:S(2)}) collective-permute-start(f32[512,128]{1,0:T(8,128)S(1)} %add.43), channel_id=1, source_target_pairs={{0,2},{2,0},{4,6},{6,4},{8,10},{10,8},{12,14},{14,12},{16,18},{18,... | collective-permute-start | bytes 786440 | tf_op jit(solution)/shard_map/ppermute | solution.py:22
  14.2 0.0 collective-permute-done.3
  14.2 0.6 %convolution_add_fusion = f32[512,128]{1,0:T(8,128)S(1)} fusion(f32[512,128]{1,0:T(8,128)S(1)} %collective-permute-done.3, f32[512,128]{1,0:T(8,128)S(1)} %get-tuple-element.20, f32[1024,512]{1,0:T(8,128)S(1)} %bitcast.23, s32[]{:T(128)S(6)} %select_n.51), kind=kOutput, calls=%fused_computation.4 | convolution fusion | flops 201392128 | bytes 1835012 | tf_op jit(solution)/shard_map/dot_general | solution.py:26
  14.8 6.4 %collective-permute-done.2 = f32[512,128]{1,0:T(8,128)S(1)} collective-permute-done((f32[512,128]{1,0:T(8,128)S(1)}, f32[512,128]{1,0:T(8,128)S(1)}, u32[]{:S(2)}, u32[]{:S(2)}) %collective-permute-start.2) | collective-permute-done | bytes 262176 | tf_op jit(solution)/shard_map/ppermute | solution.py:22
  21.2 0.0 copy-done.4
  21.2 0.0 copy-done.6
  21.2 0.6 %fusion.13 = f32[512,128]{1,0:T(8,128)S(1)} fusion(f32[512,1024]{1,0:T(8,128)S(1)} %copy-done.4, s32[]{:T(128)S(6)} %select_n.51, f32[512,128]{1,0:T(8,128)S(1)} %copy-done.6, f32[512,128]{1,0:T(8,128)S(1)} %convolution_add_fusion, f32[512,128]{1,0:T(8,128)S(1)} %collective-permute-done.2), kind=kOutput, calls=%fused_computation.17 | convolution fusion | flops 201457664 | bytes 2097156 | tf_op jit(solution)/shard_map/dot_general | solution.py:26
  21.8 0.1 collective-permute-start.4
  21.9 1.0 %fusion.1 = f32[512,512]{1,0:T(8,128)S(1)} fusion(f32[512,1024]{1,0:T(8,128)S(1)} %copy-done.4, s32[]{:T(128)S(6)} %select_n.51, pred[]{:T(512)S(6)} %gt.4), kind=kOutput, calls=%fused_computation.5 | convolution fusion | flops 805568512 | bytes 3145733 | tf_op jit(solution)/shard_map/dot_general | solution.py:26
  22.9 0.5 %collective-permute-done.4 = f32[512,128]{1,0:T(8,128)S(1)} collective-permute-done((f32[512,128]{1,0:T(8,128)S(1)}, f32[512,128]{1,0:T(8,128)S(1)}, u32[]{:S(2)}, u32[]{:S(2)}) %collective-permute-start.4) | collective-permute-done | bytes 262176 | tf_op jit(solution)/shard_map/ppermute | solution.py:77
  23.4 1.3 %convolution_subtract_fusion = f32[512,128]{1,0:T(8,128)} fusion(f32[512,128]{1,0:T(8,128)S(1)} %fusion.13, f32[512,512]{1,0:T(8,128)S(1)} %fusion.1, f32[512,128]{1,0:T(8,128)S(1)} %collective-permute-done.4), kind=kOutput, calls=%fused_computation.3 | convolution fusion | flops 201392128 | bytes 1835008 | tf_op jit(solution)/shard_map/dot_general | solution.py:26
  (4 shorter events, 0.1 us)
Async XLA Ops:
  0.6 2.8 %copy-start = (f32[1024,512]{1,0:T(8,128)S(1)}, f32[1024,512]{1,0:T(8,128)}, u32[]{:S(2)}) copy-start(f32[1024,512]{1,0:T(8,128)} %param.8) | copy-start | bytes 6291460
  0.6 2.6 %copy-start.7 = (s32[1,8]{1,0:T(1,128)S(1)}, s32[1,8]{1,0:T(1,128)}, u32[]{:S(2)}) copy-start(s32[1,8]{1,0:T(1,128)} %param.9) | copy-start | bytes 100
  2.8 2.7 %collective-permute-start = (f32[512,256]{1,0:T(8,128)S(1)}, f32[512,256]{1,0:T(8,128)}, u32[]{:S(2)}, u32[]{:S(2)}) collective-permute-start(f32[512,256]{1,0:T(8,128)S(1)} %fusion.17), channel_id=1, source_target_pairs={{0,1},{1,0},{2,3},{3,2},{4,5},{5,4},{6,7},{7,6},{8,9},{9,8},{10,11... | collective-permute-start | bytes 1572872 | tf_op jit(solution)/shard_map/ppermute | solution.py:77
  3.4 2.0 %copy-start.5 = (f32[512,256]{1,0:T(8,128)S(1)}, f32[512,256]{1,0:T(8,128)}, u32[]{:S(2)}) copy-start(f32[512,256]{1,0:T(8,128)} %param.7) | copy-start | bytes 1572868
  5.4 2.0 %copy-start.2 = (f32[512,1024]{1,0:T(8,128)S(1)}, f32[512,1024]{1,0:T(8,128)}, u32[]{:S(2)}) copy-start(f32[512,1024]{1,0:T(8,128)} %param.6) | copy-start | bytes 6291460
  7.4 1.6 %copy-start.1 = (f32[8,128,512]{2,1,0:T(8,128)S(1)}, f32[8,128,512]{2,1,0:T(8,128)}, u32[]{:S(2)}) copy-start(f32[8,128,512]{2,1,0:T(8,128)} %gather_fusion) | copy-start | bytes 6291460
  8.1 2.4 %copy-start.3 = (f32[512,256]{1,0:T(8,128)}, f32[512,256]{1,0:T(8,128)S(1)}, u32[]{:S(2)}) copy-start(f32[512,256]{1,0:T(8,128)S(1)} %fusion.15) | copy-start | bytes 1572868
  9.6 1.9 %collective-permute-start.1 = (f32[512,128]{1,0:T(8,128)S(1)}, f32[512,128]{1,0:T(8,128)S(1)}, u32[]{:S(2)}, u32[]{:S(2)}) collective-permute-start(f32[512,128]{1,0:T(8,128)S(1)} %fusion.5), channel_id=1, source_target_pairs={{0,1},{1,0},{2,3},{3,2},{4,5},{5,4},{6,7},{7,6},{8,9},{9,8},{10,11... | collective-permute-start | bytes 786440 | tf_op jit(solution)/shard_map/ppermute | solution.py:77
  10.5 10.7 %copy-start.4 = (f32[512,1024]{1,0:T(8,128)S(1)}, f32[512,1024]{1,0:T(8,128)}, u32[]{:S(2)}) copy-start(f32[512,1024]{1,0:T(8,128)} %param.10) | copy-start | bytes 6291460
  10.5 10.7 %copy-start.6 = (f32[512,128]{1,0:T(8,128)S(1)}, f32[512,128]{1,0:T(8,128)}, u32[]{:S(2)}) copy-start(f32[512,128]{1,0:T(8,128)} %param.11) | copy-start | bytes 786436
  10.5 3.7 %collective-permute-start.3 = (f32[512,128]{1,0:T(8,128)S(1)}, f32[512,128]{1,0:T(8,128)S(1)}, u32[]{:S(2)}, u32[]{:S(2)}) collective-permute-start(f32[512,128]{1,0:T(8,128)S(1)} %fusion.7), channel_id=1, source_target_pairs={{0,1},{1,0},{2,3},{3,2},{4,5},{5,4},{6,7},{7,6},{8,9},{9,8},{10,11... | collective-permute-start | bytes 786440 | tf_op jit(solution)/shard_map/ppermute | solution.py:77
  11.5 9.7 %collective-permute-start.2 = (f32[512,128]{1,0:T(8,128)S(1)}, f32[512,128]{1,0:T(8,128)S(1)}, u32[]{:S(2)}, u32[]{:S(2)}) collective-permute-start(f32[512,128]{1,0:T(8,128)S(1)} %add.43), channel_id=1, source_target_pairs={{0,2},{2,0},{4,6},{6,4},{8,10},{10,8},{12,14},{14,12},{16,18},{18,... | collective-permute-start | bytes 786440 | tf_op jit(solution)/shard_map/ppermute | solution.py:22
  21.8 1.6 %collective-permute-start.4 = (f32[512,128]{1,0:T(8,128)S(1)}, f32[512,128]{1,0:T(8,128)S(1)}, u32[]{:S(2)}, u32[]{:S(2)}) collective-permute-start(f32[512,128]{1,0:T(8,128)S(1)} %fusion.13), channel_id=1, source_target_pairs={{0,1},{1,0},{2,3},{3,2},{4,5},{5,4},{6,7},{7,6},{8,9},{9,8},{10,11... | collective-permute-start | bytes 786440 | tf_op jit(solution)/shard_map/ppermute | solution.py:77

commit v29 on v20

--- a/solution.py
+++ b/solution.py
@@ -128,13 +128,14 @@
     kept = matmul(panel_own, solution_kept, precision) + arrived_kept
     tile_rows = parent_rhs.shape[0]
     diagonal = lax.dynamic_slice_in_dim(parent_factor, section * tile_rows, tile_rows, 1)
-    coupling = lower_coupling(parent_factor, diagonal, section, precision)
+    coupling = matmul(diagonal, parent_factor[:, :tile_rows], precision)
     arrived = swapped(sent, "leaf", 0)
     arrived, kept = lax.optimization_barrier((arrived, kept))
     pending = parent_rhs - (kept + arrived)
     first = matmul(diagonal, pending, precision)
     arrived = pair_swap(first, "rows")
     arrived, coupling = lax.optimization_barrier((arrived, coupling))
+    arrived = jnp.where(section > 0, arrived, jnp.zeros_like(arrived))
     parent_solution = first - matmul(coupling, arrived, precision)
     return (leaf_solution, parent_solution)
 

time: 24.8 us -> 24.8 us (level)
  no operation moved by 1% of the time
where the time goes in v29:
time: 24.8 us; the launch traced here: 24.7 us
  matrix products  10 us (40%)
  waiting for transfers between devices  6.85 us (28%)
  starting transfers between devices  3.84 us (15%)
  local copies, waits for them, and re-layouts  3.02 us (12%)
  between operations  0.82 us (3%)
    dot_general x10, matrix products, matmul(): jnp.dot(left, right, precision=precision, preferred_element_type=jnp.floa...  10 us
    ppermute x1, waiting for transfers between devices, swapped(): return lax.ppermute(block, axis, route)  6.34 us
    ppermute x1, starting transfers between devices, swapped(): return lax.ppermute(block, axis, route)  2.61 us
    gather x1, local copies, waits for them, and re-layouts, two_section_shards(): jnp.take(blocks, order, axis=0, mode='clip').reshape(update_panel.shape)  2.01 us
    ppermute x4, starting transfers between devices, pair_swap(): return lax.ppermute(block, axis, [(0, 1), (1, 0)])  1.23 us
    unnamed x16, local copies, waits for them, and re-layouts  0.96 us
    ppermute x4, waiting for transfers between devices, pair_swap(): return lax.ppermute(block, axis, [(0, 1), (1, 0)])  0.51 us
  transfers between devices with their start and end apart: 5, of which 2 were waited for; matrix products, arithmetic and copies ran while one was open for 20% of the time, Pallas kernels for 0%

profile of v29, /device:TPU:0, one launch (start us, length us, event | category | flops | bytes accessed | tf_op | source)
XLA Modules:
  0.0 24.7 jit_solution(3680298840880905438)
XLA Ops:
  0.6 0.0 copy-start
  0.6 0.0 copy-start.7
  0.7 2.1 %fusion.16 = f32[512,256]{1,0:T(8,128)S(1)} fusion(f32[512,256]{1,0:T(8,128)} %param.7, f32[512,1024]{1,0:T(8,128)} %param.6, s32[]{:T(128)S(6)} %select_n.41), kind=kOutput, calls=%fused_computation.20 | convolution fusion | flops 402653184 | bytes 2097156 | tf_op jit(solution)/shard_map/dot_general | solution.py:26
  2.8 0.5 %collective-permute-start = (f32[512,256]{1,0:T(8,128)S(1)}, f32[512,256]{1,0:T(8,128)}, u32[]{:S(2)}, u32[]{:S(2)}) collective-permute-start(f32[512,256]{1,0:T(8,128)S(1)} %fusion.16), channel_id=1, source_target_pairs={{0,1},{1,0},{2,3},{3,2},{4,5},{5,4},{6,7},{7,6},{8,9},{9,8},{10,11... | collective-permute-start | bytes 1572872 | tf_op jit(solution)/shard_map/ppermute | solution.py:77
  3.3 0.0 copy-done.7
  3.3 0.1 select_reduce_fusion
  3.4 0.0 copy-done
  3.4 0.0 copy-start.5
  3.4 2.0 %gather_fusion = f32[8,128,512]{2,1,0:T(8,128)} fusion(f32[8,128,512]{2,1,0:T(8,128)S(1)} %bitcast.11, s32[1024]{0:T(1024)S(1)} %pad_clamp_fusion), kind=kCustom, calls=%fused_computation | custom fusion | bytes 4194336 | tf_op jit(solution)/shard_map/jit(_take)/gather | solution.py:109
  5.4 0.0 copy-start.2
  5.4 0.0 collective-permute-done
  5.4 0.0 copy-done.5
  5.4 2.1 %convolution_subtract_fusion = f32[512,256]{1,0:T(8,128)S(1)} fusion(f32[512,256]{1,0:T(8,128)S(1)} %copy-done.5, f32[512,256]{1,0:T(8,128)} %collective-permute-done, f32[512,1024]{1,0:T(8,128)} %param.6, pred[]{:T(512)S(6)} %gt.4), kind=kOutput, calls=%fused_computation.1 | convolution fusion | flops 403046400 | bytes 2621441 | tf_op jit(solution)/shard_map/dot_general | solution.py:26
  7.5 0.0 copy-done.2
  7.5 0.0 copy-start.1
  7.5 0.6 %fusion.14 = f32[512,256]{1,0:T(8,128)S(1)} fusion(f32[512,256]{1,0:T(8,128)S(1)} %convolution_subtract_fusion, f32[512,1024]{1,0:T(8,128)S(1)} %copy-done.2, s32[]{:T(128)S(6)} %select_n.41), kind=kOutput, calls=%fused_computation.18 | convolution fusion | flops 402653184 | bytes 2097156 | tf_op jit(solution)/shard_map/dot_general | solution.py:26
  8.1 0.0 copy-start.3
  8.2 0.9 %copy-done.1 = f32[8,128,512]{2,1,0:T(8,128)S(1)} copy-done((f32[8,128,512]{2,1,0:T(8,128)S(1)}, f32[8,128,512]{2,1,0:T(8,128)}, u32[]{:S(2)}) %copy-start.1) | copy-done | bytes 2097176
  9.1 0.6 %fusion.4 = f32[512,128]{1,0:T(8,128)S(1)} fusion(f32[512,128]{1,0:T(8,128)S(1)} %get-tuple-element.16, f32[1024,512]{1,0:T(8,128)S(1)} %bitcast.12, s32[]{:T(128)S(6)} %select_n.47), kind=kOutput, calls=%fused_computation.8 | convolution fusion | flops 201326592 | bytes 1572868 | tf_op jit(solution)/shard_map/dot_general | solution.py:26
  9.7 0.1 collective-permute-start.1
  9.8 0.6 %fusion.6 = f32[512,128]{1,0:T(8,128)S(1)} fusion(f32[512,128]{1,0:T(8,128)S(1)} %get-tuple-element.20, f32[1024,512]{1,0:T(8,128)S(1)} %bitcast.13, s32[]{:T(128)S(6)} %select_n.47), kind=kOutput, calls=%fused_computation.10 | convolution fusion | flops 201326592 | bytes 1572868 | tf_op jit(solution)/shard_map/dot_general | solution.py:26
  10.4 0.0 copy-done.3
  10.4 0.0 copy-start.4
  10.5 0.0 copy-start.6
  10.5 0.5 %collective-permute-start.3 = (f32[512,128]{1,0:T(8,128)S(1)}, f32[512,128]{1,0:T(8,128)S(1)}, u32[]{:S(2)}, u32[]{:S(2)}) collective-permute-start(f32[512,128]{1,0:T(8,128)S(1)} %fusion.6), channel_id=1, source_target_pairs={{0,1},{1,0},{2,3},{3,2},{4,5},{5,4},{6,7},{7,6},{8,9},{9,8},{10,11... | collective-permute-start | bytes 786440 | tf_op jit(solution)/shard_map/ppermute | solution.py:77
  11.0 0.6 %fusion.9 = f32[512,128]{1,0:T(8,128)S(1)} fusion(f32[512,128]{1,0:T(8,128)S(1)} %get-tuple-element.16, f32[1024,512]{1,0:T(8,128)S(1)} %bitcast.14, s32[]{:T(128)S(6)} %select_n.41), kind=kOutput, calls=%fused_computation.13 | convolution fusion | flops 201326592 | bytes 1572868 | tf_op jit(solution)/shard_map/dot_general | solution.py:26
  11.6 0.0 collective-permute-done.1
  11.6 2.6 %collective-permute-start.2 = (f32[512,128]{1,0:T(8,128)S(1)}, f32[512,128]{1,0:T(8,128)S(1)}, u32[]{:S(2)}, u32[]{:S(2)}) collective-permute-start(f32[512,128]{1,0:T(8,128)S(1)} %add.32), channel_id=1, source_target_pairs={{0,2},{2,0},{4,6},{6,4},{8,10},{10,8},{12,14},{14,12},{16,18},{18,... | collective-permute-start | bytes 786440 | tf_op jit(solution)/shard_map/ppermute | solution.py:22
  14.2 0.0 collective-permute-done.3
  14.2 0.6 %convolution_add_fusion = f32[512,128]{1,0:T(8,128)S(1)} fusion(f32[512,128]{1,0:T(8,128)S(1)} %collective-permute-done.3, f32[512,128]{1,0:T(8,128)S(1)} %get-tuple-element.20, f32[1024,512]{1,0:T(8,128)S(1)} %bitcast.15, s32[]{:T(128)S(6)} %select_n.41), kind=kOutput, calls=%fused_computation.3 | convolution fusion | flops 201392128 | bytes 1835012 | tf_op jit(solution)/shard_map/dot_general | solution.py:26
  14.8 6.3 %collective-permute-done.2 = f32[512,128]{1,0:T(8,128)S(1)} collective-permute-done((f32[512,128]{1,0:T(8,128)S(1)}, f32[512,128]{1,0:T(8,128)S(1)}, u32[]{:S(2)}, u32[]{:S(2)}) %collective-permute-start.2) | collective-permute-done | bytes 262176 | tf_op jit(solution)/shard_map/ppermute | solution.py:22
  21.2 0.0 copy-done.4
  21.2 0.0 copy-done.6
  21.2 0.6 %fusion.12 = f32[512,128]{1,0:T(8,128)S(1)} fusion(f32[512,1024]{1,0:T(8,128)S(1)} %copy-done.4, s32[]{:T(128)S(6)} %select_n.41, f32[512,128]{1,0:T(8,128)S(1)} %copy-done.6, f32[512,128]{1,0:T(8,128)S(1)} %convolution_add_fusion, f32[512,128]{1,0:T(8,128)S(1)} %collective-permute-done.2), kind=kOutput, calls=%fused_computation.16 | convolution fusion | flops 201457664 | bytes 2097156 | tf_op jit(solution)/shard_map/dot_general | solution.py:26
  21.8 0.1 collective-permute-start.4
  21.8 1.0 %fusion = f32[512,512]{1,0:T(8,128)S(1)} fusion(f32[512,1024]{1,0:T(8,128)S(1)} %copy-done.4, s32[]{:T(128)S(6)} %select_n.41), kind=kOutput, calls=%fused_computation.4 | convolution fusion | flops 805306368 | bytes 3145732 | tf_op jit(solution)/shard_map/dot_general | solution.py:26
  22.9 0.5 %collective-permute-done.4 = f32[512,128]{1,0:T(8,128)S(1)} collective-permute-done((f32[512,128]{1,0:T(8,128)S(1)}, f32[512,128]{1,0:T(8,128)S(1)}, u32[]{:S(2)}, u32[]{:S(2)}) %collective-permute-start.4) | collective-permute-done | bytes 262176 | tf_op jit(solution)/shard_map/ppermute | solution.py:77
  23.4 1.3 %convolution_subtract_fusion.1 = f32[512,128]{1,0:T(8,128)} fusion(f32[512,128]{1,0:T(8,128)S(1)} %fusion.12, f32[512,512]{1,0:T(8,128)S(1)} %fusion, f32[512,128]{1,0:T(8,128)S(1)} %collective-permute-done.4, pred[]{:T(512)S(6)} %gt.4), kind=kOutput, calls=%fused_computation.2 | convolution fusion | flops 201457664 | bytes 1835009 | tf_op jit(solution)/shard_map/dot_general | solution.py:26
  (3 shorter events, 0.1 us)
Async XLA Ops:
  0.6 2.8 %copy-start = (f32[1024,512]{1,0:T(8,128)S(1)}, f32[1024,512]{1,0:T(8,128)}, u32[]{:S(2)}) copy-start(f32[1024,512]{1,0:T(8,128)} %param.8) | copy-start | bytes 6291460
  0.6 2.6 %copy-start.7 = (s32[1,8]{1,0:T(1,128)S(1)}, s32[1,8]{1,0:T(1,128)}, u32[]{:S(2)}) copy-start(s32[1,8]{1,0:T(1,128)} %param.9) | copy-start | bytes 100
  2.8 2.6 %collective-permute-start = (f32[512,256]{1,0:T(8,128)S(1)}, f32[512,256]{1,0:T(8,128)}, u32[]{:S(2)}, u32[]{:S(2)}) collective-permute-start(f32[512,256]{1,0:T(8,128)S(1)} %fusion.16), channel_id=1, source_target_pairs={{0,1},{1,0},{2,3},{3,2},{4,5},{5,4},{6,7},{7,6},{8,9},{9,8},{10,11... | collective-permute-start | bytes 1572872 | tf_op jit(solution)/shard_map/ppermute | solution.py:77
  3.4 2.0 %copy-start.5 = (f32[512,256]{1,0:T(8,128)S(1)}, f32[512,256]{1,0:T(8,128)}, u32[]{:S(2)}) copy-start(f32[512,256]{1,0:T(8,128)} %param.7) | copy-start | bytes 1572868
  5.4 2.1 %copy-start.2 = (f32[512,1024]{1,0:T(8,128)S(1)}, f32[512,1024]{1,0:T(8,128)}, u32[]{:S(2)}) copy-start(f32[512,1024]{1,0:T(8,128)} %param.6) | copy-start | bytes 6291460
  7.5 1.6 %copy-start.1 = (f32[8,128,512]{2,1,0:T(8,128)S(1)}, f32[8,128,512]{2,1,0:T(8,128)}, u32[]{:S(2)}) copy-start(f32[8,128,512]{2,1,0:T(8,128)} %gather_fusion) | copy-start | bytes 6291460
  8.1 2.3 %copy-start.3 = (f32[512,256]{1,0:T(8,128)}, f32[512,256]{1,0:T(8,128)S(1)}, u32[]{:S(2)}) copy-start(f32[512,256]{1,0:T(8,128)S(1)} %fusion.14) | copy-start | bytes 1572868
  9.7 1.9 %collective-permute-start.1 = (f32[512,128]{1,0:T(8,128)S(1)}, f32[512,128]{1,0:T(8,128)S(1)}, u32[]{:S(2)}, u32[]{:S(2)}) collective-permute-start(f32[512,128]{1,0:T(8,128)S(1)} %fusion.4), channel_id=1, source_target_pairs={{0,1},{1,0},{2,3},{3,2},{4,5},{5,4},{6,7},{7,6},{8,9},{9,8},{10,11... | collective-permute-start | bytes 786440 | tf_op jit(solution)/shard_map/ppermute | solution.py:77
  10.4 10.7 %copy-start.4 = (f32[512,1024]{1,0:T(8,128)S(1)}, f32[512,1024]{1,0:T(8,128)}, u32[]{:S(2)}) copy-start(f32[512,1024]{1,0:T(8,128)} %param.10) | copy-start | bytes 6291460
  10.5 10.7 %copy-start.6 = (f32[512,128]{1,0:T(8,128)S(1)}, f32[512,128]{1,0:T(8,128)}, u32[]{:S(2)}) copy-start(f32[512,128]{1,0:T(8,128)} %param.11) | copy-start | bytes 786436
  10.5 3.8 %collective-permute-start.3 = (f32[512,128]{1,0:T(8,128)S(1)}, f32[512,128]{1,0:T(8,128)S(1)}, u32[]{:S(2)}, u32[]{:S(2)}) collective-permute-start(f32[512,128]{1,0:T(8,128)S(1)} %fusion.6), channel_id=1, source_target_pairs={{0,1},{1,0},{2,3},{3,2},{4,5},{5,4},{6,7},{7,6},{8,9},{9,8},{10,11... | collective-permute-start | bytes 786440 | tf_op jit(solution)/shard_map/ppermute | solution.py:77
  11.6 9.5 %collective-permute-start.2 = (f32[512,128]{1,0:T(8,128)S(1)}, f32[512,128]{1,0:T(8,128)S(1)}, u32[]{:S(2)}, u32[]{:S(2)}) collective-permute-start(f32[512,128]{1,0:T(8,128)S(1)} %add.32), channel_id=1, source_target_pairs={{0,2},{2,0},{4,6},{6,4},{8,10},{10,8},{12,14},{14,12},{16,18},{18,... | collective-permute-start | bytes 786440 | tf_op jit(solution)/shard_map/ppermute | solution.py:22
  21.8 1.6 %collective-permute-start.4 = (f32[512,128]{1,0:T(8,128)S(1)}, f32[512,128]{1,0:T(8,128)S(1)}, u32[]{:S(2)}, u32[]{:S(2)}) collective-permute-start(f32[512,128]{1,0:T(8,128)S(1)} %fusion.12), channel_id=1, source_target_pairs={{0,1},{1,0},{2,3},{3,2},{4,5},{5,4},{6,7},{7,6},{8,9},{9,8},{10,11... | collective-permute-start | bytes 786440 | tf_op jit(solution)/shard_map/ppermute | solution.py:77
